TPU v7x, 32 devices: a whole 2x2x4 slice. The times are simulated.
32 devices in a mesh: region: 2 (over y), tile: 4 (over z), corner: 2 (over x), kern: 2 (over core).
Axes of the slice: x: 2, y: 2, z: 4, core: 2. Of those that a mesh axis runs over, the one named last changes fastest.
Arguments:
- tile_mask: bfloat16 [16, 256, 256], P(('region', 'tile')), parts along dimension 0, may hold values from -1 to 1
- master_mask: bfloat16 [8, 256, 256], P(('region', 'tile')), parts along dimension 0, may hold values from -1 to 1
- target: bfloat16 [16, 256, 256], P(('region', 'tile')), parts along dimension 0, may hold values from 0 to 1
- inst_master: int32 [16], P(('region', 'tile')), parts along dimension 0, may hold values from 0 to 3, as said below
- inst_shift: int32 [16, 2], P(('region', 'tile')), parts along dimension 0, may hold values from 0 to 255
- kernels: float32 [2, 12, 2, 32, 32], P('corner'), may hold values from -24 to 24
- kernel_weight: float32 [2, 12], P('corner'), may hold values from 0.05 to 1
- corner_dose: float32 [2], P('corner'), may hold values from 0.6 to 1.6
Outputs:
- tile_grad: float32 [16, 256, 256], P(('region', 'tile')), parts along dimension 0
- master_grad: float32 [8, 256, 256], P(('region', 'tile')), parts along dimension 0
There are 2 independent parts, one for each index of `region`. A program takes and returns all parts, laid end to end along the dimension named above; an argument that names none is the same for every part. Nothing has to cross between parts.
Inputs may be any that keep to these rules, and one draw needn't show every extreme that they name: `inst_master`: each master cell is placed in exactly 2 tiles.
All inputs are finite; a program needn't handle non-finite values.
Results may differ from a plain program's by a relative error of at most 0.0003.
Values may be sent and summed in bfloat16 or wider, within the bound.
No kernel may reach another device: no remote copies, remote signals or barrier semaphores. Data moves between devices by JAX's collectives and lax.ppermute only.
A program may use at most 64 MiB of HBM per device.

v0:
```python
import math

import jax
import jax.numpy as jnp
from jax import lax
from jax.sharding import PartitionSpec as P

P_SIZE = 256
B = 32


precise = lax.Precision.HIGHEST
steepness = 3.0
threshold = 1.0


def band_tables():
    freq = jnp.arange(B, dtype=jnp.int32) - B // 2
    pixel = jnp.arange(P_SIZE, dtype=jnp.int32)
    angle = (
        2.0 * math.pi / P_SIZE * jnp.mod(freq[:, None] * pixel[None, :], P_SIZE).astype(jnp.float32)
    )
    return (jnp.cos(angle), -jnp.sin(angle))


def phase_ramp(shift):
    freq = jnp.arange(B, dtype=jnp.int32) - B // 2
    total = (
        freq[None, :, None] * shift[:, 0][:, None, None]
        + freq[None, None, :] * shift[:, 1][:, None, None]
    )
    angle = 2.0 * math.pi / P_SIZE * jnp.mod(total, P_SIZE).astype(jnp.float32)
    return (jnp.cos(angle), -jnp.sin(angle))


def spectra(masks, cos_tab, sin_tab):
    rows_re = jnp.einsum("bx,nxy->nby", cos_tab, masks, precision=precise)
    rows_im = jnp.einsum("bx,nxy->nby", sin_tab, masks, precision=precise)
    spec_re = jnp.einsum("nby,cy->nbc", rows_re, cos_tab, precision=precise) - jnp.einsum(
        "nby,cy->nbc", rows_im, sin_tab, precision=precise
    )
    spec_im = jnp.einsum("nby,cy->nbc", rows_re, sin_tab, precision=precise) + jnp.einsum(
        "nby,cy->nbc", rows_im, cos_tab, precision=precise
    )
    return (spec_re, spec_im)


def to_field(x_re, x_im, cos_tab, sin_tab, scale):
    half_re = jnp.einsum("bx,nbc->nxc", cos_tab, x_re, precision=precise) + jnp.einsum(
        "bx,nbc->nxc", sin_tab, x_im, precision=precise
    )
    half_im = jnp.einsum("bx,nbc->nxc", cos_tab, x_im, precision=precise) - jnp.einsum(
        "bx,nbc->nxc", sin_tab, x_re, precision=precise
    )
    out_re = (
        jnp.einsum("nxc,cy->nxy", half_re, cos_tab, precision=precise)
        + jnp.einsum("nxc,cy->nxy", half_im, sin_tab, precision=precise)
    ) * scale
    out_im = (
        jnp.einsum("nxc,cy->nxy", half_im, cos_tab, precision=precise)
        - jnp.einsum("nxc,cy->nxy", half_re, sin_tab, precision=precise)
    ) * scale
    return (out_re, out_im)


def back_pixels(x_re, x_im, cos_tab, sin_tab):
    half_re = jnp.einsum("bx,nbc->nxc", cos_tab, x_re, precision=precise) + jnp.einsum(
        "bx,nbc->nxc", sin_tab, x_im, precision=precise
    )
    half_im = jnp.einsum("bx,nbc->nxc", cos_tab, x_im, precision=precise) - jnp.einsum(
        "bx,nbc->nxc", sin_tab, x_re, precision=precise
    )
    return jnp.einsum("nxc,cy->nxy", half_re, cos_tab, precision=precise) + jnp.einsum(
        "nxc,cy->nxy", half_im, sin_tab, precision=precise
    )


def adjoint(g_re, g_im, cos_tab, sin_tab, scale):
    mid_re = jnp.einsum("bx,nxy->nby", cos_tab, g_re, precision=precise) - jnp.einsum(
        "bx,nxy->nby", sin_tab, g_im, precision=precise
    )
    mid_im = jnp.einsum("bx,nxy->nby", cos_tab, g_im, precision=precise) + jnp.einsum(
        "bx,nxy->nby", sin_tab, g_re, precision=precise
    )
    out_re = (
        jnp.einsum("nby,cy->nbc", mid_re, cos_tab, precision=precise)
        - jnp.einsum("nby,cy->nbc", mid_im, sin_tab, precision=precise)
    ) * scale
    out_im = (
        jnp.einsum("nby,cy->nbc", mid_re, sin_tab, precision=precise)
        + jnp.einsum("nby,cy->nbc", mid_im, cos_tab, precision=precise)
    ) * scale
    return (out_re, out_im)


def on_device(
    tile_mask, master_mask, target, inst_master, inst_shift, kernels, kernel_weight, corner_dose
):
    cos_tab, sin_tab = band_tables()
    scale = 1.0 / (P_SIZE * P_SIZE)
    local_tiles = tile_mask.shape[0]
    tile_re, tile_im = spectra(tile_mask.astype(jnp.float32), cos_tab, sin_tab)
    ph_re, ph_im = phase_ramp(inst_shift)

    def picker(count):
        index = jnp.arange(count, dtype=jnp.int32)
        return (inst_master[:, None] == index[None, :]).astype(jnp.float32)

    piece = lax.all_gather(master_mask, "tile", axis=0, tiled=True)
    chosen = picker(piece.shape[0])
    placed = jnp.einsum("tr,rxy->txy", chosen, piece.astype(jnp.float32), precision=precise)
    sel_re, sel_im = spectra(placed, cos_tab, sin_tab)
    spec_re = tile_re + (ph_re * sel_re - ph_im * sel_im)
    spec_im = tile_im + (ph_re * sel_im + ph_im * sel_re)
    goal = target.astype(jnp.float32)
    dose = corner_dose[0]
    kern_count = lax.axis_size("kern")
    kern_pos = lax.axis_index("kern")
    per_dev = kernels.shape[1] // kern_count
    first = kern_pos * per_dev
    mine_kern = lax.dynamic_slice_in_dim(kernels[0], first, per_dev, 0)
    kern_re = mine_kern[:, 0]
    kern_im = mine_kern[:, 1]
    weights = lax.dynamic_slice_in_dim(kernel_weight[0], first, per_dev, 0)

    def make_field(h_re, h_im):
        x_re = h_re * spec_re - h_im * spec_im
        x_im = h_re * spec_im + h_im * spec_re
        return to_field(x_re, x_im, cos_tab, sin_tab, scale)

    def forward(total, item):
        h_re, h_im, weight = item
        f_re, f_im = make_field(h_re, h_im)
        return (total + weight * (f_re * f_re + f_im * f_im), None)

    partial_light, unused = lax.scan(
        forward, jnp.zeros((local_tiles, P_SIZE, P_SIZE), jnp.float32), (kern_re, kern_im, weights)
    )
    intensity = lax.psum(partial_light, "kern")
    resist = jax.nn.sigmoid(steepness * (dose * intensity - threshold))
    sens = 2.0 * (resist - goal) * resist * (1.0 - resist) * steepness * dose

    def backward(acc, item):
        h_re, h_im, weight = item
        f_re, f_im = make_field(h_re, h_im)
        g_re = 2.0 * weight * sens * f_re
        g_im = 2.0 * weight * sens * f_im
        x_re, x_im = adjoint(g_re, g_im, cos_tab, sin_tab, scale)
        return ((acc[0] + h_re * x_re + h_im * x_im, acc[1] + h_re * x_im - h_im * x_re), None)

    zero = jnp.zeros((local_tiles, B, B), jnp.float32)
    grads, unused = lax.scan(backward, (zero, zero), (kern_re, kern_im, weights))
    partial_grad = jnp.stack([grads[0], grads[1]], axis=1)
    summed = lax.psum(partial_grad, ("corner", "kern"))
    tile_grad = back_pixels(summed[:, 0], summed[:, 1], cos_tab, sin_tab)
    back_re = ph_re * summed[:, 0] + ph_im * summed[:, 1]
    back_im = ph_re * summed[:, 1] - ph_im * summed[:, 0]
    masters_all = lax.axis_size("tile") * master_mask.shape[0]
    owner_pick = picker(masters_all)
    terms = jnp.stack(
        [
            jnp.einsum("tm,tbc->mbc", owner_pick, back_re, precision=precise),
            jnp.einsum("tm,tbc->mbc", owner_pick, back_im, precision=precise),
        ],
        axis=1,
    )
    mine = lax.psum_scatter(terms, "tile", scatter_dimension=0, tiled=True)
    master_grad = back_pixels(mine[:, 0], mine[:, 1], cos_tab, sin_tab)
    return (tile_grad, master_grad)


def solution(mesh):
    return jax.shard_map(
        on_device,
        mesh=mesh,
        in_specs=(
            P(("region", "tile"), None, None),
            P(("region", "tile"), None, None),
            P(("region", "tile"), None, None),
            P(("region", "tile")),
            P(("region", "tile"), None),
            P("corner", None, None, None, None),
            P("corner", None),
            P("corner"),
        ),
        out_specs=(P(("region", "tile"), None, None), P(("region", "tile"), None, None)),
        check_vma=False,
    )
```

profile of v0, /device:TPU:0, one launch (start us, length us, event | category | flops | bytes accessed | tf_op | source)
XLA Modules:
  0.0 199.7 jit_solution(11332372084410168777)
XLA Ops:
  7.2 17.7 %all_gather.3 = bf16[4,256,256]{2,1,0:T(8,128)(2,1)S(1)} all-gather(bf16[1,256,256]{2,1,0:T(8,128)(2,1)} %param.13), channel_id=1, replica_groups=mesh['region'=2,'tile'=4,'corner'=2,'kern'=2] {'tile'}, dimensions={0}, use_global_device_ids=true | all-gather | bytes 655360 | tf_op jit(solution)/shard_map/all_gather | solution.py:109
  32.3 37.9 %while.30 = (s32[]{:T(128)}, f32[2,256,256]{2,1,0:T(8,128)S(1)}, f32[6]{0:T(128)S(1)}, f32[6,32,32]{2,1,0:T(8,128)S(1)}, f32[2,32,32]{1,2,0:T(8,128)S(1)}, /*ind...) while((s32[]{:T(128)}, f32[2,256,256]{2,1,0:T(8,128)S(1)}, ...), condition=%wide.region_1.2_spmd.clone.clone.clone.clone, body=%wide.region_0.1_spmd.clone.clone.clone.clone.sunk | while | flops 228810752 | bytes 4981891 | solution.py:136
  37.0 1.6 fusion.466
  41.2 0.8 fusion.464
  43.3 1.6 fusion.466
  47.5 0.8 fusion.464
  49.7 1.6 fusion.466
  53.9 0.8 fusion.464
  56.0 1.6 fusion.466
  60.2 0.8 fusion.464
  62.3 1.6 fusion.466
  66.5 0.8 fusion.464
  68.6 1.6 fusion.466
  70.3 0.8 copy-done.1
  72.0 19.7 %all-reduce.2.cloned.1.call-done = f32[2,256,256]{2,1,0:T(8,128)} async-done(((f32[2,256,256]{2,1,0:T(8,128)}), f32[2,256,256]{2,1,0:T(8,128)}) %all-reduce.2.cloned.1.call-update) | async-done | bytes 524304 | tf_op jit(solution)/shard_map/psum | solution.py:139
  91.7 1.3 multiply_multiply_fusion
  93.0 61.6 %while.31 = (s32[]{:T(128)}, f32[2,32,32]{2,1,0:T(8,128)S(1)}, f32[2,32,32]{2,1,0:T(8,128)S(1)}, f32[6]{0:T(128)S(1)}, f32[2,256,256]{2,1,0:T(8,128)S(1)}, /*ind...) while((s32[]{:T(128)}, f32[2,32,32]{2,1,0:T(8,128)S(1)}, ...), condition=%wide.region_4.5_spmd.clone.clone.clone.clone, body=%wide.region_3.4_spmd.clone.clone.clone.clone.sunk | while | flops 456050688 | bytes 7833771 | solution.py:152
  96.8 0.8 fusion.502
  99.0 0.8 fusion.499
  107.1 0.8 fusion.502
  109.3 0.8 fusion.499
  119.5 0.8 fusion.499
  127.6 0.8 fusion.502
  129.8 0.8 fusion.499
  137.9 0.8 fusion.502
  140.1 0.8 fusion.499
  150.4 0.8 fusion.499
  154.7 12.2 %psum.15 = f32[2,2,32,32]{3,2,0,1:T(8,128)S(1)} all-reduce(f32[2,2,32,32]{3,2,0,1:T(8,128)S(1)} %pad_maximum_fusion.1), channel_id=1, replica_groups=mesh['region'=2,'tile'=4,'corner'=2,'kern'=2] {'corner','kern'}, use_global_device_ids=true, to_apply=%region_5.6 | all-reduce | flops 4096 | bytes 32768 | tf_op jit(solution)/shard_map/psum | solution.py:154
  170.9 1.6 convolution_add_fusion.6
  172.5 16.2 %reduce-scatter.2.cloned.1.call-done = f32[1,2,32,32]{3,2,1,0:T(8,128)} async-done(((f32[4,2,32,32]{3,2,1,0:T(8,128)}), f32[1,2,32,32]{3,2,1,0:T(8,128)}) %reduce-scatter.2.cloned.1.call-update) | async-done | bytes 8208 | tf_op jit(solution)/shard_map/reduce_scatter | solution.py:167
  188.7 1.1 fusion.250
  191.6 1.3 fusion.189
  (229 shorter events, 86.2 us)
Async XLA Ops:
  7.2 24.4 %copy-start = (f32[1,12,2,32,32]{4,3,2,1,0:T(8,128)S(1)}, f32[1,12,2,32,32]{4,3,2,1,0:T(8,128)}, u32[]{:S(2)}) copy-start(f32[1,12,2,32,32]{4,3,2,1,0:T(8,128)} %param.17) | copy-start | bytes 294916
  7.2 84.5 %all-reduce.2.cloned.1.call-start = ((), (), s32[]{:S(2)}) async-start(), calls=%async_computation.1 | async-start | bytes 1048576 | tf_op jit(solution)/shard_map/psum | solution.py:139
  7.2 17.7 %copy-start.4 = (s32[2]{0:T(128)S(1)}, s32[2]{0:T(128)}, u32[]{:S(2)}) copy-start(s32[2]{0:T(128)} %param.15) | copy-start | bytes 28
  26.7 1.0 copy-start.2
  29.7 0.7 copy-start.5
  31.6 0.7 copy-start.7
  70.3 0.8 copy-start.1
  70.3 21.4 %copy-start.3 = (bf16[2,256,256]{2,1,0:T(8,128)(2,1)S(1)}, bf16[2,256,256]{2,1,0:T(8,128)(2,1)}, u32[]{:S(2)}) copy-start(bf16[2,256,256]{2,1,0:T(8,128)(2,1)} %param.14) | copy-start | bytes 786436
  71.1 117.6 %reduce-scatter.2.cloned.1.call-start = ((), (), s32[]{:S(2)}) async-start(), calls=%async_computation.2 | async-start | bytes 163840 | tf_op jit(solution)/shard_map/reduce_scatter | solution.py:167
  188.7 1.2 copy-start.6
Sparse Core Ops, SparseCore 0:
  71.2 20.4 all-reduce.1
  169.5 19.2 reduce-scatter.1
where the time goes:
time: 200 us
  matrix products  99.7 us (50%)
  waiting for transfers between devices  36 us (18%)
  blocking collectives  29.9 us (15%)
  between operations  15 us (8%)
  local copies, waits for them, and re-layouts  11.7 us (6%)
  loops' own time  5.29 us (3%)
    psum x1, waiting for transfers between devices, on_device(): intensity = lax.psum(partial_light, 'kern')  19.7 us
    all_gather x1, blocking collectives, on_device(): piece = lax.all_gather(master_mask, 'tile', axis=0, tiled=True)  17.7 us
    reduce_scatter x1, waiting for transfers between devices, on_device(): mine = lax.psum_scatter(terms, 'tile', scatter_dimension=0, tiled=True)  16.2 us
    dot_general x12, matrix products, to_field(): jnp.einsum('nxc,cy->nxy', half_im, sin_tab, precision=precise)  14.3 us
    psum x1, blocking collectives, on_device(): summed = lax.psum(partial_grad, ('corner', 'kern'))  12.2 us
    dot_general x12, matrix products, to_field(): jnp.einsum('nxc,cy->nxy', half_re, sin_tab, precision=precise)  9.2 us
    dot_general x12, matrix products, to_field(): jnp.einsum('nxc,cy->nxy', half_im, cos_tab, precision=precise)  9.12 us
    dot_general x12, matrix products, to_field(): jnp.einsum('nxc,cy->nxy', half_re, cos_tab, precision=precise)  9.1 us
  transfers between devices with their start and end apart: 2, of which 2 were waited for; matrix products, arithmetic and copies ran while one was open for 2% of the time, Pallas kernels for 0%

commit v1 on v0

v1 whole, which is shorter than its diff:
```python
import math

import numpy as np
import jax
import jax.numpy as jnp
from jax import lax
from jax.sharding import PartitionSpec as P

P_SIZE = 256
B = 32


precise = lax.Precision.HIGHEST
steepness = 3.0
threshold = 1.0


def band_tables():
    freq = np.arange(B, dtype=np.int64) - B // 2
    pixel = np.arange(P_SIZE, dtype=np.int64)
    angle = (2.0 * math.pi / P_SIZE) * np.mod(freq[:, None] * pixel[None, :], P_SIZE).astype(np.float64)
    return (jnp.asarray(np.cos(angle), jnp.float32), jnp.asarray(-np.sin(angle), jnp.float32))


def phase_ramp(shift):
    freq = jnp.arange(B, dtype=jnp.int32) - B // 2
    total = (
        freq[None, :, None] * shift[:, 0][:, None, None]
        + freq[None, None, :] * shift[:, 1][:, None, None]
    )
    angle = 2.0 * math.pi / P_SIZE * jnp.mod(total, P_SIZE).astype(jnp.float32)
    return (jnp.cos(angle), -jnp.sin(angle))


def spectra(masks, cos_tab, sin_tab):
    rows_re = jnp.einsum("bx,nxy->nby", cos_tab, masks, precision=precise)
    rows_im = jnp.einsum("bx,nxy->nby", sin_tab, masks, precision=precise)
    spec_re = jnp.einsum("nby,cy->nbc", rows_re, cos_tab, precision=precise) - jnp.einsum(
        "nby,cy->nbc", rows_im, sin_tab, precision=precise
    )
    spec_im = jnp.einsum("nby,cy->nbc", rows_re, sin_tab, precision=precise) + jnp.einsum(
        "nby,cy->nbc", rows_im, cos_tab, precision=precise
    )
    return (spec_re, spec_im)


def back_pixels(x_re, x_im, cos_tab, sin_tab):
    half_re = jnp.einsum("bx,nbc->nxc", cos_tab, x_re, precision=precise) + jnp.einsum(
        "bx,nbc->nxc", sin_tab, x_im, precision=precise
    )
    half_im = jnp.einsum("bx,nbc->nxc", cos_tab, x_im, precision=precise) - jnp.einsum(
        "bx,nbc->nxc", sin_tab, x_re, precision=precise
    )
    return jnp.einsum("nxc,cy->nxy", half_re, cos_tab, precision=precise) + jnp.einsum(
        "nxc,cy->nxy", half_im, sin_tab, precision=precise
    )


def on_device(
    tile_mask, master_mask, target, inst_master, inst_shift, kernels, kernel_weight, corner_dose
):
    cos_tab, sin_tab = band_tables()
    scale = 1.0 / (P_SIZE * P_SIZE)
    local_tiles = tile_mask.shape[0]
    local_masters = master_mask.shape[0]
    tile_count = lax.axis_size("tile")
    tile_pos = lax.axis_index("tile")
    kern_count = lax.axis_size("kern")
    kern_pos = lax.axis_index("kern")
    per_dev = local_tiles // kern_count
    first = kern_pos * per_dev
    region_tiles = tile_count * local_tiles
    region_masters = tile_count * local_masters

    with jax.named_scope("master_spectra"):
        own_re, own_im = spectra(master_mask.astype(jnp.float32), cos_tab, sin_tab)
        own = jnp.stack([own_re, own_im], axis=1)
        every = lax.all_gather(own, "tile", axis=0, tiled=True)

    with jax.named_scope("tile_spectra"):
        mine_mask = lax.dynamic_slice_in_dim(tile_mask, first, per_dev, 0)
        goal = lax.dynamic_slice_in_dim(target, first, per_dev, 0).astype(jnp.float32)
        mine_master = lax.dynamic_slice_in_dim(inst_master, first, per_dev, 0)
        mine_shift = lax.dynamic_slice_in_dim(inst_shift, first, per_dev, 0)
        tile_re, tile_im = spectra(mine_mask.astype(jnp.float32), cos_tab, sin_tab)
        ph_re, ph_im = phase_ramp(mine_shift)
        pick = (mine_master[:, None] == jnp.arange(region_masters, dtype=jnp.int32)[None, :]).astype(
            jnp.float32
        )
        sel = jnp.sum(pick[:, :, None, None, None] * every[None], axis=1)
        sel_re = sel[:, 0]
        sel_im = sel[:, 1]
        spec_re = tile_re + (ph_re * sel_re - ph_im * sel_im)
        spec_im = tile_im + (ph_re * sel_im + ph_im * sel_re)

    dose = corner_dose[0]
    h_re = kernels[0, :, 0]
    h_im = kernels[0, :, 1]
    weights = kernel_weight[0]

    with jax.named_scope("forward_fields"):
        x_re = h_re[:, None] * spec_re[None] - h_im[:, None] * spec_im[None]
        x_im = h_re[:, None] * spec_im[None] + h_im[:, None] * spec_re[None]
        half_re = jnp.einsum("bx,knbc->knxc", cos_tab, x_re, precision=precise) + jnp.einsum(
            "bx,knbc->knxc", sin_tab, x_im, precision=precise
        )
        half_im = jnp.einsum("bx,knbc->knxc", cos_tab, x_im, precision=precise) - jnp.einsum(
            "bx,knbc->knxc", sin_tab, x_re, precision=precise
        )
        f_re = (
            jnp.einsum("knxc,cy->knxy", half_re, cos_tab, precision=precise)
            + jnp.einsum("knxc,cy->knxy", half_im, sin_tab, precision=precise)
        ) * scale
        f_im = (
            jnp.einsum("knxc,cy->knxy", half_im, cos_tab, precision=precise)
            - jnp.einsum("knxc,cy->knxy", half_re, sin_tab, precision=precise)
        ) * scale

    with jax.named_scope("resist_sensitivity"):
        intensity = jnp.sum(weights[:, None, None, None] * (f_re * f_re + f_im * f_im), axis=0)
        resist = jax.nn.sigmoid(steepness * (dose * intensity - threshold))
        sens = 2.0 * (resist - goal) * resist * (1.0 - resist) * steepness * dose

    with jax.named_scope("adjoint_spectra"):
        g_re = (2.0 * weights)[:, None, None, None] * sens[None] * f_re
        g_im = (2.0 * weights)[:, None, None, None] * sens[None] * f_im
        mid_re = jnp.einsum("knxy,cy->knxc", g_re, cos_tab, precision=precise) - jnp.einsum(
            "knxy,cy->knxc", g_im, sin_tab, precision=precise
        )
        mid_im = jnp.einsum("knxy,cy->knxc", g_re, sin_tab, precision=precise) + jnp.einsum(
            "knxy,cy->knxc", g_im, cos_tab, precision=precise
        )
        out_re = (
            jnp.einsum("bx,knxc->knbc", cos_tab, mid_re, precision=precise)
            - jnp.einsum("bx,knxc->knbc", sin_tab, mid_im, precision=precise)
        ) * scale
        out_im = (
            jnp.einsum("bx,knxc->knbc", cos_tab, mid_im, precision=precise)
            + jnp.einsum("bx,knxc->knbc", sin_tab, mid_re, precision=precise)
        ) * scale
        grad_re = jnp.sum(h_re[:, None] * out_re + h_im[:, None] * out_im, axis=0)
        grad_im = jnp.sum(h_re[:, None] * out_im - h_im[:, None] * out_re, axis=0)

    with jax.named_scope("gradient_exchange"):
        back_re = ph_re * grad_re + ph_im * grad_im
        back_im = ph_re * grad_im - ph_im * grad_re
        tile_slot = tile_pos * local_tiles + first + jnp.arange(per_dev, dtype=jnp.int32)
        tile_pick = (
            tile_slot[:, None] == jnp.arange(region_tiles, dtype=jnp.int32)[None, :]
        ).astype(jnp.float32)
        own_grad = jnp.stack([grad_re, grad_im], axis=1)
        own_back = jnp.stack([back_re, back_im], axis=1)
        tile_part = jnp.sum(tile_pick[:, :, None, None, None] * own_grad[:, None], axis=0)
        master_part = jnp.sum(pick[:, :, None, None, None] * own_back[:, None], axis=0)
        slots = jnp.concatenate([tile_part, master_part], axis=0)
        summed = lax.psum(slots, ("tile", "corner", "kern"))
        mine_tiles = lax.dynamic_slice_in_dim(summed, tile_pos * local_tiles, local_tiles, 0)
        mine_masters = lax.dynamic_slice_in_dim(
            summed, region_tiles + tile_pos * local_masters, local_masters, 0
        )

    with jax.named_scope("pixel_gradients"):
        tile_grad = back_pixels(mine_tiles[:, 0], mine_tiles[:, 1], cos_tab, sin_tab)
        master_grad = back_pixels(mine_masters[:, 0], mine_masters[:, 1], cos_tab, sin_tab)
    return (tile_grad, master_grad)


def solution(mesh):
    return jax.shard_map(
        on_device,
        mesh=mesh,
        in_specs=(
            P(("region", "tile"), None, None),
            P(("region", "tile"), None, None),
            P(("region", "tile"), None, None),
            P(("region", "tile")),
            P(("region", "tile"), None),
            P("corner", None, None, None, None),
            P("corner", None),
            P("corner"),
        ),
        out_specs=(P(("region", "tile"), None, None), P(("region", "tile"), None, None)),
        check_vma=False,
    )
```

time: 200 us -> 187 us (0.935)
  waiting for transfers between devices: 36 us -> 91.9 us
  matrix products: 99.7 us -> 55.3 us
  blocking collectives: 29.9 us -> 15.1 us
  local copies, waits for them, and re-layouts: 11.7 us -> 4.24 us
  loops' own time: 5.29 us -> 0 us
    psum x1, waiting for transfers between devices: 19.7 us -> 91.9 us  [on_device(): summed = lax.psum(slots, ('tile', 'corner', 'kern'))]
    dot_general x147 -> x16, matrix products: 86.5 us -> 32.3 us  [the longest x1 5.58 us: on_device(): jnp.einsum('knxc,cy->knxy', half_re, sin_tab, precision=precise)]
    reduce_scatter x1 -> x0, waiting for transfers between devices: 16.2 us -> none  [on_device(): mine = lax.psum_scatter(terms, 'tile', scatter_dimension=0, tiled=True)]
    psum x1 -> x0, blocking collectives: 12.2 us -> none  [on_device(): summed = lax.psum(partial_grad, ('corner', 'kern'))]
    dynamic_slice x32 -> x2, local copies, waits for them, and re-layouts: 8.06 us -> 2.01 us  [the longest x1 1.32 us: on_device(): mine_master = lax.dynamic_slice_in_dim(inst_master, first, per_dev, 0)]
    another operation x2 -> x0, loops' own time: 5.29 us -> none  [the longest x1 4.8 us: on_device(): lax.scan(backward, (zero, zero), (kern_re, kern_im, weights))]
    all_gather x1, blocking collectives: 17.7 us -> 15.1 us  [on_device(): every = lax.all_gather(own, 'tile', axis=0, tiled=True)]
  transfers between devices with their start and end apart: 2 -> 1, of which waited for: 2 -> 1; matrix products, arithmetic and copies ran while one was open for 2% -> 0% of each run, Pallas kernels for 0% -> 0%
where the time goes in v1:
time: 187 us; the launch traced here: 185 us
  waiting for transfers between devices  91.9 us (49%)
  matrix products  55.3 us (30%)
  between operations  15.2 us (8%)
  blocking collectives  15.1 us (8%)
  local copies, waits for them, and re-layouts  4.24 us (2%)
  other arithmetic  3.34 us (2%)
    psum x1, waiting for transfers between devices, on_device(): summed = lax.psum(slots, ('tile', 'corner', 'kern'))  91.9 us
    all_gather x1, blocking collectives, on_device(): every = lax.all_gather(own, 'tile', axis=0, tiled=True)  15.1 us
    dot_general x1, matrix products, on_device(): jnp.einsum('knxc,cy->knxy', half_re, sin_tab, precision=precise)  5.58 us
    dot_general x1, matrix products, on_device(): jnp.einsum('knxc,cy->knxy', half_im, cos_tab, precision=precise)  4.34 us
  transfers between devices with their start and end apart: 1, of which 1 were waited for; matrix products, arithmetic and copies ran while one was open for 0% of the time, Pallas kernels for 0%

profile of v1, /device:TPU:0, one launch (start us, length us, event | category | flops | bytes accessed | tf_op | source)
XLA Modules:
  0.0 185.2 jit_solution(1260496238623281663)
XLA Ops:
  7.3 1.1 fusion.41
  8.4 1.1 fusion.39
  10.5 0.9 fusion.80
  11.4 1.0 convolution_bitcast_fusion.1
  12.4 1.0 convolution_bitcast_fusion
  16.5 1.3 dynamic_slice.20
  18.5 0.9 fusion.26
  19.4 0.9 fusion.27
  20.4 15.1 %all_gather.3 = f32[4,2,32,32]{3,2,1,0:T(8,128)S(1)} all-gather(f32[1,2,32,32]{3,2,1,0:T(8,128)S(1)} %pad_maximum_fusion.1), channel_id=1, replica_groups=mesh['region'=2,'tile'=4,'corner'=2,'kern'=2] {'tile'}, dimensions={0}, use_global_device_ids=true | all-gather | bytes 40960 | tf_op jit(solution)/shard_map/master_spectra/all_gather | solution.py:78
  35.4 1.3 fusion.75
  36.8 0.9 fusion.28
  37.8 0.9 fusion.25
  38.8 1.1 fusion.77
  42.0 2.7 %fusion.83 = f32[12,256,256]{2,1,0:T(8,128)S(1)} fusion(f32[12,256,32]{1,2,0:T(8,128)S(1)} %fusion.15, f32[32,256,1]{1,0,2:T(8,128)S(1)} %copy-done.6), kind=kOutput, calls=%fused_computation.143 | convolution fusion | flops 301989888 | bytes 3571712 | tf_op jit(solution)/shard_map/forward_fields/knxc,cy->knxy/dot_general | solution.py:111
  44.8 4.3 %fusion.84 = f32[12,256,256]{2,1,0:T(8,128)} fusion(f32[12,256,32]{1,2,0:T(8,128)S(1)} %fusion.14, f32[32,256,1]{1,0,2:T(8,128)S(1)} %copy-done.6), kind=kOutput, calls=%fused_computation.144 | convolution fusion | flops 301989888 | bytes 3571712 | tf_op jit(solution)/shard_map/forward_fields/knxc,cy->knxy/dot_general | solution.py:115
  49.1 2.7 %add_multiply_fusion = f32[12,256,256]{2,1,0:T(8,128)S(1)} fusion(f32[12,256,256]{2,1,0:T(8,128)S(1)} %fusion.83, f32[12,256,32]{1,2,0:T(8,128)S(1)} %fusion.14, f32[32,256,1]{1,0,2:T(8,128)S(1)} %copy-done.5), kind=kOutput, calls=%fused_computation.4 | convolution fusion | flops 303562752 | bytes 6717440 | tf_op jit(solution)/shard_map/forward_fields/knxc,cy->knxy/dot_general | solution.py:112
  52.5 5.6 %multiply_reduce_fusion = (f32[256,256]{1,0:T(8,128)S(1)}, f32[12,256,256]{2,1,0:T(8,128)S(1)}) fusion(f32[12,256,256]{2,1,0:T(8,128)S(1)} %add_multiply_fusion, f32[12]{0:T(128)S(1)} %bitcast.235, f32[12,256,256]{2,1,0:T(8,128)} %fusion.84, f32[12,256,32]{1,2,0:T(8,128)} %copy-done.7, f32[32,256,1]{1,0,2:T(8,128)S(1)} %copy-done.5), kind=kOutput, calls=%fused_computation.2 | convolution fusion | flops 307429376 | bytes 10125360 | tf_op jit(solution)/shard_map/forward_fields/knxc,cy->knxy/dot_general | solution.py:116
  58.3 3.3 %fusion = f32[12,256,32]{1,2,0:T(8,128)S(1)} fusion(f32[32,256,1]{1,0,2:T(8,128)S(1)} %copy-done.5, f32[12,256,256]{2,1,0:T(8,128)S(1)} %add_multiply_fusion, f32[256,256]{1,0:T(8,128)S(1)} %fusion.32, f32[12]{0:T(128)S(1)} %broadcast_multiply_fusion.2), kind=kOutput, calls=%fused_computation.5 | convolution fusion | flops 303562752 | bytes 3833904 | tf_op jit(solution)/shard_map/adjoint_spectra/knxy,cy->knxc/dot_general | solution.py:130
  61.6 3.3 %fusion.1 = f32[12,256,32]{1,2,0:T(8,128)S(1)} fusion(f32[32,256,1]{1,0,2:T(8,128)S(1)} %copy-done.6, f32[12,256,256]{2,1,0:T(8,128)S(1)} %add_multiply_fusion, f32[256,256]{1,0:T(8,128)S(1)} %fusion.32, f32[12]{0:T(128)S(1)} %broadcast_multiply_fusion.2), kind=kOutput, calls=%fused_computation.6 | convolution fusion | flops 303562752 | bytes 3833904 | tf_op jit(solution)/shard_map/adjoint_spectra/knxy,cy->knxc/dot_general | solution.py:127
  64.8 3.3 %fusion.13 = f32[12,256,32]{1,2,0:T(8,128)S(1)} fusion(f32[12,256,32]{1,2,0:T(8,128)S(1)} %fusion, f32[32,256,1]{1,0,2:T(8,128)S(1)} %copy-done.6, f32[12,256,256]{2,1,0:T(8,128)S(1)} %get-tuple-element.11, f32[256,256]{1,0:T(8,128)S(1)} %fusion.32, f32[12]{0:T(128)S(1)} %broadcast_multiply_fusion.2), kind=kOutput, calls=%fused_computation.19 | convolution fusion | flops 303661056 | bytes 4227120 | tf_op jit(solution)/shard_map/adjoint_spectra/knxy,cy->knxc/dot_general | solution.py:130
  68.2 3.5 %fusion.12 = f32[12,256,32]{1,2,0:T(8,128)S(1)} fusion(f32[12,256,32]{1,2,0:T(8,128)S(1)} %fusion.1, f32[32,256,1]{1,0,2:T(8,128)S(1)} %copy-done.5, f32[12,256,256]{2,1,0:T(8,128)S(1)} %get-tuple-element.11, f32[256,256]{1,0:T(8,128)S(1)} %fusion.32, f32[12]{0:T(128)S(1)} %broadcast_multiply_fusion.2), kind=kOutput, calls=%fused_computation.18 | convolution fusion | flops 303661056 | bytes 4227120 | tf_op jit(solution)/shard_map/adjoint_spectra/knxy,cy->knxc/dot_general | solution.py:127
  74.9 91.9 %all-reduce.2.cloned.1.call-done = f32[12,2,32,32]{3,2,1,0:T(8,128)} async-done(((f32[12,2,32,32]{3,2,1,0:T(8,128)}), f32[12,2,32,32]{3,2,1,0:T(8,128)}) %all-reduce.2.cloned.1.call-update) | async-done | bytes 98320 | tf_op jit(solution)/shard_map/gradient_exchange/psum | solution.py:156
  166.8 0.9 fusion.61
  167.8 0.9 fusion.24
  169.2 1.0 fusion.53
  170.2 1.0 fusion.22
  171.8 0.9 fusion.62
  172.8 0.9 fusion.23
  173.7 1.1 fusion.16
  174.9 1.0 fusion.54
  175.9 1.0 fusion.21
  176.9 1.4 convolution_add_fusion
  (59 shorter events, 11.4 us)
Async XLA Ops:
  7.2 4.2 %copy-start = (bf16[2,256,256]{2,1,0:T(8,128)(2,1)S(1)}, bf16[2,256,256]{2,1,0:T(8,128)(2,1)}, u32[]{:S(2)}) copy-start(bf16[2,256,256]{2,1,0:T(8,128)(2,1)} %param.10) | copy-start | bytes 786436
  7.2 33.0 %copy-start.6 = (f32[32,256,1]{1,0,2:T(8,128)S(1)}, f32[32,256,1]{1,0,2:T(8,128)}, u32[]{:S(2)}) copy-start(f32[32,256,1]{1,0,2:T(8,128)} %constant.68) | copy-start | bytes 98308
  7.2 33.9 %copy-start.5 = (f32[32,256,1]{1,0,2:T(8,128)S(1)}, f32[32,256,1]{1,0,2:T(8,128)}, u32[]{:S(2)}) copy-start(f32[32,256,1]{1,0,2:T(8,128)} %constant.69) | copy-start | bytes 98308
  7.2 159.6 %all-reduce.2.cloned.1.call-start = ((), (), s32[]{:S(2)}) async-start(), calls=%async_computation | async-start | bytes 786432 | tf_op jit(solution)/shard_map/gradient_exchange/psum | solution.py:156
  40.0 4.8 %copy-start.1 = (f32[1,12,1,32,32]{3,4,1,2,0:T(8,128)}, f32[1,12,1,32,32]{3,4,1,2,0:T(8,128)S(1)}, u32[]{:S(2)}) copy-start(f32[1,12,1,32,32]{3,4,1,2,0:T(8,128)S(1)} %copy.22) | copy-start | bytes 147460
  40.1 4.6 %copy-start.3 = (f32[1,12,1,32,32]{3,4,1,2,0:T(8,128)}, f32[1,12,1,32,32]{3,4,1,2,0:T(8,128)S(1)}, u32[]{:S(2)}) copy-start(f32[1,12,1,32,32]{3,4,1,2,0:T(8,128)S(1)} %copy.23) | copy-start | bytes 147460
  42.0 2.8 %copy-start.7 = (f32[12,256,32]{1,2,0:T(8,128)}, f32[12,256,32]{1,2,0:T(8,128)S(1)}, u32[]{:S(2)}) copy-start(f32[12,256,32]{1,2,0:T(8,128)S(1)} %fusion.15) | copy-start | bytes 1179652
  49.1 3.4 %copy-start.11 = (f32[1,12]{1,0:T(1,128)S(1)}, f32[1,12]{1,0:T(1,128)}, u32[]{:S(2)}) copy-start(f32[1,12]{1,0:T(1,128)} %param.16) | copy-start | bytes 148
  52.5 5.6 %copy-start.10 = (bf16[2,256,256]{2,1,0:T(8,128)(2,1)S(1)}, bf16[2,256,256]{2,1,0:T(8,128)(2,1)}, u32[]{:S(2)}) copy-start(bf16[2,256,256]{2,1,0:T(8,128)(2,1)} %param.12) | copy-start | bytes 786436
  68.1 4.9 %copy-start.2 = (f32[1,12,1,32,32]{3,4,1,2,0:T(8,128)S(1)}, f32[1,12,1,32,32]{3,4,1,2,0:T(8,128)}, u32[]{:S(2)}) copy-start(f32[1,12,1,32,32]{3,4,1,2,0:T(8,128)} %copy-done.1) | copy-start | bytes 147460
  68.1 4.9 %copy-start.4 = (f32[1,12,1,32,32]{3,4,1,2,0:T(8,128)S(1)}, f32[1,12,1,32,32]{3,4,1,2,0:T(8,128)}, u32[]{:S(2)}) copy-start(f32[1,12,1,32,32]{3,4,1,2,0:T(8,128)} %copy-done.3) | copy-start | bytes 147460
  71.6 95.2 %copy-start.9 = (f32[32,256]{1,0:T(8,128)S(1)}, f32[32,256]{1,0:T(8,128)}, u32[]{:S(2)}) copy-start(f32[32,256]{1,0:T(8,128)} %constant.58.clone) | copy-start | bytes 98308
  71.7 96.1 %copy-start.8 = (f32[32,256]{1,0:T(8,128)S(1)}, f32[32,256]{1,0:T(8,128)}, u32[]{:S(2)}) copy-start(f32[32,256]{1,0:T(8,128)} %constant.59.clone) | copy-start | bytes 98308
Sparse Core Ops, SparseCore 0:
  75.0 91.7 all-reduce.1

commit v2 on v1

--- a/solution.py
+++ b/solution.py
@@ -54,6 +54,43 @@
     return jnp.einsum("nxc,cy->nxy", half_re, cos_tab, precision=precise) + jnp.einsum(
         "nxc,cy->nxy", half_im, sin_tab, precision=precise
     )
+
+
+def xor_partners(count):
+    return count & (count - 1) == 0 and count <= 8
+
+
+def gather_all(x, axis, count, pos):
+    if not xor_partners(count):
+        return lax.all_gather(x, axis, axis=0, tiled=True)
+    size = x.shape[0]
+    slot = jnp.arange(count * size, dtype=jnp.int32) // size
+    total = jnp.where((slot == pos)[:, None, None, None], jnp.tile(x, (count, 1, 1, 1)), 0.0)
+    for step in range(1, count):
+        got = lax.ppermute(x, axis, [(i, i ^ step) for i in range(count)])
+        hit = (slot == (pos ^ step))[:, None, None, None]
+        total = total + jnp.where(hit, jnp.tile(got, (count, 1, 1, 1)), 0.0)
+    return total
+
+
+def sum_all(x, axis, count, pos):
+    if not xor_partners(count):
+        return lax.psum(x, axis)
+    step = 1
+    while step < count:
+        x = x + lax.ppermute(x, axis, [(i, i ^ step) for i in range(count)])
+        step *= 2
+    return x
+
+
+def scatter_sum(x, axis, count, pos, size):
+    if not xor_partners(count):
+        return lax.psum_scatter(x, axis, scatter_dimension=0, tiled=True)
+    total = lax.dynamic_slice_in_dim(x, pos * size, size, 0)
+    for step in range(1, count):
+        part = lax.dynamic_slice_in_dim(x, (pos ^ step) * size, size, 0)
+        total = total + lax.ppermute(part, axis, [(i, i ^ step) for i in range(count)])
+    return total
 
 
 def on_device(
@@ -75,7 +112,7 @@
     with jax.named_scope("master_spectra"):
         own_re, own_im = spectra(master_mask.astype(jnp.float32), cos_tab, sin_tab)
         own = jnp.stack([own_re, own_im], axis=1)
-        every = lax.all_gather(own, "tile", axis=0, tiled=True)
+        every = gather_all(own, "tile", tile_count, tile_pos)
 
     with jax.named_scope("tile_spectra"):
         mine_mask = lax.dynamic_slice_in_dim(tile_mask, first, per_dev, 0)
@@ -142,22 +179,19 @@
         grad_im = jnp.sum(h_re[:, None] * out_im - h_im[:, None] * out_re, axis=0)
 
     with jax.named_scope("gradient_exchange"):
-        back_re = ph_re * grad_re + ph_im * grad_im
-        back_im = ph_re * grad_im - ph_im * grad_re
-        tile_slot = tile_pos * local_tiles + first + jnp.arange(per_dev, dtype=jnp.int32)
-        tile_pick = (
-            tile_slot[:, None] == jnp.arange(region_tiles, dtype=jnp.int32)[None, :]
+        own_grad = jnp.stack([grad_re, grad_im], axis=1)
+        both = gather_all(own_grad, "kern", kern_count, kern_pos)
+        corner_count = lax.axis_size("corner")
+        mine_tiles = sum_all(both, "corner", corner_count, lax.axis_index("corner"))
+        all_re, all_im = phase_ramp(inst_shift)
+        back_re = all_re * mine_tiles[:, 0] + all_im * mine_tiles[:, 1]
+        back_im = all_re * mine_tiles[:, 1] - all_im * mine_tiles[:, 0]
+        own_back = jnp.stack([back_re, back_im], axis=1)
+        owner_pick = (
+            inst_master[:, None] == jnp.arange(region_masters, dtype=jnp.int32)[None, :]
         ).astype(jnp.float32)
-        own_grad = jnp.stack([grad_re, grad_im], axis=1)
-        own_back = jnp.stack([back_re, back_im], axis=1)
-        tile_part = jnp.sum(tile_pick[:, :, None, None, None] * own_grad[:, None], axis=0)
-        master_part = jnp.sum(pick[:, :, None, None, None] * own_back[:, None], axis=0)
-        slots = jnp.concatenate([tile_part, master_part], axis=0)
-        summed = lax.psum(slots, ("tile", "corner", "kern"))
-        mine_tiles = lax.dynamic_slice_in_dim(summed, tile_pos * local_tiles, local_tiles, 0)
-        mine_masters = lax.dynamic_slice_in_dim(
-            summed, region_tiles + tile_pos * local_masters, local_masters, 0
-        )
+        terms = jnp.sum(owner_pick[:, :, None, None, None] * own_back[:, None], axis=0)
+        mine_masters = scatter_sum(terms, "tile", tile_count, tile_pos, local_masters)
 
     with jax.named_scope("pixel_gradients"):
         tile_grad = back_pixels(mine_tiles[:, 0], mine_tiles[:, 1], cos_tab, sin_tab)

time: 187 us -> 74.4 us (0.40)
  waiting for transfers between devices: 91.9 us -> 6.93 us
  blocking collectives: 15.1 us -> 0 us
  between operations: 15.2 us -> 1.84 us
  starting transfers between devices: 0.04 us -> 12 us
  matrix products: 55.3 us -> 44.2 us
    psum x1 -> x0, waiting for transfers between devices: 91.9 us -> none  [on_device(): summed = lax.psum(slots, ('tile', 'corner', 'kern'))]
    all_gather x1 -> x0, blocking collectives: 15.1 us -> none  [on_device(): every = lax.all_gather(own, 'tile', axis=0, tiled=True)]
    ppermute x0 -> x8, starting transfers between devices: none -> 12 us  [the longest x4 5.75 us: gather_all(): got = lax.ppermute(x, axis, [(i, i ^ step) for i in range(count)])]
    ppermute x0 -> x8, waiting for transfers between devices: none -> 6.93 us  [the longest x3 3.27 us: scatter_sum(): lax.ppermute(part, axis, [(i, i ^ step) for i in range(count)])]
    dot_general x1, matrix products: 5.58 us -> 3.61 us  [on_device(): jnp.einsum('knxc,cy->knxy', half_re, sin_tab, precision=precise)]
  transfers between devices with their start and end apart: 1 -> 8, of which waited for: 1 -> 3; matrix products, arithmetic and copies ran while one was open for 0% -> 19% of each run, Pallas kernels for 0% -> 0%
where the time goes in v2:
time: 74.4 us; the launch traced here: 73.6 us
  matrix products  44.2 us (59%)
  starting transfers between devices  12 us (16%)
  waiting for transfers between devices  6.93 us (9%)
  local copies, waits for them, and re-layouts  5.1 us (7%)
  other arithmetic  3.51 us (5%)
  between operations  1.84 us (2%)
    ppermute x4, starting transfers between devices, gather_all(): got = lax.ppermute(x, axis, [(i, i ^ step) for i in range(count)])  5.75 us
    ppermute x3, starting transfers between devices, scatter_sum(): lax.ppermute(part, axis, [(i, i ^ step) for i in range(count)])  4.46 us
    dot_general x1, matrix products, on_device(): jnp.einsum('knxc,cy->knxy', half_re, sin_tab, precision=precise)  3.61 us
    dot_general x1, matrix products, on_device(): jnp.einsum('knxy,cy->knxc', g_im, sin_tab, precision=precise)  3.49 us
    dot_general x1, matrix products, on_device(): jnp.einsum('knxy,cy->knxc', g_re, cos_tab, precision=precise)  3.28 us
    dot_general x1, matrix products, on_device(): jnp.einsum('knxy,cy->knxc', g_im, cos_tab, precision=precise)  3.27 us
    dot_general x1, matrix products, on_device(): jnp.einsum('knxy,cy->knxc', g_re, sin_tab, precision=precise)  3.27 us
    ppermute x3, waiting for transfers between devices, scatter_sum(): lax.ppermute(part, axis, [(i, i ^ step) for i in range(count)])  3.27 us
  transfers between devices with their start and end apart: 8, of which 3 were waited for; matrix products, arithmetic and copies ran while one was open for 19% of the time, Pallas kernels for 0%

profile of v2, /device:TPU:0, one launch (start us, length us, event | category | flops | bytes accessed | tf_op | source)
XLA Modules:
  0.0 73.6 jit_solution(3441830529996323901)
XLA Ops:
  0.7 1.2 %fusion.41 = f32[32,256]{1,0:T(8,128)S(1)} fusion(f32[32,256]{1,0:T(8,128)} %constant.92.clone, bf16[1,256,256]{2,1,0:T(8,128)(2,1)} %param.11), kind=kOutput, calls=%fused_computation.74 | convolution fusion | flops 25165824 | bytes 196608 | tf_op jit(solution)/shard_map/master_spectra/bx,nxy->nby/dot_general | solution.py:36
  1.9 1.1 %fusion.39 = f32[32,256]{1,0:T(8,128)S(1)} fusion(f32[32,256]{1,0:T(8,128)} %constant.93.clone, bf16[1,256,256]{2,1,0:T(8,128)(2,1)} %param.11), kind=kOutput, calls=%fused_computation.72 | convolution fusion | flops 25165824 | bytes 196608 | tf_op jit(solution)/shard_map/master_spectra/bx,nxy->nby/dot_general | solution.py:37
  3.0 0.9 %fusion.81 = f32[32,32]{1,0:T(8,128)S(1)} fusion(f32[32,256]{1,0:T(8,128)S(1)} %fusion.41, f32[32,256]{1,0:T(8,128)} %constant.93.clone), kind=kOutput, calls=%fused_computation.154 | convolution fusion | flops 3145728 | bytes 69632 | tf_op jit(solution)/shard_map/master_spectra/nby,cy->nbc/dot_general | solution.py:41
  3.9 0.9 %fusion.80 = f32[32,32]{1,0:T(8,128)S(1)} fusion(f32[32,256]{1,0:T(8,128)S(1)} %fusion.41, f32[32,256]{1,0:T(8,128)} %constant.92.clone), kind=kOutput, calls=%fused_computation.153 | convolution fusion | flops 3145728 | bytes 69632 | tf_op jit(solution)/shard_map/master_spectra/nby,cy->nbc/dot_general | solution.py:38
  4.8 0.9 %fusion.26 = f32[1,1,32,32]{3,2,1,0:T(8,128)S(1)} fusion(f32[32,32]{1,0:T(8,128)S(1)} %fusion.81, f32[32,256]{1,0:T(8,128)S(1)} %fusion.39, f32[32,256]{1,0:T(8,128)} %constant.92.clone), kind=kOutput, calls=%fused_computation.45 | convolution fusion | flops 3146752 | bytes 73728 | tf_op jit(solution)/shard_map/master_spectra/nby,cy->nbc/dot_general | solution.py:41
  5.8 0.9 %fusion.27 = f32[1,1,32,32]{3,2,1,0:T(8,128)S(1)} fusion(f32[32,32]{1,0:T(8,128)S(1)} %fusion.80, f32[32,256]{1,0:T(8,128)S(1)} %fusion.39, f32[32,256]{1,0:T(8,128)} %constant.93.clone), kind=kOutput, calls=%fused_computation.47 | convolution fusion | flops 3146752 | bytes 73728 | tf_op jit(solution)/shard_map/master_spectra/nby,cy->nbc/dot_general | solution.py:38
  6.7 3.1 %collective-permute-start = (f32[1,2,32,32]{3,2,1,0:T(8,128)S(1)}, f32[1,2,32,32]{3,2,1,0:T(8,128)S(1)}, u32[]{:S(2)}, u32[]{:S(2)}) collective-permute-start(f32[1,2,32,32]{3,2,1,0:T(8,128)S(1)} %get-tuple-element.16), channel_id=1, source_target_pairs={{0,4},{4,0},{8,12},{12,8},{1,5},{5,1},{9,13},{13,9},{2,6},{6,2},{1... | collective-permute-start | bytes 24584 | tf_op jit(solution)/shard_map/master_spectra/ppermute | solution.py:70
  9.8 2.6 %collective-permute-start.1 = (f32[1,2,32,32]{3,2,1,0:T(8,128)S(1)}, f32[1,2,32,32]{3,2,1,0:T(8,128)S(1)}, u32[]{:S(2)}, u32[]{:S(2)}) collective-permute-start(f32[1,2,32,32]{3,2,1,0:T(8,128)S(1)} %get-tuple-element.16), channel_id=1, source_target_pairs={{0,8},{4,12},{8,0},{12,4},{1,9},{5,13},{9,1},{13,5},{2,10},{6,14},... | collective-permute-start | bytes 24584 | tf_op jit(solution)/shard_map/master_spectra/ppermute | solution.py:70
  12.4 1.0 %convolution_bitcast_fusion.1 = f32[32,256]{1,0:T(8,128)S(1)} fusion(f32[32,256]{1,0:T(8,128)} %constant.92.clone, bf16[2,256,256]{2,1,0:T(8,128)(2,1)S(1)} %copy-done, s32[]{:T(128)S(6)} %select_n.103), kind=kOutput, calls=%fused_computation.41 | convolution fusion | flops 25165824 | bytes 196612 | tf_op jit(solution)/shard_map/tile_spectra/bx,nxy->nby/dot_general | solution.py:36
  13.4 1.0 %convolution_bitcast_fusion = f32[32,256]{1,0:T(8,128)S(1)} fusion(f32[32,256]{1,0:T(8,128)} %constant.93.clone, bf16[2,256,256]{2,1,0:T(8,128)(2,1)S(1)} %copy-done, s32[]{:T(128)S(6)} %select_n.103), kind=kOutput, calls=%fused_computation.40 | convolution fusion | flops 25165824 | bytes 196612 | tf_op jit(solution)/shard_map/tile_spectra/bx,nxy->nby/dot_general | solution.py:37
  14.3 0.9 %fusion.79 = f32[32,32]{1,0:T(8,128)S(1)} fusion(f32[32,256]{1,0:T(8,128)S(1)} %convolution_bitcast_fusion.1, f32[32,256]{1,0:T(8,128)} %constant.92.clone), kind=kOutput, calls=%fused_computation.152 | convolution fusion | flops 3145728 | bytes 69632 | tf_op jit(solution)/shard_map/tile_spectra/nby,cy->nbc/dot_general | solution.py:38
  15.3 0.9 %fusion.82 = f32[32,32]{1,0:T(8,128)S(1)} fusion(f32[32,256]{1,0:T(8,128)S(1)} %convolution_bitcast_fusion.1, f32[32,256]{1,0:T(8,128)} %constant.93.clone), kind=kOutput, calls=%fused_computation.155 | convolution fusion | flops 3145728 | bytes 69632 | tf_op jit(solution)/shard_map/tile_spectra/nby,cy->nbc/dot_general | solution.py:41
  16.9 1.0 %slice_reduce_fusion.1 = (s32[2]{0:T(128)S(1)}, s32[2]{0:T(128)S(1)}) fusion(s32[2,2]{1,0:T(2,128)} %param.14), kind=kLoop, calls=%fused_computation.135 | loop fusion | bytes 32 | tf_op jit(solution)/shard_map/gradient_exchange/slice | solution.py:28
  17.8 1.2 %dynamic_slice.26 = s32[1]{0:T(128)} dynamic-slice(s32[2]{0:T(128)} %param.13, s32[]{:T(128)S(6)} %select_n.103), dynamic_slice_sizes={1} | dynamic-slice | bytes 12 | tf_op jit(solution)/shard_map/tile_spectra/dynamic_slice | solution.py:120
  19.7 1.0 %fusion.77 = (f32[1,12,1,32,32]{4,3,2,1,0:T(8,128)S(1)}, f32[1,12,1,32,32]{4,3,2,1,0:T(8,128)S(1)}) fusion(f32[1,12,2,32,32]{4,3,2,1,0:T(8,128)} %param.15), kind=kLoop, calls=%fused_computation.150 | loop fusion | bytes 196608 | tf_op jit(solution)/shard_map/slice | solution.py:134
  22.1 1.3 %broadcast_multiply_fusion.2 = (s32[32]{0:T(128)S(1)}, s32[32]{0:T(128)S(1)}) fusion(s32[]{:T(128)} %bitcast.12, s32[]{:T(128)} %bitcast.11), kind=kLoop, calls=%fused_computation.145 | loop fusion | flops 96 | bytes 264 | tf_op jit(solution)/shard_map/tile_spectra/mul | solution.py:29
  26.9 2.8 %fusion.83 = f32[12,256,256]{2,1,0:T(8,128)S(1)} fusion(f32[12,256,32]{1,2,0:T(8,128)S(1)} %fusion.15, f32[32,256,1]{1,0,2:T(8,128)S(1)} %copy-done.2), kind=kOutput, calls=%fused_computation.156 | convolution fusion | flops 301989888 | bytes 3571712 | tf_op jit(solution)/shard_map/forward_fields/knxc,cy->knxy/dot_general | solution.py:148
  29.7 2.8 %fusion.84 = f32[12,256,256]{2,1,0:T(8,128)S(1)} fusion(f32[12,256,32]{1,2,0:T(8,128)S(1)} %fusion.14, f32[32,256,1]{1,0,2:T(8,128)S(1)} %copy-done.2), kind=kOutput, calls=%fused_computation.157 | convolution fusion | flops 301989888 | bytes 3571712 | tf_op jit(solution)/shard_map/forward_fields/knxc,cy->knxy/dot_general | solution.py:152
  32.5 2.8 %add_multiply_fusion = f32[12,256,256]{2,1,0:T(8,128)S(1)} fusion(f32[12,256,256]{2,1,0:T(8,128)S(1)} %fusion.83, f32[12,256,32]{1,2,0:T(8,128)S(1)} %fusion.14, f32[32,256,1]{1,0,2:T(8,128)S(1)} %copy-done.1), kind=kOutput, calls=%fused_computation.4 | convolution fusion | flops 303562752 | bytes 6717440 | tf_op jit(solution)/shard_map/forward_fields/knxc,cy->knxy/dot_general | solution.py:149
  35.3 3.6 %multiply_reduce_fusion = (f32[256,256]{1,0:T(8,128)S(1)}, f32[12,256,256]{2,1,0:T(8,128)S(1)}) fusion(f32[12,256,256]{2,1,0:T(8,128)S(1)} %add_multiply_fusion, f32[12]{0:T(128)S(1)} %bitcast.242, f32[12,256,256]{2,1,0:T(8,128)S(1)} %fusion.84, f32[12,256,32]{1,2,0:T(8,128)S(1)} %fusion.15, f32[32,256,1]{1,0,2:T(8,128)S(1)} %copy-done.1), kind=kOutput, calls=%fused_computation.2 | convolution fusion | flops 307429376 | bytes 10125360 | tf_op jit(solution)/shard_map/forward_fields/knxc,cy->knxy/dot_general | solution.py:153
  39.1 3.3 %fusion = f32[12,256,32]{1,2,0:T(8,128)S(1)} fusion(f32[32,256,1]{1,0,2:T(8,128)S(1)} %copy-done.1, f32[12,256,256]{2,1,0:T(8,128)S(1)} %add_multiply_fusion, f32[256,256]{1,0:T(8,128)S(1)} %fusion.32, f32[12]{0:T(128)S(1)} %broadcast_multiply_fusion.4), kind=kOutput, calls=%fused_computation.5 | convolution fusion | flops 303562752 | bytes 3833904 | tf_op jit(solution)/shard_map/adjoint_spectra/knxy,cy->knxc/dot_general | solution.py:167
  42.4 3.3 %fusion.1 = f32[12,256,32]{1,2,0:T(8,128)S(1)} fusion(f32[32,256,1]{1,0,2:T(8,128)S(1)} %copy-done.2, f32[12,256,256]{2,1,0:T(8,128)S(1)} %add_multiply_fusion, f32[256,256]{1,0:T(8,128)S(1)} %fusion.32, f32[12]{0:T(128)S(1)} %broadcast_multiply_fusion.4), kind=kOutput, calls=%fused_computation.6 | convolution fusion | flops 303562752 | bytes 3833904 | tf_op jit(solution)/shard_map/adjoint_spectra/knxy,cy->knxc/dot_general | solution.py:164
  45.7 3.3 %fusion.13 = f32[12,256,32]{1,2,0:T(8,128)S(1)} fusion(f32[12,256,32]{1,2,0:T(8,128)S(1)} %fusion, f32[32,256,1]{1,0,2:T(8,128)S(1)} %copy-done.2, f32[12,256,256]{2,1,0:T(8,128)S(1)} %get-tuple-element.22, f32[256,256]{1,0:T(8,128)S(1)} %fusion.32, f32[12]{0:T(128)S(1)} %broadcast_multiply_fusion.4), kind=kOutput, calls=%fused_computation.19 | convolution fusion | flops 303661056 | bytes 4227120 | tf_op jit(solution)/shard_map/adjoint_spectra/knxy,cy->knxc/dot_general | solution.py:167
  48.9 3.5 %fusion.12 = f32[12,256,32]{1,2,0:T(8,128)S(1)} fusion(f32[12,256,32]{1,2,0:T(8,128)S(1)} %fusion.1, f32[32,256,1]{1,0,2:T(8,128)S(1)} %copy-done.1, f32[12,256,256]{2,1,0:T(8,128)S(1)} %get-tuple-element.22, f32[256,256]{1,0:T(8,128)S(1)} %fusion.32, f32[12]{0:T(128)S(1)} %broadcast_multiply_fusion.4), kind=kOutput, calls=%fused_computation.18 | convolution fusion | flops 303661056 | bytes 4227120 | tf_op jit(solution)/shard_map/adjoint_spectra/knxy,cy->knxc/dot_general | solution.py:164
  54.4 1.2 %collective-permute-done.3 = f32[1,2,32,32]{2,3,1,0:T(8,128)S(1)} collective-permute-done((f32[1,2,32,32]{2,3,1,0:T(8,128)S(1)}, f32[1,2,32,32]{2,3,1,0:T(8,128)S(1)}, u32[]{:S(2)}, u32[]{:S(2)}) %collective-permute-start.3) | collective-permute-done | bytes 8224 | tf_op jit(solution)/shard_map/gradient_exchange/ppermute | solution.py:70
  55.7 1.8 %collective-permute-start.4 = (f32[2,2,32,32]{2,3,0,1:T(8,128)S(1)}, f32[2,2,32,32]{2,3,0,1:T(8,128)S(1)}, u32[]{:S(2)}, u32[]{:S(2)}) collective-permute-start(f32[2,2,32,32]{2,3,0,1:T(8,128)S(1)} %select_add_fusion), channel_id=1, source_target_pairs={{0,2},{2,0},{1,3},{3,1},{4,6},{6,4},{5,7},{7,5},{8,10},{10,8},{9,1... | collective-permute-start | bytes 49160 | tf_op jit(solution)/shard_map/gradient_exchange/ppermute | solution.py:81
  57.5 2.5 %collective-permute-done.4 = f32[2,2,32,32]{2,3,0,1:T(8,128)S(1)} collective-permute-done((f32[2,2,32,32]{2,3,0,1:T(8,128)S(1)}, f32[2,2,32,32]{2,3,0,1:T(8,128)S(1)}, u32[]{:S(2)}, u32[]{:S(2)}) %collective-permute-start.4) | collective-permute-done | bytes 16416 | tf_op jit(solution)/shard_map/gradient_exchange/ppermute | solution.py:81
  60.9 1.0 %collective-permute-start.5 = (f32[1,2,32,32]{3,2,1,0:T(8,128)S(1)}, f32[1,2,32,32]{3,2,1,0:T(8,128)S(1)}, u32[]{:S(2)}, u32[]{:S(2)}) collective-permute-start(f32[1,2,32,32]{3,2,1,0:T(8,128)S(1)} %get-tuple-element.8), channel_id=1, source_target_pairs={{0,4},{4,0},{8,12},{12,8},{1,5},{5,1},{9,13},{13,9},{2,6},{6,2},{1... | collective-permute-start | bytes 24584 | tf_op jit(solution)/shard_map/gradient_exchange/ppermute | solution.py:92
  61.9 3.5 %collective-permute-start.6 = (f32[1,2,32,32]{3,2,1,0:T(8,128)S(1)}, f32[1,2,32,32]{3,2,1,0:T(8,128)S(1)}, u32[]{:S(2)}, u32[]{:S(2)}) collective-permute-start(f32[1,2,32,32]{3,2,1,0:T(8,128)S(1)} %get-tuple-element.10), channel_id=1, source_target_pairs={{0,8},{4,12},{8,0},{12,4},{1,9},{5,13},{9,1},{13,5},{2,10},{6,14},... | collective-permute-start | bytes 24584 | tf_op jit(solution)/shard_map/gradient_exchange/ppermute | solution.py:92
  66.4 1.4 %convolution_add_fusion = f32[2,256,256]{2,1,0:T(8,128)} fusion(f32[2,256,256]{2,1,0:T(8,128)S(1)} %fusion.87, f32[2,256,32]{1,2,0:T(8,128)S(1)} %fusion.21, f32[32,256,1]{1,0,2:T(8,128)S(1)} %copy-done.1), kind=kOutput, calls=%fused_computation.17 | convolution fusion | flops 50462720 | bytes 1146880 | tf_op jit(solution)/shard_map/pixel_gradients/nxc,cy->nxy/dot_general | solution.py:54
  67.8 3.3 %collective-permute-done.7 = f32[1,2,32,32]{3,2,1,0:T(8,128)S(1)} collective-permute-done((f32[1,2,32,32]{3,2,1,0:T(8,128)S(1)}, f32[1,2,32,32]{3,2,1,0:T(8,128)S(1)}, u32[]{:S(2)}, u32[]{:S(2)}) %collective-permute-start.7) | collective-permute-done | bytes 8224 | tf_op jit(solution)/shard_map/gradient_exchange/ppermute | solution.py:92
  72.4 1.1 %fusion.16 = f32[1,256,256]{2,1,0:T(8,128)} fusion(f32[256,256]{1,0:T(8,128)S(1)} %fusion.88, f32[256,32]{0,1:T(8,128)S(1)} %fusion.23, f32[32,256]{1,0:T(8,128)S(1)} %copy-done.4), kind=kOutput, calls=%fused_computation.25 | convolution fusion | flops 25231360 | bytes 589824 | tf_op jit(solution)/shard_map/pixel_gradients/nxc,cy->nxy/dot_general | solution.py:54
  (70 shorter events, 10.8 us)
Async XLA Ops:
  0.6 11.8 %copy-start = (bf16[2,256,256]{2,1,0:T(8,128)(2,1)S(1)}, bf16[2,256,256]{2,1,0:T(8,128)(2,1)}, u32[]{:S(2)}) copy-start(bf16[2,256,256]{2,1,0:T(8,128)(2,1)} %param.10) | copy-start | bytes 786436
  0.6 24.1 %copy-start.3 = (f32[32,256]{1,0:T(8,128)S(1)}, f32[32,256]{1,0:T(8,128)}, u32[]{:S(2)}) copy-start(f32[32,256]{1,0:T(8,128)} %constant.92.clone) | copy-start | bytes 98308
  0.7 23.9 %copy-start.4 = (f32[32,256]{1,0:T(8,128)S(1)}, f32[32,256]{1,0:T(8,128)}, u32[]{:S(2)}) copy-start(f32[32,256]{1,0:T(8,128)} %constant.93.clone) | copy-start | bytes 98308
  0.7 24.4 %copy-start.2 = (f32[32,256,1]{1,0,2:T(8,128)S(1)}, f32[32,256,1]{1,0,2:T(8,128)}, u32[]{:S(2)}) copy-start(f32[32,256,1]{1,0,2:T(8,128)} %constant.102) | copy-start | bytes 98308
  0.7 25.3 %copy-start.1 = (f32[32,256,1]{1,0,2:T(8,128)S(1)}, f32[32,256,1]{1,0,2:T(8,128)}, u32[]{:S(2)}) copy-start(f32[32,256,1]{1,0,2:T(8,128)} %constant.103) | copy-start | bytes 98308
  6.7 17.6 %collective-permute-start = (f32[1,2,32,32]{3,2,1,0:T(8,128)S(1)}, f32[1,2,32,32]{3,2,1,0:T(8,128)S(1)}, u32[]{:S(2)}, u32[]{:S(2)}) collective-permute-start(f32[1,2,32,32]{3,2,1,0:T(8,128)S(1)} %get-tuple-element.16), channel_id=1, source_target_pairs={{0,4},{4,0},{8,12},{12,8},{1,5},{5,1},{9,13},{13,9},{2,6},{6,2},{1... | collective-permute-start | bytes 24584 | tf_op jit(solution)/shard_map/master_spectra/ppermute | solution.py:70
  9.8 14.6 %collective-permute-start.1 = (f32[1,2,32,32]{3,2,1,0:T(8,128)S(1)}, f32[1,2,32,32]{3,2,1,0:T(8,128)S(1)}, u32[]{:S(2)}, u32[]{:S(2)}) collective-permute-start(f32[1,2,32,32]{3,2,1,0:T(8,128)S(1)} %get-tuple-element.16), channel_id=1, source_target_pairs={{0,8},{4,12},{8,0},{12,4},{1,9},{5,13},{9,1},{13,5},{2,10},{6,14},... | collective-permute-start | bytes 24584 | tf_op jit(solution)/shard_map/master_spectra/ppermute | solution.py:70
  12.4 12.0 %collective-permute-start.2 = (f32[1,2,32,32]{3,2,1,0:T(8,128)S(1)}, f32[1,2,32,32]{3,2,1,0:T(8,128)S(1)}, u32[]{:S(2)}, u32[]{:S(2)}) collective-permute-start(f32[1,2,32,32]{3,2,1,0:T(8,128)S(1)} %get-tuple-element.16), channel_id=1, source_target_pairs={{0,12},{4,8},{8,4},{12,0},{1,13},{5,9},{9,5},{13,1},{2,14},{6,10},... | collective-permute-start | bytes 24584 | tf_op jit(solution)/shard_map/master_spectra/ppermute | solution.py:70
  32.5 2.8 %copy-start.6 = (f32[1,12]{1,0:T(1,128)S(1)}, f32[1,12]{1,0:T(1,128)}, u32[]{:S(2)}) copy-start(f32[1,12]{1,0:T(1,128)} %param.16) | copy-start | bytes 148
  35.3 3.6 %copy-start.5 = (bf16[2,256,256]{2,1,0:T(8,128)(2,1)S(1)}, bf16[2,256,256]{2,1,0:T(8,128)(2,1)}, u32[]{:S(2)}) copy-start(bf16[2,256,256]{2,1,0:T(8,128)(2,1)} %param.12) | copy-start | bytes 786436
  48.9 8.5 %copy-start.7 = (s32[2]{0:T(128)S(1)}, s32[2]{0:T(128)}, u32[]{:S(2)}) copy-start(s32[2]{0:T(128)} %param.13) | copy-start | bytes 28
  54.3 1.3 %collective-permute-start.3 = (f32[1,2,32,32]{2,3,1,0:T(8,128)S(1)}, f32[1,2,32,32]{2,3,1,0:T(8,128)S(1)}, u32[]{:S(2)}, u32[]{:S(2)}) collective-permute-start(f32[1,2,32,32]{2,3,1,0:T(8,128)S(1)} %get-tuple-element.14), channel_id=1, source_target_pairs={{0,1},{1,0},{2,3},{3,2},{4,5},{5,4},{6,7},{7,6},{8,9},{9,8},{10,11... | collective-permute-start | bytes 24584 | tf_op jit(solution)/shard_map/gradient_exchange/ppermute | solution.py:70
  55.7 4.3 %collective-permute-start.4 = (f32[2,2,32,32]{2,3,0,1:T(8,128)S(1)}, f32[2,2,32,32]{2,3,0,1:T(8,128)S(1)}, u32[]{:S(2)}, u32[]{:S(2)}) collective-permute-start(f32[2,2,32,32]{2,3,0,1:T(8,128)S(1)} %select_add_fusion), channel_id=1, source_target_pairs={{0,2},{2,0},{1,3},{3,1},{4,6},{6,4},{5,7},{7,5},{8,10},{10,8},{9,1... | collective-permute-start | bytes 49160 | tf_op jit(solution)/shard_map/gradient_exchange/ppermute | solution.py:81
  60.9 6.9 %collective-permute-start.5 = (f32[1,2,32,32]{3,2,1,0:T(8,128)S(1)}, f32[1,2,32,32]{3,2,1,0:T(8,128)S(1)}, u32[]{:S(2)}, u32[]{:S(2)}) collective-permute-start(f32[1,2,32,32]{3,2,1,0:T(8,128)S(1)} %get-tuple-element.8), channel_id=1, source_target_pairs={{0,4},{4,0},{8,12},{12,8},{1,5},{5,1},{9,13},{13,9},{2,6},{6,2},{1... | collective-permute-start | bytes 24584 | tf_op jit(solution)/shard_map/gradient_exchange/ppermute | solution.py:92
  61.9 5.9 %collective-permute-start.6 = (f32[1,2,32,32]{3,2,1,0:T(8,128)S(1)}, f32[1,2,32,32]{3,2,1,0:T(8,128)S(1)}, u32[]{:S(2)}, u32[]{:S(2)}) collective-permute-start(f32[1,2,32,32]{3,2,1,0:T(8,128)S(1)} %get-tuple-element.10), channel_id=1, source_target_pairs={{0,8},{4,12},{8,0},{12,4},{1,9},{5,13},{9,1},{13,5},{2,10},{6,14},... | collective-permute-start | bytes 24584 | tf_op jit(solution)/shard_map/gradient_exchange/ppermute | solution.py:92
  65.4 5.7 %collective-permute-start.7 = (f32[1,2,32,32]{3,2,1,0:T(8,128)S(1)}, f32[1,2,32,32]{3,2,1,0:T(8,128)S(1)}, u32[]{:S(2)}, u32[]{:S(2)}) collective-permute-start(f32[1,2,32,32]{3,2,1,0:T(8,128)S(1)} %get-tuple-element.9), channel_id=1, source_target_pairs={{0,12},{4,8},{8,4},{12,0},{1,13},{5,9},{9,5},{13,1},{2,14},{6,10},... | collective-permute-start | bytes 24584 | tf_op jit(solution)/shard_map/gradient_exchange/ppermute | solution.py:92

commit v3 on v2

--- a/solution.py
+++ b/solution.py
@@ -5,6 +5,8 @@
 import jax.numpy as jnp
 from jax import lax
 from jax.sharding import PartitionSpec as P
+from jax.experimental import pallas as pl
+from jax.experimental.pallas import tpu as pltpu
 
 P_SIZE = 256
 B = 32
@@ -54,6 +56,105 @@
     return jnp.einsum("nxc,cy->nxy", half_re, cos_tab, precision=precise) + jnp.einsum(
         "nxc,cy->nxy", half_im, sin_tab, precision=precise
     )
+
+
+def split_bf16(a):
+    hi = a.astype(jnp.bfloat16)
+    lo = (a - hi.astype(jnp.float32)).astype(jnp.bfloat16)
+    return hi, lo
+
+
+def dot3(a, b_hi, b_lo):
+    a_hi, a_lo = split_bf16(a)
+    out = jnp.dot(a_hi, b_hi, preferred_element_type=jnp.float32)
+    out = out + jnp.dot(a_hi, b_lo, preferred_element_type=jnp.float32)
+    return out + jnp.dot(a_lo, b_hi, preferred_element_type=jnp.float32)
+
+
+def dot3_left(a_hi, a_lo, b):
+    b_hi, b_lo = split_bf16(b)
+    out = jnp.dot(a_hi, b_hi, preferred_element_type=jnp.float32)
+    out = out + jnp.dot(a_hi, b_lo, preferred_element_type=jnp.float32)
+    return out + jnp.dot(a_lo, b_hi, preferred_element_type=jnp.float32)
+
+
+def imaging_tables():
+    freq = np.arange(B, dtype=np.int64) - B // 2
+    pixel = np.arange(P_SIZE, dtype=np.int64)
+    angle = (2.0 * math.pi / P_SIZE) * np.mod(freq[:, None] * pixel[None, :], P_SIZE).astype(np.float64)
+    c_re = np.cos(angle)
+    c_im = -np.sin(angle)
+    scale = 1.0 / (P_SIZE * P_SIZE)
+    right_w = np.zeros((128, 2 * P_SIZE))
+    right_w[:B, :P_SIZE] = c_re
+    right_w[:B, P_SIZE:] = -c_im
+    right_w[B : 2 * B, :P_SIZE] = c_im
+    right_w[B : 2 * B, P_SIZE:] = c_re
+    left_a = np.zeros((P_SIZE, 128))
+    left_a[:, :B] = c_re.T * scale
+    left_a[:, B : 2 * B] = -c_im.T * scale
+    right_b = np.zeros((2 * P_SIZE, 128))
+    right_b[:P_SIZE, :B] = c_re.T * scale
+    right_b[:P_SIZE, B : 2 * B] = c_im.T * scale
+    right_b[P_SIZE:, :B] = -c_im.T * scale
+    right_b[P_SIZE:, B : 2 * B] = c_re.T * scale
+    out = []
+    for table in (right_w, left_a, right_b):
+        hi = table.astype(jnp.bfloat16)
+        lo = (table - hi.astype(np.float64)).astype(jnp.bfloat16)
+        out += [jnp.asarray(hi), jnp.asarray(lo)]
+    return out
+
+
+def imaging_body(
+    x_ref, goal_ref, w_ref, dose_ref, rw_hi, rw_lo, la_hi, la_lo, rb_hi, rb_lo, u_ref, w_buf, f_buf, i_buf
+):
+    count = f_buf.shape[0]
+    w_buf[...] = dot3(x_ref[...], rw_hi[...], rw_lo[...])
+    i_buf[...] = jnp.zeros(i_buf.shape, jnp.float32)
+    pad = jnp.zeros((128 - 2 * B, 2 * P_SIZE), jnp.float32)
+
+    def forward(k, carry):
+        rows = w_buf[pl.ds(pl.multiple_of(k * B, B), B), :]
+        swap = jnp.concatenate([-rows[:, P_SIZE:], rows[:, :P_SIZE]], axis=1)
+        stacked = jnp.concatenate([rows, swap, pad], axis=0)
+        field = dot3_left(la_hi[...], la_lo[...], stacked)
+        f_buf[k] = field
+        power = field * field
+        i_buf[...] += w_ref[k] * (power[:, :P_SIZE] + power[:, P_SIZE:])
+        return carry
+
+    lax.fori_loop(0, count, forward, 0)
+    dose = dose_ref[0]
+    resist = 1.0 / (1.0 + jnp.exp(-(steepness * (dose * i_buf[...] - threshold))))
+    sens = 2.0 * (resist - goal_ref[...]) * resist * (1.0 - resist) * steepness * dose
+    i_buf[...] = sens
+
+    def backward(k, carry):
+        sens = i_buf[...]
+        weighted = f_buf[k] * jnp.concatenate([sens, sens], axis=1)
+        u_ref[k] = dot3(weighted, rb_hi[...], rb_lo[...])
+        return carry
+
+    lax.fori_loop(0, count, backward, 0)
+
+
+def imaging(x_cat, goal, weights, dose):
+    count = weights.shape[0]
+    tables = imaging_tables()
+    vmem = pl.BlockSpec(memory_space=pltpu.VMEM)
+    smem = pl.BlockSpec(memory_space=pltpu.SMEM)
+    return pl.pallas_call(
+        imaging_body,
+        out_shape=jax.ShapeDtypeStruct((count, P_SIZE, 128), jnp.float32),
+        in_specs=[vmem, vmem, smem, smem] + [vmem] * 6,
+        out_specs=vmem,
+        scratch_shapes=[
+            pltpu.VMEM((count * B, 2 * P_SIZE), jnp.float32),
+            pltpu.VMEM((count, P_SIZE, 2 * P_SIZE), jnp.float32),
+            pltpu.VMEM((P_SIZE, P_SIZE), jnp.float32),
+        ],
+    )(x_cat, goal, weights, dose, *tables)
 
 
 def xor_partners(count):
@@ -135,48 +236,30 @@
     h_im = kernels[0, :, 1]
     weights = kernel_weight[0]
 
-    with jax.named_scope("forward_fields"):
+    with jax.named_scope("imaging_kernel"):
         x_re = h_re[:, None] * spec_re[None] - h_im[:, None] * spec_im[None]
         x_im = h_re[:, None] * spec_im[None] + h_im[:, None] * spec_re[None]
-        half_re = jnp.einsum("bx,knbc->knxc", cos_tab, x_re, precision=precise) + jnp.einsum(
-            "bx,knbc->knxc", sin_tab, x_im, precision=precise
+        count = h_re.shape[0]
+        outs = []
+        for j in range(per_dev):
+            x_cat = jnp.concatenate(
+                [x_re[:, j], x_im[:, j], jnp.zeros((count, B, 128 - 2 * B), jnp.float32)], axis=-1
+            ).reshape(count * B, 128)
+            outs.append(imaging(x_cat, goal[j], weights, corner_dose))
+        u_all = jnp.stack(outs, axis=1)
+        u_re = u_all[..., :B]
+        u_im = u_all[..., B : 2 * B]
+
+    with jax.named_scope("adjoint_spectra"):
+        out_re = jnp.einsum("bx,knxc->knbc", cos_tab, u_re, precision=precise) - jnp.einsum(
+            "bx,knxc->knbc", sin_tab, u_im, precision=precise
         )
-        half_im = jnp.einsum("bx,knbc->knxc", cos_tab, x_im, precision=precise) - jnp.einsum(
-            "bx,knbc->knxc", sin_tab, x_re, precision=precise
+        out_im = jnp.einsum("bx,knxc->knbc", cos_tab, u_im, precision=precise) + jnp.einsum(
+            "bx,knxc->knbc", sin_tab, u_re, precision=precise
         )
-        f_re = (
-            jnp.einsum("knxc,cy->knxy", half_re, cos_tab, precision=precise)
-            + jnp.einsum("knxc,cy->knxy", half_im, sin_tab, precision=precise)
-        ) * scale
-        f_im = (
-            jnp.einsum("knxc,cy->knxy", half_im, cos_tab, precision=precise)
-            - jnp.einsum("knxc,cy->knxy", half_re, sin_tab, precision=precise)
-        ) * scale
-
-    with jax.named_scope("resist_sensitivity"):
-        intensity = jnp.sum(weights[:, None, None, None] * (f_re * f_re + f_im * f_im), axis=0)
-        resist = jax.nn.sigmoid(steepness * (dose * intensity - threshold))
-        sens = 2.0 * (resist - goal) * resist * (1.0 - resist) * steepness * dose
-
-    with jax.named_scope("adjoint_spectra"):
-        g_re = (2.0 * weights)[:, None, None, None] * sens[None] * f_re
-        g_im = (2.0 * weights)[:, None, None, None] * sens[None] * f_im
-        mid_re = jnp.einsum("knxy,cy->knxc", g_re, cos_tab, precision=precise) - jnp.einsum(
-            "knxy,cy->knxc", g_im, sin_tab, precision=precise
-        )
-        mid_im = jnp.einsum("knxy,cy->knxc", g_re, sin_tab, precision=precise) + jnp.einsum(
-            "knxy,cy->knxc", g_im, cos_tab, precision=precise
-        )
-        out_re = (
-            jnp.einsum("bx,knxc->knbc", cos_tab, mid_re, precision=precise)
-            - jnp.einsum("bx,knxc->knbc", sin_tab, mid_im, precision=precise)
-        ) * scale
-        out_im = (
-            jnp.einsum("bx,knxc->knbc", cos_tab, mid_im, precision=precise)
-            + jnp.einsum("bx,knxc->knbc", sin_tab, mid_re, precision=precise)
-        ) * scale
-        grad_re = jnp.sum(h_re[:, None] * out_re + h_im[:, None] * out_im, axis=0)
-        grad_im = jnp.sum(h_re[:, None] * out_im - h_im[:, None] * out_re, axis=0)
+        twice = (2.0 * weights)[:, None, None, None]
+        grad_re = jnp.sum(twice * (h_re[:, None] * out_re + h_im[:, None] * out_im), axis=0)
+        grad_im = jnp.sum(twice * (h_re[:, None] * out_im - h_im[:, None] * out_re), axis=0)
 
     with jax.named_scope("gradient_exchange"):
         own_grad = jnp.stack([grad_re, grad_im], axis=1)

time: 74.4 us -> 68.7 us (0.923)
  matrix products: 44.2 us -> 28.3 us
  Pallas kernels: 0 us -> 11.7 us
  local copies, waits for them, and re-layouts: 5.1 us -> 3.37 us
  other arithmetic: 3.51 us -> 4.27 us
    dot_general x16 -> x4, matrix products: 28.9 us -> 12.9 us  [the longest x1 4.12 us: on_device(): jnp.einsum('bx,knxc->knbc', cos_tab, u_re, precision=precise)]
    pallas_call x0 -> x1, Pallas kernels: none -> 11.7 us  [imaging(): pl.pallas_call(imaging_body, out_shape=jax.ShapeDtypeStruct((count, P_SIZ...]
    slice x1, local copies, waits for them, and re-layouts: 1.05 us -> 0.03 us  [on_device(): h_re = kernels[0, :, 0]]
    concatenate x0 -> x1, other arithmetic: none -> 0.8 us  [on_device(): jnp.concatenate([x_re[:, j], x_im[:, j], jnp.zeros((count, B, 128 - 2 * B...]
    mul x2 -> x1, other arithmetic: 0.8 us -> 0.01 us  [on_device(): twice = (2.0 * weights)[:, None, None, None]]
  transfers between devices with their start and end apart: 8 -> 8, of which waited for: 3 -> 3; matrix products, arithmetic and copies ran while one was open for 19% -> 16% of each run, Pallas kernels for 0% -> 0%
where the time goes in v3:
time: 68.7 us; the launch traced here: 67.8 us
  matrix products  28.3 us (41%)
  starting transfers between devices  12 us (17%)
  Pallas kernels  11.7 us (17%)
  waiting for transfers between devices  6.5 us (9%)
  other arithmetic  4.27 us (6%)
  local copies, waits for them, and re-layouts  3.37 us (5%)
  between operations  1.73 us (3%)
    pallas_call x1, Pallas kernels, imaging(): pl.pallas_call(imaging_body, out_shape=jax.ShapeDtypeStruct((count, P_SIZ...  11.7 us
    ppermute x4, starting transfers between devices, gather_all(): got = lax.ppermute(x, axis, [(i, i ^ step) for i in range(count)])  5.83 us
    ppermute x3, starting transfers between devices, scatter_sum(): lax.ppermute(part, axis, [(i, i ^ step) for i in range(count)])  4.46 us
    dot_general x1, matrix products, on_device(): jnp.einsum('bx,knxc->knbc', cos_tab, u_re, precision=precise)  4.12 us
    dot_general x1, matrix products, on_device(): jnp.einsum('bx,knxc->knbc', sin_tab, u_im, precision=precise)  3.08 us
    dot_general x1, matrix products, on_device(): jnp.einsum('bx,knxc->knbc', cos_tab, u_im, precision=precise)  3.08 us
    ppermute x3, waiting for transfers between devices, scatter_sum(): lax.ppermute(part, axis, [(i, i ^ step) for i in range(count)])  2.76 us
    dot_general x1, matrix products, on_device(): jnp.einsum('bx,knxc->knbc', sin_tab, u_re, precision=precise)  2.6 us
  transfers between devices with their start and end apart: 8, of which 3 were waited for; matrix products, arithmetic and copies ran while one was open for 16% of the time, Pallas kernels for 0%

profile of v3, /device:TPU:0, one launch (start us, length us, event | category | flops | bytes accessed | tf_op | source)
XLA Modules:
  0.0 67.8 jit_solution(5568104550960318130)
XLA Ops:
  0.7 1.2 %fusion.27 = f32[32,256]{1,0:T(8,128)S(1)} fusion(f32[32,256]{1,0:T(8,128)} %constant.95.clone, bf16[1,256,256]{2,1,0:T(8,128)(2,1)} %param.17), kind=kOutput, calls=%fused_computation.52 | convolution fusion | flops 25165824 | bytes 196608 | tf_op jit(solution)/shard_map/master_spectra/bx,nxy->nby/dot_general | solution.py:38
  1.9 1.1 %fusion.25 = f32[32,256]{1,0:T(8,128)S(1)} fusion(f32[32,256]{1,0:T(8,128)} %constant.96.clone, bf16[1,256,256]{2,1,0:T(8,128)(2,1)} %param.17), kind=kOutput, calls=%fused_computation.50 | convolution fusion | flops 25165824 | bytes 196608 | tf_op jit(solution)/shard_map/master_spectra/bx,nxy->nby/dot_general | solution.py:39
  3.0 0.9 %fusion.61 = f32[32,32]{1,0:T(8,128)S(1)} fusion(f32[32,256]{1,0:T(8,128)S(1)} %fusion.27, f32[32,256]{1,0:T(8,128)} %constant.96.clone), kind=kOutput, calls=%fused_computation.130 | convolution fusion | flops 3145728 | bytes 69632 | tf_op jit(solution)/shard_map/master_spectra/nby,cy->nbc/dot_general | solution.py:43
  4.0 1.0 %fusion.60 = f32[32,32]{1,0:T(8,128)S(1)} fusion(f32[32,256]{1,0:T(8,128)S(1)} %fusion.27, f32[32,256]{1,0:T(8,128)} %constant.95.clone), kind=kOutput, calls=%fused_computation.129 | convolution fusion | flops 3145728 | bytes 69632 | tf_op jit(solution)/shard_map/master_spectra/nby,cy->nbc/dot_general | solution.py:40
  4.9 0.9 %fusion.14 = f32[1,1,32,32]{3,2,1,0:T(8,128)S(1)} fusion(f32[32,32]{1,0:T(8,128)S(1)} %fusion.61, f32[32,256]{1,0:T(8,128)S(1)} %fusion.25, f32[32,256]{1,0:T(8,128)} %constant.95.clone), kind=kOutput, calls=%fused_computation.26 | convolution fusion | flops 3146752 | bytes 73728 | tf_op jit(solution)/shard_map/master_spectra/nby,cy->nbc/dot_general | solution.py:43
  5.9 1.0 %fusion.15 = f32[1,1,32,32]{3,2,1,0:T(8,128)S(1)} fusion(f32[32,32]{1,0:T(8,128)S(1)} %fusion.60, f32[32,256]{1,0:T(8,128)S(1)} %fusion.25, f32[32,256]{1,0:T(8,128)} %constant.96.clone), kind=kOutput, calls=%fused_computation.28 | convolution fusion | flops 3146752 | bytes 73728 | tf_op jit(solution)/shard_map/master_spectra/nby,cy->nbc/dot_general | solution.py:40
  6.9 5.1 %collective-permute-start.2 = (f32[1,2,32,32]{3,2,1,0:T(8,128)S(1)}, f32[1,2,32,32]{3,2,1,0:T(8,128)S(1)}, u32[]{:S(2)}, u32[]{:S(2)}) collective-permute-start(f32[1,2,32,32]{3,2,1,0:T(8,128)S(1)} %get-tuple-element.18), channel_id=1, source_target_pairs={{0,12},{4,8},{8,4},{12,0},{1,13},{5,9},{9,5},{13,1},{2,14},{6,10},... | collective-permute-start | bytes 24584 | tf_op jit(solution)/shard_map/master_spectra/ppermute | solution.py:171
  12.0 0.6 collective-permute-start
  12.7 1.0 %convolution_bitcast_fusion.1 = f32[32,256]{1,0:T(8,128)S(1)} fusion(f32[32,256]{1,0:T(8,128)} %constant.95.clone, bf16[2,256,256]{2,1,0:T(8,128)(2,1)S(1)} %copy-done, s32[]{:T(128)S(6)} %select_n.103), kind=kOutput, calls=%fused_computation.22 | convolution fusion | flops 25165824 | bytes 196612 | tf_op jit(solution)/shard_map/tile_spectra/bx,nxy->nby/dot_general | solution.py:38
  13.6 1.0 %convolution_bitcast_fusion = f32[32,256]{1,0:T(8,128)S(1)} fusion(f32[32,256]{1,0:T(8,128)} %constant.96.clone, bf16[2,256,256]{2,1,0:T(8,128)(2,1)S(1)} %copy-done, s32[]{:T(128)S(6)} %select_n.103), kind=kOutput, calls=%fused_computation.21 | convolution fusion | flops 25165824 | bytes 196612 | tf_op jit(solution)/shard_map/tile_spectra/bx,nxy->nby/dot_general | solution.py:39
  14.6 0.9 %fusion.62 = f32[32,32]{1,0:T(8,128)S(1)} fusion(f32[32,256]{1,0:T(8,128)S(1)} %convolution_bitcast_fusion.1, f32[32,256]{1,0:T(8,128)} %constant.96.clone), kind=kOutput, calls=%fused_computation.131 | convolution fusion | flops 3145728 | bytes 69632 | tf_op jit(solution)/shard_map/tile_spectra/nby,cy->nbc/dot_general | solution.py:43
  15.5 0.9 %fusion.59 = f32[32,32]{1,0:T(8,128)S(1)} fusion(f32[32,256]{1,0:T(8,128)S(1)} %convolution_bitcast_fusion.1, f32[32,256]{1,0:T(8,128)} %constant.95.clone), kind=kOutput, calls=%fused_computation.128 | convolution fusion | flops 3145728 | bytes 69632 | tf_op jit(solution)/shard_map/tile_spectra/nby,cy->nbc/dot_general | solution.py:40
  16.4 0.7 %constant_dynamic-slice_fusion.3 = s32[1,2]{1,0:T(1,128)S(1)} fusion(s32[2,2]{1,0:T(2,128)} %param.20, s32[]{:T(128)S(6)} %select_n.103), kind=kLoop, calls=%fused_computation.108 | loop fusion | bytes 20 | tf_op jit(solution)/shard_map/tile_spectra/dynamic_slice | solution.py:222
  17.1 1.0 %slice_reduce_fusion.1 = (s32[2]{0:T(128)S(1)}, s32[2]{0:T(128)S(1)}) fusion(s32[2,2]{1,0:T(2,128)} %param.20), kind=kLoop, calls=%fused_computation.111 | loop fusion | bytes 32 | tf_op jit(solution)/shard_map/gradient_exchange/slice | solution.py:30
  18.7 0.6 fusion.58
  19.4 0.7 %bitcast_convert_fusion.goal_ref = f32[256,256]{1,0:T(8,128)} fusion(bf16[2,256,256]{2,1,0:T(8,128)(2,1)S(1)} %copy-done.7, s32[]{:T(128)S(6)} %select_n.103), kind=kLoop, calls=%fused_computation.49 | loop fusion | flops 65536 | bytes 393220 | tf_op jit(solution)/shard_map/imaging_kernel/squeeze | solution.py:248
  20.1 0.6 compare_convert_fusion.1
  20.8 1.3 %broadcast_multiply_fusion.2 = (s32[32]{0:T(128)S(1)}, s32[32]{0:T(128)S(1)}) fusion(s32[]{:T(128)} %bitcast.11, s32[]{:T(128)} %bitcast.10), kind=kLoop, calls=%fused_computation.121 | loop fusion | flops 96 | bytes 264 | tf_op jit(solution)/shard_map/tile_spectra/mul | solution.py:31
  23.7 0.8 %maximum_maximum_fusion.x_ref = f32[384,128]{1,0:T(8,128)} fusion(f32[384,32]{1,0:T(8,128)S(1)} %get-tuple-element.7, f32[384,32]{1,0:T(8,128)S(1)} %get-tuple-element.6, f32[128]{0:T(128)S(1)} %pad.6.clone), kind=kLoop, calls=%fused_computation.38 | loop fusion | flops 98304 | bytes 295424 | tf_op jit(solution)/shard_map/imaging_kernel/concatenate | solution.py:245
  24.5 11.7 %imaging_kernel.1 = f32[12,256,128]{2,1,0:T(8,128)} custom-call(f32[384,128]{1,0:T(8,128)} %maximum_maximum_fusion.x_ref, f32[256,256]{1,0:T(8,128)} %bitcast_convert_fusion.goal_ref, f32[12]{0:T(128)} %bitcast.221, f32[1]{0:T(128)S(6)} %copy.53.dose_ref, bf16[128,512]{1,0:T(8,128)(2,1)} %constant.97.clone.rw_hi, bf16[128,512]{1,0:T(8,128)(2,1)} %constant.98.clone.rw_lo, ...), custom_call_target="tpu_custom_call" | custom-call | tf_op jit(solution)/shard_map/imaging_kernel/pallas_call | solution.py:147
  36.2 4.1 %fusion.1 = f32[12,32,32]{2,1,0:T(8,128)S(1)} fusion(f32[32,256,1]{1,0,2:T(8,128)S(1)} %copy-done.5, f32[12,1,256,128]{3,2,0,1:T(8,128)} %bitcast.208), kind=kOutput, calls=%fused_computation.3 | convolution fusion | flops 37748736 | bytes 1654784 | tf_op jit(solution)/shard_map/adjoint_spectra/bx,knxc->knbc/dot_general | solution.py:254
  40.3 2.6 %fusion = f32[12,32,32]{2,1,0:T(8,128)S(1)} fusion(f32[32,256,1]{1,0,2:T(8,128)S(1)} %copy-done.4, f32[12,1,256,128]{3,2,0,1:T(8,128)S(1)} %bitcast.209), kind=kOutput, calls=%fused_computation.2 | convolution fusion | flops 37748736 | bytes 1654784 | tf_op jit(solution)/shard_map/adjoint_spectra/bx,knxc->knbc/dot_general | solution.py:257
  42.9 3.1 %fusion.8 = f32[12,1,32,32]{2,3,0,1:T(8,128)S(1)} fusion(f32[12,32,32]{2,1,0:T(8,128)S(1)} %fusion.1, f32[32,256,1]{1,0,2:T(8,128)S(1)} %copy-done.4, f32[12,1,256,128]{3,2,0,1:T(8,128)S(1)} %bitcast.210), kind=kOutput, calls=%fused_computation.12 | convolution fusion | flops 37761024 | bytes 1703936 | tf_op jit(solution)/shard_map/adjoint_spectra/bx,knxc->knbc/dot_general | solution.py:254
  46.0 3.1 %fusion.21 = (f32[32,32]{0,1:T(8,128)S(1)}, f32[32,32]{0,1:T(8,128)S(1)}) fusion(f32[1,12,1,32,32]{3,4,1,2,0:T(8,128)S(1)} %copy.50, f32[12,1,32,32]{2,3,0,1:T(8,128)S(1)} %fusion.8, f32[1,12,1,32,32]{3,4,1,2,0:T(8,128)S(1)} %copy.49, f32[12]{0:T(128)S(1)} %broadcast_multiply_fusion.4, f32[12,32,32]{2,1,0:T(8,128)S(1)} %fusion, ...), kind=kOutput, calls=%fused_computation.43 | convolution fusion | flops 37881856 | bytes 1810480 | tf_op jit(solution)/shard_map/adjoint_spectra/bx,knxc->knbc/dot_general | solution.py:257
  49.2 1.2 %collective-permute-done.3 = f32[1,2,32,32]{2,3,1,0:T(8,128)S(1)} collective-permute-done((f32[1,2,32,32]{2,3,1,0:T(8,128)S(1)}, f32[1,2,32,32]{2,3,1,0:T(8,128)S(1)}, u32[]{:S(2)}, u32[]{:S(2)}) %collective-permute-start.3) | collective-permute-done | bytes 8224 | tf_op jit(solution)/shard_map/gradient_exchange/ppermute | solution.py:171
  50.5 1.7 %collective-permute-start.4 = (f32[2,2,32,32]{2,3,0,1:T(8,128)S(1)}, f32[2,2,32,32]{2,3,0,1:T(8,128)S(1)}, u32[]{:S(2)}, u32[]{:S(2)}) collective-permute-start(f32[2,2,32,32]{2,3,0,1:T(8,128)S(1)} %select_add_fusion), channel_id=1, source_target_pairs={{0,2},{2,0},{1,3},{3,1},{4,6},{6,4},{5,7},{7,5},{8,10},{10,8},{9,1... | collective-permute-start | bytes 49160 | tf_op jit(solution)/shard_map/gradient_exchange/ppermute | solution.py:182
  52.2 2.6 %collective-permute-done.4 = f32[2,2,32,32]{2,3,0,1:T(8,128)S(1)} collective-permute-done((f32[2,2,32,32]{2,3,0,1:T(8,128)S(1)}, f32[2,2,32,32]{2,3,0,1:T(8,128)S(1)}, u32[]{:S(2)}, u32[]{:S(2)}) %collective-permute-start.4) | collective-permute-done | bytes 16416 | tf_op jit(solution)/shard_map/gradient_exchange/ppermute | solution.py:182
  56.7 3.8 %collective-permute-start.7 = (f32[1,2,32,32]{3,2,1,0:T(8,128)S(1)}, f32[1,2,32,32]{3,2,1,0:T(8,128)S(1)}, u32[]{:S(2)}, u32[]{:S(2)}) collective-permute-start(f32[1,2,32,32]{3,2,1,0:T(8,128)S(1)} %get-tuple-element.11), channel_id=1, source_target_pairs={{0,12},{4,8},{8,4},{12,0},{1,13},{5,9},{9,5},{13,1},{2,14},{6,10},... | collective-permute-start | bytes 24584 | tf_op jit(solution)/shard_map/gradient_exchange/ppermute | solution.py:193
  60.6 0.6 collective-permute-start.5
  61.2 1.4 %convolution_add_fusion = f32[2,256,256]{2,1,0:T(8,128)} fusion(f32[2,256,256]{2,1,0:T(8,128)S(1)} %fusion.63, f32[2,256,32]{1,2,0:T(8,128)S(1)} %fusion.9, f32[32,256,1]{1,0,2:T(8,128)S(1)} %copy-done.4), kind=kOutput, calls=%fused_computation.6 | convolution fusion | flops 50462720 | bytes 1146880 | tf_op jit(solution)/shard_map/pixel_gradients/nxc,cy->nxy/dot_general | solution.py:56
  62.6 2.8 %collective-permute-done.6 = f32[1,2,32,32]{3,2,1,0:T(8,128)S(1)} collective-permute-done((f32[1,2,32,32]{3,2,1,0:T(8,128)S(1)}, f32[1,2,32,32]{3,2,1,0:T(8,128)S(1)}, u32[]{:S(2)}, u32[]{:S(2)}) %collective-permute-start.6) | collective-permute-done | bytes 8224 | tf_op jit(solution)/shard_map/gradient_exchange/ppermute | solution.py:193
  66.7 1.1 %fusion.4 = f32[1,256,256]{2,1,0:T(8,128)} fusion(f32[256,256]{1,0:T(8,128)S(1)} %fusion.64, f32[256,32]{0,1:T(8,128)S(1)} %fusion.11, f32[32,256]{1,0:T(8,128)S(1)} %copy-done.3), kind=kOutput, calls=%fused_computation.8 | convolution fusion | flops 25231360 | bytes 589824 | tf_op jit(solution)/shard_map/pixel_gradients/nxc,cy->nxy/dot_general | solution.py:56
  (65 shorter events, 5.0 us)
Async XLA Ops:
  0.6 12.0 %copy-start = (bf16[2,256,256]{2,1,0:T(8,128)(2,1)S(1)}, bf16[2,256,256]{2,1,0:T(8,128)(2,1)}, u32[]{:S(2)}) copy-start(bf16[2,256,256]{2,1,0:T(8,128)(2,1)} %param.16) | copy-start | bytes 786436
  0.6 17.5 %copy-start.6 = (f32[1,12,2,32,32]{4,3,2,1,0:T(8,128)S(1)}, f32[1,12,2,32,32]{4,3,2,1,0:T(8,128)}, u32[]{:S(2)}) copy-start(f32[1,12,2,32,32]{4,3,2,1,0:T(8,128)} %param.21) | copy-start | bytes 294916
  0.7 17.5 %copy-start.9 = (s32[2]{0:T(128)S(1)}, s32[2]{0:T(128)}, u32[]{:S(2)}) copy-start(s32[2]{0:T(128)} %param.19) | copy-start | bytes 28
  0.7 18.7 %copy-start.7 = (bf16[2,256,256]{2,1,0:T(8,128)(2,1)S(1)}, bf16[2,256,256]{2,1,0:T(8,128)(2,1)}, u32[]{:S(2)}) copy-start(bf16[2,256,256]{2,1,0:T(8,128)(2,1)} %param.18) | copy-start | bytes 786436
  0.7 19.4 %copy-start.8 = (f32[1,12]{1,0:T(1,128)S(1)}, f32[1,12]{1,0:T(1,128)}, u32[]{:S(2)}) copy-start(f32[1,12]{1,0:T(1,128)} %param.22) | copy-start | bytes 148
  3.9 19.3 %copy-start.2 = (f32[32,256]{1,0:T(8,128)S(1)}, f32[32,256]{1,0:T(8,128)}, u32[]{:S(2)}) copy-start(f32[32,256]{1,0:T(8,128)} %constant.95.clone) | copy-start | bytes 98308
  5.9 17.6 %copy-start.3 = (f32[32,256]{1,0:T(8,128)S(1)}, f32[32,256]{1,0:T(8,128)}, u32[]{:S(2)}) copy-start(f32[32,256]{1,0:T(8,128)} %constant.96.clone) | copy-start | bytes 98308
  6.9 16.2 %collective-permute-start.2 = (f32[1,2,32,32]{3,2,1,0:T(8,128)S(1)}, f32[1,2,32,32]{3,2,1,0:T(8,128)S(1)}, u32[]{:S(2)}, u32[]{:S(2)}) collective-permute-start(f32[1,2,32,32]{3,2,1,0:T(8,128)S(1)} %get-tuple-element.18), channel_id=1, source_target_pairs={{0,12},{4,8},{8,4},{12,0},{1,13},{5,9},{9,5},{13,1},{2,14},{6,10},... | collective-permute-start | bytes 24584 | tf_op jit(solution)/shard_map/master_spectra/ppermute | solution.py:171
  12.0 11.1 %collective-permute-start.1 = (f32[1,2,32,32]{3,2,1,0:T(8,128)S(1)}, f32[1,2,32,32]{3,2,1,0:T(8,128)S(1)}, u32[]{:S(2)}, u32[]{:S(2)}) collective-permute-start(f32[1,2,32,32]{3,2,1,0:T(8,128)S(1)} %get-tuple-element.18), channel_id=1, source_target_pairs={{0,8},{4,12},{8,0},{12,4},{1,9},{5,13},{9,1},{13,5},{2,10},{6,14},... | collective-permute-start | bytes 24584 | tf_op jit(solution)/shard_map/master_spectra/ppermute | solution.py:171
  12.0 11.1 %collective-permute-start = (f32[1,2,32,32]{3,2,1,0:T(8,128)S(1)}, f32[1,2,32,32]{3,2,1,0:T(8,128)S(1)}, u32[]{:S(2)}, u32[]{:S(2)}) collective-permute-start(f32[1,2,32,32]{3,2,1,0:T(8,128)S(1)} %get-tuple-element.18), channel_id=1, source_target_pairs={{0,4},{4,0},{8,12},{12,8},{1,5},{5,1},{9,13},{13,9},{2,6},{6,2},{1... | collective-permute-start | bytes 24584 | tf_op jit(solution)/shard_map/master_spectra/ppermute | solution.py:171
  23.7 12.5 %copy-start.5 = (f32[32,256,1]{1,0,2:T(8,128)S(1)}, f32[32,256,1]{1,0,2:T(8,128)}, u32[]{:S(2)}) copy-start(f32[32,256,1]{1,0,2:T(8,128)} %constant.111) | copy-start | bytes 98308
  36.2 4.1 %copy-start.1 = (f32[12,256,128]{2,1,0:T(8,128)S(1)}, f32[12,256,128]{2,1,0:T(8,128)}, u32[]{:S(2)}) copy-start(f32[12,256,128]{2,1,0:T(8,128)} %imaging_kernel.1) | copy-start | bytes 4718596
  36.2 4.1 %copy-start.4 = (f32[32,256,1]{1,0,2:T(8,128)S(1)}, f32[32,256,1]{1,0,2:T(8,128)}, u32[]{:S(2)}) copy-start(f32[32,256,1]{1,0,2:T(8,128)} %constant.112) | copy-start | bytes 98308
  49.1 1.3 %collective-permute-start.3 = (f32[1,2,32,32]{2,3,1,0:T(8,128)S(1)}, f32[1,2,32,32]{2,3,1,0:T(8,128)S(1)}, u32[]{:S(2)}, u32[]{:S(2)}) collective-permute-start(f32[1,2,32,32]{2,3,1,0:T(8,128)S(1)} %get-tuple-element.16), channel_id=1, source_target_pairs={{0,1},{1,0},{2,3},{3,2},{4,5},{5,4},{6,7},{7,6},{8,9},{9,8},{10,11... | collective-permute-start | bytes 24584 | tf_op jit(solution)/shard_map/gradient_exchange/ppermute | solution.py:171
  50.5 4.3 %collective-permute-start.4 = (f32[2,2,32,32]{2,3,0,1:T(8,128)S(1)}, f32[2,2,32,32]{2,3,0,1:T(8,128)S(1)}, u32[]{:S(2)}, u32[]{:S(2)}) collective-permute-start(f32[2,2,32,32]{2,3,0,1:T(8,128)S(1)} %select_add_fusion), channel_id=1, source_target_pairs={{0,2},{2,0},{1,3},{3,1},{4,6},{6,4},{5,7},{7,5},{8,10},{10,8},{9,1... | collective-permute-start | bytes 49160 | tf_op jit(solution)/shard_map/gradient_exchange/ppermute | solution.py:182
  56.7 5.9 %collective-permute-start.7 = (f32[1,2,32,32]{3,2,1,0:T(8,128)S(1)}, f32[1,2,32,32]{3,2,1,0:T(8,128)S(1)}, u32[]{:S(2)}, u32[]{:S(2)}) collective-permute-start(f32[1,2,32,32]{3,2,1,0:T(8,128)S(1)} %get-tuple-element.11), channel_id=1, source_target_pairs={{0,12},{4,8},{8,4},{12,0},{1,13},{5,9},{9,5},{13,1},{2,14},{6,10},... | collective-permute-start | bytes 24584 | tf_op jit(solution)/shard_map/gradient_exchange/ppermute | solution.py:193
  60.6 4.8 %collective-permute-start.6 = (f32[1,2,32,32]{3,2,1,0:T(8,128)S(1)}, f32[1,2,32,32]{3,2,1,0:T(8,128)S(1)}, u32[]{:S(2)}, u32[]{:S(2)}) collective-permute-start(f32[1,2,32,32]{3,2,1,0:T(8,128)S(1)} %get-tuple-element.12), channel_id=1, source_target_pairs={{0,8},{4,12},{8,0},{12,4},{1,9},{5,13},{9,1},{13,5},{2,10},{6,14},... | collective-permute-start | bytes 24584 | tf_op jit(solution)/shard_map/gradient_exchange/ppermute | solution.py:193
  60.6 4.8 %collective-permute-start.5 = (f32[1,2,32,32]{3,2,1,0:T(8,128)S(1)}, f32[1,2,32,32]{3,2,1,0:T(8,128)S(1)}, u32[]{:S(2)}, u32[]{:S(2)}) collective-permute-start(f32[1,2,32,32]{3,2,1,0:T(8,128)S(1)} %get-tuple-element.10), channel_id=1, source_target_pairs={{0,4},{4,0},{8,12},{12,8},{1,5},{5,1},{9,13},{13,9},{2,6},{6,2},{1... | collective-permute-start | bytes 24584 | tf_op jit(solution)/shard_map/gradient_exchange/ppermute | solution.py:193

commit v4 on v3

--- a/solution.py
+++ b/solution.py
@@ -58,24 +58,8 @@
     )
 
 
-def split_bf16(a):
-    hi = a.astype(jnp.bfloat16)
-    lo = (a - hi.astype(jnp.float32)).astype(jnp.bfloat16)
-    return hi, lo
-
-
-def dot3(a, b_hi, b_lo):
-    a_hi, a_lo = split_bf16(a)
-    out = jnp.dot(a_hi, b_hi, preferred_element_type=jnp.float32)
-    out = out + jnp.dot(a_hi, b_lo, preferred_element_type=jnp.float32)
-    return out + jnp.dot(a_lo, b_hi, preferred_element_type=jnp.float32)
-
-
-def dot3_left(a_hi, a_lo, b):
-    b_hi, b_lo = split_bf16(b)
-    out = jnp.dot(a_hi, b_hi, preferred_element_type=jnp.float32)
-    out = out + jnp.dot(a_hi, b_lo, preferred_element_type=jnp.float32)
-    return out + jnp.dot(a_lo, b_hi, preferred_element_type=jnp.float32)
+def dot_full(a, b):
+    return jnp.dot(a, b, precision=precise, preferred_element_type=jnp.float32)
 
 
 def imaging_tables():
@@ -98,19 +82,23 @@
     right_b[:P_SIZE, B : 2 * B] = c_im.T * scale
     right_b[P_SIZE:, :B] = -c_im.T * scale
     right_b[P_SIZE:, B : 2 * B] = c_re.T * scale
-    out = []
-    for table in (right_w, left_a, right_b):
-        hi = table.astype(jnp.bfloat16)
-        lo = (table - hi.astype(np.float64)).astype(jnp.bfloat16)
-        out += [jnp.asarray(hi), jnp.asarray(lo)]
-    return out
+    ct_re = c_re.T
+    ct_im = c_im.T
+    right_c = np.zeros((2 * P_SIZE, 128))
+    for col, (top, bottom) in enumerate(
+        ((ct_re, -ct_im), (ct_im, ct_re), (ct_im, ct_re), (ct_re, -ct_im))
+    ):
+        right_c[:P_SIZE, col * B : (col + 1) * B] = top
+        right_c[P_SIZE:, col * B : (col + 1) * B] = bottom
+    return [jnp.asarray(table, jnp.float32) for table in (right_w, left_a, right_b, right_c)]
 
 
 def imaging_body(
-    x_ref, goal_ref, w_ref, dose_ref, rw_hi, rw_lo, la_hi, la_lo, rb_hi, rb_lo, u_ref, w_buf, f_buf, i_buf
+    x_ref, goal_ref, h_ref, w_ref, dose_ref, rw_ref, la_ref, rb_ref, rc_ref,
+    acc_ref, w_buf, f_buf, i_buf, u_buf,
 ):
     count = f_buf.shape[0]
-    w_buf[...] = dot3(x_ref[...], rw_hi[...], rw_lo[...])
+    w_buf[...] = dot_full(x_ref[...], rw_ref[...])
     i_buf[...] = jnp.zeros(i_buf.shape, jnp.float32)
     pad = jnp.zeros((128 - 2 * B, 2 * P_SIZE), jnp.float32)
 
@@ -118,7 +106,7 @@
         rows = w_buf[pl.ds(pl.multiple_of(k * B, B), B), :]
         swap = jnp.concatenate([-rows[:, P_SIZE:], rows[:, :P_SIZE]], axis=1)
         stacked = jnp.concatenate([rows, swap, pad], axis=0)
-        field = dot3_left(la_hi[...], la_lo[...], stacked)
+        field = dot_full(la_ref[...], stacked)
         f_buf[k] = field
         power = field * field
         i_buf[...] += w_ref[k] * (power[:, :P_SIZE] + power[:, P_SIZE:])
@@ -133,28 +121,33 @@
     def backward(k, carry):
         sens = i_buf[...]
         weighted = f_buf[k] * jnp.concatenate([sens, sens], axis=1)
-        u_ref[k] = dot3(weighted, rb_hi[...], rb_lo[...])
+        half = dot_full(weighted, rb_ref[...])
+        flip = half.T
+        u_buf[pl.ds(pl.multiple_of(k * B, B), B), :] = jnp.concatenate([flip[:B], flip[B : 2 * B]], axis=1)
         return carry
 
     lax.fori_loop(0, count, backward, 0)
-
-
-def imaging(x_cat, goal, weights, dose):
+    out = dot_full(u_buf[...], rc_ref[...])
+    acc_ref[...] = jnp.sum((h_ref[...] * out).reshape(count, B, 128), axis=0)
+
+
+def imaging(x_cat, goal, h_cat, weights, dose):
     count = weights.shape[0]
     tables = imaging_tables()
     vmem = pl.BlockSpec(memory_space=pltpu.VMEM)
     smem = pl.BlockSpec(memory_space=pltpu.SMEM)
     return pl.pallas_call(
         imaging_body,
-        out_shape=jax.ShapeDtypeStruct((count, P_SIZE, 128), jnp.float32),
-        in_specs=[vmem, vmem, smem, smem] + [vmem] * 6,
+        out_shape=jax.ShapeDtypeStruct((B, 128), jnp.float32),
+        in_specs=[vmem, vmem, vmem, smem, smem] + [vmem] * 4,
         out_specs=vmem,
         scratch_shapes=[
             pltpu.VMEM((count * B, 2 * P_SIZE), jnp.float32),
             pltpu.VMEM((count, P_SIZE, 2 * P_SIZE), jnp.float32),
             pltpu.VMEM((P_SIZE, P_SIZE), jnp.float32),
+            pltpu.VMEM((count * B, 2 * P_SIZE), jnp.float32),
         ],
-    )(x_cat, goal, weights, dose, *tables)
+    )(x_cat, goal, h_cat, weights, dose, *tables)
 
 
 def xor_partners(count):
@@ -240,26 +233,21 @@
         x_re = h_re[:, None] * spec_re[None] - h_im[:, None] * spec_im[None]
         x_im = h_re[:, None] * spec_im[None] + h_im[:, None] * spec_re[None]
         count = h_re.shape[0]
-        outs = []
+        twice = (2.0 * weights)[:, None, None]
+        ht_re = jnp.swapaxes(h_re, 1, 2) * twice
+        ht_im = jnp.swapaxes(h_im, 1, 2) * twice
+        h_cat = jnp.concatenate([ht_re, ht_re, ht_im, -ht_im], axis=-1).reshape(count * B, 128)
+        grads_re = []
+        grads_im = []
         for j in range(per_dev):
             x_cat = jnp.concatenate(
                 [x_re[:, j], x_im[:, j], jnp.zeros((count, B, 128 - 2 * B), jnp.float32)], axis=-1
             ).reshape(count * B, 128)
-            outs.append(imaging(x_cat, goal[j], weights, corner_dose))
-        u_all = jnp.stack(outs, axis=1)
-        u_re = u_all[..., :B]
-        u_im = u_all[..., B : 2 * B]
-
-    with jax.named_scope("adjoint_spectra"):
-        out_re = jnp.einsum("bx,knxc->knbc", cos_tab, u_re, precision=precise) - jnp.einsum(
-            "bx,knxc->knbc", sin_tab, u_im, precision=precise
-        )
-        out_im = jnp.einsum("bx,knxc->knbc", cos_tab, u_im, precision=precise) + jnp.einsum(
-            "bx,knxc->knbc", sin_tab, u_re, precision=precise
-        )
-        twice = (2.0 * weights)[:, None, None, None]
-        grad_re = jnp.sum(twice * (h_re[:, None] * out_re + h_im[:, None] * out_im), axis=0)
-        grad_im = jnp.sum(twice * (h_re[:, None] * out_im - h_im[:, None] * out_re), axis=0)
+            acc = imaging(x_cat, goal[j], h_cat, weights, corner_dose)
+            grads_re.append((acc[:, :B] + acc[:, 2 * B : 3 * B]).T)
+            grads_im.append((acc[:, B : 2 * B] + acc[:, 3 * B :]).T)
+        grad_re = jnp.stack(grads_re)
+        grad_im = jnp.stack(grads_im)
 
     with jax.named_scope("gradient_exchange"):
         own_grad = jnp.stack([grad_re, grad_im], axis=1)

time: 68.7 us -> 59.3 us (0.86)
  matrix products: 28.3 us -> 8.21 us
  Pallas kernels: 11.7 us -> 18.6 us
  other arithmetic: 4.27 us -> 6.28 us
  local copies, waits for them, and re-layouts: 3.37 us -> 5.24 us
    dot_general x4 -> x0, matrix products: 12.9 us -> none  [the longest x1 4.12 us: on_device(): jnp.einsum('bx,knxc->knbc', cos_tab, u_re, precision=precise)]
    pallas_call x1, Pallas kernels: 11.7 us -> 18.6 us  [imaging(): pl.pallas_call(imaging_body, out_shape=jax.ShapeDtypeStruct((B, 128), jnp...]
    unnamed x22 -> x24, local copies, waits for them, and re-layouts: 0.28 us -> 3.64 us
    dot_general x2, matrix products: 2.08 us -> 0.4 us  [spectra(): rows_im = jnp.einsum('bx,nxy->nby', sin_tab, masks, precision=precise)]
    dot_general x2, matrix products: 1.9 us -> 0.32 us  [spectra(): jnp.einsum('nby,cy->nbc', rows_re, cos_tab, precision=precise)]
    dot_general x2, matrix products: 1.84 us -> 0.32 us  [spectra(): jnp.einsum('nby,cy->nbc', rows_re, sin_tab, precision=precise)]
    another operation x0 -> x1, other arithmetic: none -> 0.94 us  [on_device(): own_grad = jnp.stack([grad_re, grad_im], axis=1)]
    concatenate x0 -> x1, other arithmetic: none -> 0.9 us  [on_device(): jnp.concatenate([ht_re, ht_re, ht_im, -ht_im], axis=-1)]
  transfers between devices with their start and end apart: 8 -> 8, of which waited for: 3 -> 3; matrix products, arithmetic and copies ran while one was open for 16% -> 15% of each run, Pallas kernels for 0% -> 0%
where the time goes in v4:
time: 59.3 us; the launch traced here: 58.9 us
  Pallas kernels  18.6 us (31%)
  starting transfers between devices  12 us (20%)
  matrix products  8.21 us (14%)
  waiting for transfers between devices  6.93 us (12%)
  other arithmetic  6.28 us (11%)
  local copies, waits for them, and re-layouts  5.24 us (9%)
  between operations  1.73 us (3%)
    pallas_call x1, Pallas kernels, imaging(): pl.pallas_call(imaging_body, out_shape=jax.ShapeDtypeStruct((B, 128), jnp...  18.6 us
    ppermute x4, starting transfers between devices, gather_all(): got = lax.ppermute(x, axis, [(i, i ^ step) for i in range(count)])  5.75 us
    ppermute x3, starting transfers between devices, scatter_sum(): lax.ppermute(part, axis, [(i, i ^ step) for i in range(count)])  4.45 us
    unnamed x24, local copies, waits for them, and re-layouts  3.64 us
    ppermute x3, waiting for transfers between devices, scatter_sum(): lax.ppermute(part, axis, [(i, i ^ step) for i in range(count)])  3.26 us
    dot_general x2, matrix products, back_pixels(): jnp.einsum('nxc,cy->nxy', half_im, sin_tab, precision=precise)  2.54 us
    ppermute x1, waiting for transfers between devices, sum_all(): x = x + lax.ppermute(x, axis, [(i, i ^ step) for i in range(count)])  2.48 us
    ppermute x1, starting transfers between devices, sum_all(): x = x + lax.ppermute(x, axis, [(i, i ^ step) for i in range(count)])  1.77 us
  transfers between devices with their start and end apart: 8, of which 3 were waited for; matrix products, arithmetic and copies ran while one was open for 15% of the time, Pallas kernels for 0%

profile of v4, /device:TPU:0, one launch (start us, length us, event | category | flops | bytes accessed | tf_op | source)
XLA Modules:
  0.0 58.9 jit_solution(12927602861680705284)
XLA Ops:
  0.7 0.8 %copy-done.1 = f32[32,256]{1,0:T(8,128)S(1)} copy-done((f32[32,256]{1,0:T(8,128)S(1)}, f32[32,256]{1,0:T(8,128)}, u32[]{:S(2)}) %copy-start.1) | copy-done | bytes 32792
  1.4 1.1 %fusion.15 = f32[32,256]{1,0:T(8,128)S(1)} fusion(f32[32,256]{1,0:T(8,128)S(1)} %copy-done.1, bf16[1,256,256]{2,1,0:T(8,128)(2,1)} %param.15), kind=kOutput, calls=%fused_computation.37 | convolution fusion | flops 25165824 | bytes 196608 | tf_op jit(solution)/shard_map/master_spectra/bx,nxy->nby/dot_general | solution.py:38
  3.5 3.1 %collective-permute-start = (f32[1,2,32,32]{3,2,1,0:T(8,128)S(1)}, f32[1,2,32,32]{3,2,1,0:T(8,128)S(1)}, u32[]{:S(2)}, u32[]{:S(2)}) collective-permute-start(f32[1,2,32,32]{3,2,1,0:T(8,128)S(1)} %get-tuple-element.18), channel_id=1, source_target_pairs={{0,4},{4,0},{8,12},{12,8},{1,5},{5,1},{9,13},{13,9},{2,6},{6,2},{1... | collective-permute-start | bytes 24584 | tf_op jit(solution)/shard_map/master_spectra/ppermute | solution.py:164
  6.6 2.6 %collective-permute-start.1 = (f32[1,2,32,32]{3,2,1,0:T(8,128)S(1)}, f32[1,2,32,32]{3,2,1,0:T(8,128)S(1)}, u32[]{:S(2)}, u32[]{:S(2)}) collective-permute-start(f32[1,2,32,32]{3,2,1,0:T(8,128)S(1)} %get-tuple-element.18), channel_id=1, source_target_pairs={{0,8},{4,12},{8,0},{12,4},{1,9},{5,13},{9,1},{13,5},{2,10},{6,14},... | collective-permute-start | bytes 24584 | tf_op jit(solution)/shard_map/master_spectra/ppermute | solution.py:164
  9.9 0.5 copy-done.8
  10.6 0.6 %copy-done.10 = s32[2]{0:T(128)S(1)} copy-done((s32[2]{0:T(128)S(1)}, s32[2]{0:T(128)}, u32[]{:S(2)}) %copy-start.10) | copy-done | bytes 32
  11.3 0.6 dynamic_slice.26
  11.9 0.6 %fusion.50 = (s32[1,1]{1,0:T(1,128)}, s32[1,1]{1,0:T(1,128)}) fusion(s32[1,2]{1,0:T(1,128)S(1)} %constant_dynamic-slice_fusion.3), kind=kLoop, calls=%fused_computation.117 | loop fusion | bytes 16 | tf_op jit(solution)/shard_map/tile_spectra/slice | solution.py:30
  12.5 0.9 %copy-done.7 = bf16[2,256,256]{2,1,0:T(8,128)(2,1)S(1)} copy-done((bf16[2,256,256]{2,1,0:T(8,128)(2,1)S(1)}, bf16[2,256,256]{2,1,0:T(8,128)(2,1)}, u32[]{:S(2)}) %copy-start.7) | copy-done | bytes 262168
  13.5 0.7 %bitcast_convert_fusion.goal_ref = f32[256,256]{1,0:T(8,128)} fusion(bf16[2,256,256]{2,1,0:T(8,128)(2,1)S(1)} %copy-done.7, s32[]{:T(128)S(6)} %select_n.103), kind=kLoop, calls=%fused_computation.34 | loop fusion | flops 65536 | bytes 393220 | tf_op jit(solution)/shard_map/imaging_kernel/squeeze | solution.py:246
  14.3 0.5 copy-done.9
  15.1 0.7 %compare_convert_fusion.1 = (f32[4]{0:T(128)S(1)}, pred[4]{0:T(512)(128)(4,1)S(1)}) fusion(s32[]{:T(128)} %bitcast.10, s32[]{:T(128)S(6)} %xor.17), kind=kLoop, calls=%fused_computation.92 | loop fusion | flops 12 | bytes 28 | tf_op jit(solution)/shard_map/tile_spectra/convert_element_type | solution.py:218
  15.8 1.3 %broadcast_multiply_fusion.3 = (s32[32]{0:T(128)S(1)}, s32[32]{0:T(128)S(1)}) fusion(s32[]{:T(128)} %bitcast.9, s32[]{:T(128)} %bitcast.8), kind=kLoop, calls=%fused_computation.111 | loop fusion | flops 96 | bytes 264 | tf_op jit(solution)/shard_map/tile_spectra/mul | solution.py:31
  17.1 0.9 %pad_maximum_fusion = f32[12,32,128]{2,1,0:T(8,128)} fusion(f32[12,32,32]{2,1,0:T(8,128)S(1)} %get-tuple-element.4, f32[12,32,32]{2,1,0:T(8,128)S(1)} %get-tuple-element.5, f32[12,32,32]{2,1,0:T(8,128)S(1)} %fusion.12), kind=kLoop, calls=%fused_computation.29 | loop fusion | flops 147456 | bytes 344064 | tf_op jit(solution)/shard_map/imaging_kernel/concatenate | solution.py:239
  19.3 0.8 %maximum_maximum_fusion.x_ref = f32[384,128]{1,0:T(8,128)} fusion(f32[384,32]{1,0:T(8,128)S(1)} %get-tuple-element.7, f32[384,32]{1,0:T(8,128)S(1)} %get-tuple-element.6, f32[128]{0:T(128)S(1)} %pad.10.clone), kind=kLoop, calls=%fused_computation.28 | loop fusion | flops 98304 | bytes 295424 | tf_op jit(solution)/shard_map/imaging_kernel/concatenate | solution.py:243
  20.1 18.6 %imaging_kernel.1 = f32[32,128]{1,0:T(8,128)} custom-call(f32[384,128]{1,0:T(8,128)} %maximum_maximum_fusion.x_ref, f32[256,256]{1,0:T(8,128)} %bitcast_convert_fusion.goal_ref, f32[384,128]{1,0:T(8,128)} %bitcast.176, f32[12]{0:T(128)} %bitcast.184, f32[1]{0:T(128)S(6)} %copy.35.dose_ref, f32[128,512]{1,0:T(8,128)} %constant.93.clone.rw_ref, ...), custom_call_target="tpu_custom_call" | custom-call | tf_op jit(solution)/shard_map/imaging_kernel/pallas_call | solution.py:139
  38.7 0.9 %fusion.38 = (f32[1,1,32,32]{2,3,1,0:T(8,128)S(1)}, f32[1,1,32,32]{2,3,1,0:T(8,128)S(1)}) fusion(f32[32,128]{1,0:T(8,128)} %imaging_kernel.1), kind=kLoop, calls=%fused_computation.83 | loop fusion | flops 2048 | bytes 24576 | tf_op jit(solution)/shard_map/gradient_exchange/stack;imaging_kernel/stack | solution.py:253
  39.8 1.2 %collective-permute-done.3 = f32[1,2,32,32]{2,3,1,0:T(8,128)S(1)} collective-permute-done((f32[1,2,32,32]{2,3,1,0:T(8,128)S(1)}, f32[1,2,32,32]{2,3,1,0:T(8,128)S(1)}, u32[]{:S(2)}, u32[]{:S(2)}) %collective-permute-start.3) | collective-permute-done | bytes 8224 | tf_op jit(solution)/shard_map/gradient_exchange/ppermute | solution.py:164
  41.0 1.8 %collective-permute-start.4 = (f32[2,2,32,32]{2,3,0,1:T(8,128)S(1)}, f32[2,2,32,32]{2,3,0,1:T(8,128)S(1)}, u32[]{:S(2)}, u32[]{:S(2)}) collective-permute-start(f32[2,2,32,32]{2,3,0,1:T(8,128)S(1)} %select_add_fusion), channel_id=1, source_target_pairs={{0,2},{2,0},{1,3},{3,1},{4,6},{6,4},{5,7},{7,5},{8,10},{10,8},{9,1... | collective-permute-start | bytes 49160 | tf_op jit(solution)/shard_map/gradient_exchange/ppermute | solution.py:175
  42.9 2.5 %collective-permute-done.4 = f32[2,2,32,32]{2,3,0,1:T(8,128)S(1)} collective-permute-done((f32[2,2,32,32]{2,3,0,1:T(8,128)S(1)}, f32[2,2,32,32]{2,3,0,1:T(8,128)S(1)}, u32[]{:S(2)}, u32[]{:S(2)}) %collective-permute-start.4) | collective-permute-done | bytes 16416 | tf_op jit(solution)/shard_map/gradient_exchange/ppermute | solution.py:175
  45.8 0.2 multiply_add_fusion
  46.3 1.0 %collective-permute-start.5 = (f32[1,2,32,32]{3,2,1,0:T(8,128)S(1)}, f32[1,2,32,32]{3,2,1,0:T(8,128)S(1)}, u32[]{:S(2)}, u32[]{:S(2)}) collective-permute-start(f32[1,2,32,32]{3,2,1,0:T(8,128)S(1)} %get-tuple-element.10), channel_id=1, source_target_pairs={{0,4},{4,0},{8,12},{12,8},{1,5},{5,1},{9,13},{13,9},{2,6},{6,2},{1... | collective-permute-start | bytes 24584 | tf_op jit(solution)/shard_map/gradient_exchange/ppermute | solution.py:186
  47.3 3.5 %collective-permute-start.6 = (f32[1,2,32,32]{3,2,1,0:T(8,128)S(1)}, f32[1,2,32,32]{3,2,1,0:T(8,128)S(1)}, u32[]{:S(2)}, u32[]{:S(2)}) collective-permute-start(f32[1,2,32,32]{3,2,1,0:T(8,128)S(1)} %get-tuple-element.12), channel_id=1, source_target_pairs={{0,8},{4,12},{8,0},{12,4},{1,9},{5,13},{9,1},{13,5},{2,10},{6,14},... | collective-permute-start | bytes 24584 | tf_op jit(solution)/shard_map/gradient_exchange/ppermute | solution.py:186
  51.2 0.6 %fusion.55 = f32[2,256,256]{2,1,0:T(8,128)S(1)} fusion(f32[2,256,32]{1,2,0:T(8,128)S(1)} %fusion.2, f32[32,256,1]{1,0,2:T(8,128)S(1)} %copy-done.6), kind=kOutput, calls=%fused_computation.122 | convolution fusion | flops 50331648 | bytes 622592 | tf_op jit(solution)/shard_map/pixel_gradients/nxc,cy->nxy/dot_general | solution.py:56
  51.8 1.4 %convolution_add_fusion = f32[2,256,256]{2,1,0:T(8,128)} fusion(f32[2,256,256]{2,1,0:T(8,128)S(1)} %fusion.55, f32[2,256,32]{1,2,0:T(8,128)S(1)} %fusion.1, f32[32,256,1]{1,0,2:T(8,128)S(1)} %copy-done.5), kind=kOutput, calls=%fused_computation | convolution fusion | flops 50462720 | bytes 1146880 | tf_op jit(solution)/shard_map/pixel_gradients/nxc,cy->nxy/dot_general | solution.py:56
  53.2 3.3 %collective-permute-done.7 = f32[1,2,32,32]{3,2,1,0:T(8,128)S(1)} collective-permute-done((f32[1,2,32,32]{3,2,1,0:T(8,128)S(1)}, f32[1,2,32,32]{3,2,1,0:T(8,128)S(1)}, u32[]{:S(2)}, u32[]{:S(2)}) %collective-permute-start.7) | collective-permute-done | bytes 8224 | tf_op jit(solution)/shard_map/gradient_exchange/ppermute | solution.py:186
  56.5 0.2 fusion.40
  56.7 0.2 fusion.41
  56.9 0.2 fusion.3
  57.1 0.2 fusion.4
  57.4 0.4 fusion.56
  57.8 1.1 %fusion = f32[1,256,256]{2,1,0:T(8,128)} fusion(f32[256,256]{1,0:T(8,128)S(1)} %fusion.56, f32[256,32]{0,1:T(8,128)S(1)} %fusion.3, f32[32,256]{1,0:T(8,128)S(1)} %copy-done.2), kind=kOutput, calls=%fused_computation.2 | convolution fusion | flops 25231360 | bytes 589824 | tf_op jit(solution)/shard_map/pixel_gradients/nxc,cy->nxy/dot_general | solution.py:56
  (67 shorter events, 4.2 us)
Async XLA Ops:
  0.6 8.5 %copy-start = (bf16[2,256,256]{2,1,0:T(8,128)(2,1)S(1)}, bf16[2,256,256]{2,1,0:T(8,128)(2,1)}, u32[]{:S(2)}) copy-start(bf16[2,256,256]{2,1,0:T(8,128)(2,1)} %param.14) | copy-start | bytes 786436
  0.6 0.8 %copy-start.1 = (f32[32,256]{1,0:T(8,128)S(1)}, f32[32,256]{1,0:T(8,128)}, u32[]{:S(2)}) copy-start(f32[32,256]{1,0:T(8,128)} %constant.91.clone) | copy-start | bytes 98308
  0.7 1.9 %copy-start.2 = (f32[32,256]{1,0:T(8,128)S(1)}, f32[32,256]{1,0:T(8,128)}, u32[]{:S(2)}) copy-start(f32[32,256]{1,0:T(8,128)} %constant.92.clone) | copy-start | bytes 98308
  0.7 1.9 %copy-start.3 = (bf16[1,256,256]{2,1,0:T(8,128)(2,1)S(1)}, bf16[1,256,256]{2,1,0:T(8,128)(2,1)}, u32[]{:S(2)}) copy-start(bf16[1,256,256]{2,1,0:T(8,128)(2,1)} %param.15) | copy-start | bytes 393220
  3.3 9.2 %copy-start.4 = (f32[1,12,2,32,32]{4,3,2,1,0:T(8,128)S(1)}, f32[1,12,2,32,32]{4,3,2,1,0:T(8,128)}, u32[]{:S(2)}) copy-start(f32[1,12,2,32,32]{4,3,2,1,0:T(8,128)} %param.19) | copy-start | bytes 294916
  3.5 15.3 %collective-permute-start = (f32[1,2,32,32]{3,2,1,0:T(8,128)S(1)}, f32[1,2,32,32]{3,2,1,0:T(8,128)S(1)}, u32[]{:S(2)}, u32[]{:S(2)}) collective-permute-start(f32[1,2,32,32]{3,2,1,0:T(8,128)S(1)} %get-tuple-element.18), channel_id=1, source_target_pairs={{0,4},{4,0},{8,12},{12,8},{1,5},{5,1},{9,13},{13,9},{2,6},{6,2},{1... | collective-permute-start | bytes 24584 | tf_op jit(solution)/shard_map/master_spectra/ppermute | solution.py:164
  6.6 12.2 %collective-permute-start.1 = (f32[1,2,32,32]{3,2,1,0:T(8,128)S(1)}, f32[1,2,32,32]{3,2,1,0:T(8,128)S(1)}, u32[]{:S(2)}, u32[]{:S(2)}) collective-permute-start(f32[1,2,32,32]{3,2,1,0:T(8,128)S(1)} %get-tuple-element.18), channel_id=1, source_target_pairs={{0,8},{4,12},{8,0},{12,4},{1,9},{5,13},{9,1},{13,5},{2,10},{6,14},... | collective-permute-start | bytes 24584 | tf_op jit(solution)/shard_map/master_spectra/ppermute | solution.py:164
  9.2 9.6 %collective-permute-start.2 = (f32[1,2,32,32]{3,2,1,0:T(8,128)S(1)}, f32[1,2,32,32]{3,2,1,0:T(8,128)S(1)}, u32[]{:S(2)}, u32[]{:S(2)}) collective-permute-start(f32[1,2,32,32]{3,2,1,0:T(8,128)S(1)} %get-tuple-element.18), channel_id=1, source_target_pairs={{0,12},{4,8},{8,4},{12,0},{1,13},{5,9},{9,5},{13,1},{2,14},{6,10},... | collective-permute-start | bytes 24584 | tf_op jit(solution)/shard_map/master_spectra/ppermute | solution.py:164
  9.8 0.7 %copy-start.8 = (s32[2,2]{1,0:T(2,128)S(1)}, s32[2,2]{1,0:T(2,128)}, u32[]{:S(2)}) copy-start(s32[2,2]{1,0:T(2,128)} %param.18) | copy-start | bytes 52
  10.6 0.7 %copy-start.10 = (s32[2]{0:T(128)S(1)}, s32[2]{0:T(128)}, u32[]{:S(2)}) copy-start(s32[2]{0:T(128)} %param.17) | copy-start | bytes 28
  12.5 1.0 %copy-start.7 = (bf16[2,256,256]{2,1,0:T(8,128)(2,1)S(1)}, bf16[2,256,256]{2,1,0:T(8,128)(2,1)}, u32[]{:S(2)}) copy-start(bf16[2,256,256]{2,1,0:T(8,128)(2,1)} %param.16) | copy-start | bytes 786436
  14.2 0.7 %copy-start.9 = (f32[1,12]{1,0:T(1,128)S(1)}, f32[1,12]{1,0:T(1,128)}, u32[]{:S(2)}) copy-start(f32[1,12]{1,0:T(1,128)} %param.20) | copy-start | bytes 148
  39.7 1.3 %collective-permute-start.3 = (f32[1,2,32,32]{2,3,1,0:T(8,128)S(1)}, f32[1,2,32,32]{2,3,1,0:T(8,128)S(1)}, u32[]{:S(2)}, u32[]{:S(2)}) collective-permute-start(f32[1,2,32,32]{2,3,1,0:T(8,128)S(1)} %get-tuple-element.16), channel_id=1, source_target_pairs={{0,1},{1,0},{2,3},{3,2},{4,5},{5,4},{6,7},{7,6},{8,9},{9,8},{10,11... | collective-permute-start | bytes 24584 | tf_op jit(solution)/shard_map/gradient_exchange/ppermute | solution.py:164
  41.0 4.3 %collective-permute-start.4 = (f32[2,2,32,32]{2,3,0,1:T(8,128)S(1)}, f32[2,2,32,32]{2,3,0,1:T(8,128)S(1)}, u32[]{:S(2)}, u32[]{:S(2)}) collective-permute-start(f32[2,2,32,32]{2,3,0,1:T(8,128)S(1)} %select_add_fusion), channel_id=1, source_target_pairs={{0,2},{2,0},{1,3},{3,1},{4,6},{6,4},{5,7},{7,5},{8,10},{10,8},{9,1... | collective-permute-start | bytes 49160 | tf_op jit(solution)/shard_map/gradient_exchange/ppermute | solution.py:175
  42.9 2.6 %copy-start.5 = (f32[32,256,1]{1,0,2:T(8,128)S(1)}, f32[32,256,1]{1,0,2:T(8,128)}, u32[]{:S(2)}) copy-start(f32[32,256,1]{1,0,2:T(8,128)} %constant.106) | copy-start | bytes 98308
  46.3 4.5 %copy-start.6 = (f32[32,256,1]{1,0,2:T(8,128)S(1)}, f32[32,256,1]{1,0,2:T(8,128)}, u32[]{:S(2)}) copy-start(f32[32,256,1]{1,0,2:T(8,128)} %constant.105) | copy-start | bytes 98308
  46.3 6.9 %collective-permute-start.5 = (f32[1,2,32,32]{3,2,1,0:T(8,128)S(1)}, f32[1,2,32,32]{3,2,1,0:T(8,128)S(1)}, u32[]{:S(2)}, u32[]{:S(2)}) collective-permute-start(f32[1,2,32,32]{3,2,1,0:T(8,128)S(1)} %get-tuple-element.10), channel_id=1, source_target_pairs={{0,4},{4,0},{8,12},{12,8},{1,5},{5,1},{9,13},{13,9},{2,6},{6,2},{1... | collective-permute-start | bytes 24584 | tf_op jit(solution)/shard_map/gradient_exchange/ppermute | solution.py:186
  47.3 5.9 %collective-permute-start.6 = (f32[1,2,32,32]{3,2,1,0:T(8,128)S(1)}, f32[1,2,32,32]{3,2,1,0:T(8,128)S(1)}, u32[]{:S(2)}, u32[]{:S(2)}) collective-permute-start(f32[1,2,32,32]{3,2,1,0:T(8,128)S(1)} %get-tuple-element.12), channel_id=1, source_target_pairs={{0,8},{4,12},{8,0},{12,4},{1,9},{5,13},{9,1},{13,5},{2,10},{6,14},... | collective-permute-start | bytes 24584 | tf_op jit(solution)/shard_map/gradient_exchange/ppermute | solution.py:186
  50.7 5.7 %collective-permute-start.7 = (f32[1,2,32,32]{3,2,1,0:T(8,128)S(1)}, f32[1,2,32,32]{3,2,1,0:T(8,128)S(1)}, u32[]{:S(2)}, u32[]{:S(2)}) collective-permute-start(f32[1,2,32,32]{3,2,1,0:T(8,128)S(1)} %get-tuple-element.11), channel_id=1, source_target_pairs={{0,12},{4,8},{8,4},{12,0},{1,13},{5,9},{9,5},{13,1},{2,14},{6,10},... | collective-permute-start | bytes 24584 | tf_op jit(solution)/shard_map/gradient_exchange/ppermute | solution.py:186

commit v5 on v4

--- a/solution.py
+++ b/solution.py
@@ -60,6 +60,26 @@
 
 def dot_full(a, b):
     return jnp.dot(a, b, precision=precise, preferred_element_type=jnp.float32)
+
+
+def dot_parts(a, b):
+    return jnp.dot(a, b, preferred_element_type=jnp.float32)
+
+
+def split_three(a):
+    hi = a.astype(jnp.bfloat16)
+    rest = a - hi.astype(jnp.float32)
+    mid = rest.astype(jnp.bfloat16)
+    lo = (rest - mid.astype(jnp.float32)).astype(jnp.bfloat16)
+    return hi, mid, lo
+
+
+def table_three(table):
+    hi = table.astype(jnp.bfloat16)
+    rest = table - hi.astype(np.float64)
+    mid = rest.astype(jnp.bfloat16)
+    lo = (rest - mid.astype(np.float64)).astype(jnp.bfloat16)
+    return hi, mid, lo
 
 
 def imaging_tables():
@@ -90,23 +110,29 @@
     ):
         right_c[:P_SIZE, col * B : (col + 1) * B] = top
         right_c[P_SIZE:, col * B : (col + 1) * B] = bottom
-    return [jnp.asarray(table, jnp.float32) for table in (right_w, left_a, right_b, right_c)]
+    a_hi, a_mid, a_lo = table_three(left_a[:, : 2 * B])
+    left_three = np.concatenate([a_hi, a_hi, a_mid, a_hi, a_lo, a_mid], axis=1)
+    b_hi, b_mid, b_lo = table_three(right_b)
+    right_hm = np.concatenate([b_hi, b_mid], axis=1)
+    right_lh = np.concatenate([b_lo, b_hi], axis=0)
+    out = [jnp.asarray(table, jnp.float32) for table in (right_w, right_c)]
+    return out + [jnp.asarray(table) for table in (left_three, right_hm, right_lh)]
 
 
 def imaging_body(
-    x_ref, goal_ref, h_ref, w_ref, dose_ref, rw_ref, la_ref, rb_ref, rc_ref,
+    x_ref, goal_ref, h_ref, w_ref, dose_ref, rw_ref, rc_ref, la_ref, rhm_ref, rlh_ref,
     acc_ref, w_buf, f_buf, i_buf, u_buf,
 ):
     count = f_buf.shape[0]
     w_buf[...] = dot_full(x_ref[...], rw_ref[...])
     i_buf[...] = jnp.zeros(i_buf.shape, jnp.float32)
-    pad = jnp.zeros((128 - 2 * B, 2 * P_SIZE), jnp.float32)
 
     def forward(k, carry):
         rows = w_buf[pl.ds(pl.multiple_of(k * B, B), B), :]
         swap = jnp.concatenate([-rows[:, P_SIZE:], rows[:, :P_SIZE]], axis=1)
-        stacked = jnp.concatenate([rows, swap, pad], axis=0)
-        field = dot_full(la_ref[...], stacked)
+        s_hi, s_mid, s_lo = split_three(jnp.concatenate([rows, swap], axis=0))
+        stacked = jnp.concatenate([s_hi, s_mid, s_hi, s_lo, s_hi, s_mid], axis=0)
+        field = dot_parts(la_ref[...], stacked)
         f_buf[k] = field
         power = field * field
         i_buf[...] += w_ref[k] * (power[:, :P_SIZE] + power[:, P_SIZE:])
@@ -121,7 +147,10 @@
     def backward(k, carry):
         sens = i_buf[...]
         weighted = f_buf[k] * jnp.concatenate([sens, sens], axis=1)
-        half = dot_full(weighted, rb_ref[...])
+        q_hi, q_mid, q_lo = split_three(weighted)
+        first = dot_parts(q_hi, rhm_ref[...]) + dot_parts(q_mid, rhm_ref[...])
+        rest = dot_parts(jnp.concatenate([q_hi, q_lo], axis=1), rlh_ref[...])
+        half = first[:, :128] + first[:, 128:] + rest
         flip = half.T
         u_buf[pl.ds(pl.multiple_of(k * B, B), B), :] = jnp.concatenate([flip[:B], flip[B : 2 * B]], axis=1)
         return carry
@@ -139,7 +168,7 @@
     return pl.pallas_call(
         imaging_body,
         out_shape=jax.ShapeDtypeStruct((B, 128), jnp.float32),
-        in_specs=[vmem, vmem, vmem, smem, smem] + [vmem] * 4,
+        in_specs=[vmem, vmem, vmem, smem, smem] + [vmem] * 5,
         out_specs=vmem,
         scratch_shapes=[
             pltpu.VMEM((count * B, 2 * P_SIZE), jnp.float32),

time: 59.3 us -> 54.1 us (0.912)
  Pallas kernels: 18.6 us -> 13.4 us
    pallas_call x1, Pallas kernels: 18.6 us -> 13.4 us  [imaging(): pl.pallas_call(imaging_body, out_shape=jax.ShapeDtypeStruct((B, 128), jnp...]
  transfers between devices with their start and end apart: 8 -> 8, of which waited for: 3 -> 3; matrix products, arithmetic and copies ran while one was open for 15% -> 16% of each run, Pallas kernels for 0% -> 0%
where the time goes in v5:
time: 54.1 us; the launch traced here: 53.7 us
  Pallas kernels  13.4 us (25%)
  starting transfers between devices  12 us (22%)
  matrix products  8.2 us (15%)
  waiting for transfers between devices  6.93 us (13%)
  other arithmetic  6.28 us (12%)
  local copies, waits for them, and re-layouts  5.24 us (10%)
  between operations  1.73 us (3%)
    pallas_call x1, Pallas kernels, imaging(): pl.pallas_call(imaging_body, out_shape=jax.ShapeDtypeStruct((B, 128), jnp...  13.4 us
    ppermute x4, starting transfers between devices, gather_all(): got = lax.ppermute(x, axis, [(i, i ^ step) for i in range(count)])  5.75 us
    ppermute x3, starting transfers between devices, scatter_sum(): lax.ppermute(part, axis, [(i, i ^ step) for i in range(count)])  4.46 us
    unnamed x24, local copies, waits for them, and re-layouts  3.64 us
    ppermute x3, waiting for transfers between devices, scatter_sum(): lax.ppermute(part, axis, [(i, i ^ step) for i in range(count)])  3.27 us
    dot_general x2, matrix products, back_pixels(): jnp.einsum('nxc,cy->nxy', half_im, sin_tab, precision=precise)  2.53 us
    ppermute x1, waiting for transfers between devices, sum_all(): x = x + lax.ppermute(x, axis, [(i, i ^ step) for i in range(count)])  2.48 us
    ppermute x1, starting transfers between devices, sum_all(): x = x + lax.ppermute(x, axis, [(i, i ^ step) for i in range(count)])  1.78 us
  transfers between devices with their start and end apart: 8, of which 3 were waited for; matrix products, arithmetic and copies ran while one was open for 16% of the time, Pallas kernels for 0%

profile of v5, /device:TPU:0, one launch (start us, length us, event | category | flops | bytes accessed | tf_op | source)
XLA Modules:
  0.0 53.7 jit_solution(14117954726569246456)
XLA Ops:
  0.7 0.8 %copy-done.1 = f32[32,256]{1,0:T(8,128)S(1)} copy-done((f32[32,256]{1,0:T(8,128)S(1)}, f32[32,256]{1,0:T(8,128)}, u32[]{:S(2)}) %copy-start.1) | copy-done | bytes 32792
  1.4 1.1 %fusion.15 = f32[32,256]{1,0:T(8,128)S(1)} fusion(f32[32,256]{1,0:T(8,128)S(1)} %copy-done.1, bf16[1,256,256]{2,1,0:T(8,128)(2,1)} %param.16), kind=kOutput, calls=%fused_computation.37 | convolution fusion | flops 25165824 | bytes 196608 | tf_op jit(solution)/shard_map/master_spectra/bx,nxy->nby/dot_general | solution.py:38
  3.5 3.1 %collective-permute-start = (f32[1,2,32,32]{3,2,1,0:T(8,128)S(1)}, f32[1,2,32,32]{3,2,1,0:T(8,128)S(1)}, u32[]{:S(2)}, u32[]{:S(2)}) collective-permute-start(f32[1,2,32,32]{3,2,1,0:T(8,128)S(1)} %get-tuple-element.18), channel_id=1, source_target_pairs={{0,4},{4,0},{8,12},{12,8},{1,5},{5,1},{9,13},{13,9},{2,6},{6,2},{1... | collective-permute-start | bytes 24584 | tf_op jit(solution)/shard_map/master_spectra/ppermute | solution.py:193
  6.6 2.6 %collective-permute-start.1 = (f32[1,2,32,32]{3,2,1,0:T(8,128)S(1)}, f32[1,2,32,32]{3,2,1,0:T(8,128)S(1)}, u32[]{:S(2)}, u32[]{:S(2)}) collective-permute-start(f32[1,2,32,32]{3,2,1,0:T(8,128)S(1)} %get-tuple-element.18), channel_id=1, source_target_pairs={{0,8},{4,12},{8,0},{12,4},{1,9},{5,13},{9,1},{13,5},{2,10},{6,14},... | collective-permute-start | bytes 24584 | tf_op jit(solution)/shard_map/master_spectra/ppermute | solution.py:193
  9.9 0.5 copy-done.8
  10.6 0.6 %copy-done.10 = s32[2]{0:T(128)S(1)} copy-done((s32[2]{0:T(128)S(1)}, s32[2]{0:T(128)}, u32[]{:S(2)}) %copy-start.10) | copy-done | bytes 32
  11.3 0.6 %dynamic_slice.26 = s32[1]{0:T(128)} dynamic-slice(s32[2]{0:T(128)S(1)} %copy-done.10, s32[]{:T(128)S(6)} %select_n.103), dynamic_slice_sizes={1} | dynamic-slice | bytes 12 | tf_op jit(solution)/shard_map/tile_spectra/dynamic_slice | solution.py:243
  11.9 0.6 %fusion.50 = (s32[1,1]{1,0:T(1,128)}, s32[1,1]{1,0:T(1,128)}) fusion(s32[1,2]{1,0:T(1,128)S(1)} %constant_dynamic-slice_fusion.3), kind=kLoop, calls=%fused_computation.117 | loop fusion | bytes 16 | tf_op jit(solution)/shard_map/tile_spectra/slice | solution.py:30
  12.5 0.9 %copy-done.7 = bf16[2,256,256]{2,1,0:T(8,128)(2,1)S(1)} copy-done((bf16[2,256,256]{2,1,0:T(8,128)(2,1)S(1)}, bf16[2,256,256]{2,1,0:T(8,128)(2,1)}, u32[]{:S(2)}) %copy-start.7) | copy-done | bytes 262168
  13.5 0.7 %bitcast_convert_fusion.goal_ref = f32[256,256]{1,0:T(8,128)} fusion(bf16[2,256,256]{2,1,0:T(8,128)(2,1)S(1)} %copy-done.7, s32[]{:T(128)S(6)} %select_n.103), kind=kLoop, calls=%fused_computation.34 | loop fusion | flops 65536 | bytes 393220 | tf_op jit(solution)/shard_map/imaging_kernel/squeeze | solution.py:275
  14.3 0.5 copy-done.9
  15.1 0.7 %compare_convert_fusion.1 = (f32[4]{0:T(128)S(1)}, pred[4]{0:T(512)(128)(4,1)S(1)}) fusion(s32[]{:T(128)} %bitcast.10, s32[]{:T(128)S(6)} %xor.17), kind=kLoop, calls=%fused_computation.92 | loop fusion | flops 12 | bytes 28 | tf_op jit(solution)/shard_map/tile_spectra/convert_element_type | solution.py:247
  15.8 1.3 %broadcast_multiply_fusion.3 = (s32[32]{0:T(128)S(1)}, s32[32]{0:T(128)S(1)}) fusion(s32[]{:T(128)} %bitcast.9, s32[]{:T(128)} %bitcast.8), kind=kLoop, calls=%fused_computation.111 | loop fusion | flops 96 | bytes 264 | tf_op jit(solution)/shard_map/tile_spectra/mul | solution.py:31
  17.1 0.9 %pad_maximum_fusion = f32[12,32,128]{2,1,0:T(8,128)} fusion(f32[12,32,32]{2,1,0:T(8,128)S(1)} %get-tuple-element.4, f32[12,32,32]{2,1,0:T(8,128)S(1)} %get-tuple-element.5, f32[12,32,32]{2,1,0:T(8,128)S(1)} %fusion.12), kind=kLoop, calls=%fused_computation.29 | loop fusion | flops 147456 | bytes 344064 | tf_op jit(solution)/shard_map/imaging_kernel/concatenate | solution.py:268
  19.3 0.8 %maximum_maximum_fusion.x_ref = f32[384,128]{1,0:T(8,128)} fusion(f32[384,32]{1,0:T(8,128)S(1)} %get-tuple-element.7, f32[384,32]{1,0:T(8,128)S(1)} %get-tuple-element.6, f32[128]{0:T(128)S(1)} %pad.10.clone), kind=kLoop, calls=%fused_computation.28 | loop fusion | flops 98304 | bytes 295424 | tf_op jit(solution)/shard_map/imaging_kernel/concatenate | solution.py:272
  20.1 13.4 %imaging_kernel.1 = f32[32,128]{1,0:T(8,128)} custom-call(f32[384,128]{1,0:T(8,128)} %maximum_maximum_fusion.x_ref, f32[256,256]{1,0:T(8,128)} %bitcast_convert_fusion.goal_ref, f32[384,128]{1,0:T(8,128)} %bitcast.176, f32[12]{0:T(128)} %bitcast.184, f32[1]{0:T(128)S(6)} %copy.36.dose_ref, f32[128,512]{1,0:T(8,128)} %constant.95.clone.rw_ref, ...), custom_call_target="tpu_custom_call" | custom-call | tf_op jit(solution)/shard_map/imaging_kernel/pallas_call | solution.py:168
  33.5 0.9 %fusion.38 = (f32[1,1,32,32]{2,3,1,0:T(8,128)S(1)}, f32[1,1,32,32]{2,3,1,0:T(8,128)S(1)}) fusion(f32[32,128]{1,0:T(8,128)} %imaging_kernel.1), kind=kLoop, calls=%fused_computation.83 | loop fusion | flops 2048 | bytes 24576 | tf_op jit(solution)/shard_map/gradient_exchange/stack;imaging_kernel/stack | solution.py:282
  34.6 1.2 %collective-permute-done.3 = f32[1,2,32,32]{2,3,1,0:T(8,128)S(1)} collective-permute-done((f32[1,2,32,32]{2,3,1,0:T(8,128)S(1)}, f32[1,2,32,32]{2,3,1,0:T(8,128)S(1)}, u32[]{:S(2)}, u32[]{:S(2)}) %collective-permute-start.3) | collective-permute-done | bytes 8224 | tf_op jit(solution)/shard_map/gradient_exchange/ppermute | solution.py:193
  35.8 1.8 %collective-permute-start.4 = (f32[2,2,32,32]{2,3,0,1:T(8,128)S(1)}, f32[2,2,32,32]{2,3,0,1:T(8,128)S(1)}, u32[]{:S(2)}, u32[]{:S(2)}) collective-permute-start(f32[2,2,32,32]{2,3,0,1:T(8,128)S(1)} %select_add_fusion), channel_id=1, source_target_pairs={{0,2},{2,0},{1,3},{3,1},{4,6},{6,4},{5,7},{7,5},{8,10},{10,8},{9,1... | collective-permute-start | bytes 49160 | tf_op jit(solution)/shard_map/gradient_exchange/ppermute | solution.py:204
  37.7 2.5 %collective-permute-done.4 = f32[2,2,32,32]{2,3,0,1:T(8,128)S(1)} collective-permute-done((f32[2,2,32,32]{2,3,0,1:T(8,128)S(1)}, f32[2,2,32,32]{2,3,0,1:T(8,128)S(1)}, u32[]{:S(2)}, u32[]{:S(2)}) %collective-permute-start.4) | collective-permute-done | bytes 16416 | tf_op jit(solution)/shard_map/gradient_exchange/ppermute | solution.py:204
  40.6 0.2 multiply_add_fusion
  41.1 1.0 %collective-permute-start.5 = (f32[1,2,32,32]{3,2,1,0:T(8,128)S(1)}, f32[1,2,32,32]{3,2,1,0:T(8,128)S(1)}, u32[]{:S(2)}, u32[]{:S(2)}) collective-permute-start(f32[1,2,32,32]{3,2,1,0:T(8,128)S(1)} %get-tuple-element.10), channel_id=1, source_target_pairs={{0,4},{4,0},{8,12},{12,8},{1,5},{5,1},{9,13},{13,9},{2,6},{6,2},{1... | collective-permute-start | bytes 24584 | tf_op jit(solution)/shard_map/gradient_exchange/ppermute | solution.py:215
  42.1 3.5 %collective-permute-start.6 = (f32[1,2,32,32]{3,2,1,0:T(8,128)S(1)}, f32[1,2,32,32]{3,2,1,0:T(8,128)S(1)}, u32[]{:S(2)}, u32[]{:S(2)}) collective-permute-start(f32[1,2,32,32]{3,2,1,0:T(8,128)S(1)} %get-tuple-element.12), channel_id=1, source_target_pairs={{0,8},{4,12},{8,0},{12,4},{1,9},{5,13},{9,1},{13,5},{2,10},{6,14},... | collective-permute-start | bytes 24584 | tf_op jit(solution)/shard_map/gradient_exchange/ppermute | solution.py:215
  45.9 0.6 %fusion.55 = f32[2,256,256]{2,1,0:T(8,128)S(1)} fusion(f32[2,256,32]{1,2,0:T(8,128)S(1)} %fusion.2, f32[32,256,1]{1,0,2:T(8,128)S(1)} %copy-done.6), kind=kOutput, calls=%fused_computation.122 | convolution fusion | flops 50331648 | bytes 622592 | tf_op jit(solution)/shard_map/pixel_gradients/nxc,cy->nxy/dot_general | solution.py:56
  46.6 1.4 %convolution_add_fusion = f32[2,256,256]{2,1,0:T(8,128)} fusion(f32[2,256,256]{2,1,0:T(8,128)S(1)} %fusion.55, f32[2,256,32]{1,2,0:T(8,128)S(1)} %fusion.1, f32[32,256,1]{1,0,2:T(8,128)S(1)} %copy-done.5), kind=kOutput, calls=%fused_computation | convolution fusion | flops 50462720 | bytes 1146880 | tf_op jit(solution)/shard_map/pixel_gradients/nxc,cy->nxy/dot_general | solution.py:56
  48.0 3.3 %collective-permute-done.7 = f32[1,2,32,32]{3,2,1,0:T(8,128)S(1)} collective-permute-done((f32[1,2,32,32]{3,2,1,0:T(8,128)S(1)}, f32[1,2,32,32]{3,2,1,0:T(8,128)S(1)}, u32[]{:S(2)}, u32[]{:S(2)}) %collective-permute-start.7) | collective-permute-done | bytes 8224 | tf_op jit(solution)/shard_map/gradient_exchange/ppermute | solution.py:215
  51.3 0.2 fusion.40
  51.5 0.2 fusion.41
  51.7 0.2 fusion.3
  52.0 0.2 fusion.4
  52.2 0.4 fusion.56
  52.6 1.1 %fusion = f32[1,256,256]{2,1,0:T(8,128)} fusion(f32[256,256]{1,0:T(8,128)S(1)} %fusion.56, f32[256,32]{0,1:T(8,128)S(1)} %fusion.3, f32[32,256]{1,0:T(8,128)S(1)} %copy-done.2), kind=kOutput, calls=%fused_computation.2 | convolution fusion | flops 25231360 | bytes 589824 | tf_op jit(solution)/shard_map/pixel_gradients/nxc,cy->nxy/dot_general | solution.py:56
  (67 shorter events, 4.2 us)
Async XLA Ops:
  0.6 8.5 %copy-start = (bf16[2,256,256]{2,1,0:T(8,128)(2,1)S(1)}, bf16[2,256,256]{2,1,0:T(8,128)(2,1)}, u32[]{:S(2)}) copy-start(bf16[2,256,256]{2,1,0:T(8,128)(2,1)} %param.15) | copy-start | bytes 786436
  0.6 0.8 %copy-start.1 = (f32[32,256]{1,0:T(8,128)S(1)}, f32[32,256]{1,0:T(8,128)}, u32[]{:S(2)}) copy-start(f32[32,256]{1,0:T(8,128)} %constant.93.clone) | copy-start | bytes 98308
  0.7 1.9 %copy-start.2 = (f32[32,256]{1,0:T(8,128)S(1)}, f32[32,256]{1,0:T(8,128)}, u32[]{:S(2)}) copy-start(f32[32,256]{1,0:T(8,128)} %constant.94.clone) | copy-start | bytes 98308
  0.7 1.9 %copy-start.3 = (bf16[1,256,256]{2,1,0:T(8,128)(2,1)S(1)}, bf16[1,256,256]{2,1,0:T(8,128)(2,1)}, u32[]{:S(2)}) copy-start(bf16[1,256,256]{2,1,0:T(8,128)(2,1)} %param.16) | copy-start | bytes 393220
  3.3 9.2 %copy-start.4 = (f32[1,12,2,32,32]{4,3,2,1,0:T(8,128)S(1)}, f32[1,12,2,32,32]{4,3,2,1,0:T(8,128)}, u32[]{:S(2)}) copy-start(f32[1,12,2,32,32]{4,3,2,1,0:T(8,128)} %param.20) | copy-start | bytes 294916
  3.5 15.3 %collective-permute-start = (f32[1,2,32,32]{3,2,1,0:T(8,128)S(1)}, f32[1,2,32,32]{3,2,1,0:T(8,128)S(1)}, u32[]{:S(2)}, u32[]{:S(2)}) collective-permute-start(f32[1,2,32,32]{3,2,1,0:T(8,128)S(1)} %get-tuple-element.18), channel_id=1, source_target_pairs={{0,4},{4,0},{8,12},{12,8},{1,5},{5,1},{9,13},{13,9},{2,6},{6,2},{1... | collective-permute-start | bytes 24584 | tf_op jit(solution)/shard_map/master_spectra/ppermute | solution.py:193
  6.6 12.2 %collective-permute-start.1 = (f32[1,2,32,32]{3,2,1,0:T(8,128)S(1)}, f32[1,2,32,32]{3,2,1,0:T(8,128)S(1)}, u32[]{:S(2)}, u32[]{:S(2)}) collective-permute-start(f32[1,2,32,32]{3,2,1,0:T(8,128)S(1)} %get-tuple-element.18), channel_id=1, source_target_pairs={{0,8},{4,12},{8,0},{12,4},{1,9},{5,13},{9,1},{13,5},{2,10},{6,14},... | collective-permute-start | bytes 24584 | tf_op jit(solution)/shard_map/master_spectra/ppermute | solution.py:193
  9.2 9.6 %collective-permute-start.2 = (f32[1,2,32,32]{3,2,1,0:T(8,128)S(1)}, f32[1,2,32,32]{3,2,1,0:T(8,128)S(1)}, u32[]{:S(2)}, u32[]{:S(2)}) collective-permute-start(f32[1,2,32,32]{3,2,1,0:T(8,128)S(1)} %get-tuple-element.18), channel_id=1, source_target_pairs={{0,12},{4,8},{8,4},{12,0},{1,13},{5,9},{9,5},{13,1},{2,14},{6,10},... | collective-permute-start | bytes 24584 | tf_op jit(solution)/shard_map/master_spectra/ppermute | solution.py:193
  9.8 0.7 %copy-start.8 = (s32[2,2]{1,0:T(2,128)S(1)}, s32[2,2]{1,0:T(2,128)}, u32[]{:S(2)}) copy-start(s32[2,2]{1,0:T(2,128)} %param.19) | copy-start | bytes 52
  10.6 0.7 %copy-start.10 = (s32[2]{0:T(128)S(1)}, s32[2]{0:T(128)}, u32[]{:S(2)}) copy-start(s32[2]{0:T(128)} %param.18) | copy-start | bytes 28
  12.5 1.0 %copy-start.7 = (bf16[2,256,256]{2,1,0:T(8,128)(2,1)S(1)}, bf16[2,256,256]{2,1,0:T(8,128)(2,1)}, u32[]{:S(2)}) copy-start(bf16[2,256,256]{2,1,0:T(8,128)(2,1)} %param.17) | copy-start | bytes 786436
  14.2 0.7 %copy-start.9 = (f32[1,12]{1,0:T(1,128)S(1)}, f32[1,12]{1,0:T(1,128)}, u32[]{:S(2)}) copy-start(f32[1,12]{1,0:T(1,128)} %param.21) | copy-start | bytes 148
  34.5 1.3 %collective-permute-start.3 = (f32[1,2,32,32]{2,3,1,0:T(8,128)S(1)}, f32[1,2,32,32]{2,3,1,0:T(8,128)S(1)}, u32[]{:S(2)}, u32[]{:S(2)}) collective-permute-start(f32[1,2,32,32]{2,3,1,0:T(8,128)S(1)} %get-tuple-element.16), channel_id=1, source_target_pairs={{0,1},{1,0},{2,3},{3,2},{4,5},{5,4},{6,7},{7,6},{8,9},{9,8},{10,11... | collective-permute-start | bytes 24584 | tf_op jit(solution)/shard_map/gradient_exchange/ppermute | solution.py:193
  35.8 4.3 %collective-permute-start.4 = (f32[2,2,32,32]{2,3,0,1:T(8,128)S(1)}, f32[2,2,32,32]{2,3,0,1:T(8,128)S(1)}, u32[]{:S(2)}, u32[]{:S(2)}) collective-permute-start(f32[2,2,32,32]{2,3,0,1:T(8,128)S(1)} %select_add_fusion), channel_id=1, source_target_pairs={{0,2},{2,0},{1,3},{3,1},{4,6},{6,4},{5,7},{7,5},{8,10},{10,8},{9,1... | collective-permute-start | bytes 49160 | tf_op jit(solution)/shard_map/gradient_exchange/ppermute | solution.py:204
  37.7 2.6 %copy-start.5 = (f32[32,256,1]{1,0,2:T(8,128)S(1)}, f32[32,256,1]{1,0,2:T(8,128)}, u32[]{:S(2)}) copy-start(f32[32,256,1]{1,0,2:T(8,128)} %constant.109) | copy-start | bytes 98308
  41.1 4.5 %copy-start.6 = (f32[32,256,1]{1,0,2:T(8,128)S(1)}, f32[32,256,1]{1,0,2:T(8,128)}, u32[]{:S(2)}) copy-start(f32[32,256,1]{1,0,2:T(8,128)} %constant.108) | copy-start | bytes 98308
  41.1 6.9 %collective-permute-start.5 = (f32[1,2,32,32]{3,2,1,0:T(8,128)S(1)}, f32[1,2,32,32]{3,2,1,0:T(8,128)S(1)}, u32[]{:S(2)}, u32[]{:S(2)}) collective-permute-start(f32[1,2,32,32]{3,2,1,0:T(8,128)S(1)} %get-tuple-element.10), channel_id=1, source_target_pairs={{0,4},{4,0},{8,12},{12,8},{1,5},{5,1},{9,13},{13,9},{2,6},{6,2},{1... | collective-permute-start | bytes 24584 | tf_op jit(solution)/shard_map/gradient_exchange/ppermute | solution.py:215
  42.1 5.9 %collective-permute-start.6 = (f32[1,2,32,32]{3,2,1,0:T(8,128)S(1)}, f32[1,2,32,32]{3,2,1,0:T(8,128)S(1)}, u32[]{:S(2)}, u32[]{:S(2)}) collective-permute-start(f32[1,2,32,32]{3,2,1,0:T(8,128)S(1)} %get-tuple-element.12), channel_id=1, source_target_pairs={{0,8},{4,12},{8,0},{12,4},{1,9},{5,13},{9,1},{13,5},{2,10},{6,14},... | collective-permute-start | bytes 24584 | tf_op jit(solution)/shard_map/gradient_exchange/ppermute | solution.py:215
  45.5 5.7 %collective-permute-start.7 = (f32[1,2,32,32]{3,2,1,0:T(8,128)S(1)}, f32[1,2,32,32]{3,2,1,0:T(8,128)S(1)}, u32[]{:S(2)}, u32[]{:S(2)}) collective-permute-start(f32[1,2,32,32]{3,2,1,0:T(8,128)S(1)} %get-tuple-element.11), channel_id=1, source_target_pairs={{0,12},{4,8},{8,4},{12,0},{1,13},{5,9},{9,5},{13,1},{2,14},{6,10},... | collective-permute-start | bytes 24584 | tf_op jit(solution)/shard_map/gradient_exchange/ppermute | solution.py:215

commit v6 on v5

--- a/solution.py
+++ b/solution.py
@@ -216,6 +216,56 @@
     return total
 
 
+def partner_lists(count, kern_count):
+    lists = [[] for _ in range(kern_count)]
+    for step in range(1, count):
+        lists[step % kern_count].append(step)
+    return lists
+
+
+def chosen_step(lists, round_index, kern_pos):
+    pick = jnp.int32(-1)
+    for k, steps in enumerate(lists):
+        if round_index < len(steps):
+            pick = jnp.where(kern_pos == k, jnp.int32(steps[round_index]), pick)
+    return pick
+
+
+def gather_split(x, count, pos, kern_count, kern_pos):
+    size = x.shape[0]
+    lists = partner_lists(count, kern_count)
+    slot = jnp.arange(count * size, dtype=jnp.int32) // size
+    spread = lambda part: jnp.tile(part, (count, 1, 1, 1))
+    collected = jnp.zeros((count * size,) + x.shape[1:], x.dtype)
+    for r in range(max(len(steps) for steps in lists)):
+        pairs = []
+        for k, steps in enumerate(lists):
+            if r < len(steps):
+                pairs += [((t ^ steps[r]) * kern_count + k, t * kern_count + k) for t in range(count)]
+        got = lax.ppermute(x, ("tile", "kern"), pairs)
+        step = chosen_step(lists, r, kern_pos)
+        source = jnp.where(step >= 0, pos ^ step, -1)
+        collected = collected + jnp.where((slot == source)[:, None, None, None], spread(got), 0.0)
+    collected = sum_all(collected, "kern", kern_count, kern_pos)
+    return collected + jnp.where((slot == pos)[:, None, None, None], spread(x), 0.0)
+
+
+def scatter_split(x, count, pos, kern_count, kern_pos, size):
+    lists = partner_lists(count, kern_count)
+    own = lax.dynamic_slice_in_dim(x, pos * size, size, 0)
+    total = jnp.where(kern_pos == 0, own, 0.0)
+    for r in range(max(len(steps) for steps in lists)):
+        pairs = []
+        for k, steps in enumerate(lists):
+            if r < len(steps):
+                pairs += [(t * kern_count + k, (t ^ steps[r]) * kern_count + k) for t in range(count)]
+        step = chosen_step(lists, r, kern_pos)
+        target = jnp.where(step >= 0, pos ^ step, 0)
+        part = lax.dynamic_slice_in_dim(x, target * size, size, 0)
+        total = total + lax.ppermute(part, ("tile", "kern"), pairs)
+    return sum_all(total, "kern", kern_count, kern_pos)
+
+
 def on_device(
     tile_mask, master_mask, target, inst_master, inst_shift, kernels, kernel_weight, corner_dose
 ):
@@ -235,7 +285,10 @@
     with jax.named_scope("master_spectra"):
         own_re, own_im = spectra(master_mask.astype(jnp.float32), cos_tab, sin_tab)
         own = jnp.stack([own_re, own_im], axis=1)
-        every = gather_all(own, "tile", tile_count, tile_pos)
+        if xor_partners(tile_count) and xor_partners(kern_count) and tile_count > 2:
+            every = gather_split(own, tile_count, tile_pos, kern_count, kern_pos)
+        else:
+            every = gather_all(own, "tile", tile_count, tile_pos)
 
     with jax.named_scope("tile_spectra"):
         mine_mask = lax.dynamic_slice_in_dim(tile_mask, first, per_dev, 0)
@@ -291,7 +344,10 @@
             inst_master[:, None] == jnp.arange(region_masters, dtype=jnp.int32)[None, :]
         ).astype(jnp.float32)
         terms = jnp.sum(owner_pick[:, :, None, None, None] * own_back[:, None], axis=0)
-        mine_masters = scatter_sum(terms, "tile", tile_count, tile_pos, local_masters)
+        if xor_partners(tile_count) and xor_partners(kern_count) and tile_count > 2:
+            mine_masters = scatter_split(terms, tile_count, tile_pos, kern_count, kern_pos, local_masters)
+        else:
+            mine_masters = scatter_sum(terms, "tile", tile_count, tile_pos, local_masters)
 
     with jax.named_scope("pixel_gradients"):
         tile_grad = back_pixels(mine_tiles[:, 0], mine_tiles[:, 1], cos_tab, sin_tab)

time: 54.1 us -> 52.6 us (0.972)
  starting transfers between devices: 12 us -> 10.1 us
    ppermute x4 -> x1, starting transfers between devices: 5.75 us -> 0.08 us  [gather_all(): got = lax.ppermute(x, axis, [(i, i ^ step) for i in range(count)])]
    ppermute x1 -> x3, starting transfers between devices: 1.78 us -> 4.19 us  [sum_all(): x = x + lax.ppermute(x, axis, [(i, i ^ step) for i in range(count)])]
    ppermute x3 -> x4, starting transfers between devices: 4.46 us -> 5.87 us  [the longest x2 4.75 us: gather_split(): got = lax.ppermute(x, ('tile', 'kern'), pairs)]
    ppermute x1 -> x3, waiting for transfers between devices: 2.48 us -> 2.71 us  [sum_all(): x = x + lax.ppermute(x, axis, [(i, i ^ step) for i in range(count)])]
    ppermute x3 -> x4, waiting for transfers between devices: 3.27 us -> 3.23 us  [the longest x2 3.23 us: scatter_split(): total = total + lax.ppermute(part, ('tile', 'kern'), pairs)]
    ppermute x4 -> x1, waiting for transfers between devices: 1.19 us -> 1.18 us  [gather_all(): got = lax.ppermute(x, axis, [(i, i ^ step) for i in range(count)])]
  transfers between devices with their start and end apart: 8 -> 8, of which waited for: 3 -> 3; matrix products, arithmetic and copies ran while one was open for 16% -> 17% of each run, Pallas kernels for 0% -> 0%
where the time goes in v6:
time: 52.6 us; the launch traced here: 52.2 us
  Pallas kernels  13.4 us (25%)
  starting transfers between devices  10.1 us (19%)
  matrix products  8.22 us (16%)
  waiting for transfers between devices  7.12 us (14%)
  other arithmetic  6.35 us (12%)
  local copies, waits for them, and re-layouts  5.21 us (10%)
  between operations  1.8 us (3%)
    pallas_call x1, Pallas kernels, imaging(): pl.pallas_call(imaging_body, out_shape=jax.ShapeDtypeStruct((B, 128), jnp...  13.4 us
    ppermute x2, starting transfers between devices, gather_split(): got = lax.ppermute(x, ('tile', 'kern'), pairs)  4.75 us
    ppermute x3, starting transfers between devices, sum_all(): x = x + lax.ppermute(x, axis, [(i, i ^ step) for i in range(count)])  4.19 us
    unnamed x24, local copies, waits for them, and re-layouts  3.64 us
    ppermute x2, waiting for transfers between devices, scatter_split(): total = total + lax.ppermute(part, ('tile', 'kern'), pairs)  3.23 us
    ppermute x3, waiting for transfers between devices, sum_all(): x = x + lax.ppermute(x, axis, [(i, i ^ step) for i in range(count)])  2.71 us
    dot_general x2, matrix products, back_pixels(): jnp.einsum('nxc,cy->nxy', half_im, sin_tab, precision=precise)  2.54 us
    dot_general x2, matrix products, spectra(): rows_re = jnp.einsum('bx,nxy->nby', cos_tab, masks, precision=precise)  1.3 us
  transfers between devices with their start and end apart: 8, of which 3 were waited for; matrix products, arithmetic and copies ran while one was open for 17% of the time, Pallas kernels for 0%

profile of v6, /device:TPU:0, one launch (start us, length us, event | category | flops | bytes accessed | tf_op | source)
XLA Modules:
  0.0 52.2 jit_solution(9875954883605003185)
XLA Ops:
  0.7 0.8 %copy-done.1 = f32[32,256]{1,0:T(8,128)S(1)} copy-done((f32[32,256]{1,0:T(8,128)S(1)}, f32[32,256]{1,0:T(8,128)}, u32[]{:S(2)}) %copy-start.1) | copy-done | bytes 32792
  1.4 1.1 %fusion.15 = f32[32,256]{1,0:T(8,128)S(1)} fusion(f32[32,256]{1,0:T(8,128)S(1)} %copy-done.1, bf16[1,256,256]{2,1,0:T(8,128)(2,1)} %param.16), kind=kOutput, calls=%fused_computation.37 | convolution fusion | flops 25165824 | bytes 196608 | tf_op jit(solution)/shard_map/master_spectra/bx,nxy->nby/dot_general | solution.py:38
  3.5 4.1 %collective-permute-start = (f32[1,2,32,32]{3,2,1,0:T(8,128)S(1)}, f32[1,2,32,32]{3,2,1,0:T(8,128)S(1)}, u32[]{:S(2)}, u32[]{:S(2)}) collective-permute-start(f32[1,2,32,32]{3,2,1,0:T(8,128)S(1)} %get-tuple-element.17), channel_id=1, source_target_pairs={{8,0},{12,4},{0,8},{4,12},{5,1},{1,5},{13,9},{9,13},{10,2},{14,6},... | collective-permute-start | bytes 24584 | tf_op jit(solution)/shard_map/master_spectra/ppermute | solution.py:245
  7.6 0.7 %collective-permute-start.1 = (f32[1,2,32,32]{3,2,1,0:T(8,128)S(1)}, f32[1,2,32,32]{3,2,1,0:T(8,128)S(1)}, u32[]{:S(2)}, u32[]{:S(2)}) collective-permute-start(f32[1,2,32,32]{3,2,1,0:T(8,128)S(1)} %get-tuple-element.17), channel_id=1, source_target_pairs={{13,1},{9,5},{5,9},{1,13},{15,3},{11,7},{7,11},{3,15},{29,17},{25,... | collective-permute-start | bytes 24584 | tf_op jit(solution)/shard_map/master_spectra/ppermute | solution.py:245
  9.0 0.5 copy-done.8
  9.7 0.6 %copy-done.10 = s32[2]{0:T(128)S(1)} copy-done((s32[2]{0:T(128)S(1)}, s32[2]{0:T(128)}, u32[]{:S(2)}) %copy-start.10) | copy-done | bytes 32
  10.4 0.6 %dynamic_slice.23 = s32[1]{0:T(128)} dynamic-slice(s32[2]{0:T(128)S(1)} %copy-done.10, s32[]{:T(128)S(6)} %select_n.101), dynamic_slice_sizes={1} | dynamic-slice | bytes 12 | tf_op jit(solution)/shard_map/tile_spectra/dynamic_slice | solution.py:296
  11.0 0.6 %compare_convert_fusion.1 = (f32[4]{0:T(128)S(1)}, pred[4]{0:T(512)(128)(4,1)S(1)}) fusion(s32[]{:T(128)} %bitcast.10, s32[]{:T(128)S(6)} %axis_index.25), kind=kLoop, calls=%fused_computation.93 | loop fusion | flops 12 | bytes 28 | tf_op jit(solution)/shard_map/tile_spectra/convert_element_type | solution.py:300
  11.6 0.6 %fusion.50 = (s32[1,1]{1,0:T(1,128)}, s32[1,1]{1,0:T(1,128)}) fusion(s32[1,2]{1,0:T(1,128)S(1)} %constant_dynamic-slice_fusion.2), kind=kLoop, calls=%fused_computation.116 | loop fusion | bytes 16 | tf_op jit(solution)/shard_map/tile_spectra/slice | solution.py:30
  12.3 0.9 %copy-done.7 = bf16[2,256,256]{2,1,0:T(8,128)(2,1)S(1)} copy-done((bf16[2,256,256]{2,1,0:T(8,128)(2,1)S(1)}, bf16[2,256,256]{2,1,0:T(8,128)(2,1)}, u32[]{:S(2)}) %copy-start.7) | copy-done | bytes 262168
  13.2 0.7 %bitcast_convert_fusion.goal_ref = f32[256,256]{1,0:T(8,128)} fusion(bf16[2,256,256]{2,1,0:T(8,128)(2,1)S(1)} %copy-done.7, s32[]{:T(128)S(6)} %select_n.101), kind=kLoop, calls=%fused_computation.34 | loop fusion | flops 65536 | bytes 393220 | tf_op jit(solution)/shard_map/imaging_kernel/squeeze | solution.py:328
  14.0 0.5 %copy-done.9 = f32[1,12]{1,0:T(1,128)S(1)} copy-done((f32[1,12]{1,0:T(1,128)S(1)}, f32[1,12]{1,0:T(1,128)}, u32[]{:S(2)}) %copy-start.9) | copy-done | bytes 72
  14.9 0.9 %pad_maximum_fusion = f32[12,32,128]{2,1,0:T(8,128)} fusion(f32[12,32,32]{2,1,0:T(8,128)S(1)} %get-tuple-element.4, f32[12,32,32]{2,1,0:T(8,128)S(1)} %get-tuple-element.5, f32[12,32,32]{2,1,0:T(8,128)S(1)} %fusion.12), kind=kLoop, calls=%fused_computation.29 | loop fusion | flops 147456 | bytes 344064 | tf_op jit(solution)/shard_map/imaging_kernel/concatenate | solution.py:321
  16.0 2.0 %collective-permute-start.2 = (f32[4,2,32,32]{3,2,1,0:T(8,128)S(1)}, f32[4,2,32,32]{3,2,1,0:T(8,128)S(1)}, u32[]{:S(2)}, u32[]{:S(2)}) collective-permute-start(f32[4,2,32,32]{3,2,1,0:T(8,128)S(1)} %select_add_fusion), channel_id=1, source_target_pairs={{0,1},{1,0},{2,3},{3,2},{4,5},{5,4},{6,7},{7,6},{8,9},{9,8},{10,11... | collective-permute-start | bytes 98312 | tf_op jit(solution)/shard_map/master_spectra/ppermute | solution.py:204
  18.0 1.3 %broadcast_multiply_fusion.3 = (s32[32]{0:T(128)S(1)}, s32[32]{0:T(128)S(1)}) fusion(s32[]{:T(128)} %bitcast.9, s32[]{:T(128)} %bitcast.8), kind=kLoop, calls=%fused_computation.110 | loop fusion | flops 96 | bytes 264 | tf_op jit(solution)/shard_map/tile_spectra/mul | solution.py:31
  20.5 0.8 %maximum_maximum_fusion.x_ref = f32[384,128]{1,0:T(8,128)} fusion(f32[384,32]{1,0:T(8,128)S(1)} %get-tuple-element.7, f32[384,32]{1,0:T(8,128)S(1)} %get-tuple-element.6, f32[128]{0:T(128)S(1)} %pad.10.clone), kind=kLoop, calls=%fused_computation.28 | loop fusion | flops 98304 | bytes 295424 | tf_op jit(solution)/shard_map/imaging_kernel/concatenate | solution.py:325
  21.4 13.4 %imaging_kernel.1 = f32[32,128]{1,0:T(8,128)} custom-call(f32[384,128]{1,0:T(8,128)} %maximum_maximum_fusion.x_ref, f32[256,256]{1,0:T(8,128)} %bitcast_convert_fusion.goal_ref, f32[384,128]{1,0:T(8,128)} %bitcast.175, f32[12]{0:T(128)} %bitcast.184, f32[1]{0:T(128)S(6)} %copy.36.dose_ref, f32[128,512]{1,0:T(8,128)} %constant.95.clone.rw_ref, ...), custom_call_target="tpu_custom_call" | custom-call | tf_op jit(solution)/shard_map/imaging_kernel/pallas_call | solution.py:168
  34.7 0.9 %fusion.38 = (f32[1,1,32,32]{2,3,1,0:T(8,128)S(1)}, f32[1,1,32,32]{2,3,1,0:T(8,128)S(1)}) fusion(f32[32,128]{1,0:T(8,128)} %imaging_kernel.1), kind=kLoop, calls=%fused_computation.84 | loop fusion | flops 2048 | bytes 24576 | tf_op jit(solution)/shard_map/gradient_exchange/stack;imaging_kernel/stack | solution.py:335
  35.8 1.2 %collective-permute-done.3 = f32[1,2,32,32]{2,3,1,0:T(8,128)S(1)} collective-permute-done((f32[1,2,32,32]{2,3,1,0:T(8,128)S(1)}, f32[1,2,32,32]{2,3,1,0:T(8,128)S(1)}, u32[]{:S(2)}, u32[]{:S(2)}) %collective-permute-start.3) | collective-permute-done | bytes 8224 | tf_op jit(solution)/shard_map/gradient_exchange/ppermute | solution.py:193
  37.0 1.5 %collective-permute-start.4 = (f32[2,2,32,32]{2,3,0,1:T(8,128)S(1)}, f32[2,2,32,32]{2,3,0,1:T(8,128)S(1)}, u32[]{:S(2)}, u32[]{:S(2)}) collective-permute-start(f32[2,2,32,32]{2,3,0,1:T(8,128)S(1)} %select_add_fusion.1), channel_id=1, source_target_pairs={{0,2},{2,0},{1,3},{3,1},{4,6},{6,4},{5,7},{7,5},{8,10},{10,8},{9,1... | collective-permute-start | bytes 49160 | tf_op jit(solution)/shard_map/gradient_exchange/ppermute | solution.py:204
  38.7 2.7 %collective-permute-done.4 = f32[2,2,32,32]{2,3,0,1:T(8,128)S(1)} collective-permute-done((f32[2,2,32,32]{2,3,0,1:T(8,128)S(1)}, f32[2,2,32,32]{2,3,0,1:T(8,128)S(1)}, u32[]{:S(2)}, u32[]{:S(2)}) %collective-permute-start.4) | collective-permute-done | bytes 16416 | tf_op jit(solution)/shard_map/gradient_exchange/ppermute | solution.py:204
  41.9 0.2 multiply_add_fusion
  42.3 0.5 collective-permute-start.5
  42.8 0.7 %collective-permute-start.6 = (f32[1,2,32,32]{3,2,1,0:T(8,128)S(1)}, f32[1,2,32,32]{3,2,1,0:T(8,128)S(1)}, u32[]{:S(2)}, u32[]{:S(2)}) collective-permute-start(f32[1,2,32,32]{3,2,1,0:T(8,128)S(1)} %get-tuple-element.11), channel_id=1, source_target_pairs={{1,13},{5,9},{9,5},{13,1},{3,15},{7,11},{11,7},{15,3},{17,29},{21,... | collective-permute-start | bytes 24584 | tf_op jit(solution)/shard_map/gradient_exchange/ppermute | solution.py:265
  43.6 0.6 %fusion.55 = f32[2,256,256]{2,1,0:T(8,128)S(1)} fusion(f32[2,256,32]{1,2,0:T(8,128)S(1)} %fusion.2, f32[32,256,1]{1,0,2:T(8,128)S(1)} %copy-done.6), kind=kOutput, calls=%fused_computation.121 | convolution fusion | flops 50331648 | bytes 622592 | tf_op jit(solution)/shard_map/pixel_gradients/nxc,cy->nxy/dot_general | solution.py:56
  44.5 3.2 %collective-permute-done.5 = f32[1,2,32,32]{3,2,1,0:T(8,128)S(1)} collective-permute-done((f32[1,2,32,32]{3,2,1,0:T(8,128)S(1)}, f32[1,2,32,32]{3,2,1,0:T(8,128)S(1)}, u32[]{:S(2)}, u32[]{:S(2)}) %collective-permute-start.5) | collective-permute-done | bytes 8224 | tf_op jit(solution)/shard_map/gradient_exchange/ppermute | solution.py:265
  47.7 0.6 %collective-permute-start.7 = (f32[1,2,32,32]{3,2,1,0:T(8,128)S(1)}, f32[1,2,32,32]{3,2,1,0:T(8,128)S(1)}, u32[]{:S(2)}, u32[]{:S(2)}) collective-permute-start(f32[1,2,32,32]{3,2,1,0:T(8,128)S(1)} %add_add_fusion), channel_id=1, source_target_pairs={{0,1},{1,0},{2,3},{3,2},{4,5},{5,4},{6,7},{7,6},{8,9},{9,8},{10,11... | collective-permute-start | bytes 24584 | tf_op jit(solution)/shard_map/gradient_exchange/ppermute | solution.py:204
  48.3 1.4 %convolution_add_fusion = f32[2,256,256]{2,1,0:T(8,128)} fusion(f32[2,256,256]{2,1,0:T(8,128)S(1)} %fusion.55, f32[2,256,32]{1,2,0:T(8,128)S(1)} %fusion.1, f32[32,256,1]{1,0,2:T(8,128)S(1)} %copy-done.5), kind=kOutput, calls=%fused_computation | convolution fusion | flops 50462720 | bytes 1146880 | tf_op jit(solution)/shard_map/pixel_gradients/nxc,cy->nxy/dot_general | solution.py:56
  50.2 0.2 fusion.3
  50.4 0.2 fusion.4
  50.6 0.4 fusion.56
  51.1 1.1 %fusion = f32[1,256,256]{2,1,0:T(8,128)} fusion(f32[256,256]{1,0:T(8,128)S(1)} %fusion.56, f32[256,32]{0,1:T(8,128)S(1)} %fusion.3, f32[32,256]{1,0:T(8,128)S(1)} %copy-done.2), kind=kOutput, calls=%fused_computation.2 | convolution fusion | flops 25231360 | bytes 589824 | tf_op jit(solution)/shard_map/pixel_gradients/nxc,cy->nxy/dot_general | solution.py:56
  (68 shorter events, 4.7 us)
Async XLA Ops:
  0.6 7.6 %copy-start = (bf16[2,256,256]{2,1,0:T(8,128)(2,1)S(1)}, bf16[2,256,256]{2,1,0:T(8,128)(2,1)}, u32[]{:S(2)}) copy-start(bf16[2,256,256]{2,1,0:T(8,128)(2,1)} %param.15) | copy-start | bytes 786436
  0.6 0.8 %copy-start.1 = (f32[32,256]{1,0:T(8,128)S(1)}, f32[32,256]{1,0:T(8,128)}, u32[]{:S(2)}) copy-start(f32[32,256]{1,0:T(8,128)} %constant.93.clone) | copy-start | bytes 98308
  0.7 1.9 %copy-start.2 = (f32[32,256]{1,0:T(8,128)S(1)}, f32[32,256]{1,0:T(8,128)}, u32[]{:S(2)}) copy-start(f32[32,256]{1,0:T(8,128)} %constant.94.clone) | copy-start | bytes 98308
  0.7 1.9 %copy-start.3 = (bf16[1,256,256]{2,1,0:T(8,128)(2,1)S(1)}, bf16[1,256,256]{2,1,0:T(8,128)(2,1)}, u32[]{:S(2)}) copy-start(bf16[1,256,256]{2,1,0:T(8,128)(2,1)} %param.16) | copy-start | bytes 393220
  3.3 9.0 %copy-start.4 = (f32[1,12,2,32,32]{4,3,2,1,0:T(8,128)S(1)}, f32[1,12,2,32,32]{4,3,2,1,0:T(8,128)}, u32[]{:S(2)}) copy-start(f32[1,12,2,32,32]{4,3,2,1,0:T(8,128)} %param.20) | copy-start | bytes 294916
  3.5 12.4 %collective-permute-start = (f32[1,2,32,32]{3,2,1,0:T(8,128)S(1)}, f32[1,2,32,32]{3,2,1,0:T(8,128)S(1)}, u32[]{:S(2)}, u32[]{:S(2)}) collective-permute-start(f32[1,2,32,32]{3,2,1,0:T(8,128)S(1)} %get-tuple-element.17), channel_id=1, source_target_pairs={{8,0},{12,4},{0,8},{4,12},{5,1},{1,5},{13,9},{9,13},{10,2},{14,6},... | collective-permute-start | bytes 24584 | tf_op jit(solution)/shard_map/master_spectra/ppermute | solution.py:245
  7.6 8.3 %collective-permute-start.1 = (f32[1,2,32,32]{3,2,1,0:T(8,128)S(1)}, f32[1,2,32,32]{3,2,1,0:T(8,128)S(1)}, u32[]{:S(2)}, u32[]{:S(2)}) collective-permute-start(f32[1,2,32,32]{3,2,1,0:T(8,128)S(1)} %get-tuple-element.17), channel_id=1, source_target_pairs={{13,1},{9,5},{5,9},{1,13},{15,3},{11,7},{7,11},{3,15},{29,17},{25,... | collective-permute-start | bytes 24584 | tf_op jit(solution)/shard_map/master_spectra/ppermute | solution.py:245
  8.9 0.7 %copy-start.8 = (s32[2,2]{1,0:T(2,128)S(1)}, s32[2,2]{1,0:T(2,128)}, u32[]{:S(2)}) copy-start(s32[2,2]{1,0:T(2,128)} %param.19) | copy-start | bytes 52
  9.7 0.7 %copy-start.10 = (s32[2]{0:T(128)S(1)}, s32[2]{0:T(128)}, u32[]{:S(2)}) copy-start(s32[2]{0:T(128)} %param.18) | copy-start | bytes 28
  12.2 1.0 %copy-start.7 = (bf16[2,256,256]{2,1,0:T(8,128)(2,1)S(1)}, bf16[2,256,256]{2,1,0:T(8,128)(2,1)}, u32[]{:S(2)}) copy-start(bf16[2,256,256]{2,1,0:T(8,128)(2,1)} %param.17) | copy-start | bytes 786436
  13.9 0.7 %copy-start.9 = (f32[1,12]{1,0:T(1,128)S(1)}, f32[1,12]{1,0:T(1,128)}, u32[]{:S(2)}) copy-start(f32[1,12]{1,0:T(1,128)} %param.21) | copy-start | bytes 148
  16.0 4.0 %collective-permute-start.2 = (f32[4,2,32,32]{3,2,1,0:T(8,128)S(1)}, f32[4,2,32,32]{3,2,1,0:T(8,128)S(1)}, u32[]{:S(2)}, u32[]{:S(2)}) collective-permute-start(f32[4,2,32,32]{3,2,1,0:T(8,128)S(1)} %select_add_fusion), channel_id=1, source_target_pairs={{0,1},{1,0},{2,3},{3,2},{4,5},{5,4},{6,7},{7,6},{8,9},{9,8},{10,11... | collective-permute-start | bytes 98312 | tf_op jit(solution)/shard_map/master_spectra/ppermute | solution.py:204
  35.7 1.3 %collective-permute-start.3 = (f32[1,2,32,32]{2,3,1,0:T(8,128)S(1)}, f32[1,2,32,32]{2,3,1,0:T(8,128)S(1)}, u32[]{:S(2)}, u32[]{:S(2)}) collective-permute-start(f32[1,2,32,32]{2,3,1,0:T(8,128)S(1)} %get-tuple-element.15), channel_id=1, source_target_pairs={{0,1},{1,0},{2,3},{3,2},{4,5},{5,4},{6,7},{7,6},{8,9},{9,8},{10,11... | collective-permute-start | bytes 24584 | tf_op jit(solution)/shard_map/gradient_exchange/ppermute | solution.py:193
  37.0 4.3 %collective-permute-start.4 = (f32[2,2,32,32]{2,3,0,1:T(8,128)S(1)}, f32[2,2,32,32]{2,3,0,1:T(8,128)S(1)}, u32[]{:S(2)}, u32[]{:S(2)}) collective-permute-start(f32[2,2,32,32]{2,3,0,1:T(8,128)S(1)} %select_add_fusion.1), channel_id=1, source_target_pairs={{0,2},{2,0},{1,3},{3,1},{4,6},{6,4},{5,7},{7,5},{8,10},{10,8},{9,1... | collective-permute-start | bytes 49160 | tf_op jit(solution)/shard_map/gradient_exchange/ppermute | solution.py:204
  38.7 2.8 %copy-start.5 = (f32[32,256,1]{1,0,2:T(8,128)S(1)}, f32[32,256,1]{1,0,2:T(8,128)}, u32[]{:S(2)}) copy-start(f32[32,256,1]{1,0,2:T(8,128)} %constant.109) | copy-start | bytes 98308
  42.3 1.2 %copy-start.6 = (f32[32,256,1]{1,0,2:T(8,128)S(1)}, f32[32,256,1]{1,0,2:T(8,128)}, u32[]{:S(2)}) copy-start(f32[32,256,1]{1,0,2:T(8,128)} %constant.108) | copy-start | bytes 98308
  42.3 5.4 %collective-permute-start.5 = (f32[1,2,32,32]{3,2,1,0:T(8,128)S(1)}, f32[1,2,32,32]{3,2,1,0:T(8,128)S(1)}, u32[]{:S(2)}, u32[]{:S(2)}) collective-permute-start(f32[1,2,32,32]{3,2,1,0:T(8,128)S(1)} %get-tuple-element.10), channel_id=1, source_target_pairs={{0,8},{4,12},{8,0},{12,4},{1,5},{5,1},{9,13},{13,9},{2,10},{6,14},... | collective-permute-start | bytes 24584 | tf_op jit(solution)/shard_map/gradient_exchange/ppermute | solution.py:265
  42.8 4.9 %collective-permute-start.6 = (f32[1,2,32,32]{3,2,1,0:T(8,128)S(1)}, f32[1,2,32,32]{3,2,1,0:T(8,128)S(1)}, u32[]{:S(2)}, u32[]{:S(2)}) collective-permute-start(f32[1,2,32,32]{3,2,1,0:T(8,128)S(1)} %get-tuple-element.11), channel_id=1, source_target_pairs={{1,13},{5,9},{9,5},{13,1},{3,15},{7,11},{11,7},{15,3},{17,29},{21,... | collective-permute-start | bytes 24584 | tf_op jit(solution)/shard_map/gradient_exchange/ppermute | solution.py:265
  47.7 2.0 %collective-permute-start.7 = (f32[1,2,32,32]{3,2,1,0:T(8,128)S(1)}, f32[1,2,32,32]{3,2,1,0:T(8,128)S(1)}, u32[]{:S(2)}, u32[]{:S(2)}) collective-permute-start(f32[1,2,32,32]{3,2,1,0:T(8,128)S(1)} %add_add_fusion), channel_id=1, source_target_pairs={{0,1},{1,0},{2,3},{3,2},{4,5},{5,4},{6,7},{7,6},{8,9},{9,8},{10,11... | collective-permute-start | bytes 24584 | tf_op jit(solution)/shard_map/gradient_exchange/ppermute | solution.py:204

commit v7 on v6

--- a/solution.py
+++ b/solution.py
@@ -115,20 +115,40 @@
     b_hi, b_mid, b_lo = table_three(right_b)
     right_hm = np.concatenate([b_hi, b_mid], axis=1)
     right_lh = np.concatenate([b_lo, b_hi], axis=0)
-    out = [jnp.asarray(table, jnp.float32) for table in (right_w, right_c)]
+    plain = (c_re, c_im, c_re.T, c_im.T, right_w[:B], right_w[B : 2 * B], right_c)
+    out = [jnp.asarray(table, jnp.float32) for table in plain]
     return out + [jnp.asarray(table) for table in (left_three, right_hm, right_lh)]
 
 
 def imaging_body(
-    x_ref, goal_ref, h_ref, w_ref, dose_ref, rw_ref, rc_ref, la_ref, rhm_ref, rlh_ref,
-    acc_ref, w_buf, f_buf, i_buf, u_buf,
+    pos_ref, im_ref, sh_ref, w_ref, dose_ref, t_ref, ev_ref, goal_ref, h_ref, hc_ref,
+    c_re_ref, c_im_ref, ct_re_ref, ct_im_ref, rw_top, rw_bot, rc_ref, la_ref, rhm_ref, rlh_ref,
+    slots_ref, f_buf, i_buf, u_buf,
 ):
     count = f_buf.shape[0]
-    w_buf[...] = dot_full(x_ref[...], rw_ref[...])
+    local_tiles = goal_ref.shape[0]
+    pos = pos_ref[0]
+    master = im_ref[pos]
+    pick0 = (lax.broadcasted_iota(jnp.int32, (P_SIZE, 128), 0) == sh_ref[2 * pos]).astype(jnp.float32)
+    pick1 = (lax.broadcasted_iota(jnp.int32, (8, P_SIZE), 1) == sh_ref[2 * pos + 1]).astype(jnp.float32)
+    e0_re = dot_full(c_re_ref[...], pick0)[:, 0:1]
+    e0_im = dot_full(c_im_ref[...], pick0)[:, 0:1]
+    e1_re = dot_full(pick1, ct_re_ref[...])[0:1, :]
+    e1_im = dot_full(pick1, ct_im_ref[...])[0:1, :]
+    ph_re = e0_re * e1_re - e0_im * e1_im
+    ph_im = e0_re * e1_im + e0_im * e1_re
+    m_re = ev_ref[master, 0]
+    m_im = ev_ref[master, 1]
+    s_re = t_ref[pos, 0] + (ph_re * m_re - ph_im * m_im)
+    s_im = t_ref[pos, 1] + (ph_re * m_im + ph_im * m_re)
     i_buf[...] = jnp.zeros(i_buf.shape, jnp.float32)
 
     def forward(k, carry):
-        rows = w_buf[pl.ds(pl.multiple_of(k * B, B), B), :]
+        h_re = h_ref[k, 0]
+        h_im = h_ref[k, 1]
+        x_re = h_re * s_re - h_im * s_im
+        x_im = h_re * s_im + h_im * s_re
+        rows = dot_full(x_re, rw_top[...]) + dot_full(x_im, rw_bot[...])
         swap = jnp.concatenate([-rows[:, P_SIZE:], rows[:, :P_SIZE]], axis=1)
         s_hi, s_mid, s_lo = split_three(jnp.concatenate([rows, swap], axis=0))
         stacked = jnp.concatenate([s_hi, s_mid, s_hi, s_lo, s_hi, s_mid], axis=0)
@@ -141,8 +161,8 @@
     lax.fori_loop(0, count, forward, 0)
     dose = dose_ref[0]
     resist = 1.0 / (1.0 + jnp.exp(-(steepness * (dose * i_buf[...] - threshold))))
-    sens = 2.0 * (resist - goal_ref[...]) * resist * (1.0 - resist) * steepness * dose
-    i_buf[...] = sens
+    goal = goal_ref[pos].astype(jnp.float32)
+    i_buf[...] = 2.0 * (resist - goal) * resist * (1.0 - resist) * steepness * dose
 
     def backward(k, carry):
         sens = i_buf[...]
@@ -157,26 +177,34 @@
 
     lax.fori_loop(0, count, backward, 0)
     out = dot_full(u_buf[...], rc_ref[...])
-    acc_ref[...] = jnp.sum((h_ref[...] * out).reshape(count, B, 128), axis=0)
-
-
-def imaging(x_cat, goal, h_cat, weights, dose):
+    acc = jnp.sum((hc_ref[...] * out).reshape(count, B, 128), axis=0)
+    flip = jnp.concatenate([acc, jnp.zeros((128 - B, 128), jnp.float32)], axis=0).T
+    g_re = flip[0:B, 0:B] + flip[2 * B : 3 * B, 0:B]
+    g_im = flip[B : 2 * B, 0:B] + flip[3 * B : 4 * B, 0:B]
+    slots_ref[...] = jnp.zeros(slots_ref.shape, jnp.float32)
+    slots_ref[pos, 0] = g_re
+    slots_ref[pos, 1] = g_im
+    slots_ref[local_tiles + master, 0] = ph_re * g_re + ph_im * g_im
+    slots_ref[local_tiles + master, 1] = ph_re * g_im - ph_im * g_re
+
+
+def imaging(pos, inst_master, inst_shift, weights, dose, tile_spec, every, target, kerns, h_cat):
     count = weights.shape[0]
     tables = imaging_tables()
+    slots = target.shape[0] + every.shape[0]
     vmem = pl.BlockSpec(memory_space=pltpu.VMEM)
     smem = pl.BlockSpec(memory_space=pltpu.SMEM)
     return pl.pallas_call(
         imaging_body,
-        out_shape=jax.ShapeDtypeStruct((B, 128), jnp.float32),
-        in_specs=[vmem, vmem, vmem, smem, smem] + [vmem] * 5,
+        out_shape=jax.ShapeDtypeStruct((slots, 2, B, B), jnp.float32),
+        in_specs=[smem] * 5 + [vmem] * 5 + [vmem] * len(tables),
         out_specs=vmem,
         scratch_shapes=[
-            pltpu.VMEM((count * B, 2 * P_SIZE), jnp.float32),
             pltpu.VMEM((count, P_SIZE, 2 * P_SIZE), jnp.float32),
             pltpu.VMEM((P_SIZE, P_SIZE), jnp.float32),
             pltpu.VMEM((count * B, 2 * P_SIZE), jnp.float32),
         ],
-    )(x_cat, goal, h_cat, weights, dose, *tables)
+    )(pos, inst_master, inst_shift, weights, dose, tile_spec, every, target, kerns, h_cat, *tables)
 
 
 def xor_partners(count):
@@ -291,59 +319,36 @@
             every = gather_all(own, "tile", tile_count, tile_pos)
 
     with jax.named_scope("tile_spectra"):
-        mine_mask = lax.dynamic_slice_in_dim(tile_mask, first, per_dev, 0)
-        goal = lax.dynamic_slice_in_dim(target, first, per_dev, 0).astype(jnp.float32)
-        mine_master = lax.dynamic_slice_in_dim(inst_master, first, per_dev, 0)
-        mine_shift = lax.dynamic_slice_in_dim(inst_shift, first, per_dev, 0)
-        tile_re, tile_im = spectra(mine_mask.astype(jnp.float32), cos_tab, sin_tab)
-        ph_re, ph_im = phase_ramp(mine_shift)
-        pick = (mine_master[:, None] == jnp.arange(region_masters, dtype=jnp.int32)[None, :]).astype(
-            jnp.float32
-        )
-        sel = jnp.sum(pick[:, :, None, None, None] * every[None], axis=1)
-        sel_re = sel[:, 0]
-        sel_im = sel[:, 1]
-        spec_re = tile_re + (ph_re * sel_re - ph_im * sel_im)
-        spec_im = tile_im + (ph_re * sel_im + ph_im * sel_re)
+        tile_re, tile_im = spectra(tile_mask.astype(jnp.float32), cos_tab, sin_tab)
+        tile_spec = jnp.stack([tile_re, tile_im], axis=1)
 
     dose = corner_dose[0]
-    h_re = kernels[0, :, 0]
-    h_im = kernels[0, :, 1]
+    kerns = kernels[0]
+    h_re = kerns[:, 0]
+    h_im = kerns[:, 1]
     weights = kernel_weight[0]
 
     with jax.named_scope("imaging_kernel"):
-        x_re = h_re[:, None] * spec_re[None] - h_im[:, None] * spec_im[None]
-        x_im = h_re[:, None] * spec_im[None] + h_im[:, None] * spec_re[None]
         count = h_re.shape[0]
         twice = (2.0 * weights)[:, None, None]
         ht_re = jnp.swapaxes(h_re, 1, 2) * twice
         ht_im = jnp.swapaxes(h_im, 1, 2) * twice
         h_cat = jnp.concatenate([ht_re, ht_re, ht_im, -ht_im], axis=-1).reshape(count * B, 128)
-        grads_re = []
-        grads_im = []
+        shifts = inst_shift.reshape(-1)
+        slots = None
         for j in range(per_dev):
-            x_cat = jnp.concatenate(
-                [x_re[:, j], x_im[:, j], jnp.zeros((count, B, 128 - 2 * B), jnp.float32)], axis=-1
-            ).reshape(count * B, 128)
-            acc = imaging(x_cat, goal[j], h_cat, weights, corner_dose)
-            grads_re.append((acc[:, :B] + acc[:, 2 * B : 3 * B]).T)
-            grads_im.append((acc[:, B : 2 * B] + acc[:, 3 * B :]).T)
-        grad_re = jnp.stack(grads_re)
-        grad_im = jnp.stack(grads_im)
+            pos = jnp.reshape(first + j, (1,)).astype(jnp.int32)
+            part = imaging(
+                pos, inst_master, shifts, weights, corner_dose, tile_spec, every, target, kerns, h_cat
+            )
+            slots = part if slots is None else slots + part
 
     with jax.named_scope("gradient_exchange"):
-        own_grad = jnp.stack([grad_re, grad_im], axis=1)
-        both = gather_all(own_grad, "kern", kern_count, kern_pos)
         corner_count = lax.axis_size("corner")
-        mine_tiles = sum_all(both, "corner", corner_count, lax.axis_index("corner"))
-        all_re, all_im = phase_ramp(inst_shift)
-        back_re = all_re * mine_tiles[:, 0] + all_im * mine_tiles[:, 1]
-        back_im = all_re * mine_tiles[:, 1] - all_im * mine_tiles[:, 0]
-        own_back = jnp.stack([back_re, back_im], axis=1)
-        owner_pick = (
-            inst_master[:, None] == jnp.arange(region_masters, dtype=jnp.int32)[None, :]
-        ).astype(jnp.float32)
-        terms = jnp.sum(owner_pick[:, :, None, None, None] * own_back[:, None], axis=0)
+        slots = sum_all(slots, "kern", kern_count, kern_pos)
+        slots = sum_all(slots, "corner", corner_count, lax.axis_index("corner"))
+        mine_tiles = slots[:local_tiles]
+        terms = slots[local_tiles:]
         if xor_partners(tile_count) and xor_partners(kern_count) and tile_count > 2:
             mine_masters = scatter_split(terms, tile_count, tile_pos, kern_count, kern_pos, local_masters)
         else:

time: 52.6 us -> 56.2 us (1.068)
  waiting for transfers between devices: 7.12 us -> 10.1 us
  Pallas kernels: 13.4 us -> 16.3 us
  other arithmetic: 6.35 us -> 3.56 us
    ppermute x3 -> x4, waiting for transfers between devices: 2.71 us -> 7.01 us  [sum_all(): x = x + lax.ppermute(x, axis, [(i, i ^ step) for i in range(count)])]
    pallas_call x1, Pallas kernels: 13.4 us -> 16.3 us  [imaging(): pl.pallas_call(imaging_body, out_shape=jax.ShapeDtypeStruct((slots, 2, B,...]
    mul x2 -> x0, other arithmetic: 1.33 us -> none  [the longest x1 1.26 us: phase_ramp(): freq[None, None, :] * shift[:, 1][:, None, None]]
    ppermute x1 -> x0, waiting for transfers between devices: 1.18 us -> none  [gather_all(): got = lax.ppermute(x, axis, [(i, i ^ step) for i in range(count)])]
    add x2 -> x3, other arithmetic: 0.09 us -> 0.99 us  [sum_all(): x = x + lax.ppermute(x, axis, [(i, i ^ step) for i in range(count)])]
    slice x3 -> x1, local copies, waits for them, and re-layouts: 0.81 us -> 0.01 us  [on_device(): terms = slots[local_tiles:]]
    concatenate x1 -> x0, other arithmetic: 0.8 us -> none  [on_device(): jnp.concatenate([x_re[:, j], x_im[:, j], jnp.zeros((count, B, 128 - 2 * B...]
    squeeze x1 -> x0, other arithmetic: 0.72 us -> none  [on_device(): acc = imaging(x_cat, goal[j], h_cat, weights, corner_dose)]
  transfers between devices with their start and end apart: 8 -> 8, of which waited for: 3 -> 3; matrix products, arithmetic and copies ran while one was open for 17% -> 12% of each run, Pallas kernels for 0% -> 0%
where the time goes in v7:
time: 56.2 us; the launch traced here: 55.7 us
  Pallas kernels  16.3 us (29%)
  starting transfers between devices  10.5 us (19%)
  waiting for transfers between devices  10.1 us (18%)
  matrix products  8.64 us (15%)
  local copies, waits for them, and re-layouts  4.86 us (9%)
  other arithmetic  3.56 us (6%)
  between operations  1.7 us (3%)
    pallas_call x1, Pallas kernels, imaging(): pl.pallas_call(imaging_body, out_shape=jax.ShapeDtypeStruct((slots, 2, B,...  16.3 us
    ppermute x4, waiting for transfers between devices, sum_all(): x = x + lax.ppermute(x, axis, [(i, i ^ step) for i in range(count)])  7.01 us
    ppermute x2, starting transfers between devices, gather_split(): got = lax.ppermute(x, ('tile', 'kern'), pairs)  4.75 us
    ppermute x4, starting transfers between devices, sum_all(): x = x + lax.ppermute(x, axis, [(i, i ^ step) for i in range(count)])  4.65 us
    unnamed x22, local copies, waits for them, and re-layouts  3.92 us
    ppermute x2, waiting for transfers between devices, scatter_split(): total = total + lax.ppermute(part, ('tile', 'kern'), pairs)  3.06 us
    dot_general x2, matrix products, back_pixels(): jnp.einsum('nxc,cy->nxy', half_im, sin_tab, precision=precise)  2.54 us
    dot_general x2, matrix products, spectra(): rows_re = jnp.einsum('bx,nxy->nby', cos_tab, masks, precision=precise)  1.33 us
  transfers between devices with their start and end apart: 8, of which 3 were waited for; matrix products, arithmetic and copies ran while one was open for 12% of the time, Pallas kernels for 0%

profile of v7, /device:TPU:0, one launch (start us, length us, event | category | flops | bytes accessed | tf_op | source)
XLA Modules:
  0.0 55.7 jit_solution(7309538254125202103)
XLA Ops:
  0.7 0.8 %copy-done.1 = f32[32,256]{1,0:T(8,128)S(1)} copy-done((f32[32,256]{1,0:T(8,128)S(1)}, f32[32,256]{1,0:T(8,128)}, u32[]{:S(2)}) %copy-start.1) | copy-done | bytes 32792
  1.4 1.1 %fusion.15 = f32[32,256]{1,0:T(8,128)S(1)} fusion(f32[32,256]{1,0:T(8,128)S(1)} %copy-done.1, bf16[1,256,256]{2,1,0:T(8,128)(2,1)} %param.21), kind=kOutput, calls=%fused_computation.30 | convolution fusion | flops 25165824 | bytes 196608 | tf_op jit(solution)/shard_map/master_spectra/bx,nxy->nby/dot_general | solution.py:38
  3.5 4.1 %collective-permute-start = (f32[1,2,32,32]{3,2,1,0:T(8,128)S(1)}, f32[1,2,32,32]{3,2,1,0:T(8,128)S(1)}, u32[]{:S(2)}, u32[]{:S(2)}) collective-permute-start(f32[1,2,32,32]{3,2,1,0:T(8,128)S(1)} %get-tuple-element.7), channel_id=1, source_target_pairs={{8,0},{12,4},{0,8},{4,12},{5,1},{1,5},{13,9},{9,13},{10,2},{14,6},... | collective-permute-start | bytes 24584 | tf_op jit(solution)/shard_map/master_spectra/ppermute | solution.py:273
  7.6 0.7 %collective-permute-start.1 = (f32[1,2,32,32]{3,2,1,0:T(8,128)S(1)}, f32[1,2,32,32]{3,2,1,0:T(8,128)S(1)}, u32[]{:S(2)}, u32[]{:S(2)}) collective-permute-start(f32[1,2,32,32]{3,2,1,0:T(8,128)S(1)} %get-tuple-element.7), channel_id=1, source_target_pairs={{13,1},{9,5},{5,9},{1,13},{15,3},{11,7},{7,11},{3,15},{29,17},{25,... | collective-permute-start | bytes 24584 | tf_op jit(solution)/shard_map/master_spectra/ppermute | solution.py:273
  8.3 0.6 %copy-done.9 = f32[1,12]{1,0:T(1,128)S(1)} copy-done((f32[1,12]{1,0:T(1,128)S(1)}, f32[1,12]{1,0:T(1,128)}, u32[]{:S(2)}) %copy-start.9) | copy-done | bytes 72
  9.1 0.7 %copy-done.7 = f32[32,256,1]{1,0,2:T(8,128)S(1)} copy-done((f32[32,256,1]{1,0,2:T(8,128)S(1)}, f32[32,256,1]{1,0,2:T(8,128)}, u32[]{:S(2)}) %copy-start.7) | copy-done | bytes 32792
  9.8 0.2 convolution_bitcast_fusion.1
  10.0 0.5 copy-done.6
  12.0 0.6 %pad_maximum_fusion.1.t_ref = f32[2,2,32,32]{3,2,1,0:T(8,128)} fusion(f32[2,1,32,32]{3,2,1,0:T(8,128)S(1)} %fusion.5, f32[2,1,32,32]{3,2,1,0:T(8,128)S(1)} %fusion.6), kind=kLoop, calls=%fused_computation.34 | loop fusion | flops 4096 | bytes 32768 | tf_op jit(solution)/shard_map/tile_spectra/stack | solution.py:323
  12.6 0.9 %pad_maximum_fusion = f32[12,32,128]{2,1,0:T(8,128)} fusion(f32[12,32,32]{2,1,0:T(8,128)S(1)} %copy.28, f32[12,32,32]{2,1,0:T(8,128)S(1)} %copy.27, f32[12,32,32]{2,1,0:T(8,128)S(1)} %copy.25), kind=kLoop, calls=%fused_computation.27 | loop fusion | flops 147456 | bytes 344064 | tf_op jit(solution)/shard_map/imaging_kernel/concatenate | solution.py:336
  13.6 2.0 %collective-permute-start.2 = (f32[4,2,32,32]{3,2,1,0:T(8,128)S(1)}, f32[4,2,32,32]{3,2,1,0:T(8,128)S(1)}, u32[]{:S(2)}, u32[]{:S(2)}) collective-permute-start(f32[4,2,32,32]{3,2,1,0:T(8,128)S(1)} %select_add_fusion.1), channel_id=1, source_target_pairs={{0,1},{1,0},{2,3},{3,2},{4,5},{5,4},{6,7},{7,6},{8,9},{9,8},{10,11... | collective-permute-start | bytes 98312 | tf_op jit(solution)/shard_map/master_spectra/ppermute | solution.py:232
  16.3 0.6 %reshape.89.sh_ref = s32[4]{0:T(128)} reshape(s32[2,2]{1,0:T(2,128)S(1)} %copy-done.10) | data formatting | bytes 32 | tf_op jit(solution)/shard_map/imaging_kernel/reshape | solution.py:337
  16.9 0.7 %select_add_fusion.ev_ref = f32[4,2,32,32]{3,2,1,0:T(8,128)} fusion(f32[4,2,32,32]{3,2,1,0:T(8,128)S(1)} %collective-permute-done.2, f32[2,32,32]{2,1,0:T(8,128)S(1)} %get-tuple-element.6, pred[4]{0:T(512)(128)(4,1)S(1)} %iota_compare_fusion, f32[2,32,32]{2,1,0:T(8,128)S(1)} %bitcast.127, pred[4]{0:T(512)(128)(4,1)S(1)} %get-tuple-element.8, ...), kind=kLoop, calls=%fused_computation.32 | loop fusion | flops 49152 | bytes 90124 | tf_op jit(solution)/shard_map/master_spectra/add | solution.py:278
  17.7 16.3 %imaging_kernel.1 = f32[6,2,32,32]{3,2,1,0:T(8,128)} custom-call(s32[1]{0:T(128)} %bitcast.pos_ref, s32[2]{0:T(128)} %im_ref.1, s32[4]{0:T(128)} %reshape.89.sh_ref, f32[12]{0:T(128)} %bitcast.128, f32[1]{0:T(128)S(6)} %copy.30.dose_ref, f32[2,2,32,32]{3,2,1,0:T(8,128)} %pad_maximum_fusion.1.t_ref, f32[4,2,32,32]{3,2,1,0:T(8,128)} %select_add_fusion.ev_ref, ...), custom_call_target="tpu_custom_call" | custom-call | tf_op jit(solution)/shard_map/imaging_kernel/pallas_call | solution.py:197
  34.1 1.6 %collective-permute-done.3 = f32[6,2,32,32]{3,2,1,0:T(8,128)S(1)} collective-permute-done((f32[6,2,32,32]{3,2,1,0:T(8,128)}, f32[6,2,32,32]{3,2,1,0:T(8,128)S(1)}, u32[]{:S(2)}, u32[]{:S(2)}) %collective-permute-start.3) | collective-permute-done | bytes 49184 | tf_op jit(solution)/shard_map/gradient_exchange/ppermute | solution.py:232
  35.6 1.0 %add.73 = f32[6,2,32,32]{3,2,1,0:T(8,128)S(1)} add(f32[6,2,32,32]{3,2,1,0:T(8,128)} %imaging_kernel.1, f32[6,2,32,32]{3,2,1,0:T(8,128)S(1)} %collective-permute-done.3) | non-fusion elementwise | flops 12288 | bytes 147456 | tf_op jit(solution)/shard_map/gradient_exchange/add | solution.py:232
  36.6 1.6 %collective-permute-start.4 = (f32[6,2,32,32]{3,2,1,0:T(8,128)S(1)}, f32[6,2,32,32]{3,2,1,0:T(8,128)S(1)}, u32[]{:S(2)}, u32[]{:S(2)}) collective-permute-start(f32[6,2,32,32]{3,2,1,0:T(8,128)S(1)} %add.73), channel_id=1, source_target_pairs={{0,2},{2,0},{1,3},{3,1},{4,6},{6,4},{5,7},{7,5},{8,10},{10,8},{9,1... | collective-permute-start | bytes 147464 | tf_op jit(solution)/shard_map/gradient_exchange/ppermute | solution.py:232
  38.2 5.4 %collective-permute-done.4 = f32[6,2,32,32]{3,2,1,0:T(8,128)S(1)} collective-permute-done((f32[6,2,32,32]{3,2,1,0:T(8,128)S(1)}, f32[6,2,32,32]{3,2,1,0:T(8,128)S(1)}, u32[]{:S(2)}, u32[]{:S(2)}) %collective-permute-start.4) | collective-permute-done | bytes 49184 | tf_op jit(solution)/shard_map/gradient_exchange/ppermute | solution.py:232
  43.7 0.3 fusion.17
  43.9 0.3 fusion.18
  44.2 0.5 collective-permute-start.5
  44.7 0.7 %collective-permute-start.6 = (f32[1,2,32,32]{3,2,1,0:T(8,128)S(1)}, f32[1,2,32,32]{3,2,1,0:T(8,128)S(1)}, u32[]{:S(2)}, u32[]{:S(2)}) collective-permute-start(f32[1,2,32,32]{3,2,1,0:T(8,128)S(1)} %get-tuple-element.5), channel_id=1, source_target_pairs={{1,13},{5,9},{9,5},{13,1},{3,15},{7,11},{11,7},{15,3},{17,29},{21,... | collective-permute-start | bytes 24584 | tf_op jit(solution)/shard_map/gradient_exchange/ppermute | solution.py:293
  45.4 0.3 fusion.2
  45.6 0.6 %fusion.28 = f32[2,256,256]{2,1,0:T(8,128)S(1)} fusion(f32[2,256,32]{1,2,0:T(8,128)S(1)} %fusion.2, f32[32,256,1]{1,0,2:T(8,128)S(1)} %copy-done.7), kind=kOutput, calls=%fused_computation.57 | convolution fusion | flops 50331648 | bytes 622592 | tf_op jit(solution)/shard_map/pixel_gradients/nxc,cy->nxy/dot_general | solution.py:56
  46.2 0.3 fusion.1
  46.5 3.1 %collective-permute-done.5 = f32[1,2,32,32]{3,2,1,0:T(8,128)S(1)} collective-permute-done((f32[1,2,32,32]{3,2,1,0:T(8,128)S(1)}, f32[1,2,32,32]{3,2,1,0:T(8,128)S(1)}, u32[]{:S(2)}, u32[]{:S(2)}) %collective-permute-start.5) | collective-permute-done | bytes 8224 | tf_op jit(solution)/shard_map/gradient_exchange/ppermute | solution.py:293
  49.6 0.9 %collective-permute-start.7 = (f32[1,2,32,32]{3,2,1,0:T(8,128)S(1)}, f32[1,2,32,32]{3,2,1,0:T(8,128)S(1)}, u32[]{:S(2)}, u32[]{:S(2)}) collective-permute-start(f32[1,2,32,32]{3,2,1,0:T(8,128)S(1)} %add_add_fusion), channel_id=1, source_target_pairs={{0,1},{1,0},{2,3},{3,2},{4,5},{5,4},{6,7},{7,6},{8,9},{9,8},{10,11... | collective-permute-start | bytes 24584 | tf_op jit(solution)/shard_map/gradient_exchange/ppermute | solution.py:232
  50.5 1.4 %convolution_add_fusion = f32[2,256,256]{2,1,0:T(8,128)} fusion(f32[2,256,256]{2,1,0:T(8,128)S(1)} %fusion.28, f32[2,256,32]{1,2,0:T(8,128)S(1)} %fusion.1, f32[32,256,1]{1,0,2:T(8,128)S(1)} %copy-done.6), kind=kOutput, calls=%fused_computation | convolution fusion | flops 50462720 | bytes 1146880 | tf_op jit(solution)/shard_map/pixel_gradients/nxc,cy->nxy/dot_general | solution.py:56
  51.9 0.7 %copy-done.4 = f32[32,256]{1,0:T(8,128)S(1)} copy-done((f32[32,256]{1,0:T(8,128)S(1)}, f32[32,256]{1,0:T(8,128)}, u32[]{:S(2)}) %copy-start.4) | copy-done | bytes 32792
  53.2 0.5 copy-done.2
  54.1 0.4 fusion.29
  54.6 1.1 %fusion = f32[1,256,256]{2,1,0:T(8,128)} fusion(f32[256,256]{1,0:T(8,128)S(1)} %fusion.29, f32[256,32]{0,1:T(8,128)S(1)} %fusion.3, f32[32,256]{1,0:T(8,128)S(1)} %copy-done.4), kind=kOutput, calls=%fused_computation.2 | convolution fusion | flops 25231360 | bytes 589824 | tf_op jit(solution)/shard_map/pixel_gradients/nxc,cy->nxy/dot_general | solution.py:56
  (51 shorter events, 3.6 us)
Async XLA Ops:
  0.6 8.5 %copy-start = (bf16[2,256,256]{2,1,0:T(8,128)(2,1)S(1)}, bf16[2,256,256]{2,1,0:T(8,128)(2,1)}, u32[]{:S(2)}) copy-start(bf16[2,256,256]{2,1,0:T(8,128)(2,1)} %param.20) | copy-start | bytes 786436
  0.6 0.8 %copy-start.1 = (f32[32,256]{1,0:T(8,128)S(1)}, f32[32,256]{1,0:T(8,128)}, u32[]{:S(2)}) copy-start(f32[32,256]{1,0:T(8,128)} %constant.59.clone.c_re_ref) | copy-start | bytes 98308
  0.7 1.9 %copy-start.3 = (f32[32,256]{1,0:T(8,128)S(1)}, f32[32,256]{1,0:T(8,128)}, u32[]{:S(2)}) copy-start(f32[32,256]{1,0:T(8,128)} %constant.60.clone.c_im_ref) | copy-start | bytes 98308
  0.7 1.9 %copy-start.8 = (bf16[1,256,256]{2,1,0:T(8,128)(2,1)S(1)}, bf16[1,256,256]{2,1,0:T(8,128)(2,1)}, u32[]{:S(2)}) copy-start(bf16[1,256,256]{2,1,0:T(8,128)(2,1)} %param.21) | copy-start | bytes 393220
  2.6 6.4 %copy-start.5 = (f32[1,12,2,32,32]{4,3,2,1,0:T(8,128)S(1)}, f32[1,12,2,32,32]{4,3,2,1,0:T(8,128)}, u32[]{:S(2)}) copy-start(f32[1,12,2,32,32]{4,3,2,1,0:T(8,128)} %param.25) | copy-start | bytes 294916
  3.5 10.0 %collective-permute-start = (f32[1,2,32,32]{3,2,1,0:T(8,128)S(1)}, f32[1,2,32,32]{3,2,1,0:T(8,128)S(1)}, u32[]{:S(2)}, u32[]{:S(2)}) collective-permute-start(f32[1,2,32,32]{3,2,1,0:T(8,128)S(1)} %get-tuple-element.7), channel_id=1, source_target_pairs={{8,0},{12,4},{0,8},{4,12},{5,1},{1,5},{13,9},{9,13},{10,2},{14,6},... | collective-permute-start | bytes 24584 | tf_op jit(solution)/shard_map/master_spectra/ppermute | solution.py:273
  7.6 5.9 %collective-permute-start.1 = (f32[1,2,32,32]{3,2,1,0:T(8,128)S(1)}, f32[1,2,32,32]{3,2,1,0:T(8,128)S(1)}, u32[]{:S(2)}, u32[]{:S(2)}) collective-permute-start(f32[1,2,32,32]{3,2,1,0:T(8,128)S(1)} %get-tuple-element.7), channel_id=1, source_target_pairs={{13,1},{9,5},{5,9},{1,13},{15,3},{11,7},{7,11},{3,15},{29,17},{25,... | collective-permute-start | bytes 24584 | tf_op jit(solution)/shard_map/master_spectra/ppermute | solution.py:273
  8.3 0.7 %copy-start.9 = (f32[1,12]{1,0:T(1,128)S(1)}, f32[1,12]{1,0:T(1,128)}, u32[]{:S(2)}) copy-start(f32[1,12]{1,0:T(1,128)} %param.26) | copy-start | bytes 148
  9.0 0.8 %copy-start.7 = (f32[32,256,1]{1,0,2:T(8,128)S(1)}, f32[32,256,1]{1,0,2:T(8,128)}, u32[]{:S(2)}) copy-start(f32[32,256,1]{1,0,2:T(8,128)} %constant.77) | copy-start | bytes 98308
  9.8 0.8 %copy-start.6 = (f32[32,256,1]{1,0,2:T(8,128)S(1)}, f32[32,256,1]{1,0,2:T(8,128)}, u32[]{:S(2)}) copy-start(f32[32,256,1]{1,0,2:T(8,128)} %constant.78) | copy-start | bytes 98308
  13.6 3.3 %collective-permute-start.2 = (f32[4,2,32,32]{3,2,1,0:T(8,128)S(1)}, f32[4,2,32,32]{3,2,1,0:T(8,128)S(1)}, u32[]{:S(2)}, u32[]{:S(2)}) collective-permute-start(f32[4,2,32,32]{3,2,1,0:T(8,128)S(1)} %select_add_fusion.1), channel_id=1, source_target_pairs={{0,1},{1,0},{2,3},{3,2},{4,5},{5,4},{6,7},{7,6},{8,9},{9,8},{10,11... | collective-permute-start | bytes 98312 | tf_op jit(solution)/shard_map/master_spectra/ppermute | solution.py:232
  15.7 0.7 %copy-start.10 = (s32[2,2]{1,0:T(2,128)S(1)}, s32[2,2]{1,0:T(2,128)}, u32[]{:S(2)}) copy-start(s32[2,2]{1,0:T(2,128)} %param.24) | copy-start | bytes 52
  34.0 1.7 %collective-permute-start.3 = (f32[6,2,32,32]{3,2,1,0:T(8,128)}, f32[6,2,32,32]{3,2,1,0:T(8,128)S(1)}, u32[]{:S(2)}, u32[]{:S(2)}) collective-permute-start(f32[6,2,32,32]{3,2,1,0:T(8,128)} %imaging_kernel.1), channel_id=1, source_target_pairs={{0,1},{1,0},{2,3},{3,2},{4,5},{5,4},{6,7},{7,6},{8,9},{9,8},{10,11... | collective-permute-start | bytes 147464 | tf_op jit(solution)/shard_map/gradient_exchange/ppermute | solution.py:232
  36.6 7.0 %collective-permute-start.4 = (f32[6,2,32,32]{3,2,1,0:T(8,128)S(1)}, f32[6,2,32,32]{3,2,1,0:T(8,128)S(1)}, u32[]{:S(2)}, u32[]{:S(2)}) collective-permute-start(f32[6,2,32,32]{3,2,1,0:T(8,128)S(1)} %add.73), channel_id=1, source_target_pairs={{0,2},{2,0},{1,3},{3,1},{4,6},{6,4},{5,7},{7,5},{8,10},{10,8},{9,1... | collective-permute-start | bytes 147464 | tf_op jit(solution)/shard_map/gradient_exchange/ppermute | solution.py:232
  44.2 5.4 %collective-permute-start.5 = (f32[1,2,32,32]{3,2,1,0:T(8,128)S(1)}, f32[1,2,32,32]{3,2,1,0:T(8,128)S(1)}, u32[]{:S(2)}, u32[]{:S(2)}) collective-permute-start(f32[1,2,32,32]{3,2,1,0:T(8,128)S(1)} %get-tuple-element.4), channel_id=1, source_target_pairs={{0,8},{4,12},{8,0},{12,4},{1,5},{5,1},{9,13},{13,9},{2,10},{6,14},... | collective-permute-start | bytes 24584 | tf_op jit(solution)/shard_map/gradient_exchange/ppermute | solution.py:293
  44.7 4.9 %collective-permute-start.6 = (f32[1,2,32,32]{3,2,1,0:T(8,128)S(1)}, f32[1,2,32,32]{3,2,1,0:T(8,128)S(1)}, u32[]{:S(2)}, u32[]{:S(2)}) collective-permute-start(f32[1,2,32,32]{3,2,1,0:T(8,128)S(1)} %get-tuple-element.5), channel_id=1, source_target_pairs={{1,13},{5,9},{9,5},{13,1},{3,15},{7,11},{11,7},{15,3},{17,29},{21,... | collective-permute-start | bytes 24584 | tf_op jit(solution)/shard_map/gradient_exchange/ppermute | solution.py:293
  49.6 2.4 %collective-permute-start.7 = (f32[1,2,32,32]{3,2,1,0:T(8,128)S(1)}, f32[1,2,32,32]{3,2,1,0:T(8,128)S(1)}, u32[]{:S(2)}, u32[]{:S(2)}) collective-permute-start(f32[1,2,32,32]{3,2,1,0:T(8,128)S(1)} %add_add_fusion), channel_id=1, source_target_pairs={{0,1},{1,0},{2,3},{3,2},{4,5},{5,4},{6,7},{7,6},{8,9},{9,8},{10,11... | collective-permute-start | bytes 24584 | tf_op jit(solution)/shard_map/gradient_exchange/ppermute | solution.py:232
  51.9 0.8 %copy-start.4 = (f32[32,256]{1,0:T(8,128)S(1)}, f32[32,256]{1,0:T(8,128)}, u32[]{:S(2)}) copy-start(f32[32,256]{1,0:T(8,128)} %constant.60.clone.c_im_ref) | copy-start | bytes 98308
  52.9 0.8 %copy-start.2 = (f32[32,256]{1,0:T(8,128)S(1)}, f32[32,256]{1,0:T(8,128)}, u32[]{:S(2)}) copy-start(f32[32,256]{1,0:T(8,128)} %constant.59.clone.c_re_ref) | copy-start | bytes 98308

commit v8 on v7

--- a/solution.py
+++ b/solution.py
@@ -123,10 +123,9 @@
 def imaging_body(
     pos_ref, im_ref, sh_ref, w_ref, dose_ref, t_ref, ev_ref, goal_ref, h_ref, hc_ref,
     c_re_ref, c_im_ref, ct_re_ref, ct_im_ref, rw_top, rw_bot, rc_ref, la_ref, rhm_ref, rlh_ref,
-    slots_ref, f_buf, i_buf, u_buf,
+    slots_ref, f_buf, i_buf, u_buf, w_buf, xr_buf, xi_buf,
 ):
     count = f_buf.shape[0]
-    local_tiles = goal_ref.shape[0]
     pos = pos_ref[0]
     master = im_ref[pos]
     pick0 = (lax.broadcasted_iota(jnp.int32, (P_SIZE, 128), 0) == sh_ref[2 * pos]).astype(jnp.float32)
@@ -143,12 +142,19 @@
     s_im = t_ref[pos, 1] + (ph_re * m_im + ph_im * m_re)
     i_buf[...] = jnp.zeros(i_buf.shape, jnp.float32)
 
-    def forward(k, carry):
+    def spectrum(k, carry):
         h_re = h_ref[k, 0]
         h_im = h_ref[k, 1]
-        x_re = h_re * s_re - h_im * s_im
-        x_im = h_re * s_im + h_im * s_re
-        rows = dot_full(x_re, rw_top[...]) + dot_full(x_im, rw_bot[...])
+        rows = pl.ds(pl.multiple_of(k * B, B), B)
+        xr_buf[rows, :] = h_re * s_re - h_im * s_im
+        xi_buf[rows, :] = h_re * s_im + h_im * s_re
+        return carry
+
+    lax.fori_loop(0, count, spectrum, 0)
+    w_buf[...] = dot_full(xr_buf[...], rw_top[...]) + dot_full(xi_buf[...], rw_bot[...])
+
+    def forward(k, carry):
+        rows = w_buf[pl.ds(pl.multiple_of(k * B, B), B), :]
         swap = jnp.concatenate([-rows[:, P_SIZE:], rows[:, :P_SIZE]], axis=1)
         s_hi, s_mid, s_lo = split_three(jnp.concatenate([rows, swap], axis=0))
         stacked = jnp.concatenate([s_hi, s_mid, s_hi, s_lo, s_hi, s_mid], axis=0)
@@ -181,28 +187,29 @@
     flip = jnp.concatenate([acc, jnp.zeros((128 - B, 128), jnp.float32)], axis=0).T
     g_re = flip[0:B, 0:B] + flip[2 * B : 3 * B, 0:B]
     g_im = flip[B : 2 * B, 0:B] + flip[3 * B : 4 * B, 0:B]
-    slots_ref[...] = jnp.zeros(slots_ref.shape, jnp.float32)
-    slots_ref[pos, 0] = g_re
-    slots_ref[pos, 1] = g_im
-    slots_ref[local_tiles + master, 0] = ph_re * g_re + ph_im * g_im
-    slots_ref[local_tiles + master, 1] = ph_re * g_im - ph_im * g_re
+    slots_ref[0] = g_re
+    slots_ref[1] = g_im
+    slots_ref[2] = ph_re * g_re + ph_im * g_im
+    slots_ref[3] = ph_re * g_im - ph_im * g_re
 
 
 def imaging(pos, inst_master, inst_shift, weights, dose, tile_spec, every, target, kerns, h_cat):
     count = weights.shape[0]
     tables = imaging_tables()
-    slots = target.shape[0] + every.shape[0]
     vmem = pl.BlockSpec(memory_space=pltpu.VMEM)
     smem = pl.BlockSpec(memory_space=pltpu.SMEM)
     return pl.pallas_call(
         imaging_body,
-        out_shape=jax.ShapeDtypeStruct((slots, 2, B, B), jnp.float32),
+        out_shape=jax.ShapeDtypeStruct((4, B, B), jnp.float32),
         in_specs=[smem] * 5 + [vmem] * 5 + [vmem] * len(tables),
         out_specs=vmem,
         scratch_shapes=[
             pltpu.VMEM((count, P_SIZE, 2 * P_SIZE), jnp.float32),
             pltpu.VMEM((P_SIZE, P_SIZE), jnp.float32),
             pltpu.VMEM((count * B, 2 * P_SIZE), jnp.float32),
+            pltpu.VMEM((count * B, 2 * P_SIZE), jnp.float32),
+            pltpu.VMEM((count * B, B), jnp.float32),
+            pltpu.VMEM((count * B, B), jnp.float32),
         ],
     )(pos, inst_master, inst_shift, weights, dose, tile_spec, every, target, kerns, h_cat, *tables)
 
@@ -335,20 +342,23 @@
         ht_im = jnp.swapaxes(h_im, 1, 2) * twice
         h_cat = jnp.concatenate([ht_re, ht_re, ht_im, -ht_im], axis=-1).reshape(count * B, 128)
         shifts = inst_shift.reshape(-1)
-        slots = None
+        parts = []
         for j in range(per_dev):
             pos = jnp.reshape(first + j, (1,)).astype(jnp.int32)
-            part = imaging(
-                pos, inst_master, shifts, weights, corner_dose, tile_spec, every, target, kerns, h_cat
+            parts.append(
+                imaging(pos, inst_master, shifts, weights, corner_dose, tile_spec, every, target, kerns, h_cat)
             )
-            slots = part if slots is None else slots + part
+        comp = jnp.stack(parts)
 
     with jax.named_scope("gradient_exchange"):
         corner_count = lax.axis_size("corner")
-        slots = sum_all(slots, "kern", kern_count, kern_pos)
-        slots = sum_all(slots, "corner", corner_count, lax.axis_index("corner"))
-        mine_tiles = slots[:local_tiles]
-        terms = slots[local_tiles:]
+        comp = sum_all(comp, "corner", corner_count, lax.axis_index("corner"))
+        both = gather_all(comp, "kern", kern_count, kern_pos)
+        mine_tiles = both[:, 0:2]
+        owner_pick = (
+            inst_master[:, None] == jnp.arange(region_masters, dtype=jnp.int32)[None, :]
+        ).astype(jnp.float32)
+        terms = jnp.sum(owner_pick[:, :, None, None, None] * both[:, None, 2:4], axis=0)
         if xor_partners(tile_count) and xor_partners(kern_count) and tile_count > 2:
             mine_masters = scatter_split(terms, tile_count, tile_pos, kern_count, kern_pos, local_masters)
         else:

time: 56.2 us -> 53.3 us (0.948)
  waiting for transfers between devices: 10.1 us -> 7.2 us
  Pallas kernels: 16.3 us -> 14.7 us
  starting transfers between devices: 10.5 us -> 11.4 us
  local copies, waits for them, and re-layouts: 4.86 us -> 5.58 us
    ppermute x4 -> x3, waiting for transfers between devices: 7.01 us -> 2.99 us  [sum_all(): x = x + lax.ppermute(x, axis, [(i, i ^ step) for i in range(count)])]
    pallas_call x1, Pallas kernels: 16.3 us -> 14.7 us  [imaging(): pl.pallas_call(imaging_body, out_shape=jax.ShapeDtypeStruct((4, B, B), jn...]
    ppermute x0 -> x1, waiting for transfers between devices: none -> 1.12 us  [gather_all(): got = lax.ppermute(x, axis, [(i, i ^ step) for i in range(count)])]
    ppermute x4 -> x3, starting transfers between devices: 4.65 us -> 5.42 us  [sum_all(): x = x + lax.ppermute(x, axis, [(i, i ^ step) for i in range(count)])]
    unnamed x22 -> x24, local copies, waits for them, and re-layouts: 3.92 us -> 4.37 us
where the time goes in v8:
time: 53.3 us; the launch traced here: 52.7 us
  Pallas kernels  14.7 us (28%)
  starting transfers between devices  11.4 us (21%)
  matrix products  8.38 us (16%)
  waiting for transfers between devices  7.2 us (14%)
  local copies, waits for them, and re-layouts  5.58 us (10%)
  other arithmetic  3.68 us (7%)
  between operations  1.76 us (3%)
    pallas_call x1, Pallas kernels, imaging(): pl.pallas_call(imaging_body, out_shape=jax.ShapeDtypeStruct((4, B, B), jn...  14.7 us
    ppermute x3, starting transfers between devices, sum_all(): x = x + lax.ppermute(x, axis, [(i, i ^ step) for i in range(count)])  5.42 us
    ppermute x2, starting transfers between devices, gather_split(): got = lax.ppermute(x, ('tile', 'kern'), pairs)  4.75 us
    unnamed x24, local copies, waits for them, and re-layouts  4.37 us
    ppermute x2, waiting for transfers between devices, scatter_split(): total = total + lax.ppermute(part, ('tile', 'kern'), pairs)  3.09 us
    ppermute x3, waiting for transfers between devices, sum_all(): x = x + lax.ppermute(x, axis, [(i, i ^ step) for i in range(count)])  2.99 us
    dot_general x2, matrix products, back_pixels(): jnp.einsum('nxc,cy->nxy', half_im, sin_tab, precision=precise)  2.53 us
    dot_general x2, matrix products, spectra(): rows_re = jnp.einsum('bx,nxy->nby', cos_tab, masks, precision=precise)  1.32 us
  transfers between devices with their start and end apart: 8, of which 3 were waited for; matrix products, arithmetic and copies ran while one was open for 12% of the time, Pallas kernels for 0%

profile of v8, /device:TPU:0, one launch (start us, length us, event | category | flops | bytes accessed | tf_op | source)
XLA Modules:
  0.0 52.7 jit_solution(1189895802834140582)
XLA Ops:
  0.7 0.8 %copy-done.1 = f32[32,256]{1,0:T(8,128)S(1)} copy-done((f32[32,256]{1,0:T(8,128)S(1)}, f32[32,256]{1,0:T(8,128)}, u32[]{:S(2)}) %copy-start.1) | copy-done | bytes 32792
  1.4 1.1 %fusion.15 = f32[32,256]{1,0:T(8,128)S(1)} fusion(f32[32,256]{1,0:T(8,128)S(1)} %copy-done.1, bf16[1,256,256]{2,1,0:T(8,128)(2,1)} %param.21), kind=kOutput, calls=%fused_computation.31 | convolution fusion | flops 25165824 | bytes 196608 | tf_op jit(solution)/shard_map/master_spectra/bx,nxy->nby/dot_general | solution.py:38
  3.5 4.1 %collective-permute-start = (f32[1,2,32,32]{3,2,1,0:T(8,128)S(1)}, f32[1,2,32,32]{3,2,1,0:T(8,128)S(1)}, u32[]{:S(2)}, u32[]{:S(2)}) collective-permute-start(f32[1,2,32,32]{3,2,1,0:T(8,128)S(1)} %get-tuple-element.7), channel_id=1, source_target_pairs={{8,0},{12,4},{0,8},{4,12},{5,1},{1,5},{13,9},{9,13},{10,2},{14,6},... | collective-permute-start | bytes 24584 | tf_op jit(solution)/shard_map/master_spectra/ppermute | solution.py:280
  7.6 0.7 %collective-permute-start.1 = (f32[1,2,32,32]{3,2,1,0:T(8,128)S(1)}, f32[1,2,32,32]{3,2,1,0:T(8,128)S(1)}, u32[]{:S(2)}, u32[]{:S(2)}) collective-permute-start(f32[1,2,32,32]{3,2,1,0:T(8,128)S(1)} %get-tuple-element.7), channel_id=1, source_target_pairs={{13,1},{9,5},{5,9},{1,13},{15,3},{11,7},{7,11},{3,15},{29,17},{25,... | collective-permute-start | bytes 24584 | tf_op jit(solution)/shard_map/master_spectra/ppermute | solution.py:280
  8.3 0.6 %copy-done.10 = f32[1,12]{1,0:T(1,128)S(1)} copy-done((f32[1,12]{1,0:T(1,128)S(1)}, f32[1,12]{1,0:T(1,128)}, u32[]{:S(2)}) %copy-start.10) | copy-done | bytes 72
  9.1 0.7 %copy-done.7 = f32[32,256,1]{1,0,2:T(8,128)S(1)} copy-done((f32[32,256,1]{1,0,2:T(8,128)S(1)}, f32[32,256,1]{1,0,2:T(8,128)}, u32[]{:S(2)}) %copy-start.7) | copy-done | bytes 32792
  9.8 0.2 convolution_bitcast_fusion.1
  10.0 0.5 %copy-done.6 = f32[32,256,1]{1,0,2:T(8,128)S(1)} copy-done((f32[32,256,1]{1,0,2:T(8,128)S(1)}, f32[32,256,1]{1,0,2:T(8,128)}, u32[]{:S(2)}) %copy-start.6) | copy-done | bytes 32792
  10.6 0.2 convolution_bitcast_fusion
  12.0 0.4 copy-done.9
  12.5 0.6 %pad_maximum_fusion.1.t_ref = f32[2,2,32,32]{3,2,1,0:T(8,128)} fusion(f32[2,1,32,32]{3,2,1,0:T(8,128)S(1)} %fusion.5, f32[2,1,32,32]{3,2,1,0:T(8,128)S(1)} %fusion.6), kind=kLoop, calls=%fused_computation.36 | loop fusion | flops 4096 | bytes 32768 | tf_op jit(solution)/shard_map/tile_spectra/stack | solution.py:330
  13.1 0.9 %pad_maximum_fusion = f32[12,32,128]{2,1,0:T(8,128)} fusion(f32[12,32,32]{2,1,0:T(8,128)S(1)} %copy.33, f32[12,32,32]{2,1,0:T(8,128)S(1)} %copy.32, f32[12,32,32]{2,1,0:T(8,128)S(1)} %copy.30), kind=kLoop, calls=%fused_computation.28 | loop fusion | flops 147456 | bytes 344064 | tf_op jit(solution)/shard_map/imaging_kernel/concatenate | solution.py:343
  14.1 2.0 %collective-permute-start.2 = (f32[4,2,32,32]{3,2,1,0:T(8,128)S(1)}, f32[4,2,32,32]{3,2,1,0:T(8,128)S(1)}, u32[]{:S(2)}, u32[]{:S(2)}) collective-permute-start(f32[4,2,32,32]{3,2,1,0:T(8,128)S(1)} %select_add_fusion.2), channel_id=1, source_target_pairs={{0,1},{1,0},{2,3},{3,2},{4,5},{5,4},{6,7},{7,6},{8,9},{9,8},{10,11... | collective-permute-start | bytes 98312 | tf_op jit(solution)/shard_map/master_spectra/ppermute | solution.py:239
  16.9 0.6 %reshape.126.sh_ref = s32[4]{0:T(128)} reshape(s32[2,2]{1,0:T(2,128)S(1)} %copy-done.11) | data formatting | bytes 32 | tf_op jit(solution)/shard_map/imaging_kernel/reshape | solution.py:344
  17.5 0.8 %select_add_fusion.1.ev_ref = f32[4,2,32,32]{3,2,1,0:T(8,128)} fusion(f32[4,2,32,32]{3,2,1,0:T(8,128)S(1)} %collective-permute-done.2, f32[2,32,32]{2,1,0:T(8,128)S(1)} %get-tuple-element.6, pred[4]{0:T(512)(128)(4,1)S(1)} %iota_compare_fusion.1, f32[2,32,32]{2,1,0:T(8,128)S(1)} %bitcast.133, pred[4]{0:T(512)(128)(4,1)S(1)} %get-tuple-element.8, ...), kind=kLoop, calls=%fused_computation.34 | loop fusion | flops 49152 | bytes 90124 | tf_op jit(solution)/shard_map/master_spectra/add | solution.py:285
  18.2 14.7 %imaging_kernel.1 = f32[4,32,32]{2,1,0:T(8,128)} custom-call(s32[1]{0:T(128)} %bitcast.pos_ref, s32[2]{0:T(128)} %im_ref.1, s32[4]{0:T(128)} %reshape.126.sh_ref, f32[12]{0:T(128)} %bitcast.135, f32[1]{0:T(128)S(6)} %copy.38.dose_ref, f32[2,2,32,32]{3,2,1,0:T(8,128)} %pad_maximum_fusion.1.t_ref, f32[4,2,32,32]{3,2,1,0:T(8,128)} %select_add_fusion.1.ev_ref, ...), custom_call_target="tpu_custom_call" | custom-call | tf_op jit(solution)/shard_map/imaging_kernel/pallas_call | solution.py:201
  33.0 1.5 %collective-permute-start.3 = (f32[1,4,32,32]{3,2,1,0:T(8,128)}, f32[1,4,32,32]{3,2,1,0:T(8,128)S(1)}, u32[]{:S(2)}, u32[]{:S(2)}) collective-permute-start(f32[1,4,32,32]{3,2,1,0:T(8,128)} %bitcast.128), channel_id=1, source_target_pairs={{0,2},{2,0},{1,3},{3,1},{4,6},{6,4},{5,7},{7,5},{8,10},{10,8},{9,1... | collective-permute-start | bytes 49160 | tf_op jit(solution)/shard_map/gradient_exchange/ppermute | solution.py:239
  34.5 3.0 %collective-permute-done.3 = f32[1,4,32,32]{3,2,1,0:T(8,128)S(1)} collective-permute-done((f32[1,4,32,32]{3,2,1,0:T(8,128)}, f32[1,4,32,32]{3,2,1,0:T(8,128)S(1)}, u32[]{:S(2)}, u32[]{:S(2)}) %collective-permute-start.3) | collective-permute-done | bytes 16416 | tf_op jit(solution)/shard_map/gradient_exchange/ppermute | solution.py:239
  37.5 0.8 %bitcast_add_fusion = f32[1,4,32,32]{3,2,1,0:T(8,128)S(1)} fusion(f32[1,4,32,32]{3,2,1,0:T(8,128)S(1)} %collective-permute-done.3, f32[4,32,32]{2,1,0:T(8,128)} %imaging_kernel.1), kind=kLoop, calls=%fused_computation.56 | loop fusion | flops 4096 | bytes 49152 | tf_op jit(solution)/shard_map/gradient_exchange/add | solution.py:239
  38.5 1.1 %collective-permute-done.4 = f32[1,4,32,32]{3,2,1,0:T(8,128)S(1)} collective-permute-done((f32[1,4,32,32]{3,2,1,0:T(8,128)S(1)}, f32[1,4,32,32]{3,2,1,0:T(8,128)S(1)}, u32[]{:S(2)}, u32[]{:S(2)}) %collective-permute-start.4) | collective-permute-done | bytes 16416 | tf_op jit(solution)/shard_map/gradient_exchange/ppermute | solution.py:228
  40.4 0.5 collective-permute-start.5
  40.9 0.7 %collective-permute-start.6 = (f32[1,2,32,32]{3,2,1,0:T(8,128)S(1)}, f32[1,2,32,32]{3,2,1,0:T(8,128)S(1)}, u32[]{:S(2)}, u32[]{:S(2)}) collective-permute-start(f32[1,2,32,32]{3,2,1,0:T(8,128)S(1)} %get-tuple-element.5), channel_id=1, source_target_pairs={{1,13},{5,9},{9,5},{13,1},{3,15},{7,11},{11,7},{15,3},{17,29},{21,... | collective-permute-start | bytes 24584 | tf_op jit(solution)/shard_map/gradient_exchange/ppermute | solution.py:300
  41.7 0.6 %fusion.28 = f32[2,256,256]{2,1,0:T(8,128)S(1)} fusion(f32[2,256,32]{1,2,0:T(8,128)S(1)} %fusion.2, f32[32,256,1]{1,0,2:T(8,128)S(1)} %copy-done.7), kind=kOutput, calls=%fused_computation.63 | convolution fusion | flops 50331648 | bytes 622592 | tf_op jit(solution)/shard_map/pixel_gradients/nxc,cy->nxy/dot_general | solution.py:56
  42.6 3.1 %collective-permute-done.5 = f32[1,2,32,32]{3,2,1,0:T(8,128)S(1)} collective-permute-done((f32[1,2,32,32]{3,2,1,0:T(8,128)S(1)}, f32[1,2,32,32]{3,2,1,0:T(8,128)S(1)}, u32[]{:S(2)}, u32[]{:S(2)}) %collective-permute-start.5) | collective-permute-done | bytes 8224 | tf_op jit(solution)/shard_map/gradient_exchange/ppermute | solution.py:300
  45.7 1.9 %collective-permute-start.7 = (f32[1,2,32,32]{3,2,1,0:T(8,128)S(1)}, f32[1,2,32,32]{3,2,1,0:T(8,128)S(1)}, u32[]{:S(2)}, u32[]{:S(2)}) collective-permute-start(f32[1,2,32,32]{3,2,1,0:T(8,128)S(1)} %add_add_fusion), channel_id=1, source_target_pairs={{0,1},{1,0},{2,3},{3,2},{4,5},{5,4},{6,7},{7,6},{8,9},{9,8},{10,11... | collective-permute-start | bytes 24584 | tf_op jit(solution)/shard_map/gradient_exchange/ppermute | solution.py:239
  47.5 1.4 %convolution_add_fusion = f32[2,256,256]{2,1,0:T(8,128)} fusion(f32[2,256,256]{2,1,0:T(8,128)S(1)} %fusion.28, f32[2,256,32]{1,2,0:T(8,128)S(1)} %fusion.1, f32[32,256,1]{1,0,2:T(8,128)S(1)} %copy-done.6), kind=kOutput, calls=%fused_computation | convolution fusion | flops 50462720 | bytes 1146880 | tf_op jit(solution)/shard_map/pixel_gradients/nxc,cy->nxy/dot_general | solution.py:56
  49.0 0.7 %copy-done.4 = f32[32,256]{1,0:T(8,128)S(1)} copy-done((f32[32,256]{1,0:T(8,128)S(1)}, f32[32,256]{1,0:T(8,128)}, u32[]{:S(2)}) %copy-start.4) | copy-done | bytes 32792
  50.0 0.2 fusion.20
  50.2 0.5 copy-done.2
  50.9 0.2 fusion.4
  51.2 0.4 fusion.29
  51.6 1.1 %fusion = f32[1,256,256]{2,1,0:T(8,128)} fusion(f32[256,256]{1,0:T(8,128)S(1)} %fusion.29, f32[256,32]{0,1:T(8,128)S(1)} %fusion.3, f32[32,256]{1,0:T(8,128)S(1)} %copy-done.4), kind=kOutput, calls=%fused_computation.2 | convolution fusion | flops 25231360 | bytes 589824 | tf_op jit(solution)/shard_map/pixel_gradients/nxc,cy->nxy/dot_general | solution.py:56
  (60 shorter events, 4.1 us)
Async XLA Ops:
  0.6 8.5 %copy-start = (bf16[2,256,256]{2,1,0:T(8,128)(2,1)S(1)}, bf16[2,256,256]{2,1,0:T(8,128)(2,1)}, u32[]{:S(2)}) copy-start(bf16[2,256,256]{2,1,0:T(8,128)(2,1)} %param.20) | copy-start | bytes 786436
  0.6 0.8 %copy-start.1 = (f32[32,256]{1,0:T(8,128)S(1)}, f32[32,256]{1,0:T(8,128)}, u32[]{:S(2)}) copy-start(f32[32,256]{1,0:T(8,128)} %constant.70.clone.c_re_ref) | copy-start | bytes 98308
  0.7 1.9 %copy-start.3 = (f32[32,256]{1,0:T(8,128)S(1)}, f32[32,256]{1,0:T(8,128)}, u32[]{:S(2)}) copy-start(f32[32,256]{1,0:T(8,128)} %constant.71.clone.c_im_ref) | copy-start | bytes 98308
  0.7 1.9 %copy-start.8 = (bf16[1,256,256]{2,1,0:T(8,128)(2,1)S(1)}, bf16[1,256,256]{2,1,0:T(8,128)(2,1)}, u32[]{:S(2)}) copy-start(bf16[1,256,256]{2,1,0:T(8,128)(2,1)} %param.21) | copy-start | bytes 393220
  2.6 6.4 %copy-start.5 = (f32[1,12,2,32,32]{4,3,2,1,0:T(8,128)S(1)}, f32[1,12,2,32,32]{4,3,2,1,0:T(8,128)}, u32[]{:S(2)}) copy-start(f32[1,12,2,32,32]{4,3,2,1,0:T(8,128)} %param.25) | copy-start | bytes 294916
  3.5 10.5 %collective-permute-start = (f32[1,2,32,32]{3,2,1,0:T(8,128)S(1)}, f32[1,2,32,32]{3,2,1,0:T(8,128)S(1)}, u32[]{:S(2)}, u32[]{:S(2)}) collective-permute-start(f32[1,2,32,32]{3,2,1,0:T(8,128)S(1)} %get-tuple-element.7), channel_id=1, source_target_pairs={{8,0},{12,4},{0,8},{4,12},{5,1},{1,5},{13,9},{9,13},{10,2},{14,6},... | collective-permute-start | bytes 24584 | tf_op jit(solution)/shard_map/master_spectra/ppermute | solution.py:280
  7.6 6.4 %collective-permute-start.1 = (f32[1,2,32,32]{3,2,1,0:T(8,128)S(1)}, f32[1,2,32,32]{3,2,1,0:T(8,128)S(1)}, u32[]{:S(2)}, u32[]{:S(2)}) collective-permute-start(f32[1,2,32,32]{3,2,1,0:T(8,128)S(1)} %get-tuple-element.7), channel_id=1, source_target_pairs={{13,1},{9,5},{5,9},{1,13},{15,3},{11,7},{7,11},{3,15},{29,17},{25,... | collective-permute-start | bytes 24584 | tf_op jit(solution)/shard_map/master_spectra/ppermute | solution.py:280
  8.3 0.7 %copy-start.10 = (f32[1,12]{1,0:T(1,128)S(1)}, f32[1,12]{1,0:T(1,128)}, u32[]{:S(2)}) copy-start(f32[1,12]{1,0:T(1,128)} %param.26) | copy-start | bytes 148
  9.0 0.8 %copy-start.7 = (f32[32,256,1]{1,0,2:T(8,128)S(1)}, f32[32,256,1]{1,0,2:T(8,128)}, u32[]{:S(2)}) copy-start(f32[32,256,1]{1,0,2:T(8,128)} %constant.88) | copy-start | bytes 98308
  9.8 0.8 %copy-start.6 = (f32[32,256,1]{1,0,2:T(8,128)S(1)}, f32[32,256,1]{1,0,2:T(8,128)}, u32[]{:S(2)}) copy-start(f32[32,256,1]{1,0,2:T(8,128)} %constant.89) | copy-start | bytes 98308
  11.8 0.7 %copy-start.9 = (s32[2]{0:T(128)S(1)}, s32[2]{0:T(128)}, u32[]{:S(2)}) copy-start(s32[2]{0:T(128)} %im_ref.1) | copy-start | bytes 28
  14.1 3.4 %collective-permute-start.2 = (f32[4,2,32,32]{3,2,1,0:T(8,128)S(1)}, f32[4,2,32,32]{3,2,1,0:T(8,128)S(1)}, u32[]{:S(2)}, u32[]{:S(2)}) collective-permute-start(f32[4,2,32,32]{3,2,1,0:T(8,128)S(1)} %select_add_fusion.2), channel_id=1, source_target_pairs={{0,1},{1,0},{2,3},{3,2},{4,5},{5,4},{6,7},{7,6},{8,9},{9,8},{10,11... | collective-permute-start | bytes 98312 | tf_op jit(solution)/shard_map/master_spectra/ppermute | solution.py:239
  16.2 0.7 %copy-start.11 = (s32[2,2]{1,0:T(2,128)S(1)}, s32[2,2]{1,0:T(2,128)}, u32[]{:S(2)}) copy-start(s32[2,2]{1,0:T(2,128)} %param.24) | copy-start | bytes 52
  33.0 4.5 %collective-permute-start.3 = (f32[1,4,32,32]{3,2,1,0:T(8,128)}, f32[1,4,32,32]{3,2,1,0:T(8,128)S(1)}, u32[]{:S(2)}, u32[]{:S(2)}) collective-permute-start(f32[1,4,32,32]{3,2,1,0:T(8,128)} %bitcast.128), channel_id=1, source_target_pairs={{0,2},{2,0},{1,3},{3,1},{4,6},{6,4},{5,7},{7,5},{8,10},{10,8},{9,1... | collective-permute-start | bytes 49160 | tf_op jit(solution)/shard_map/gradient_exchange/ppermute | solution.py:239
  38.3 1.3 %collective-permute-start.4 = (f32[1,4,32,32]{3,2,1,0:T(8,128)S(1)}, f32[1,4,32,32]{3,2,1,0:T(8,128)S(1)}, u32[]{:S(2)}, u32[]{:S(2)}) collective-permute-start(f32[1,4,32,32]{3,2,1,0:T(8,128)S(1)} %bitcast_add_fusion), channel_id=1, source_target_pairs={{0,1},{1,0},{2,3},{3,2},{4,5},{5,4},{6,7},{7,6},{8,9},{9,8},{10,11... | collective-permute-start | bytes 49160 | tf_op jit(solution)/shard_map/gradient_exchange/ppermute | solution.py:228
  40.4 5.2 %collective-permute-start.5 = (f32[1,2,32,32]{3,2,1,0:T(8,128)S(1)}, f32[1,2,32,32]{3,2,1,0:T(8,128)S(1)}, u32[]{:S(2)}, u32[]{:S(2)}) collective-permute-start(f32[1,2,32,32]{3,2,1,0:T(8,128)S(1)} %get-tuple-element.4), channel_id=1, source_target_pairs={{0,8},{4,12},{8,0},{12,4},{1,5},{5,1},{9,13},{13,9},{2,10},{6,14},... | collective-permute-start | bytes 24584 | tf_op jit(solution)/shard_map/gradient_exchange/ppermute | solution.py:300
  40.9 4.8 %collective-permute-start.6 = (f32[1,2,32,32]{3,2,1,0:T(8,128)S(1)}, f32[1,2,32,32]{3,2,1,0:T(8,128)S(1)}, u32[]{:S(2)}, u32[]{:S(2)}) collective-permute-start(f32[1,2,32,32]{3,2,1,0:T(8,128)S(1)} %get-tuple-element.5), channel_id=1, source_target_pairs={{1,13},{5,9},{9,5},{13,1},{3,15},{7,11},{11,7},{15,3},{17,29},{21,... | collective-permute-start | bytes 24584 | tf_op jit(solution)/shard_map/gradient_exchange/ppermute | solution.py:300
  45.7 3.3 %collective-permute-start.7 = (f32[1,2,32,32]{3,2,1,0:T(8,128)S(1)}, f32[1,2,32,32]{3,2,1,0:T(8,128)S(1)}, u32[]{:S(2)}, u32[]{:S(2)}) collective-permute-start(f32[1,2,32,32]{3,2,1,0:T(8,128)S(1)} %add_add_fusion), channel_id=1, source_target_pairs={{0,1},{1,0},{2,3},{3,2},{4,5},{5,4},{6,7},{7,6},{8,9},{9,8},{10,11... | collective-permute-start | bytes 24584 | tf_op jit(solution)/shard_map/gradient_exchange/ppermute | solution.py:239
  49.0 0.8 %copy-start.4 = (f32[32,256]{1,0:T(8,128)S(1)}, f32[32,256]{1,0:T(8,128)}, u32[]{:S(2)}) copy-start(f32[32,256]{1,0:T(8,128)} %constant.71.clone.c_im_ref) | copy-start | bytes 98308
  49.9 0.8 %copy-start.2 = (f32[32,256]{1,0:T(8,128)S(1)}, f32[32,256]{1,0:T(8,128)}, u32[]{:S(2)}) copy-start(f32[32,256]{1,0:T(8,128)} %constant.70.clone.c_re_ref) | copy-start | bytes 98308

commit v9 on v8

--- a/solution.py
+++ b/solution.py
@@ -121,23 +121,25 @@
 
 
 def imaging_body(
-    pos_ref, im_ref, sh_ref, w_ref, dose_ref, t_ref, ev_ref, goal_ref, h_ref, hc_ref,
+    pos_ref, im_ref, sh_ref, w_ref, dose_ref, t_ref, ev_ref, own_ref, goal_ref, h_ref, hc_ref,
     c_re_ref, c_im_ref, ct_re_ref, ct_im_ref, rw_top, rw_bot, rc_ref, la_ref, rhm_ref, rlh_ref,
     slots_ref, f_buf, i_buf, u_buf, w_buf, xr_buf, xi_buf,
 ):
     count = f_buf.shape[0]
     pos = pos_ref[0]
     master = im_ref[pos]
-    pick0 = (lax.broadcasted_iota(jnp.int32, (P_SIZE, 128), 0) == sh_ref[2 * pos]).astype(jnp.float32)
-    pick1 = (lax.broadcasted_iota(jnp.int32, (8, P_SIZE), 1) == sh_ref[2 * pos + 1]).astype(jnp.float32)
+    pick0 = (lax.broadcasted_iota(jnp.int32, (P_SIZE, 128), 0) == sh_ref[pos, 0]).astype(jnp.float32)
+    pick1 = (lax.broadcasted_iota(jnp.int32, (8, P_SIZE), 1) == sh_ref[pos, 1]).astype(jnp.float32)
     e0_re = dot_full(c_re_ref[...], pick0)[:, 0:1]
     e0_im = dot_full(c_im_ref[...], pick0)[:, 0:1]
     e1_re = dot_full(pick1, ct_re_ref[...])[0:1, :]
     e1_im = dot_full(pick1, ct_im_ref[...])[0:1, :]
     ph_re = e0_re * e1_re - e0_im * e1_im
     ph_im = e0_re * e1_im + e0_im * e1_re
-    m_re = ev_ref[master, 0]
-    m_im = ev_ref[master, 1]
+    local_masters = own_ref.shape[0]
+    is_own = master // local_masters == pos_ref[1]
+    m_re = ev_ref[master, 0] + jnp.where(is_own, own_ref[master % local_masters, 0], 0.0)
+    m_im = ev_ref[master, 1] + jnp.where(is_own, own_ref[master % local_masters, 1], 0.0)
     s_re = t_ref[pos, 0] + (ph_re * m_re - ph_im * m_im)
     s_im = t_ref[pos, 1] + (ph_re * m_im + ph_im * m_re)
     i_buf[...] = jnp.zeros(i_buf.shape, jnp.float32)
@@ -193,7 +195,7 @@
     slots_ref[3] = ph_re * g_im - ph_im * g_re
 
 
-def imaging(pos, inst_master, inst_shift, weights, dose, tile_spec, every, target, kerns, h_cat):
+def imaging(pos, inst_master, inst_shift, weights, dose, tile_spec, every, own, target, kerns, h_cat):
     count = weights.shape[0]
     tables = imaging_tables()
     vmem = pl.BlockSpec(memory_space=pltpu.VMEM)
@@ -201,7 +203,7 @@
     return pl.pallas_call(
         imaging_body,
         out_shape=jax.ShapeDtypeStruct((4, B, B), jnp.float32),
-        in_specs=[smem] * 5 + [vmem] * 5 + [vmem] * len(tables),
+        in_specs=[smem] * 5 + [vmem] * 6 + [vmem] * len(tables),
         out_specs=vmem,
         scratch_shapes=[
             pltpu.VMEM((count, P_SIZE, 2 * P_SIZE), jnp.float32),
@@ -211,7 +213,33 @@
             pltpu.VMEM((count * B, B), jnp.float32),
             pltpu.VMEM((count * B, B), jnp.float32),
         ],
-    )(pos, inst_master, inst_shift, weights, dose, tile_spec, every, target, kerns, h_cat, *tables)
+    )(pos, inst_master, inst_shift, weights, dose, tile_spec, every, own, target, kerns, h_cat, *tables)
+
+
+def pixel_body(x_ref, left_ref, c_re_ref, c_im_ref, out_ref):
+    for n in range(out_ref.shape[0]):
+        x_re = x_ref[n, 0]
+        x_im = x_ref[n, 1]
+        half_re = dot_full(left_ref[...], jnp.concatenate([x_re, x_im], axis=0))
+        half_im = dot_full(left_ref[...], jnp.concatenate([x_im, -x_re], axis=0))
+        out_ref[n] = dot_full(half_re, c_re_ref[...]) + dot_full(half_im, c_im_ref[...])
+
+
+def pixels(x):
+    freq = np.arange(B, dtype=np.int64) - B // 2
+    pixel = np.arange(P_SIZE, dtype=np.int64)
+    angle = (2.0 * math.pi / P_SIZE) * np.mod(freq[:, None] * pixel[None, :], P_SIZE).astype(np.float64)
+    c_re = np.cos(angle)
+    c_im = -np.sin(angle)
+    left = np.concatenate([c_re.T, c_im.T], axis=1)
+    tables = [jnp.asarray(table, jnp.float32) for table in (left, c_re, c_im)]
+    vmem = pl.BlockSpec(memory_space=pltpu.VMEM)
+    return pl.pallas_call(
+        pixel_body,
+        out_shape=jax.ShapeDtypeStruct((x.shape[0], P_SIZE, P_SIZE), jnp.float32),
+        in_specs=[vmem] * 4,
+        out_specs=vmem,
+    )(x, *tables)
 
 
 def xor_partners(count):
@@ -281,8 +309,7 @@
         step = chosen_step(lists, r, kern_pos)
         source = jnp.where(step >= 0, pos ^ step, -1)
         collected = collected + jnp.where((slot == source)[:, None, None, None], spread(got), 0.0)
-    collected = sum_all(collected, "kern", kern_count, kern_pos)
-    return collected + jnp.where((slot == pos)[:, None, None, None], spread(x), 0.0)
+    return sum_all(collected, "kern", kern_count, kern_pos)
 
 
 def scatter_split(x, count, pos, kern_count, kern_pos, size):
@@ -322,8 +349,10 @@
         own = jnp.stack([own_re, own_im], axis=1)
         if xor_partners(tile_count) and xor_partners(kern_count) and tile_count > 2:
             every = gather_split(own, tile_count, tile_pos, kern_count, kern_pos)
+            own_part = own
         else:
             every = gather_all(own, "tile", tile_count, tile_pos)
+            own_part = jnp.zeros_like(own)
 
     with jax.named_scope("tile_spectra"):
         tile_re, tile_im = spectra(tile_mask.astype(jnp.float32), cos_tab, sin_tab)
@@ -341,12 +370,14 @@
         ht_re = jnp.swapaxes(h_re, 1, 2) * twice
         ht_im = jnp.swapaxes(h_im, 1, 2) * twice
         h_cat = jnp.concatenate([ht_re, ht_re, ht_im, -ht_im], axis=-1).reshape(count * B, 128)
-        shifts = inst_shift.reshape(-1)
         parts = []
         for j in range(per_dev):
-            pos = jnp.reshape(first + j, (1,)).astype(jnp.int32)
+            pos = jnp.stack([first + j, tile_pos]).astype(jnp.int32)
             parts.append(
-                imaging(pos, inst_master, shifts, weights, corner_dose, tile_spec, every, target, kerns, h_cat)
+                imaging(
+                    pos, inst_master, inst_shift, weights, corner_dose, tile_spec, every, own_part, target,
+                    kerns, h_cat,
+                )
             )
         comp = jnp.stack(parts)
 
@@ -365,8 +396,8 @@
             mine_masters = scatter_sum(terms, "tile", tile_count, tile_pos, local_masters)
 
     with jax.named_scope("pixel_gradients"):
-        tile_grad = back_pixels(mine_tiles[:, 0], mine_tiles[:, 1], cos_tab, sin_tab)
-        master_grad = back_pixels(mine_masters[:, 0], mine_masters[:, 1], cos_tab, sin_tab)
+        tile_grad = pixels(mine_tiles)
+        master_grad = pixels(mine_masters)
     return (tile_grad, master_grad)
 
 

time: 53.3 us -> 53.8 us (level)
  Pallas kernels: 14.7 us -> 20.4 us
  matrix products: 8.38 us -> 3.19 us
  local copies, waits for them, and re-layouts: 5.58 us -> 3.62 us
  other arithmetic: 3.68 us -> 4.84 us
  waiting for transfers between devices: 7.2 us -> 8.23 us
    pallas_call x0 -> x2, Pallas kernels: none -> 5.64 us  [pixels(): pl.pallas_call(pixel_body, out_shape=jax.ShapeDtypeStruct((x.shape[0], P_...]
    dot_general x12 -> x0, matrix products: 5.2 us -> none  [the longest x2 2.53 us: back_pixels(): jnp.einsum('nxc,cy->nxy', half_im, sin_tab, precision=precise)]
    unnamed x24 -> x20, local copies, waits for them, and re-layouts: 4.37 us -> 2.63 us
    add x2 -> x3, other arithmetic: 0.86 us -> 2.21 us  [sum_all(): x = x + lax.ppermute(x, axis, [(i, i ^ step) for i in range(count)])]
    ppermute x2, waiting for transfers between devices: 3.09 us -> 4.1 us  [scatter_split(): total = total + lax.ppermute(part, ('tile', 'kern'), pairs)]
    add x1 -> x0, other arithmetic: 0.75 us -> none  [gather_split(): collected + jnp.where((slot == pos)[:, None, None, None], spread(x), 0.0)]
    reshape x1 -> x0, local copies, waits for them, and re-layouts: 0.62 us -> none  [on_device(): shifts = inst_shift.reshape(-1)]
    another operation x1 -> x2, other arithmetic: 0.01 us -> 0.58 us  [the longest x1 0.58 us: on_device(): pos = jnp.stack([first + j, tile_pos]).astype(jnp.int32)]
  transfers between devices with their start and end apart: 8 -> 8, of which waited for: 3 -> 3; matrix products, arithmetic and copies ran while one was open for 12% -> 7% of each run, Pallas kernels for 0% -> 6%
where the time goes in v9:
time: 53.8 us; the launch traced here: 53.4 us
  Pallas kernels  20.4 us (38%)
  starting transfers between devices  11.4 us (21%)
  waiting for transfers between devices  8.23 us (15%)
  other arithmetic  4.84 us (9%)
  local copies, waits for them, and re-layouts  3.62 us (7%)
  matrix products  3.19 us (6%)
  between operations  1.64 us (3%)
    pallas_call x1, Pallas kernels, imaging(): pl.pallas_call(imaging_body, out_shape=jax.ShapeDtypeStruct((4, B, B), jn...  14.8 us
    pallas_call x2, Pallas kernels, pixels(): pl.pallas_call(pixel_body, out_shape=jax.ShapeDtypeStruct((x.shape[0], P_...  5.64 us
    ppermute x3, starting transfers between devices, sum_all(): x = x + lax.ppermute(x, axis, [(i, i ^ step) for i in range(count)])  5.51 us
    ppermute x2, starting transfers between devices, gather_split(): got = lax.ppermute(x, ('tile', 'kern'), pairs)  4.75 us
    ppermute x2, waiting for transfers between devices, scatter_split(): total = total + lax.ppermute(part, ('tile', 'kern'), pairs)  4.1 us
    ppermute x3, waiting for transfers between devices, sum_all(): x = x + lax.ppermute(x, axis, [(i, i ^ step) for i in range(count)])  2.91 us
    unnamed x20, local copies, waits for them, and re-layouts  2.63 us
    add x3, other arithmetic, sum_all(): x = x + lax.ppermute(x, axis, [(i, i ^ step) for i in range(count)])  2.21 us
  transfers between devices with their start and end apart: 8, of which 3 were waited for; matrix products, arithmetic and copies ran while one was open for 7% of the time, Pallas kernels for 6%

profile of v9, /device:TPU:0, one launch (start us, length us, event | category | flops | bytes accessed | tf_op | source)
XLA Modules:
  0.0 53.4 jit_solution(3883661968963781920)
XLA Ops:
  0.7 0.8 %copy-done.2 = f32[32,256]{1,0:T(8,128)S(1)} copy-done((f32[32,256]{1,0:T(8,128)S(1)}, f32[32,256]{1,0:T(8,128)}, u32[]{:S(2)}) %copy-start.2) | copy-done | bytes 32792
  1.4 1.1 %fusion.10 = f32[32,256]{1,0:T(8,128)S(1)} fusion(f32[32,256]{1,0:T(8,128)S(1)} %copy-done.2, bf16[1,256,256]{2,1,0:T(8,128)(2,1)} %param.27), kind=kOutput, calls=%fused_computation.20 | convolution fusion | flops 25165824 | bytes 196608 | tf_op jit(solution)/shard_map/master_spectra/bx,nxy->nby/dot_general | solution.py:38
  2.6 0.2 fusion.8
  3.5 4.1 %collective-permute-start = (f32[1,2,32,32]{3,2,1,0:T(8,128)S(1)}, f32[1,2,32,32]{3,2,1,0:T(8,128)S(1)}, u32[]{:S(2)}, u32[]{:S(2)}) collective-permute-start(f32[1,2,32,32]{3,2,1,0:T(8,128)S(1)} %pad_maximum_fusion.2.own_ref), channel_id=1, source_target_pairs={{8,0},{12,4},{0,8},{4,12},{5,1},{1,5},{13,9},{9,13},{10,2},{14,6},... | collective-permute-start | bytes 24584 | tf_op jit(solution)/shard_map/master_spectra/ppermute | solution.py:308
  7.6 0.7 %collective-permute-start.1 = (f32[1,2,32,32]{3,2,1,0:T(8,128)S(1)}, f32[1,2,32,32]{3,2,1,0:T(8,128)S(1)}, u32[]{:S(2)}, u32[]{:S(2)}) collective-permute-start(f32[1,2,32,32]{3,2,1,0:T(8,128)S(1)} %pad_maximum_fusion.2.own_ref), channel_id=1, source_target_pairs={{13,1},{9,5},{5,9},{1,13},{15,3},{11,7},{7,11},{3,15},{29,17},{25,... | collective-permute-start | bytes 24584 | tf_op jit(solution)/shard_map/master_spectra/ppermute | solution.py:308
  8.3 0.6 %copy-done.8 = f32[1,12]{1,0:T(1,128)S(1)} copy-done((f32[1,12]{1,0:T(1,128)S(1)}, f32[1,12]{1,0:T(1,128)}, u32[]{:S(2)}) %copy-start.8) | copy-done | bytes 72
  9.1 0.7 %copy-done.6 = f32[32,256,1]{1,0,2:T(8,128)S(1)} copy-done((f32[32,256,1]{1,0,2:T(8,128)S(1)}, f32[32,256,1]{1,0,2:T(8,128)}, u32[]{:S(2)}) %copy-start.6) | copy-done | bytes 32792
  9.8 0.2 convolution_bitcast_fusion.1
  10.0 0.5 copy-done.5
  10.6 0.2 convolution_bitcast_fusion
  10.8 0.2 fusion.17
  11.0 0.2 fusion.16
  11.6 0.2 fusion
  11.8 0.2 fusion.1
  12.0 0.6 %pad_maximum_fusion.1.t_ref = f32[2,2,32,32]{3,2,1,0:T(8,128)} fusion(f32[2,1,32,32]{3,2,1,0:T(8,128)S(1)} %fusion, f32[2,1,32,32]{3,2,1,0:T(8,128)S(1)} %fusion.1), kind=kLoop, calls=%fused_computation.24 | loop fusion | flops 4096 | bytes 32768 | tf_op jit(solution)/shard_map/tile_spectra/stack | solution.py:359
  12.6 0.9 %pad_maximum_fusion = f32[12,32,128]{2,1,0:T(8,128)} fusion(f32[12,32,32]{2,1,0:T(8,128)S(1)} %copy.39, f32[12,32,32]{2,1,0:T(8,128)S(1)} %copy.38, f32[12,32,32]{2,1,0:T(8,128)S(1)} %copy.36), kind=kLoop, calls=%fused_computation.17 | loop fusion | flops 147456 | bytes 344064 | tf_op jit(solution)/shard_map/imaging_kernel/concatenate | solution.py:372
  13.6 2.0 %collective-permute-start.2 = (f32[4,2,32,32]{3,2,1,0:T(8,128)S(1)}, f32[4,2,32,32]{3,2,1,0:T(8,128)S(1)}, u32[]{:S(2)}, u32[]{:S(2)}) collective-permute-start(f32[4,2,32,32]{3,2,1,0:T(8,128)S(1)} %select_add_fusion.1), channel_id=1, source_target_pairs={{0,1},{1,0},{2,3},{3,2},{4,5},{5,4},{6,7},{7,6},{8,9},{9,8},{10,11... | collective-permute-start | bytes 98312 | tf_op jit(solution)/shard_map/master_spectra/ppermute | solution.py:267
  15.6 0.6 %pad_add_fusion.pos_ref = s32[2]{0:T(128)} fusion(s32[1]{0:T(128)} %bitcast.1, s32[1]{0:T(128)} %bitcast), kind=kLoop, calls=%fused_computation.30 | loop fusion | flops 2 | bytes 16 | tf_op jit(solution)/shard_map/imaging_kernel/stack | solution.py:375
  16.9 0.7 %fusion.12.ev_ref = f32[4,2,32,32]{3,2,1,0:T(8,128)} fusion(f32[4,2,32,32]{3,2,1,0:T(8,128)S(1)} %collective-permute-done.2, f32[2,32,32]{2,1,0:T(8,128)S(1)} %bitcast.82, pred[4]{0:T(512)(128)(4,1)S(1)} %get-tuple-element.8, f32[2,32,32]{2,1,0:T(8,128)S(1)} %bitcast.80, pred[4]{0:T(512)(128)(4,1)S(1)} %get-tuple-element.9), kind=kLoop, calls=%fused_computation.37 | loop fusion | flops 32768 | bytes 81928 | tf_op jit(solution)/shard_map/master_spectra/add | solution.py:267
  17.6 14.8 %imaging_kernel.1 = f32[4,32,32]{2,1,0:T(8,128)} custom-call(s32[2]{0:T(128)} %pad_add_fusion.pos_ref, s32[2]{0:T(128)} %im_ref.1, s32[2,2]{1,0:T(2,128)} %sh_ref.1, f32[12]{0:T(128)} %bitcast.84, f32[1]{0:T(128)S(6)} %copy.41.dose_ref, f32[2,2,32,32]{3,2,1,0:T(8,128)} %pad_maximum_fusion.1.t_ref, f32[4,2,32,32]{3,2,1,0:T(8,128)} %fusion.12.ev_ref, ...), custom_call_target="tpu_custom_call" | custom-call | tf_op jit(solution)/shard_map/imaging_kernel/pallas_call | solution.py:203
  32.4 1.6 %collective-permute-start.3 = (f32[1,4,32,32]{3,2,1,0:T(8,128)}, f32[1,4,32,32]{3,2,1,0:T(8,128)S(1)}, u32[]{:S(2)}, u32[]{:S(2)}) collective-permute-start(f32[1,4,32,32]{3,2,1,0:T(8,128)} %bitcast.77), channel_id=1, source_target_pairs={{0,2},{2,0},{1,3},{3,1},{4,6},{6,4},{5,7},{7,5},{8,10},{10,8},{9,1... | collective-permute-start | bytes 49160 | tf_op jit(solution)/shard_map/gradient_exchange/ppermute | solution.py:267
  34.1 2.9 %collective-permute-done.3 = f32[1,4,32,32]{3,2,1,0:T(8,128)S(1)} collective-permute-done((f32[1,4,32,32]{3,2,1,0:T(8,128)}, f32[1,4,32,32]{3,2,1,0:T(8,128)S(1)}, u32[]{:S(2)}, u32[]{:S(2)}) %collective-permute-start.3) | collective-permute-done | bytes 16416 | tf_op jit(solution)/shard_map/gradient_exchange/ppermute | solution.py:267
  37.0 0.8 %bitcast_add_fusion = f32[1,4,32,32]{3,2,1,0:T(8,128)S(1)} fusion(f32[1,4,32,32]{3,2,1,0:T(8,128)S(1)} %collective-permute-done.3, f32[4,32,32]{2,1,0:T(8,128)} %imaging_kernel.1), kind=kLoop, calls=%fused_computation.36 | loop fusion | flops 4096 | bytes 49152 | tf_op jit(solution)/shard_map/gradient_exchange/add | solution.py:267
  37.9 1.2 %collective-permute-done.4 = f32[1,4,32,32]{3,2,1,0:T(8,128)S(1)} collective-permute-done((f32[1,4,32,32]{3,2,1,0:T(8,128)S(1)}, f32[1,4,32,32]{3,2,1,0:T(8,128)S(1)}, u32[]{:S(2)}, u32[]{:S(2)}) %collective-permute-start.4) | collective-permute-done | bytes 16416 | tf_op jit(solution)/shard_map/gradient_exchange/ppermute | solution.py:256
  39.2 0.6 %fusion.15 = (f32[2,2,32,32]{3,2,1,0:T(8,128)S(1)}, f32[2,2,32,32]{3,2,1,0:T(8,128)}) fusion(f32[2,4,32,32]{3,2,1,0:T(8,128)S(1)} %select_add_fusion), kind=kLoop, calls=%fused_computation.39 | loop fusion | bytes 65536 | tf_op jit(solution)/shard_map/gradient_exchange/slice | solution.py:392
  40.0 0.5 collective-permute-start.5
  40.5 0.7 %collective-permute-start.6 = (f32[1,2,32,32]{3,2,1,0:T(8,128)S(1)}, f32[1,2,32,32]{3,2,1,0:T(8,128)S(1)}, u32[]{:S(2)}, u32[]{:S(2)}) collective-permute-start(f32[1,2,32,32]{3,2,1,0:T(8,128)S(1)} %get-tuple-element.5), channel_id=1, source_target_pairs={{1,13},{5,9},{9,5},{13,1},{3,15},{7,11},{11,7},{15,3},{17,29},{21,... | collective-permute-start | bytes 24584 | tf_op jit(solution)/shard_map/gradient_exchange/ppermute | solution.py:327
  41.1 4.1 %collective-permute-done.5 = f32[1,2,32,32]{3,2,1,0:T(8,128)S(1)} collective-permute-done((f32[1,2,32,32]{3,2,1,0:T(8,128)S(1)}, f32[1,2,32,32]{3,2,1,0:T(8,128)S(1)}, u32[]{:S(2)}, u32[]{:S(2)}) %collective-permute-start.5) | collective-permute-done | bytes 8224 | tf_op jit(solution)/shard_map/gradient_exchange/ppermute | solution.py:327
  45.2 1.9 %collective-permute-start.7 = (f32[1,2,32,32]{3,2,1,0:T(8,128)S(1)}, f32[1,2,32,32]{3,2,1,0:T(8,128)S(1)}, u32[]{:S(2)}, u32[]{:S(2)}) collective-permute-start(f32[1,2,32,32]{3,2,1,0:T(8,128)S(1)} %add_add_fusion), channel_id=1, source_target_pairs={{0,1},{1,0},{2,3},{3,2},{4,5},{5,4},{6,7},{7,6},{8,9},{9,8},{10,11... | collective-permute-start | bytes 24584 | tf_op jit(solution)/shard_map/gradient_exchange/ppermute | solution.py:267
  47.1 3.2 %pixel_gradients.2 = f32[2,256,256]{2,1,0:T(8,128)} custom-call(f32[2,2,32,32]{3,2,1,0:T(8,128)} %get-tuple-element.7.x_ref, f32[256,64]{1,0:T(8,128)} %constant.80.clone.left_ref, f32[32,256]{1,0:T(8,128)} %constant.70.clone.c_re_ref, f32[32,256]{1,0:T(8,128)} %constant.71.clone.c_im_ref), custom_call_target="tpu_custom_call" | custom-call | tf_op jit(solution)/shard_map/pixel_gradients/pallas_call | solution.py:237
  50.3 0.6 %add.54.x_ref = f32[1,2,32,32]{3,2,1,0:T(8,128)} add(f32[1,2,32,32]{3,2,1,0:T(8,128)S(1)} %add_add_fusion, f32[1,2,32,32]{3,2,1,0:T(8,128)S(1)} %collective-permute-done.7) | non-fusion elementwise | flops 2048 | bytes 24576 | tf_op jit(solution)/shard_map/gradient_exchange/add | solution.py:267
  50.9 2.5 %pixel_gradients.3 = f32[1,256,256]{2,1,0:T(8,128)} custom-call(f32[1,2,32,32]{3,2,1,0:T(8,128)} %add.54.x_ref, f32[256,64]{1,0:T(8,128)} %constant.80.clone.left_ref, f32[32,256]{1,0:T(8,128)} %constant.70.clone.c_re_ref, f32[32,256]{1,0:T(8,128)} %constant.71.clone.c_im_ref), custom_call_target="tpu_custom_call" | custom-call | tf_op jit(solution)/shard_map/pixel_gradients/pallas_call | solution.py:237
  (41 shorter events, 1.7 us)
Async XLA Ops:
  0.6 8.5 %copy-start = (bf16[2,256,256]{2,1,0:T(8,128)(2,1)S(1)}, bf16[2,256,256]{2,1,0:T(8,128)(2,1)}, u32[]{:S(2)}) copy-start(bf16[2,256,256]{2,1,0:T(8,128)(2,1)} %param.26) | copy-start | bytes 786436
  0.6 0.8 %copy-start.2 = (f32[32,256]{1,0:T(8,128)S(1)}, f32[32,256]{1,0:T(8,128)}, u32[]{:S(2)}) copy-start(f32[32,256]{1,0:T(8,128)} %constant.70.clone.c_re_ref) | copy-start | bytes 98308
  0.7 1.9 %copy-start.3 = (f32[32,256]{1,0:T(8,128)S(1)}, f32[32,256]{1,0:T(8,128)}, u32[]{:S(2)}) copy-start(f32[32,256]{1,0:T(8,128)} %constant.71.clone.c_im_ref) | copy-start | bytes 98308
  0.7 1.9 %copy-start.4 = (bf16[1,256,256]{2,1,0:T(8,128)(2,1)S(1)}, bf16[1,256,256]{2,1,0:T(8,128)(2,1)}, u32[]{:S(2)}) copy-start(bf16[1,256,256]{2,1,0:T(8,128)(2,1)} %param.27) | copy-start | bytes 393220
  0.7 8.2 %copy-start.1 = (f32[1,12,2,32,32]{4,3,2,1,0:T(8,128)S(1)}, f32[1,12,2,32,32]{4,3,2,1,0:T(8,128)}, u32[]{:S(2)}) copy-start(f32[1,12,2,32,32]{4,3,2,1,0:T(8,128)} %param.31) | copy-start | bytes 294916
  3.5 5.6 %copy-start.7 = (f32[1,2,32,32]{3,2,1,0:T(8,128)}, f32[1,2,32,32]{3,2,1,0:T(8,128)S(1)}, u32[]{:S(2)}) copy-start(f32[1,2,32,32]{3,2,1,0:T(8,128)S(1)} %pad_maximum_fusion.2.own_ref) | copy-start | bytes 24580
  3.5 10.0 %collective-permute-start = (f32[1,2,32,32]{3,2,1,0:T(8,128)S(1)}, f32[1,2,32,32]{3,2,1,0:T(8,128)S(1)}, u32[]{:S(2)}, u32[]{:S(2)}) collective-permute-start(f32[1,2,32,32]{3,2,1,0:T(8,128)S(1)} %pad_maximum_fusion.2.own_ref), channel_id=1, source_target_pairs={{8,0},{12,4},{0,8},{4,12},{5,1},{1,5},{13,9},{9,13},{10,2},{14,6},... | collective-permute-start | bytes 24584 | tf_op jit(solution)/shard_map/master_spectra/ppermute | solution.py:308
  7.6 5.9 %collective-permute-start.1 = (f32[1,2,32,32]{3,2,1,0:T(8,128)S(1)}, f32[1,2,32,32]{3,2,1,0:T(8,128)S(1)}, u32[]{:S(2)}, u32[]{:S(2)}) collective-permute-start(f32[1,2,32,32]{3,2,1,0:T(8,128)S(1)} %pad_maximum_fusion.2.own_ref), channel_id=1, source_target_pairs={{13,1},{9,5},{5,9},{1,13},{15,3},{11,7},{7,11},{3,15},{29,17},{25,... | collective-permute-start | bytes 24584 | tf_op jit(solution)/shard_map/master_spectra/ppermute | solution.py:308
  8.3 0.7 %copy-start.8 = (f32[1,12]{1,0:T(1,128)S(1)}, f32[1,12]{1,0:T(1,128)}, u32[]{:S(2)}) copy-start(f32[1,12]{1,0:T(1,128)} %param.32) | copy-start | bytes 148
  9.0 0.8 %copy-start.6 = (f32[32,256,1]{1,0,2:T(8,128)S(1)}, f32[32,256,1]{1,0,2:T(8,128)}, u32[]{:S(2)}) copy-start(f32[32,256,1]{1,0,2:T(8,128)} %constant.89) | copy-start | bytes 98308
  9.8 0.8 %copy-start.5 = (f32[32,256,1]{1,0,2:T(8,128)S(1)}, f32[32,256,1]{1,0,2:T(8,128)}, u32[]{:S(2)}) copy-start(f32[32,256,1]{1,0,2:T(8,128)} %constant.90) | copy-start | bytes 98308
  13.6 3.3 %collective-permute-start.2 = (f32[4,2,32,32]{3,2,1,0:T(8,128)S(1)}, f32[4,2,32,32]{3,2,1,0:T(8,128)S(1)}, u32[]{:S(2)}, u32[]{:S(2)}) collective-permute-start(f32[4,2,32,32]{3,2,1,0:T(8,128)S(1)} %select_add_fusion.1), channel_id=1, source_target_pairs={{0,1},{1,0},{2,3},{3,2},{4,5},{5,4},{6,7},{7,6},{8,9},{9,8},{10,11... | collective-permute-start | bytes 98312 | tf_op jit(solution)/shard_map/master_spectra/ppermute | solution.py:267
  32.4 1.6 %copy-start.9 = (s32[2]{0:T(128)S(1)}, s32[2]{0:T(128)}, u32[]{:S(2)}) copy-start(s32[2]{0:T(128)} %im_ref.1) | copy-start | bytes 28
  32.4 4.5 %collective-permute-start.3 = (f32[1,4,32,32]{3,2,1,0:T(8,128)}, f32[1,4,32,32]{3,2,1,0:T(8,128)S(1)}, u32[]{:S(2)}, u32[]{:S(2)}) collective-permute-start(f32[1,4,32,32]{3,2,1,0:T(8,128)} %bitcast.77), channel_id=1, source_target_pairs={{0,2},{2,0},{1,3},{3,1},{4,6},{6,4},{5,7},{7,5},{8,10},{10,8},{9,1... | collective-permute-start | bytes 49160 | tf_op jit(solution)/shard_map/gradient_exchange/ppermute | solution.py:267
  37.8 1.3 %collective-permute-start.4 = (f32[1,4,32,32]{3,2,1,0:T(8,128)S(1)}, f32[1,4,32,32]{3,2,1,0:T(8,128)S(1)}, u32[]{:S(2)}, u32[]{:S(2)}) collective-permute-start(f32[1,4,32,32]{3,2,1,0:T(8,128)S(1)} %bitcast_add_fusion), channel_id=1, source_target_pairs={{0,1},{1,0},{2,3},{3,2},{4,5},{5,4},{6,7},{7,6},{8,9},{9,8},{10,11... | collective-permute-start | bytes 49160 | tf_op jit(solution)/shard_map/gradient_exchange/ppermute | solution.py:256
  40.0 5.2 %collective-permute-start.5 = (f32[1,2,32,32]{3,2,1,0:T(8,128)S(1)}, f32[1,2,32,32]{3,2,1,0:T(8,128)S(1)}, u32[]{:S(2)}, u32[]{:S(2)}) collective-permute-start(f32[1,2,32,32]{3,2,1,0:T(8,128)S(1)} %get-tuple-element.4), channel_id=1, source_target_pairs={{0,8},{4,12},{8,0},{12,4},{1,5},{5,1},{9,13},{13,9},{2,10},{6,14},... | collective-permute-start | bytes 24584 | tf_op jit(solution)/shard_map/gradient_exchange/ppermute | solution.py:327
  40.5 4.8 %collective-permute-start.6 = (f32[1,2,32,32]{3,2,1,0:T(8,128)S(1)}, f32[1,2,32,32]{3,2,1,0:T(8,128)S(1)}, u32[]{:S(2)}, u32[]{:S(2)}) collective-permute-start(f32[1,2,32,32]{3,2,1,0:T(8,128)S(1)} %get-tuple-element.5), channel_id=1, source_target_pairs={{1,13},{5,9},{9,5},{13,1},{3,15},{7,11},{11,7},{15,3},{17,29},{21,... | collective-permute-start | bytes 24584 | tf_op jit(solution)/shard_map/gradient_exchange/ppermute | solution.py:327
  45.2 5.1 %collective-permute-start.7 = (f32[1,2,32,32]{3,2,1,0:T(8,128)S(1)}, f32[1,2,32,32]{3,2,1,0:T(8,128)S(1)}, u32[]{:S(2)}, u32[]{:S(2)}) collective-permute-start(f32[1,2,32,32]{3,2,1,0:T(8,128)S(1)} %add_add_fusion), channel_id=1, source_target_pairs={{0,1},{1,0},{2,3},{3,2},{4,5},{5,4},{6,7},{7,6},{8,9},{9,8},{10,11... | collective-permute-start | bytes 24584 | tf_op jit(solution)/shard_map/gradient_exchange/ppermute | solution.py:267

commit v10 on v9

--- a/solution.py
+++ b/solution.py
@@ -121,7 +121,7 @@
 
 
 def imaging_body(
-    pos_ref, im_ref, sh_ref, w_ref, dose_ref, t_ref, ev_ref, own_ref, goal_ref, h_ref, hc_ref,
+    pos_ref, im_ref, sh_ref, w_ref, dose_ref, t_ref, ev_ref, ev2_ref, own_ref, goal_ref, h_ref, hc_ref,
     c_re_ref, c_im_ref, ct_re_ref, ct_im_ref, rw_top, rw_bot, rc_ref, la_ref, rhm_ref, rlh_ref,
     slots_ref, f_buf, i_buf, u_buf, w_buf, xr_buf, xi_buf,
 ):
@@ -138,8 +138,8 @@
     ph_im = e0_re * e1_im + e0_im * e1_re
     local_masters = own_ref.shape[0]
     is_own = master // local_masters == pos_ref[1]
-    m_re = ev_ref[master, 0] + jnp.where(is_own, own_ref[master % local_masters, 0], 0.0)
-    m_im = ev_ref[master, 1] + jnp.where(is_own, own_ref[master % local_masters, 1], 0.0)
+    m_re = ev_ref[master, 0] + ev2_ref[master, 0] + jnp.where(is_own, own_ref[master % local_masters, 0], 0.0)
+    m_im = ev_ref[master, 1] + ev2_ref[master, 1] + jnp.where(is_own, own_ref[master % local_masters, 1], 0.0)
     s_re = t_ref[pos, 0] + (ph_re * m_re - ph_im * m_im)
     s_im = t_ref[pos, 1] + (ph_re * m_im + ph_im * m_re)
     i_buf[...] = jnp.zeros(i_buf.shape, jnp.float32)
@@ -196,6 +196,8 @@
 
 
 def imaging(pos, inst_master, inst_shift, weights, dose, tile_spec, every, own, target, kerns, h_cat):
+    if len(every) == 1:
+        every = (every[0], jnp.zeros_like(every[0]))
     count = weights.shape[0]
     tables = imaging_tables()
     vmem = pl.BlockSpec(memory_space=pltpu.VMEM)
@@ -203,7 +205,7 @@
     return pl.pallas_call(
         imaging_body,
         out_shape=jax.ShapeDtypeStruct((4, B, B), jnp.float32),
-        in_specs=[smem] * 5 + [vmem] * 6 + [vmem] * len(tables),
+        in_specs=[smem] * 5 + [vmem] * 7 + [vmem] * len(tables),
         out_specs=vmem,
         scratch_shapes=[
             pltpu.VMEM((count, P_SIZE, 2 * P_SIZE), jnp.float32),
@@ -213,33 +215,42 @@
             pltpu.VMEM((count * B, B), jnp.float32),
             pltpu.VMEM((count * B, B), jnp.float32),
         ],
-    )(pos, inst_master, inst_shift, weights, dose, tile_spec, every, own, target, kerns, h_cat, *tables)
-
-
-def pixel_body(x_ref, left_ref, c_re_ref, c_im_ref, out_ref):
+    )(pos, inst_master, inst_shift, weights, dose, tile_spec, *every, own, target, kerns, h_cat, *tables)
+
+
+def pixel_body(*refs):
+    out_ref = refs[-1]
+    c_re_ref, c_im_ref, left_ref = refs[-4:-1]
+    parts = refs[:-4]
     for n in range(out_ref.shape[0]):
-        x_re = x_ref[n, 0]
-        x_im = x_ref[n, 1]
-        half_re = dot_full(left_ref[...], jnp.concatenate([x_re, x_im], axis=0))
-        half_im = dot_full(left_ref[...], jnp.concatenate([x_im, -x_re], axis=0))
-        out_ref[n] = dot_full(half_re, c_re_ref[...]) + dot_full(half_im, c_im_ref[...])
-
-
-def pixels(x):
+        x_re = sum(part[n, 0] for part in parts)
+        x_im = sum(part[n, 1] for part in parts)
+        x_both = jnp.concatenate([x_re, x_im], axis=0)
+        p_re = dot_full(x_both, c_re_ref[...])
+        p_im = dot_full(x_both, c_im_ref[...])
+        y_re = p_re[:B] + p_im[B:]
+        y_im = p_re[B:] - p_im[:B]
+        y_hi, y_mid, y_lo = split_three(jnp.concatenate([y_re, y_im], axis=0))
+        stacked = jnp.concatenate([y_hi, y_mid, y_hi, y_lo, y_hi, y_mid], axis=0)
+        out_ref[n] = dot_parts(left_ref[...], stacked)
+
+
+def pixels(*parts):
     freq = np.arange(B, dtype=np.int64) - B // 2
     pixel = np.arange(P_SIZE, dtype=np.int64)
     angle = (2.0 * math.pi / P_SIZE) * np.mod(freq[:, None] * pixel[None, :], P_SIZE).astype(np.float64)
     c_re = np.cos(angle)
     c_im = -np.sin(angle)
-    left = np.concatenate([c_re.T, c_im.T], axis=1)
-    tables = [jnp.asarray(table, jnp.float32) for table in (left, c_re, c_im)]
+    a_hi, a_mid, a_lo = table_three(np.concatenate([c_re.T, c_im.T], axis=1))
+    left = np.concatenate([a_hi, a_hi, a_mid, a_hi, a_lo, a_mid], axis=1)
+    tables = [jnp.asarray(c_re, jnp.float32), jnp.asarray(c_im, jnp.float32), jnp.asarray(left)]
     vmem = pl.BlockSpec(memory_space=pltpu.VMEM)
     return pl.pallas_call(
         pixel_body,
-        out_shape=jax.ShapeDtypeStruct((x.shape[0], P_SIZE, P_SIZE), jnp.float32),
-        in_specs=[vmem] * 4,
+        out_shape=jax.ShapeDtypeStruct((parts[0].shape[0], P_SIZE, P_SIZE), jnp.float32),
+        in_specs=[vmem] * (len(parts) + 3),
         out_specs=vmem,
-    )(x, *tables)
+    )(*parts, *tables)
 
 
 def xor_partners(count):
@@ -267,6 +278,12 @@
         x = x + lax.ppermute(x, axis, [(i, i ^ step) for i in range(count)])
         step *= 2
     return x
+
+
+def sum_parts(x, axis, count, pos):
+    if count == 2:
+        return (x, lax.ppermute(x, axis, [(0, 1), (1, 0)]))
+    return (sum_all(x, axis, count, pos),)
 
 
 def scatter_sum(x, axis, count, pos, size):
@@ -309,7 +326,7 @@
         step = chosen_step(lists, r, kern_pos)
         source = jnp.where(step >= 0, pos ^ step, -1)
         collected = collected + jnp.where((slot == source)[:, None, None, None], spread(got), 0.0)
-    return sum_all(collected, "kern", kern_count, kern_pos)
+    return sum_parts(collected, "kern", kern_count, kern_pos)
 
 
 def scatter_split(x, count, pos, kern_count, kern_pos, size):
@@ -325,7 +342,7 @@
         target = jnp.where(step >= 0, pos ^ step, 0)
         part = lax.dynamic_slice_in_dim(x, target * size, size, 0)
         total = total + lax.ppermute(part, ("tile", "kern"), pairs)
-    return sum_all(total, "kern", kern_count, kern_pos)
+    return sum_parts(total, "kern", kern_count, kern_pos)
 
 
 def on_device(
@@ -351,7 +368,7 @@
             every = gather_split(own, tile_count, tile_pos, kern_count, kern_pos)
             own_part = own
         else:
-            every = gather_all(own, "tile", tile_count, tile_pos)
+            every = (gather_all(own, "tile", tile_count, tile_pos),)
             own_part = jnp.zeros_like(own)
 
     with jax.named_scope("tile_spectra"):
@@ -393,11 +410,11 @@
         if xor_partners(tile_count) and xor_partners(kern_count) and tile_count > 2:
             mine_masters = scatter_split(terms, tile_count, tile_pos, kern_count, kern_pos, local_masters)
         else:
-            mine_masters = scatter_sum(terms, "tile", tile_count, tile_pos, local_masters)
+            mine_masters = (scatter_sum(terms, "tile", tile_count, tile_pos, local_masters),)
 
     with jax.named_scope("pixel_gradients"):
         tile_grad = pixels(mine_tiles)
-        master_grad = pixels(mine_masters)
+        master_grad = pixels(*mine_masters)
     return (tile_grad, master_grad)
 
 

time: 53.8 us -> 53.4 us (level)
  other arithmetic: 4.84 us -> 3.52 us
  local copies, waits for them, and re-layouts: 3.62 us -> 4.86 us
    ppermute x0 -> x2, starting transfers between devices: none -> 3.95 us  [sum_parts(): return (x, lax.ppermute(x, axis, [(0, 1), (1, 0)]))]
    ppermute x3 -> x1, starting transfers between devices: 5.51 us -> 1.56 us  [sum_all(): x = x + lax.ppermute(x, axis, [(i, i ^ step) for i in range(count)])]
    add x3 -> x1, other arithmetic: 2.21 us -> 0.85 us  [sum_all(): x = x + lax.ppermute(x, axis, [(i, i ^ step) for i in range(count)])]
    unnamed x20 -> x28, local copies, waits for them, and re-layouts: 2.63 us -> 3.87 us
    ppermute x3 -> x1, waiting for transfers between devices: 2.91 us -> 2.91 us  [sum_all(): x = x + lax.ppermute(x, axis, [(i, i ^ step) for i in range(count)])]
  transfers between devices with their start and end apart: 8 -> 8, of which waited for: 3 -> 3; matrix products, arithmetic and copies ran while one was open for 7% -> 8% of each run, Pallas kernels for 6% -> 5%
where the time goes in v10:
time: 53.4 us; the launch traced here: 52.9 us
  Pallas kernels  20 us (37%)
  starting transfers between devices  11.5 us (22%)
  waiting for transfers between devices  8.23 us (15%)
  local copies, waits for them, and re-layouts  4.86 us (9%)
  other arithmetic  3.52 us (7%)
  matrix products  3.19 us (6%)
  between operations  1.68 us (3%)
    pallas_call x1, Pallas kernels, imaging(): pl.pallas_call(imaging_body, out_shape=jax.ShapeDtypeStruct((4, B, B), jn...  14.8 us
    pallas_call x2, Pallas kernels, pixels(): pl.pallas_call(pixel_body, out_shape=jax.ShapeDtypeStruct((parts[0].shape...  5.19 us
    ppermute x2, starting transfers between devices, gather_split(): got = lax.ppermute(x, ('tile', 'kern'), pairs)  4.75 us
    ppermute x2, waiting for transfers between devices, scatter_split(): total = total + lax.ppermute(part, ('tile', 'kern'), pairs)  4.1 us
    ppermute x2, starting transfers between devices, sum_parts(): return (x, lax.ppermute(x, axis, [(0, 1), (1, 0)]))  3.95 us
    unnamed x28, local copies, waits for them, and re-layouts  3.87 us
    ppermute x1, waiting for transfers between devices, sum_all(): x = x + lax.ppermute(x, axis, [(i, i ^ step) for i in range(count)])  2.91 us
    ppermute x1, starting transfers between devices, sum_all(): x = x + lax.ppermute(x, axis, [(i, i ^ step) for i in range(count)])  1.56 us
  transfers between devices with their start and end apart: 8, of which 3 were waited for; matrix products, arithmetic and copies ran while one was open for 8% of the time, Pallas kernels for 5%

profile of v10, /device:TPU:0, one launch (start us, length us, event | category | flops | bytes accessed | tf_op | source)
XLA Modules:
  0.0 52.9 jit_solution(4950693912501087725)
XLA Ops:
  0.7 0.8 %copy-done.2 = f32[32,256]{1,0:T(8,128)S(1)} copy-done((f32[32,256]{1,0:T(8,128)S(1)}, f32[32,256]{1,0:T(8,128)}, u32[]{:S(2)}) %copy-start.2) | copy-done | bytes 32792
  1.4 1.1 %fusion.10 = f32[32,256]{1,0:T(8,128)S(1)} fusion(f32[32,256]{1,0:T(8,128)S(1)} %copy-done.2, bf16[1,256,256]{2,1,0:T(8,128)(2,1)} %param.27), kind=kOutput, calls=%fused_computation.20 | convolution fusion | flops 25165824 | bytes 196608 | tf_op jit(solution)/shard_map/master_spectra/bx,nxy->nby/dot_general | solution.py:38
  2.6 0.2 fusion.8
  3.5 4.1 %collective-permute-start = (f32[1,2,32,32]{3,2,1,0:T(8,128)S(1)}, f32[1,2,32,32]{3,2,1,0:T(8,128)S(1)}, u32[]{:S(2)}, u32[]{:S(2)}) collective-permute-start(f32[1,2,32,32]{3,2,1,0:T(8,128)S(1)} %pad_maximum_fusion.2.own_ref), channel_id=1, source_target_pairs={{8,0},{12,4},{0,8},{4,12},{5,1},{1,5},{13,9},{9,13},{10,2},{14,6},... | collective-permute-start | bytes 24584 | tf_op jit(solution)/shard_map/master_spectra/ppermute | solution.py:325
  7.6 0.7 %collective-permute-start.1 = (f32[1,2,32,32]{3,2,1,0:T(8,128)S(1)}, f32[1,2,32,32]{3,2,1,0:T(8,128)S(1)}, u32[]{:S(2)}, u32[]{:S(2)}) collective-permute-start(f32[1,2,32,32]{3,2,1,0:T(8,128)S(1)} %pad_maximum_fusion.2.own_ref), channel_id=1, source_target_pairs={{13,1},{9,5},{5,9},{1,13},{15,3},{11,7},{7,11},{3,15},{29,17},{25,... | collective-permute-start | bytes 24584 | tf_op jit(solution)/shard_map/master_spectra/ppermute | solution.py:325
  8.3 0.6 %copy-done.12 = f32[1,12]{1,0:T(1,128)S(1)} copy-done((f32[1,12]{1,0:T(1,128)S(1)}, f32[1,12]{1,0:T(1,128)}, u32[]{:S(2)}) %copy-start.12) | copy-done | bytes 72
  9.1 0.7 %copy-done.7 = f32[32,256,1]{1,0,2:T(8,128)S(1)} copy-done((f32[32,256,1]{1,0,2:T(8,128)S(1)}, f32[32,256,1]{1,0,2:T(8,128)}, u32[]{:S(2)}) %copy-start.7) | copy-done | bytes 32792
  9.8 0.2 convolution_bitcast_fusion.1
  10.0 0.5 copy-done.6
  10.6 0.2 convolution_bitcast_fusion
  10.8 0.2 fusion.16
  11.0 0.2 fusion.15
  11.6 0.2 fusion
  11.8 0.2 fusion.1
  12.0 0.6 %pad_maximum_fusion.1.t_ref = f32[2,2,32,32]{3,2,1,0:T(8,128)} fusion(f32[2,1,32,32]{3,2,1,0:T(8,128)S(1)} %fusion, f32[2,1,32,32]{3,2,1,0:T(8,128)S(1)} %fusion.1), kind=kLoop, calls=%fused_computation.24 | loop fusion | flops 4096 | bytes 32768 | tf_op jit(solution)/shard_map/tile_spectra/stack | solution.py:376
  12.6 0.9 %pad_maximum_fusion = f32[12,32,128]{2,1,0:T(8,128)} fusion(f32[12,32,32]{2,1,0:T(8,128)S(1)} %copy.39, f32[12,32,32]{2,1,0:T(8,128)S(1)} %copy.38, f32[12,32,32]{2,1,0:T(8,128)S(1)} %copy.36), kind=kLoop, calls=%fused_computation.17 | loop fusion | flops 147456 | bytes 344064 | tf_op jit(solution)/shard_map/imaging_kernel/concatenate | solution.py:389
  13.6 2.0 %collective-permute-start.2 = (f32[4,2,32,32]{3,2,1,0:T(8,128)S(1)}, f32[4,2,32,32]{3,2,1,0:T(8,128)S(1)}, u32[]{:S(2)}, u32[]{:S(2)}) collective-permute-start(f32[4,2,32,32]{3,2,1,0:T(8,128)S(1)} %select_add_fusion.1.ev_ref), channel_id=1, source_target_pairs={{0,1},{1,0},{2,3},{3,2},{4,5},{5,4},{6,7},{7,6},{8,9},{9,8},{10,11... | collective-permute-start | bytes 98312 | tf_op jit(solution)/shard_map/master_spectra/ppermute | solution.py:285
  15.7 0.6 %pad_add_fusion.pos_ref = s32[2]{0:T(128)} fusion(s32[1]{0:T(128)} %bitcast.1, s32[1]{0:T(128)} %bitcast), kind=kLoop, calls=%fused_computation.30 | loop fusion | flops 2 | bytes 16 | tf_op jit(solution)/shard_map/imaging_kernel/stack | solution.py:392
  17.0 0.6 %copy-done.9 = f32[4,2,32,32]{3,2,1,0:T(8,128)} copy-done((f32[4,2,32,32]{3,2,1,0:T(8,128)}, f32[4,2,32,32]{3,2,1,0:T(8,128)S(1)}, u32[]{:S(2)}) %copy-start.9) | copy-done | bytes 32792
  17.6 14.8 %imaging_kernel.1 = f32[4,32,32]{2,1,0:T(8,128)} custom-call(s32[2]{0:T(128)} %pad_add_fusion.pos_ref, s32[2]{0:T(128)} %im_ref.1, s32[2,2]{1,0:T(2,128)} %sh_ref.1, f32[12]{0:T(128)} %bitcast.82, f32[1]{0:T(128)S(6)} %copy.41.dose_ref, f32[2,2,32,32]{3,2,1,0:T(8,128)} %pad_maximum_fusion.1.t_ref, f32[4,2,32,32]{3,2,1,0:T(8,128)} %copy-done.4, ...), custom_call_target="tpu_custom_call" | custom-call | tf_op jit(solution)/shard_map/imaging_kernel/pallas_call | solution.py:205
  32.4 1.6 %collective-permute-start.3 = (f32[1,4,32,32]{3,2,1,0:T(8,128)}, f32[1,4,32,32]{3,2,1,0:T(8,128)S(1)}, u32[]{:S(2)}, u32[]{:S(2)}) collective-permute-start(f32[1,4,32,32]{3,2,1,0:T(8,128)} %bitcast.77), channel_id=1, source_target_pairs={{0,2},{2,0},{1,3},{3,1},{4,6},{6,4},{5,7},{7,5},{8,10},{10,8},{9,1... | collective-permute-start | bytes 49160 | tf_op jit(solution)/shard_map/gradient_exchange/ppermute | solution.py:278
  34.0 2.9 %collective-permute-done.3 = f32[1,4,32,32]{3,2,1,0:T(8,128)S(1)} collective-permute-done((f32[1,4,32,32]{3,2,1,0:T(8,128)}, f32[1,4,32,32]{3,2,1,0:T(8,128)S(1)}, u32[]{:S(2)}, u32[]{:S(2)}) %collective-permute-start.3) | collective-permute-done | bytes 16416 | tf_op jit(solution)/shard_map/gradient_exchange/ppermute | solution.py:278
  36.9 0.8 %bitcast_add_fusion = f32[1,4,32,32]{3,2,1,0:T(8,128)S(1)} fusion(f32[1,4,32,32]{3,2,1,0:T(8,128)S(1)} %collective-permute-done.3, f32[4,32,32]{2,1,0:T(8,128)} %imaging_kernel.1), kind=kLoop, calls=%fused_computation.36 | loop fusion | flops 4096 | bytes 49152 | tf_op jit(solution)/shard_map/gradient_exchange/add | solution.py:278
  37.9 1.2 %collective-permute-done.4 = f32[1,4,32,32]{3,2,1,0:T(8,128)S(1)} collective-permute-done((f32[1,4,32,32]{3,2,1,0:T(8,128)S(1)}, f32[1,4,32,32]{3,2,1,0:T(8,128)S(1)}, u32[]{:S(2)}, u32[]{:S(2)}) %collective-permute-start.4) | collective-permute-done | bytes 16416 | tf_op jit(solution)/shard_map/gradient_exchange/ppermute | solution.py:267
  39.2 0.6 %fusion.14 = (f32[2,2,32,32]{3,2,1,0:T(8,128)S(1)}, f32[2,2,32,32]{3,2,1,0:T(8,128)}) fusion(f32[2,4,32,32]{3,2,1,0:T(8,128)S(1)} %select_add_fusion), kind=kLoop, calls=%fused_computation.38 | loop fusion | bytes 65536 | tf_op jit(solution)/shard_map/gradient_exchange/slice | solution.py:409
  39.9 0.5 collective-permute-start.5
  40.4 0.7 %collective-permute-start.6 = (f32[1,2,32,32]{3,2,1,0:T(8,128)S(1)}, f32[1,2,32,32]{3,2,1,0:T(8,128)S(1)}, u32[]{:S(2)}, u32[]{:S(2)}) collective-permute-start(f32[1,2,32,32]{3,2,1,0:T(8,128)S(1)} %get-tuple-element.5), channel_id=1, source_target_pairs={{1,13},{5,9},{9,5},{13,1},{3,15},{7,11},{11,7},{15,3},{17,29},{21,... | collective-permute-start | bytes 24584 | tf_op jit(solution)/shard_map/gradient_exchange/ppermute | solution.py:344
  41.1 4.1 %collective-permute-done.5 = f32[1,2,32,32]{3,2,1,0:T(8,128)S(1)} collective-permute-done((f32[1,2,32,32]{3,2,1,0:T(8,128)S(1)}, f32[1,2,32,32]{3,2,1,0:T(8,128)S(1)}, u32[]{:S(2)}, u32[]{:S(2)}) %collective-permute-start.5) | collective-permute-done | bytes 8224 | tf_op jit(solution)/shard_map/gradient_exchange/ppermute | solution.py:344
  45.2 1.9 %collective-permute-start.7 = (f32[1,2,32,32]{3,2,1,0:T(8,128)S(1)}, f32[1,2,32,32]{3,2,1,0:T(8,128)S(1)}, u32[]{:S(2)}, u32[]{:S(2)}) collective-permute-start(f32[1,2,32,32]{3,2,1,0:T(8,128)S(1)} %add_add_fusion.refs_0_), channel_id=1, source_target_pairs={{0,1},{1,0},{2,3},{3,2},{4,5},{5,4},{6,7},{7,6},{8,9},{9,8},{10,11... | collective-permute-start | bytes 24584 | tf_op jit(solution)/shard_map/gradient_exchange/ppermute | solution.py:285
  47.1 2.9 %pixel_gradients.2 = f32[2,256,256]{2,1,0:T(8,128)} custom-call(f32[2,2,32,32]{3,2,1,0:T(8,128)} %get-tuple-element.7.refs_0_, f32[32,256]{1,0:T(8,128)} %constant.70.clone.c_re_ref.refs_1_.refs_2_, f32[32,256]{1,0:T(8,128)} %constant.71.clone.c_im_ref.refs_2_.refs_3_, bf16[256,384]{1,0:T(8,128)(2,1)} %constant.80.clone.refs_3_.refs_4_), custom_call_target="tpu_custom_call" | custom-call | tf_op jit(solution)/shard_map/pixel_gradients/pallas_call | solution.py:248
  50.0 0.6 %copy-done.11 = f32[1,2,32,32]{3,2,1,0:T(8,128)} copy-done((f32[1,2,32,32]{3,2,1,0:T(8,128)}, f32[1,2,32,32]{3,2,1,0:T(8,128)S(1)}, u32[]{:S(2)}) %copy-start.11) | copy-done | bytes 8216
  50.6 2.3 %pixel_gradients.3 = f32[1,256,256]{2,1,0:T(8,128)} custom-call(f32[1,2,32,32]{3,2,1,0:T(8,128)} %copy-done.10, f32[1,2,32,32]{3,2,1,0:T(8,128)} %copy-done.11, f32[32,256]{1,0:T(8,128)} %constant.70.clone.c_re_ref.refs_1_.refs_2_, f32[32,256]{1,0:T(8,128)} %constant.71.clone.c_im_ref.refs_2_.refs_3_, bf16[256,384]{1,0:T(8,128)(2,1)} %constant.80.clone.refs_3_.refs_4_), custom_call_target="tpu_custom_call" | custom-call | tf_op jit(solution)/shard_map/pixel_gradients/pallas_call | solution.py:248
  (47 shorter events, 1.7 us)
Async XLA Ops:
  0.6 8.5 %copy-start = (bf16[2,256,256]{2,1,0:T(8,128)(2,1)S(1)}, bf16[2,256,256]{2,1,0:T(8,128)(2,1)}, u32[]{:S(2)}) copy-start(bf16[2,256,256]{2,1,0:T(8,128)(2,1)} %param.26) | copy-start | bytes 786436
  0.6 0.8 %copy-start.2 = (f32[32,256]{1,0:T(8,128)S(1)}, f32[32,256]{1,0:T(8,128)}, u32[]{:S(2)}) copy-start(f32[32,256]{1,0:T(8,128)} %constant.70.clone.c_re_ref.refs_1_.refs_2_) | copy-start | bytes 98308
  0.7 1.9 %copy-start.3 = (f32[32,256]{1,0:T(8,128)S(1)}, f32[32,256]{1,0:T(8,128)}, u32[]{:S(2)}) copy-start(f32[32,256]{1,0:T(8,128)} %constant.71.clone.c_im_ref.refs_2_.refs_3_) | copy-start | bytes 98308
  0.7 1.9 %copy-start.5 = (bf16[1,256,256]{2,1,0:T(8,128)(2,1)S(1)}, bf16[1,256,256]{2,1,0:T(8,128)(2,1)}, u32[]{:S(2)}) copy-start(bf16[1,256,256]{2,1,0:T(8,128)(2,1)} %param.27) | copy-start | bytes 393220
  0.7 8.2 %copy-start.1 = (f32[1,12,2,32,32]{4,3,2,1,0:T(8,128)S(1)}, f32[1,12,2,32,32]{4,3,2,1,0:T(8,128)}, u32[]{:S(2)}) copy-start(f32[1,12,2,32,32]{4,3,2,1,0:T(8,128)} %param.31) | copy-start | bytes 294916
  3.5 5.6 %copy-start.8 = (f32[1,2,32,32]{3,2,1,0:T(8,128)}, f32[1,2,32,32]{3,2,1,0:T(8,128)S(1)}, u32[]{:S(2)}) copy-start(f32[1,2,32,32]{3,2,1,0:T(8,128)S(1)} %pad_maximum_fusion.2.own_ref) | copy-start | bytes 24580
  3.5 10.0 %collective-permute-start = (f32[1,2,32,32]{3,2,1,0:T(8,128)S(1)}, f32[1,2,32,32]{3,2,1,0:T(8,128)S(1)}, u32[]{:S(2)}, u32[]{:S(2)}) collective-permute-start(f32[1,2,32,32]{3,2,1,0:T(8,128)S(1)} %pad_maximum_fusion.2.own_ref), channel_id=1, source_target_pairs={{8,0},{12,4},{0,8},{4,12},{5,1},{1,5},{13,9},{9,13},{10,2},{14,6},... | collective-permute-start | bytes 24584 | tf_op jit(solution)/shard_map/master_spectra/ppermute | solution.py:325
  7.6 5.9 %collective-permute-start.1 = (f32[1,2,32,32]{3,2,1,0:T(8,128)S(1)}, f32[1,2,32,32]{3,2,1,0:T(8,128)S(1)}, u32[]{:S(2)}, u32[]{:S(2)}) collective-permute-start(f32[1,2,32,32]{3,2,1,0:T(8,128)S(1)} %pad_maximum_fusion.2.own_ref), channel_id=1, source_target_pairs={{13,1},{9,5},{5,9},{1,13},{15,3},{11,7},{7,11},{3,15},{29,17},{25,... | collective-permute-start | bytes 24584 | tf_op jit(solution)/shard_map/master_spectra/ppermute | solution.py:325
  8.3 0.7 %copy-start.12 = (f32[1,12]{1,0:T(1,128)S(1)}, f32[1,12]{1,0:T(1,128)}, u32[]{:S(2)}) copy-start(f32[1,12]{1,0:T(1,128)} %param.32) | copy-start | bytes 148
  9.0 0.8 %copy-start.7 = (f32[32,256,1]{1,0,2:T(8,128)S(1)}, f32[32,256,1]{1,0,2:T(8,128)}, u32[]{:S(2)}) copy-start(f32[32,256,1]{1,0,2:T(8,128)} %constant.89) | copy-start | bytes 98308
  9.8 0.8 %copy-start.6 = (f32[32,256,1]{1,0,2:T(8,128)S(1)}, f32[32,256,1]{1,0,2:T(8,128)}, u32[]{:S(2)}) copy-start(f32[32,256,1]{1,0,2:T(8,128)} %constant.90) | copy-start | bytes 98308
  13.6 3.3 %copy-start.4 = (f32[4,2,32,32]{3,2,1,0:T(8,128)}, f32[4,2,32,32]{3,2,1,0:T(8,128)S(1)}, u32[]{:S(2)}) copy-start(f32[4,2,32,32]{3,2,1,0:T(8,128)S(1)} %select_add_fusion.1.ev_ref) | copy-start | bytes 98308
  13.6 3.3 %collective-permute-start.2 = (f32[4,2,32,32]{3,2,1,0:T(8,128)S(1)}, f32[4,2,32,32]{3,2,1,0:T(8,128)S(1)}, u32[]{:S(2)}, u32[]{:S(2)}) collective-permute-start(f32[4,2,32,32]{3,2,1,0:T(8,128)S(1)} %select_add_fusion.1.ev_ref), channel_id=1, source_target_pairs={{0,1},{1,0},{2,3},{3,2},{4,5},{5,4},{6,7},{7,6},{8,9},{9,8},{10,11... | collective-permute-start | bytes 98312 | tf_op jit(solution)/shard_map/master_spectra/ppermute | solution.py:285
  16.9 0.6 %copy-start.9 = (f32[4,2,32,32]{3,2,1,0:T(8,128)}, f32[4,2,32,32]{3,2,1,0:T(8,128)S(1)}, u32[]{:S(2)}) copy-start(f32[4,2,32,32]{3,2,1,0:T(8,128)S(1)} %collective-permute-done.2.ev2_ref) | copy-start | bytes 98308
  32.4 1.6 %copy-start.13 = (s32[2]{0:T(128)S(1)}, s32[2]{0:T(128)}, u32[]{:S(2)}) copy-start(s32[2]{0:T(128)} %im_ref.1) | copy-start | bytes 28
  32.4 4.5 %collective-permute-start.3 = (f32[1,4,32,32]{3,2,1,0:T(8,128)}, f32[1,4,32,32]{3,2,1,0:T(8,128)S(1)}, u32[]{:S(2)}, u32[]{:S(2)}) collective-permute-start(f32[1,4,32,32]{3,2,1,0:T(8,128)} %bitcast.77), channel_id=1, source_target_pairs={{0,2},{2,0},{1,3},{3,1},{4,6},{6,4},{5,7},{7,5},{8,10},{10,8},{9,1... | collective-permute-start | bytes 49160 | tf_op jit(solution)/shard_map/gradient_exchange/ppermute | solution.py:278
  37.8 1.3 %collective-permute-start.4 = (f32[1,4,32,32]{3,2,1,0:T(8,128)S(1)}, f32[1,4,32,32]{3,2,1,0:T(8,128)S(1)}, u32[]{:S(2)}, u32[]{:S(2)}) collective-permute-start(f32[1,4,32,32]{3,2,1,0:T(8,128)S(1)} %bitcast_add_fusion), channel_id=1, source_target_pairs={{0,1},{1,0},{2,3},{3,2},{4,5},{5,4},{6,7},{7,6},{8,9},{9,8},{10,11... | collective-permute-start | bytes 49160 | tf_op jit(solution)/shard_map/gradient_exchange/ppermute | solution.py:267
  39.9 5.2 %collective-permute-start.5 = (f32[1,2,32,32]{3,2,1,0:T(8,128)S(1)}, f32[1,2,32,32]{3,2,1,0:T(8,128)S(1)}, u32[]{:S(2)}, u32[]{:S(2)}) collective-permute-start(f32[1,2,32,32]{3,2,1,0:T(8,128)S(1)} %get-tuple-element.4), channel_id=1, source_target_pairs={{0,8},{4,12},{8,0},{12,4},{1,5},{5,1},{9,13},{13,9},{2,10},{6,14},... | collective-permute-start | bytes 24584 | tf_op jit(solution)/shard_map/gradient_exchange/ppermute | solution.py:344
  40.4 4.8 %collective-permute-start.6 = (f32[1,2,32,32]{3,2,1,0:T(8,128)S(1)}, f32[1,2,32,32]{3,2,1,0:T(8,128)S(1)}, u32[]{:S(2)}, u32[]{:S(2)}) collective-permute-start(f32[1,2,32,32]{3,2,1,0:T(8,128)S(1)} %get-tuple-element.5), channel_id=1, source_target_pairs={{1,13},{5,9},{9,5},{13,1},{3,15},{7,11},{11,7},{15,3},{17,29},{21,... | collective-permute-start | bytes 24584 | tf_op jit(solution)/shard_map/gradient_exchange/ppermute | solution.py:344
  45.2 4.8 %copy-start.10 = (f32[1,2,32,32]{3,2,1,0:T(8,128)}, f32[1,2,32,32]{3,2,1,0:T(8,128)S(1)}, u32[]{:S(2)}) copy-start(f32[1,2,32,32]{3,2,1,0:T(8,128)S(1)} %add_add_fusion.refs_0_) | copy-start | bytes 24580
  45.2 4.8 %collective-permute-start.7 = (f32[1,2,32,32]{3,2,1,0:T(8,128)S(1)}, f32[1,2,32,32]{3,2,1,0:T(8,128)S(1)}, u32[]{:S(2)}, u32[]{:S(2)}) collective-permute-start(f32[1,2,32,32]{3,2,1,0:T(8,128)S(1)} %add_add_fusion.refs_0_), channel_id=1, source_target_pairs={{0,1},{1,0},{2,3},{3,2},{4,5},{5,4},{6,7},{7,6},{8,9},{9,8},{10,11... | collective-permute-start | bytes 24584 | tf_op jit(solution)/shard_map/gradient_exchange/ppermute | solution.py:285
  50.0 0.6 %copy-start.11 = (f32[1,2,32,32]{3,2,1,0:T(8,128)}, f32[1,2,32,32]{3,2,1,0:T(8,128)S(1)}, u32[]{:S(2)}) copy-start(f32[1,2,32,32]{3,2,1,0:T(8,128)S(1)} %collective-permute-done.7.refs_1_) | copy-start | bytes 24580

commit v11 on v10

--- a/solution.py
+++ b/solution.py
@@ -121,7 +121,7 @@
 
 
 def imaging_body(
-    pos_ref, im_ref, sh_ref, w_ref, dose_ref, t_ref, ev_ref, ev2_ref, own_ref, goal_ref, h_ref, hc_ref,
+    pos_ref, im_ref, sh_ref, w_ref, dose_ref, tr_ref, ti_ref, ev_ref, ev2_ref, own_ref, goal_ref, h_ref, hc_ref,
     c_re_ref, c_im_ref, ct_re_ref, ct_im_ref, rw_top, rw_bot, rc_ref, la_ref, rhm_ref, rlh_ref,
     slots_ref, f_buf, i_buf, u_buf, w_buf, xr_buf, xi_buf,
 ):
@@ -140,8 +140,8 @@
     is_own = master // local_masters == pos_ref[1]
     m_re = ev_ref[master, 0] + ev2_ref[master, 0] + jnp.where(is_own, own_ref[master % local_masters, 0], 0.0)
     m_im = ev_ref[master, 1] + ev2_ref[master, 1] + jnp.where(is_own, own_ref[master % local_masters, 1], 0.0)
-    s_re = t_ref[pos, 0] + (ph_re * m_re - ph_im * m_im)
-    s_im = t_ref[pos, 1] + (ph_re * m_im + ph_im * m_re)
+    s_re = tr_ref[pos] + (ph_re * m_re - ph_im * m_im)
+    s_im = ti_ref[pos] + (ph_re * m_im + ph_im * m_re)
     i_buf[...] = jnp.zeros(i_buf.shape, jnp.float32)
 
     def spectrum(k, carry):
@@ -205,7 +205,7 @@
     return pl.pallas_call(
         imaging_body,
         out_shape=jax.ShapeDtypeStruct((4, B, B), jnp.float32),
-        in_specs=[smem] * 5 + [vmem] * 7 + [vmem] * len(tables),
+        in_specs=[smem] * 5 + [vmem] * 8 + [vmem] * len(tables),
         out_specs=vmem,
         scratch_shapes=[
             pltpu.VMEM((count, P_SIZE, 2 * P_SIZE), jnp.float32),
@@ -215,7 +215,7 @@
             pltpu.VMEM((count * B, B), jnp.float32),
             pltpu.VMEM((count * B, B), jnp.float32),
         ],
-    )(pos, inst_master, inst_shift, weights, dose, tile_spec, *every, own, target, kerns, h_cat, *tables)
+    )(pos, inst_master, inst_shift, weights, dose, *tile_spec, *every, own, target, kerns, h_cat, *tables)
 
 
 def pixel_body(*refs):
@@ -329,7 +329,7 @@
     return sum_parts(collected, "kern", kern_count, kern_pos)
 
 
-def scatter_split(x, count, pos, kern_count, kern_pos, size):
+def scatter_split(x, count, pos, kern_count, kern_pos, size, after):
     lists = partner_lists(count, kern_count)
     own = lax.dynamic_slice_in_dim(x, pos * size, size, 0)
     total = jnp.where(kern_pos == 0, own, 0.0)
@@ -342,6 +342,7 @@
         target = jnp.where(step >= 0, pos ^ step, 0)
         part = lax.dynamic_slice_in_dim(x, target * size, size, 0)
         total = total + lax.ppermute(part, ("tile", "kern"), pairs)
+    total = total + 0.0 * after
     return sum_parts(total, "kern", kern_count, kern_pos)
 
 
@@ -373,7 +374,7 @@
 
     with jax.named_scope("tile_spectra"):
         tile_re, tile_im = spectra(tile_mask.astype(jnp.float32), cos_tab, sin_tab)
-        tile_spec = jnp.stack([tile_re, tile_im], axis=1)
+        tile_spec = (tile_re, tile_im)
 
     dose = corner_dose[0]
     kerns = kernels[0]
@@ -407,13 +408,15 @@
             inst_master[:, None] == jnp.arange(region_masters, dtype=jnp.int32)[None, :]
         ).astype(jnp.float32)
         terms = jnp.sum(owner_pick[:, :, None, None, None] * both[:, None, 2:4], axis=0)
+        tile_grad = pixels(mine_tiles)
         if xor_partners(tile_count) and xor_partners(kern_count) and tile_count > 2:
-            mine_masters = scatter_split(terms, tile_count, tile_pos, kern_count, kern_pos, local_masters)
+            mine_masters = scatter_split(
+                terms, tile_count, tile_pos, kern_count, kern_pos, local_masters, tile_grad[0, 0, 0]
+            )
         else:
             mine_masters = (scatter_sum(terms, "tile", tile_count, tile_pos, local_masters),)
 
     with jax.named_scope("pixel_gradients"):
-        tile_grad = pixels(mine_tiles)
         master_grad = pixels(*mine_masters)
     return (tile_grad, master_grad)
 

time: 53.4 us -> 53.1 us (level)
  waiting for transfers between devices: 8.23 us -> 4.99 us
  matrix products: 3.19 us -> 4.4 us
  local copies, waits for them, and re-layouts: 4.86 us -> 6.06 us
  other arithmetic: 3.52 us -> 2.88 us
  between operations: 1.68 us -> 2.32 us
    ppermute x2, waiting for transfers between devices: 4.1 us -> 0.01 us  [scatter_split(): total = total + lax.ppermute(part, ('tile', 'kern'), pairs)]
    slice x0 -> x1, local copies, waits for them, and re-layouts: none -> 1.2 us  [on_device(): tile_grad[0, 0, 0]]
    ppermute x2, waiting for transfers between devices: 0.01 us -> 0.86 us  [sum_parts(): return (x, lax.ppermute(x, axis, [(0, 1), (1, 0)]))]
    another operation x1 -> x0, other arithmetic: 0.65 us -> none  [on_device(): tile_spec = jnp.stack([tile_re, tile_im], axis=1)]
    dot_general x2, matrix products: 0.36 us -> 0.97 us  [spectra(): jnp.einsum('nby,cy->nbc', rows_im, sin_tab, precision=precise)]
    dot_general x2, matrix products: 0.36 us -> 0.96 us  [spectra(): jnp.einsum('nby,cy->nbc', rows_im, cos_tab, precision=precise)]
  transfers between devices with their start and end apart: 8 -> 8, of which waited for: 3 -> 3; matrix products, arithmetic and copies ran while one was open for 8% -> 11% of each run, Pallas kernels for 5% -> 5%
where the time goes in v11:
time: 53.1 us; the launch traced here: 52.6 us
  Pallas kernels  20 us (38%)
  starting transfers between devices  11.9 us (22%)
  local copies, waits for them, and re-layouts  6.06 us (11%)
  waiting for transfers between devices  4.99 us (9%)
  matrix products  4.4 us (8%)
  other arithmetic  2.88 us (5%)
  between operations  2.32 us (4%)
    pallas_call x1, Pallas kernels, imaging(): pl.pallas_call(imaging_body, out_shape=jax.ShapeDtypeStruct((4, B, B), jn...  14.9 us
    pallas_call x2, Pallas kernels, pixels(): pl.pallas_call(pixel_body, out_shape=jax.ShapeDtypeStruct((parts[0].shape...  5.19 us
    ppermute x2, starting transfers between devices, gather_split(): got = lax.ppermute(x, ('tile', 'kern'), pairs)  4.75 us
    ppermute x2, starting transfers between devices, sum_parts(): return (x, lax.ppermute(x, axis, [(0, 1), (1, 0)]))  4.42 us
    unnamed x28, local copies, waits for them, and re-layouts  3.87 us
    ppermute x1, waiting for transfers between devices, sum_all(): x = x + lax.ppermute(x, axis, [(i, i ^ step) for i in range(count)])  2.91 us
    ppermute x1, starting transfers between devices, sum_all(): x = x + lax.ppermute(x, axis, [(i, i ^ step) for i in range(count)])  1.56 us
    dot_general x2, matrix products, spectra(): rows_re = jnp.einsum('bx,nxy->nby', cos_tab, masks, precision=precise)  1.33 us
  transfers between devices with their start and end apart: 8, of which 3 were waited for; matrix products, arithmetic and copies ran while one was open for 11% of the time, Pallas kernels for 5%

profile of v11, /device:TPU:0, one launch (start us, length us, event | category | flops | bytes accessed | tf_op | source)
XLA Modules:
  0.0 52.6 jit_solution(9974587025500933057)
XLA Ops:
  0.7 0.8 %copy-done.2 = f32[32,256]{1,0:T(8,128)S(1)} copy-done((f32[32,256]{1,0:T(8,128)S(1)}, f32[32,256]{1,0:T(8,128)}, u32[]{:S(2)}) %copy-start.2) | copy-done | bytes 32792
  1.4 1.1 %fusion.8 = f32[32,256]{1,0:T(8,128)S(1)} fusion(f32[32,256]{1,0:T(8,128)S(1)} %copy-done.2, bf16[1,256,256]{2,1,0:T(8,128)(2,1)} %param.27), kind=kOutput, calls=%fused_computation.18 | convolution fusion | flops 25165824 | bytes 196608 | tf_op jit(solution)/shard_map/master_spectra/bx,nxy->nby/dot_general | solution.py:38
  2.6 0.2 fusion.6
  3.5 4.1 %collective-permute-start = (f32[1,2,32,32]{3,2,1,0:T(8,128)S(1)}, f32[1,2,32,32]{3,2,1,0:T(8,128)S(1)}, u32[]{:S(2)}, u32[]{:S(2)}) collective-permute-start(f32[1,2,32,32]{3,2,1,0:T(8,128)S(1)} %pad_maximum_fusion.1.own_ref), channel_id=1, source_target_pairs={{8,0},{12,4},{0,8},{4,12},{5,1},{1,5},{13,9},{9,13},{10,2},{14,6},... | collective-permute-start | bytes 24584 | tf_op jit(solution)/shard_map/master_spectra/ppermute | solution.py:325
  7.6 0.7 %collective-permute-start.1 = (f32[1,2,32,32]{3,2,1,0:T(8,128)S(1)}, f32[1,2,32,32]{3,2,1,0:T(8,128)S(1)}, u32[]{:S(2)}, u32[]{:S(2)}) collective-permute-start(f32[1,2,32,32]{3,2,1,0:T(8,128)S(1)} %pad_maximum_fusion.1.own_ref), channel_id=1, source_target_pairs={{13,1},{9,5},{5,9},{1,13},{15,3},{11,7},{7,11},{3,15},{29,17},{25,... | collective-permute-start | bytes 24584 | tf_op jit(solution)/shard_map/master_spectra/ppermute | solution.py:325
  8.3 0.6 %copy-done.12 = f32[1,12]{1,0:T(1,128)S(1)} copy-done((f32[1,12]{1,0:T(1,128)S(1)}, f32[1,12]{1,0:T(1,128)}, u32[]{:S(2)}) %copy-start.12) | copy-done | bytes 72
  9.1 0.7 %copy-done.7 = f32[32,256,1]{1,0,2:T(8,128)S(1)} copy-done((f32[32,256,1]{1,0,2:T(8,128)S(1)}, f32[32,256,1]{1,0,2:T(8,128)}, u32[]{:S(2)}) %copy-start.7) | copy-done | bytes 32792
  9.8 0.2 convolution_bitcast_fusion.1
  10.0 0.5 %copy-done.6 = f32[32,256,1]{1,0,2:T(8,128)S(1)} copy-done((f32[32,256,1]{1,0,2:T(8,128)S(1)}, f32[32,256,1]{1,0,2:T(8,128)}, u32[]{:S(2)}) %copy-start.6) | copy-done | bytes 32792
  10.6 0.2 convolution_bitcast_fusion
  10.8 0.2 fusion.14
  11.0 0.2 fusion.13
  11.6 0.8 %convolution_add_fusion.ti_ref = f32[2,32,32]{2,1,0:T(8,128)} fusion(f32[2,32,32]{2,1,0:T(8,128)S(1)} %fusion.14, f32[2,32,256]{2,1,0:T(8,128)S(1)} %convolution_bitcast_fusion, f32[32,256,1]{1,0,2:T(8,128)S(1)} %copy-done.7), kind=kOutput, calls=%fused_computation.2 | convolution fusion | flops 6293504 | bytes 114688 | tf_op jit(solution)/shard_map/tile_spectra/nby,cy->nbc/dot_general | solution.py:43
  12.4 0.8 %convolution_subtract_fusion.tr_ref = f32[2,32,32]{2,1,0:T(8,128)} fusion(f32[2,32,32]{2,1,0:T(8,128)S(1)} %fusion.13, f32[2,32,256]{2,1,0:T(8,128)S(1)} %convolution_bitcast_fusion, f32[32,256,1]{1,0,2:T(8,128)S(1)} %copy-done.6), kind=kOutput, calls=%fused_computation.3 | convolution fusion | flops 6293504 | bytes 114688 | tf_op jit(solution)/shard_map/tile_spectra/nby,cy->nbc/dot_general | solution.py:40
  13.2 0.9 %pad_maximum_fusion = f32[12,32,128]{2,1,0:T(8,128)} fusion(f32[12,32,32]{2,1,0:T(8,128)S(1)} %copy.39, f32[12,32,32]{2,1,0:T(8,128)S(1)} %copy.38, f32[12,32,32]{2,1,0:T(8,128)S(1)} %copy.36), kind=kLoop, calls=%fused_computation.15 | loop fusion | flops 147456 | bytes 344064 | tf_op jit(solution)/shard_map/imaging_kernel/concatenate | solution.py:390
  14.2 2.0 %collective-permute-start.2 = (f32[4,2,32,32]{3,2,1,0:T(8,128)S(1)}, f32[4,2,32,32]{3,2,1,0:T(8,128)S(1)}, u32[]{:S(2)}, u32[]{:S(2)}) collective-permute-start(f32[4,2,32,32]{3,2,1,0:T(8,128)S(1)} %select_add_fusion.1.ev_ref), channel_id=1, source_target_pairs={{0,1},{1,0},{2,3},{3,2},{4,5},{5,4},{6,7},{7,6},{8,9},{9,8},{10,11... | collective-permute-start | bytes 98312 | tf_op jit(solution)/shard_map/master_spectra/ppermute | solution.py:285
  16.2 0.6 %pad_add_fusion.pos_ref = s32[2]{0:T(128)} fusion(s32[1]{0:T(128)} %bitcast.1, s32[1]{0:T(128)} %bitcast), kind=kLoop, calls=%fused_computation.27 | loop fusion | flops 2 | bytes 16 | tf_op jit(solution)/shard_map/imaging_kernel/stack | solution.py:393
  17.5 0.6 %copy-done.9 = f32[4,2,32,32]{3,2,1,0:T(8,128)} copy-done((f32[4,2,32,32]{3,2,1,0:T(8,128)}, f32[4,2,32,32]{3,2,1,0:T(8,128)S(1)}, u32[]{:S(2)}) %copy-start.9) | copy-done | bytes 32792
  18.1 14.9 %imaging_kernel.1 = f32[4,32,32]{2,1,0:T(8,128)} custom-call(s32[2]{0:T(128)} %pad_add_fusion.pos_ref, s32[2]{0:T(128)} %im_ref.1, s32[2,2]{1,0:T(2,128)} %sh_ref.1, f32[12]{0:T(128)} %bitcast.79, f32[1]{0:T(128)S(6)} %copy.41.dose_ref, f32[2,32,32]{2,1,0:T(8,128)} %convolution_subtract_fusion.tr_ref, f32[2,32,32]{2,1,0:T(8,128)} %convolution_add_fusion.ti_ref, ...), custom_call_target="tpu_custom_call" | custom-call | tf_op jit(solution)/shard_map/imaging_kernel/pallas_call | solution.py:205
  33.0 1.6 %collective-permute-start.3 = (f32[1,4,32,32]{3,2,1,0:T(8,128)}, f32[1,4,32,32]{3,2,1,0:T(8,128)S(1)}, u32[]{:S(2)}, u32[]{:S(2)}) collective-permute-start(f32[1,4,32,32]{3,2,1,0:T(8,128)} %bitcast.74), channel_id=1, source_target_pairs={{0,2},{2,0},{1,3},{3,1},{4,6},{6,4},{5,7},{7,5},{8,10},{10,8},{9,1... | collective-permute-start | bytes 49160 | tf_op jit(solution)/shard_map/gradient_exchange/ppermute | solution.py:278
  34.6 2.9 %collective-permute-done.3 = f32[1,4,32,32]{3,2,1,0:T(8,128)S(1)} collective-permute-done((f32[1,4,32,32]{3,2,1,0:T(8,128)}, f32[1,4,32,32]{3,2,1,0:T(8,128)S(1)}, u32[]{:S(2)}, u32[]{:S(2)}) %collective-permute-start.3) | collective-permute-done | bytes 16416 | tf_op jit(solution)/shard_map/gradient_exchange/ppermute | solution.py:278
  37.5 0.8 %bitcast_add_fusion = f32[1,4,32,32]{3,2,1,0:T(8,128)S(1)} fusion(f32[1,4,32,32]{3,2,1,0:T(8,128)S(1)} %collective-permute-done.3, f32[4,32,32]{2,1,0:T(8,128)} %imaging_kernel.1), kind=kLoop, calls=%fused_computation.33 | loop fusion | flops 4096 | bytes 49152 | tf_op jit(solution)/shard_map/gradient_exchange/add | solution.py:278
  38.5 1.2 %collective-permute-done.4 = f32[1,4,32,32]{3,2,1,0:T(8,128)S(1)} collective-permute-done((f32[1,4,32,32]{3,2,1,0:T(8,128)S(1)}, f32[1,4,32,32]{3,2,1,0:T(8,128)S(1)}, u32[]{:S(2)}, u32[]{:S(2)}) %collective-permute-start.4) | collective-permute-done | bytes 16416 | tf_op jit(solution)/shard_map/gradient_exchange/ppermute | solution.py:267
  39.8 0.6 %fusion.12 = (f32[2,2,32,32]{3,2,1,0:T(8,128)S(1)}, f32[2,2,32,32]{3,2,1,0:T(8,128)}) fusion(f32[2,4,32,32]{3,2,1,0:T(8,128)S(1)} %select_add_fusion), kind=kLoop, calls=%fused_computation.35 | loop fusion | bytes 65536 | tf_op jit(solution)/shard_map/gradient_exchange/slice | solution.py:410
  40.5 0.5 collective-permute-start.5
  41.0 0.7 %collective-permute-start.6 = (f32[1,2,32,32]{3,2,1,0:T(8,128)S(1)}, f32[1,2,32,32]{3,2,1,0:T(8,128)S(1)}, u32[]{:S(2)}, u32[]{:S(2)}) collective-permute-start(f32[1,2,32,32]{3,2,1,0:T(8,128)S(1)} %get-tuple-element.5), channel_id=1, source_target_pairs={{1,13},{5,9},{9,5},{13,1},{3,15},{7,11},{11,7},{15,3},{17,29},{21,... | collective-permute-start | bytes 24584 | tf_op jit(solution)/shard_map/gradient_exchange/ppermute | solution.py:344
  41.7 2.9 %gradient_exchange.1 = f32[2,256,256]{2,1,0:T(8,128)} custom-call(f32[2,2,32,32]{3,2,1,0:T(8,128)} %get-tuple-element.7.refs_0_, f32[32,256]{1,0:T(8,128)} %constant.72.clone.c_re_ref.refs_1_.refs_2_, f32[32,256]{1,0:T(8,128)} %constant.73.clone.c_im_ref.refs_2_.refs_3_, bf16[256,384]{1,0:T(8,128)(2,1)} %constant.82.clone.refs_3_.refs_4_), custom_call_target="tpu_custom_call" | custom-call | tf_op jit(solution)/shard_map/gradient_exchange/pallas_call | solution.py:248
  44.6 1.2 %slice.24 = f32[1,1,1]{2,1,0:T(1,128)} slice(f32[2,256,256]{2,1,0:T(8,128)} %gradient_exchange.1), slice={[0:1], [0:1], [0:1]} | slice | bytes 8 | tf_op jit(solution)/shard_map/gradient_exchange/slice | solution.py:414
  46.5 2.4 %collective-permute-start.7 = (f32[1,2,32,32]{3,2,1,0:T(8,128)S(1)}, f32[1,2,32,32]{3,2,1,0:T(8,128)S(1)}, u32[]{:S(2)}, u32[]{:S(2)}) collective-permute-start(f32[1,2,32,32]{3,2,1,0:T(8,128)S(1)} %add_add_fusion.refs_0_), channel_id=1, source_target_pairs={{0,1},{1,0},{2,3},{3,2},{4,5},{5,4},{6,7},{7,6},{8,9},{9,8},{10,11... | collective-permute-start | bytes 24584 | tf_op jit(solution)/shard_map/gradient_exchange/ppermute | solution.py:285
  48.8 0.9 %collective-permute-done.7.refs_1_ = f32[1,2,32,32]{3,2,1,0:T(8,128)S(1)} collective-permute-done((f32[1,2,32,32]{3,2,1,0:T(8,128)S(1)}, f32[1,2,32,32]{3,2,1,0:T(8,128)S(1)}, u32[]{:S(2)}, u32[]{:S(2)}) %collective-permute-start.7) | collective-permute-done | bytes 8224 | tf_op jit(solution)/shard_map/gradient_exchange/ppermute | solution.py:285
  49.7 0.6 %copy-done.11 = f32[1,2,32,32]{3,2,1,0:T(8,128)} copy-done((f32[1,2,32,32]{3,2,1,0:T(8,128)}, f32[1,2,32,32]{3,2,1,0:T(8,128)S(1)}, u32[]{:S(2)}) %copy-start.11) | copy-done | bytes 8216
  50.3 2.3 %pixel_gradients.1 = f32[1,256,256]{2,1,0:T(8,128)} custom-call(f32[1,2,32,32]{3,2,1,0:T(8,128)} %copy-done.10, f32[1,2,32,32]{3,2,1,0:T(8,128)} %copy-done.11, f32[32,256]{1,0:T(8,128)} %constant.72.clone.c_re_ref.refs_1_.refs_2_, f32[32,256]{1,0:T(8,128)} %constant.73.clone.c_im_ref.refs_2_.refs_3_, bf16[256,384]{1,0:T(8,128)(2,1)} %constant.82.clone.refs_3_.refs_4_), custom_call_target="tpu_custom_call" | custom-call | tf_op jit(solution)/shard_map/pixel_gradients/pallas_call | solution.py:248
  (47 shorter events, 1.7 us)
Async XLA Ops:
  0.6 8.5 %copy-start = (bf16[2,256,256]{2,1,0:T(8,128)(2,1)S(1)}, bf16[2,256,256]{2,1,0:T(8,128)(2,1)}, u32[]{:S(2)}) copy-start(bf16[2,256,256]{2,1,0:T(8,128)(2,1)} %param.26) | copy-start | bytes 786436
  0.6 0.8 %copy-start.2 = (f32[32,256]{1,0:T(8,128)S(1)}, f32[32,256]{1,0:T(8,128)}, u32[]{:S(2)}) copy-start(f32[32,256]{1,0:T(8,128)} %constant.72.clone.c_re_ref.refs_1_.refs_2_) | copy-start | bytes 98308
  0.7 1.9 %copy-start.3 = (f32[32,256]{1,0:T(8,128)S(1)}, f32[32,256]{1,0:T(8,128)}, u32[]{:S(2)}) copy-start(f32[32,256]{1,0:T(8,128)} %constant.73.clone.c_im_ref.refs_2_.refs_3_) | copy-start | bytes 98308
  0.7 1.9 %copy-start.5 = (bf16[1,256,256]{2,1,0:T(8,128)(2,1)S(1)}, bf16[1,256,256]{2,1,0:T(8,128)(2,1)}, u32[]{:S(2)}) copy-start(bf16[1,256,256]{2,1,0:T(8,128)(2,1)} %param.27) | copy-start | bytes 393220
  0.7 8.2 %copy-start.1 = (f32[1,12,2,32,32]{4,3,2,1,0:T(8,128)S(1)}, f32[1,12,2,32,32]{4,3,2,1,0:T(8,128)}, u32[]{:S(2)}) copy-start(f32[1,12,2,32,32]{4,3,2,1,0:T(8,128)} %param.31) | copy-start | bytes 294916
  3.5 5.6 %copy-start.8 = (f32[1,2,32,32]{3,2,1,0:T(8,128)}, f32[1,2,32,32]{3,2,1,0:T(8,128)S(1)}, u32[]{:S(2)}) copy-start(f32[1,2,32,32]{3,2,1,0:T(8,128)S(1)} %pad_maximum_fusion.1.own_ref) | copy-start | bytes 24580
  3.5 10.6 %collective-permute-start = (f32[1,2,32,32]{3,2,1,0:T(8,128)S(1)}, f32[1,2,32,32]{3,2,1,0:T(8,128)S(1)}, u32[]{:S(2)}, u32[]{:S(2)}) collective-permute-start(f32[1,2,32,32]{3,2,1,0:T(8,128)S(1)} %pad_maximum_fusion.1.own_ref), channel_id=1, source_target_pairs={{8,0},{12,4},{0,8},{4,12},{5,1},{1,5},{13,9},{9,13},{10,2},{14,6},... | collective-permute-start | bytes 24584 | tf_op jit(solution)/shard_map/master_spectra/ppermute | solution.py:325
  7.6 6.5 %collective-permute-start.1 = (f32[1,2,32,32]{3,2,1,0:T(8,128)S(1)}, f32[1,2,32,32]{3,2,1,0:T(8,128)S(1)}, u32[]{:S(2)}, u32[]{:S(2)}) collective-permute-start(f32[1,2,32,32]{3,2,1,0:T(8,128)S(1)} %pad_maximum_fusion.1.own_ref), channel_id=1, source_target_pairs={{13,1},{9,5},{5,9},{1,13},{15,3},{11,7},{7,11},{3,15},{29,17},{25,... | collective-permute-start | bytes 24584 | tf_op jit(solution)/shard_map/master_spectra/ppermute | solution.py:325
  8.3 0.7 %copy-start.12 = (f32[1,12]{1,0:T(1,128)S(1)}, f32[1,12]{1,0:T(1,128)}, u32[]{:S(2)}) copy-start(f32[1,12]{1,0:T(1,128)} %param.32) | copy-start | bytes 148
  9.0 0.8 %copy-start.7 = (f32[32,256,1]{1,0,2:T(8,128)S(1)}, f32[32,256,1]{1,0,2:T(8,128)}, u32[]{:S(2)}) copy-start(f32[32,256,1]{1,0,2:T(8,128)} %constant.91) | copy-start | bytes 98308
  9.8 0.8 %copy-start.6 = (f32[32,256,1]{1,0,2:T(8,128)S(1)}, f32[32,256,1]{1,0,2:T(8,128)}, u32[]{:S(2)}) copy-start(f32[32,256,1]{1,0,2:T(8,128)} %constant.92) | copy-start | bytes 98308
  14.2 3.3 %copy-start.4 = (f32[4,2,32,32]{3,2,1,0:T(8,128)}, f32[4,2,32,32]{3,2,1,0:T(8,128)S(1)}, u32[]{:S(2)}) copy-start(f32[4,2,32,32]{3,2,1,0:T(8,128)S(1)} %select_add_fusion.1.ev_ref) | copy-start | bytes 98308
  14.2 3.3 %collective-permute-start.2 = (f32[4,2,32,32]{3,2,1,0:T(8,128)S(1)}, f32[4,2,32,32]{3,2,1,0:T(8,128)S(1)}, u32[]{:S(2)}, u32[]{:S(2)}) collective-permute-start(f32[4,2,32,32]{3,2,1,0:T(8,128)S(1)} %select_add_fusion.1.ev_ref), channel_id=1, source_target_pairs={{0,1},{1,0},{2,3},{3,2},{4,5},{5,4},{6,7},{7,6},{8,9},{9,8},{10,11... | collective-permute-start | bytes 98312 | tf_op jit(solution)/shard_map/master_spectra/ppermute | solution.py:285
  17.5 0.6 %copy-start.9 = (f32[4,2,32,32]{3,2,1,0:T(8,128)}, f32[4,2,32,32]{3,2,1,0:T(8,128)S(1)}, u32[]{:S(2)}) copy-start(f32[4,2,32,32]{3,2,1,0:T(8,128)S(1)} %collective-permute-done.2.ev2_ref) | copy-start | bytes 98308
  33.0 1.6 %copy-start.13 = (s32[2]{0:T(128)S(1)}, s32[2]{0:T(128)}, u32[]{:S(2)}) copy-start(s32[2]{0:T(128)} %im_ref.1) | copy-start | bytes 28
  33.0 4.5 %collective-permute-start.3 = (f32[1,4,32,32]{3,2,1,0:T(8,128)}, f32[1,4,32,32]{3,2,1,0:T(8,128)S(1)}, u32[]{:S(2)}, u32[]{:S(2)}) collective-permute-start(f32[1,4,32,32]{3,2,1,0:T(8,128)} %bitcast.74), channel_id=1, source_target_pairs={{0,2},{2,0},{1,3},{3,1},{4,6},{6,4},{5,7},{7,5},{8,10},{10,8},{9,1... | collective-permute-start | bytes 49160 | tf_op jit(solution)/shard_map/gradient_exchange/ppermute | solution.py:278
  38.4 1.3 %collective-permute-start.4 = (f32[1,4,32,32]{3,2,1,0:T(8,128)S(1)}, f32[1,4,32,32]{3,2,1,0:T(8,128)S(1)}, u32[]{:S(2)}, u32[]{:S(2)}) collective-permute-start(f32[1,4,32,32]{3,2,1,0:T(8,128)S(1)} %bitcast_add_fusion), channel_id=1, source_target_pairs={{0,1},{1,0},{2,3},{3,2},{4,5},{5,4},{6,7},{7,6},{8,9},{9,8},{10,11... | collective-permute-start | bytes 49160 | tf_op jit(solution)/shard_map/gradient_exchange/ppermute | solution.py:267
  40.5 5.9 %collective-permute-start.5 = (f32[1,2,32,32]{3,2,1,0:T(8,128)S(1)}, f32[1,2,32,32]{3,2,1,0:T(8,128)S(1)}, u32[]{:S(2)}, u32[]{:S(2)}) collective-permute-start(f32[1,2,32,32]{3,2,1,0:T(8,128)S(1)} %get-tuple-element.4), channel_id=1, source_target_pairs={{0,8},{4,12},{8,0},{12,4},{1,5},{5,1},{9,13},{13,9},{2,10},{6,14},... | collective-permute-start | bytes 24584 | tf_op jit(solution)/shard_map/gradient_exchange/ppermute | solution.py:344
  41.0 5.4 %collective-permute-start.6 = (f32[1,2,32,32]{3,2,1,0:T(8,128)S(1)}, f32[1,2,32,32]{3,2,1,0:T(8,128)S(1)}, u32[]{:S(2)}, u32[]{:S(2)}) collective-permute-start(f32[1,2,32,32]{3,2,1,0:T(8,128)S(1)} %get-tuple-element.5), channel_id=1, source_target_pairs={{1,13},{5,9},{9,5},{13,1},{3,15},{7,11},{11,7},{15,3},{17,29},{21,... | collective-permute-start | bytes 24584 | tf_op jit(solution)/shard_map/gradient_exchange/ppermute | solution.py:344
  46.5 3.2 %copy-start.10 = (f32[1,2,32,32]{3,2,1,0:T(8,128)}, f32[1,2,32,32]{3,2,1,0:T(8,128)S(1)}, u32[]{:S(2)}) copy-start(f32[1,2,32,32]{3,2,1,0:T(8,128)S(1)} %add_add_fusion.refs_0_) | copy-start | bytes 24580
  46.5 3.2 %collective-permute-start.7 = (f32[1,2,32,32]{3,2,1,0:T(8,128)S(1)}, f32[1,2,32,32]{3,2,1,0:T(8,128)S(1)}, u32[]{:S(2)}, u32[]{:S(2)}) collective-permute-start(f32[1,2,32,32]{3,2,1,0:T(8,128)S(1)} %add_add_fusion.refs_0_), channel_id=1, source_target_pairs={{0,1},{1,0},{2,3},{3,2},{4,5},{5,4},{6,7},{7,6},{8,9},{9,8},{10,11... | collective-permute-start | bytes 24584 | tf_op jit(solution)/shard_map/gradient_exchange/ppermute | solution.py:285
  49.7 0.6 %copy-start.11 = (f32[1,2,32,32]{3,2,1,0:T(8,128)}, f32[1,2,32,32]{3,2,1,0:T(8,128)S(1)}, u32[]{:S(2)}) copy-start(f32[1,2,32,32]{3,2,1,0:T(8,128)S(1)} %collective-permute-done.7.refs_1_) | copy-start | bytes 24580

commit v12 on v11

--- a/solution.py
+++ b/solution.py
@@ -1,3 +1,4 @@
+import functools
 import math
 
 import numpy as np
@@ -218,7 +219,11 @@
     )(pos, inst_master, inst_shift, weights, dose, *tile_spec, *every, own, target, kerns, h_cat, *tables)
 
 
-def pixel_body(*refs):
+def pixel_body(*refs, passes):
+    if passes:
+        out_ref, token_ref = refs[-2:]
+        token_ref[...] = jnp.zeros(token_ref.shape, jnp.float32)
+        refs = refs[:-2] + (out_ref,)
     out_ref = refs[-1]
     c_re_ref, c_im_ref, left_ref = refs[-4:-1]
     parts = refs[:-4]
@@ -235,7 +240,7 @@
         out_ref[n] = dot_parts(left_ref[...], stacked)
 
 
-def pixels(*parts):
+def pixels(*parts, token=False):
     freq = np.arange(B, dtype=np.int64) - B // 2
     pixel = np.arange(P_SIZE, dtype=np.int64)
     angle = (2.0 * math.pi / P_SIZE) * np.mod(freq[:, None] * pixel[None, :], P_SIZE).astype(np.float64)
@@ -245,11 +250,19 @@
     left = np.concatenate([a_hi, a_hi, a_mid, a_hi, a_lo, a_mid], axis=1)
     tables = [jnp.asarray(c_re, jnp.float32), jnp.asarray(c_im, jnp.float32), jnp.asarray(left)]
     vmem = pl.BlockSpec(memory_space=pltpu.VMEM)
+    shape = jax.ShapeDtypeStruct((parts[0].shape[0], P_SIZE, P_SIZE), jnp.float32)
+    if not token:
+        return pl.pallas_call(
+            functools.partial(pixel_body, passes=False),
+            out_shape=shape,
+            in_specs=[vmem] * (len(parts) + 3),
+            out_specs=vmem,
+        )(*parts, *tables)
     return pl.pallas_call(
-        pixel_body,
-        out_shape=jax.ShapeDtypeStruct((parts[0].shape[0], P_SIZE, P_SIZE), jnp.float32),
+        functools.partial(pixel_body, passes=True),
+        out_shape=(shape, jax.ShapeDtypeStruct((1, 1, 1, 1), jnp.float32)),
         in_specs=[vmem] * (len(parts) + 3),
-        out_specs=vmem,
+        out_specs=(vmem, vmem),
     )(*parts, *tables)
 
 
@@ -329,7 +342,7 @@
     return sum_parts(collected, "kern", kern_count, kern_pos)
 
 
-def scatter_split(x, count, pos, kern_count, kern_pos, size, after):
+def scatter_split(x, count, pos, kern_count, kern_pos, size, between):
     lists = partner_lists(count, kern_count)
     own = lax.dynamic_slice_in_dim(x, pos * size, size, 0)
     total = jnp.where(kern_pos == 0, own, 0.0)
@@ -342,8 +355,9 @@
         target = jnp.where(step >= 0, pos ^ step, 0)
         part = lax.dynamic_slice_in_dim(x, target * size, size, 0)
         total = total + lax.ppermute(part, ("tile", "kern"), pairs)
-    total = total + 0.0 * after
-    return sum_parts(total, "kern", kern_count, kern_pos)
+    done, token = between()
+    total = total + 0.0 * token
+    return done, sum_parts(total, "kern", kern_count, kern_pos)
 
 
 def on_device(
@@ -408,12 +422,13 @@
             inst_master[:, None] == jnp.arange(region_masters, dtype=jnp.int32)[None, :]
         ).astype(jnp.float32)
         terms = jnp.sum(owner_pick[:, :, None, None, None] * both[:, None, 2:4], axis=0)
-        tile_grad = pixels(mine_tiles)
         if xor_partners(tile_count) and xor_partners(kern_count) and tile_count > 2:
-            mine_masters = scatter_split(
-                terms, tile_count, tile_pos, kern_count, kern_pos, local_masters, tile_grad[0, 0, 0]
+            tile_grad, mine_masters = scatter_split(
+                terms, tile_count, tile_pos, kern_count, kern_pos, local_masters,
+                lambda: pixels(mine_tiles, token=True),
             )
         else:
+            tile_grad = pixels(mine_tiles)
             mine_masters = (scatter_sum(terms, "tile", tile_count, tile_pos, local_masters),)
 
     with jax.named_scope("pixel_gradients"):

time: 53.1 us -> 52 us (0.979)
  local copies, waits for them, and re-layouts: 6.06 us -> 4.85 us
    slice x1 -> x0, local copies, waits for them, and re-layouts: 1.2 us -> none  [on_device(): tile_grad[0, 0, 0]]
  transfers between devices with their start and end apart: 8 -> 8, of which waited for: 3 -> 4; matrix products, arithmetic and copies ran while one was open for 11% -> 9% of each run, Pallas kernels for 5% -> 6%
where the time goes in v12:
time: 52 us; the launch traced here: 51.5 us
  Pallas kernels  20 us (38%)
  starting transfers between devices  11.5 us (22%)
  waiting for transfers between devices  5.5 us (11%)
  local copies, waits for them, and re-layouts  4.85 us (9%)
  matrix products  4.4 us (8%)
  other arithmetic  2.93 us (6%)
  between operations  2.35 us (5%)
    pallas_call x1, Pallas kernels, imaging(): pl.pallas_call(imaging_body, out_shape=jax.ShapeDtypeStruct((4, B, B), jn...  14.8 us
    ppermute x2, starting transfers between devices, gather_split(): got = lax.ppermute(x, ('tile', 'kern'), pairs)  4.75 us
    ppermute x2, starting transfers between devices, sum_parts(): return (x, lax.ppermute(x, axis, [(0, 1), (1, 0)]))  3.95 us
    unnamed x28, local copies, waits for them, and re-layouts  3.86 us
    ppermute x1, waiting for transfers between devices, sum_all(): x = x + lax.ppermute(x, axis, [(i, i ^ step) for i in range(count)])  2.9 us
    pallas_call x1, Pallas kernels, pixels(): pl.pallas_call(functools.partial(pixel_body, passes=True), out_shape=(sha...  2.89 us
    pallas_call x1, Pallas kernels, pixels(): pl.pallas_call(functools.partial(pixel_body, passes=False), out_shape=sha...  2.31 us
    ppermute x1, starting transfers between devices, sum_all(): x = x + lax.ppermute(x, axis, [(i, i ^ step) for i in range(count)])  1.57 us
  transfers between devices with their start and end apart: 8, of which 4 were waited for; matrix products, arithmetic and copies ran while one was open for 9% of the time, Pallas kernels for 6%

profile of v12, /device:TPU:0, one launch (start us, length us, event | category | flops | bytes accessed | tf_op | source)
XLA Modules:
  0.0 51.5 jit_solution(10234123782006812682)
XLA Ops:
  0.7 0.8 %copy-done.2 = f32[32,256]{1,0:T(8,128)S(1)} copy-done((f32[32,256]{1,0:T(8,128)S(1)}, f32[32,256]{1,0:T(8,128)}, u32[]{:S(2)}) %copy-start.2) | copy-done | bytes 32792
  1.4 1.1 %fusion.8 = f32[32,256]{1,0:T(8,128)S(1)} fusion(f32[32,256]{1,0:T(8,128)S(1)} %copy-done.2, bf16[1,256,256]{2,1,0:T(8,128)(2,1)} %param.27), kind=kOutput, calls=%fused_computation.18 | convolution fusion | flops 25165824 | bytes 196608 | tf_op jit(solution)/shard_map/master_spectra/bx,nxy->nby/dot_general | solution.py:39
  2.6 0.2 fusion.6
  3.5 4.1 %collective-permute-start = (f32[1,2,32,32]{3,2,1,0:T(8,128)S(1)}, f32[1,2,32,32]{3,2,1,0:T(8,128)S(1)}, u32[]{:S(2)}, u32[]{:S(2)}) collective-permute-start(f32[1,2,32,32]{3,2,1,0:T(8,128)S(1)} %pad_maximum_fusion.1.own_ref), channel_id=1, source_target_pairs={{8,0},{12,4},{0,8},{4,12},{5,1},{1,5},{13,9},{9,13},{10,2},{14,6},... | collective-permute-start | bytes 24584 | tf_op jit(solution)/shard_map/master_spectra/ppermute | solution.py:338
  7.6 0.7 %collective-permute-start.1 = (f32[1,2,32,32]{3,2,1,0:T(8,128)S(1)}, f32[1,2,32,32]{3,2,1,0:T(8,128)S(1)}, u32[]{:S(2)}, u32[]{:S(2)}) collective-permute-start(f32[1,2,32,32]{3,2,1,0:T(8,128)S(1)} %pad_maximum_fusion.1.own_ref), channel_id=1, source_target_pairs={{13,1},{9,5},{5,9},{1,13},{15,3},{11,7},{7,11},{3,15},{29,17},{25,... | collective-permute-start | bytes 24584 | tf_op jit(solution)/shard_map/master_spectra/ppermute | solution.py:338
  8.3 0.6 %copy-done.12 = f32[1,12]{1,0:T(1,128)S(1)} copy-done((f32[1,12]{1,0:T(1,128)S(1)}, f32[1,12]{1,0:T(1,128)}, u32[]{:S(2)}) %copy-start.12) | copy-done | bytes 72
  9.1 0.7 %copy-done.7 = f32[32,256,1]{1,0,2:T(8,128)S(1)} copy-done((f32[32,256,1]{1,0,2:T(8,128)S(1)}, f32[32,256,1]{1,0,2:T(8,128)}, u32[]{:S(2)}) %copy-start.7) | copy-done | bytes 32792
  9.8 0.2 convolution_bitcast_fusion.1
  10.0 0.5 %copy-done.6 = f32[32,256,1]{1,0,2:T(8,128)S(1)} copy-done((f32[32,256,1]{1,0,2:T(8,128)S(1)}, f32[32,256,1]{1,0,2:T(8,128)}, u32[]{:S(2)}) %copy-start.6) | copy-done | bytes 32792
  10.6 0.2 convolution_bitcast_fusion
  10.8 0.2 fusion.14
  11.0 0.2 fusion.13
  11.6 0.8 %convolution_add_fusion.ti_ref = f32[2,32,32]{2,1,0:T(8,128)} fusion(f32[2,32,32]{2,1,0:T(8,128)S(1)} %fusion.14, f32[2,32,256]{2,1,0:T(8,128)S(1)} %convolution_bitcast_fusion, f32[32,256,1]{1,0,2:T(8,128)S(1)} %copy-done.7), kind=kOutput, calls=%fused_computation.2 | convolution fusion | flops 6293504 | bytes 114688 | tf_op jit(solution)/shard_map/tile_spectra/nby,cy->nbc/dot_general | solution.py:44
  12.4 0.8 %convolution_subtract_fusion.tr_ref = f32[2,32,32]{2,1,0:T(8,128)} fusion(f32[2,32,32]{2,1,0:T(8,128)S(1)} %fusion.13, f32[2,32,256]{2,1,0:T(8,128)S(1)} %convolution_bitcast_fusion, f32[32,256,1]{1,0,2:T(8,128)S(1)} %copy-done.6), kind=kOutput, calls=%fused_computation.3 | convolution fusion | flops 6293504 | bytes 114688 | tf_op jit(solution)/shard_map/tile_spectra/nby,cy->nbc/dot_general | solution.py:41
  13.2 0.9 %pad_maximum_fusion = f32[12,32,128]{2,1,0:T(8,128)} fusion(f32[12,32,32]{2,1,0:T(8,128)S(1)} %copy.39, f32[12,32,32]{2,1,0:T(8,128)S(1)} %copy.38, f32[12,32,32]{2,1,0:T(8,128)S(1)} %copy.36), kind=kLoop, calls=%fused_computation.15 | loop fusion | flops 147456 | bytes 344064 | tf_op jit(solution)/shard_map/imaging_kernel/concatenate | solution.py:404
  14.2 2.0 %collective-permute-start.2 = (f32[4,2,32,32]{3,2,1,0:T(8,128)S(1)}, f32[4,2,32,32]{3,2,1,0:T(8,128)S(1)}, u32[]{:S(2)}, u32[]{:S(2)}) collective-permute-start(f32[4,2,32,32]{3,2,1,0:T(8,128)S(1)} %select_add_fusion.1.ev_ref), channel_id=1, source_target_pairs={{0,1},{1,0},{2,3},{3,2},{4,5},{5,4},{6,7},{7,6},{8,9},{9,8},{10,11... | collective-permute-start | bytes 98312 | tf_op jit(solution)/shard_map/master_spectra/ppermute | solution.py:298
  16.2 0.6 %pad_add_fusion.pos_ref = s32[2]{0:T(128)} fusion(s32[1]{0:T(128)} %bitcast.1, s32[1]{0:T(128)} %bitcast), kind=kLoop, calls=%fused_computation.27 | loop fusion | flops 2 | bytes 16 | tf_op jit(solution)/shard_map/imaging_kernel/stack | solution.py:407
  17.6 0.6 %copy-done.9 = f32[4,2,32,32]{3,2,1,0:T(8,128)} copy-done((f32[4,2,32,32]{3,2,1,0:T(8,128)}, f32[4,2,32,32]{3,2,1,0:T(8,128)S(1)}, u32[]{:S(2)}) %copy-start.9) | copy-done | bytes 32792
  18.2 14.8 %imaging_kernel.1 = f32[4,32,32]{2,1,0:T(8,128)} custom-call(s32[2]{0:T(128)} %pad_add_fusion.pos_ref, s32[2]{0:T(128)} %im_ref.1, s32[2,2]{1,0:T(2,128)} %sh_ref.1, f32[12]{0:T(128)} %bitcast.79, f32[1]{0:T(128)S(6)} %copy.41.dose_ref, f32[2,32,32]{2,1,0:T(8,128)} %convolution_subtract_fusion.tr_ref, f32[2,32,32]{2,1,0:T(8,128)} %convolution_add_fusion.ti_ref, ...), custom_call_target="tpu_custom_call" | custom-call | tf_op jit(solution)/shard_map/imaging_kernel/pallas_call | solution.py:206
  33.0 1.6 %collective-permute-start.3 = (f32[1,4,32,32]{3,2,1,0:T(8,128)}, f32[1,4,32,32]{3,2,1,0:T(8,128)S(1)}, u32[]{:S(2)}, u32[]{:S(2)}) collective-permute-start(f32[1,4,32,32]{3,2,1,0:T(8,128)} %bitcast.74), channel_id=1, source_target_pairs={{0,2},{2,0},{1,3},{3,1},{4,6},{6,4},{5,7},{7,5},{8,10},{10,8},{9,1... | collective-permute-start | bytes 49160 | tf_op jit(solution)/shard_map/gradient_exchange/ppermute | solution.py:291
  34.6 2.9 %collective-permute-done.3 = f32[1,4,32,32]{3,2,1,0:T(8,128)S(1)} collective-permute-done((f32[1,4,32,32]{3,2,1,0:T(8,128)}, f32[1,4,32,32]{3,2,1,0:T(8,128)S(1)}, u32[]{:S(2)}, u32[]{:S(2)}) %collective-permute-start.3) | collective-permute-done | bytes 16416 | tf_op jit(solution)/shard_map/gradient_exchange/ppermute | solution.py:291
  37.6 0.8 %bitcast_add_fusion = f32[1,4,32,32]{3,2,1,0:T(8,128)S(1)} fusion(f32[1,4,32,32]{3,2,1,0:T(8,128)S(1)} %collective-permute-done.3, f32[4,32,32]{2,1,0:T(8,128)} %imaging_kernel.1), kind=kLoop, calls=%fused_computation.33 | loop fusion | flops 4096 | bytes 49152 | tf_op jit(solution)/shard_map/gradient_exchange/add | solution.py:291
  38.5 1.2 %collective-permute-done.4 = f32[1,4,32,32]{3,2,1,0:T(8,128)S(1)} collective-permute-done((f32[1,4,32,32]{3,2,1,0:T(8,128)S(1)}, f32[1,4,32,32]{3,2,1,0:T(8,128)S(1)}, u32[]{:S(2)}, u32[]{:S(2)}) %collective-permute-start.4) | collective-permute-done | bytes 16416 | tf_op jit(solution)/shard_map/gradient_exchange/ppermute | solution.py:280
  39.8 0.6 %fusion.12 = (f32[2,2,32,32]{3,2,1,0:T(8,128)S(1)}, f32[2,2,32,32]{3,2,1,0:T(8,128)}) fusion(f32[2,4,32,32]{3,2,1,0:T(8,128)S(1)} %select_add_fusion), kind=kLoop, calls=%fused_computation.35 | loop fusion | bytes 65536 | tf_op jit(solution)/shard_map/gradient_exchange/slice | solution.py:424
  40.6 0.5 collective-permute-start.5
  41.0 0.7 %collective-permute-start.6 = (f32[1,2,32,32]{3,2,1,0:T(8,128)S(1)}, f32[1,2,32,32]{3,2,1,0:T(8,128)S(1)}, u32[]{:S(2)}, u32[]{:S(2)}) collective-permute-start(f32[1,2,32,32]{3,2,1,0:T(8,128)S(1)} %get-tuple-element.9), channel_id=1, source_target_pairs={{1,13},{5,9},{9,5},{13,1},{3,15},{7,11},{11,7},{15,3},{17,29},{21,... | collective-permute-start | bytes 24584 | tf_op jit(solution)/shard_map/gradient_exchange/ppermute | solution.py:357
  41.7 2.9 %gradient_exchange.1 = (f32[2,256,256]{2,1,0:T(8,128)}, f32[1,1,1,1]{3,2,1,0:T(1,128)}) custom-call(f32[2,2,32,32]{3,2,1,0:T(8,128)} %get-tuple-element.11.refs_0_, f32[32,256]{1,0:T(8,128)} %constant.72.clone.c_re_ref.refs_1_.refs_2_, f32[32,256]{1,0:T(8,128)} %constant.73.clone.c_im_ref.refs_2_.refs_3_, bf16[256,384]{1,0:T(8,128)(2,1)} %constant.82.clone.refs_3_.refs_4_), custom_call_target="tpu_custom_call" | custom-call | tf_op jit(solution)/shard_map/gradient_exchange/pallas_call | solution.py:261
  45.3 0.5 %collective-permute-done.5 = f32[1,2,32,32]{3,2,1,0:T(8,128)S(1)} collective-permute-done((f32[1,2,32,32]{3,2,1,0:T(8,128)S(1)}, f32[1,2,32,32]{3,2,1,0:T(8,128)S(1)}, u32[]{:S(2)}, u32[]{:S(2)}) %collective-permute-start.5) | collective-permute-done | bytes 8224 | tf_op jit(solution)/shard_map/gradient_exchange/ppermute | solution.py:357
  45.8 1.9 %collective-permute-start.7 = (f32[1,2,32,32]{3,2,1,0:T(8,128)S(1)}, f32[1,2,32,32]{3,2,1,0:T(8,128)S(1)}, u32[]{:S(2)}, u32[]{:S(2)}) collective-permute-start(f32[1,2,32,32]{3,2,1,0:T(8,128)S(1)} %add_add_fusion.refs_0_), channel_id=1, source_target_pairs={{0,1},{1,0},{2,3},{3,2},{4,5},{5,4},{6,7},{7,6},{8,9},{9,8},{10,11... | collective-permute-start | bytes 24584 | tf_op jit(solution)/shard_map/gradient_exchange/ppermute | solution.py:298
  47.7 0.9 %collective-permute-done.7.refs_1_ = f32[1,2,32,32]{3,2,1,0:T(8,128)S(1)} collective-permute-done((f32[1,2,32,32]{3,2,1,0:T(8,128)S(1)}, f32[1,2,32,32]{3,2,1,0:T(8,128)S(1)}, u32[]{:S(2)}, u32[]{:S(2)}) %collective-permute-start.7) | collective-permute-done | bytes 8224 | tf_op jit(solution)/shard_map/gradient_exchange/ppermute | solution.py:298
  48.6 0.6 %copy-done.11 = f32[1,2,32,32]{3,2,1,0:T(8,128)} copy-done((f32[1,2,32,32]{3,2,1,0:T(8,128)}, f32[1,2,32,32]{3,2,1,0:T(8,128)S(1)}, u32[]{:S(2)}) %copy-start.11) | copy-done | bytes 8216
  49.2 2.3 %pixel_gradients.1 = f32[1,256,256]{2,1,0:T(8,128)} custom-call(f32[1,2,32,32]{3,2,1,0:T(8,128)} %copy-done.10, f32[1,2,32,32]{3,2,1,0:T(8,128)} %copy-done.11, f32[32,256]{1,0:T(8,128)} %constant.72.clone.c_re_ref.refs_1_.refs_2_, f32[32,256]{1,0:T(8,128)} %constant.73.clone.c_im_ref.refs_2_.refs_3_, bf16[256,384]{1,0:T(8,128)(2,1)} %constant.82.clone.refs_3_.refs_4_), custom_call_target="tpu_custom_call" | custom-call | tf_op jit(solution)/shard_map/pixel_gradients/pallas_call | solution.py:255
  (46 shorter events, 1.7 us)
Async XLA Ops:
  0.6 8.5 %copy-start = (bf16[2,256,256]{2,1,0:T(8,128)(2,1)S(1)}, bf16[2,256,256]{2,1,0:T(8,128)(2,1)}, u32[]{:S(2)}) copy-start(bf16[2,256,256]{2,1,0:T(8,128)(2,1)} %param.26) | copy-start | bytes 786436
  0.6 0.8 %copy-start.2 = (f32[32,256]{1,0:T(8,128)S(1)}, f32[32,256]{1,0:T(8,128)}, u32[]{:S(2)}) copy-start(f32[32,256]{1,0:T(8,128)} %constant.72.clone.c_re_ref.refs_1_.refs_2_) | copy-start | bytes 98308
  0.7 1.9 %copy-start.3 = (f32[32,256]{1,0:T(8,128)S(1)}, f32[32,256]{1,0:T(8,128)}, u32[]{:S(2)}) copy-start(f32[32,256]{1,0:T(8,128)} %constant.73.clone.c_im_ref.refs_2_.refs_3_) | copy-start | bytes 98308
  0.7 1.9 %copy-start.5 = (bf16[1,256,256]{2,1,0:T(8,128)(2,1)S(1)}, bf16[1,256,256]{2,1,0:T(8,128)(2,1)}, u32[]{:S(2)}) copy-start(bf16[1,256,256]{2,1,0:T(8,128)(2,1)} %param.27) | copy-start | bytes 393220
  0.7 8.2 %copy-start.1 = (f32[1,12,2,32,32]{4,3,2,1,0:T(8,128)S(1)}, f32[1,12,2,32,32]{4,3,2,1,0:T(8,128)}, u32[]{:S(2)}) copy-start(f32[1,12,2,32,32]{4,3,2,1,0:T(8,128)} %param.31) | copy-start | bytes 294916
  3.5 5.6 %copy-start.8 = (f32[1,2,32,32]{3,2,1,0:T(8,128)}, f32[1,2,32,32]{3,2,1,0:T(8,128)S(1)}, u32[]{:S(2)}) copy-start(f32[1,2,32,32]{3,2,1,0:T(8,128)S(1)} %pad_maximum_fusion.1.own_ref) | copy-start | bytes 24580
  3.5 10.6 %collective-permute-start = (f32[1,2,32,32]{3,2,1,0:T(8,128)S(1)}, f32[1,2,32,32]{3,2,1,0:T(8,128)S(1)}, u32[]{:S(2)}, u32[]{:S(2)}) collective-permute-start(f32[1,2,32,32]{3,2,1,0:T(8,128)S(1)} %pad_maximum_fusion.1.own_ref), channel_id=1, source_target_pairs={{8,0},{12,4},{0,8},{4,12},{5,1},{1,5},{13,9},{9,13},{10,2},{14,6},... | collective-permute-start | bytes 24584 | tf_op jit(solution)/shard_map/master_spectra/ppermute | solution.py:338
  7.6 6.5 %collective-permute-start.1 = (f32[1,2,32,32]{3,2,1,0:T(8,128)S(1)}, f32[1,2,32,32]{3,2,1,0:T(8,128)S(1)}, u32[]{:S(2)}, u32[]{:S(2)}) collective-permute-start(f32[1,2,32,32]{3,2,1,0:T(8,128)S(1)} %pad_maximum_fusion.1.own_ref), channel_id=1, source_target_pairs={{13,1},{9,5},{5,9},{1,13},{15,3},{11,7},{7,11},{3,15},{29,17},{25,... | collective-permute-start | bytes 24584 | tf_op jit(solution)/shard_map/master_spectra/ppermute | solution.py:338
  8.3 0.7 %copy-start.12 = (f32[1,12]{1,0:T(1,128)S(1)}, f32[1,12]{1,0:T(1,128)}, u32[]{:S(2)}) copy-start(f32[1,12]{1,0:T(1,128)} %param.32) | copy-start | bytes 148
  9.0 0.8 %copy-start.7 = (f32[32,256,1]{1,0,2:T(8,128)S(1)}, f32[32,256,1]{1,0,2:T(8,128)}, u32[]{:S(2)}) copy-start(f32[32,256,1]{1,0,2:T(8,128)} %constant.91) | copy-start | bytes 98308
  9.8 0.8 %copy-start.6 = (f32[32,256,1]{1,0,2:T(8,128)S(1)}, f32[32,256,1]{1,0,2:T(8,128)}, u32[]{:S(2)}) copy-start(f32[32,256,1]{1,0,2:T(8,128)} %constant.92) | copy-start | bytes 98308
  14.2 3.4 %copy-start.4 = (f32[4,2,32,32]{3,2,1,0:T(8,128)}, f32[4,2,32,32]{3,2,1,0:T(8,128)S(1)}, u32[]{:S(2)}) copy-start(f32[4,2,32,32]{3,2,1,0:T(8,128)S(1)} %select_add_fusion.1.ev_ref) | copy-start | bytes 98308
  14.2 3.4 %collective-permute-start.2 = (f32[4,2,32,32]{3,2,1,0:T(8,128)S(1)}, f32[4,2,32,32]{3,2,1,0:T(8,128)S(1)}, u32[]{:S(2)}, u32[]{:S(2)}) collective-permute-start(f32[4,2,32,32]{3,2,1,0:T(8,128)S(1)} %select_add_fusion.1.ev_ref), channel_id=1, source_target_pairs={{0,1},{1,0},{2,3},{3,2},{4,5},{5,4},{6,7},{7,6},{8,9},{9,8},{10,11... | collective-permute-start | bytes 98312 | tf_op jit(solution)/shard_map/master_spectra/ppermute | solution.py:298
  17.5 0.6 %copy-start.9 = (f32[4,2,32,32]{3,2,1,0:T(8,128)}, f32[4,2,32,32]{3,2,1,0:T(8,128)S(1)}, u32[]{:S(2)}) copy-start(f32[4,2,32,32]{3,2,1,0:T(8,128)S(1)} %collective-permute-done.2.ev2_ref) | copy-start | bytes 98308
  33.0 1.6 %copy-start.13 = (s32[2]{0:T(128)S(1)}, s32[2]{0:T(128)}, u32[]{:S(2)}) copy-start(s32[2]{0:T(128)} %im_ref.1) | copy-start | bytes 28
  33.0 4.5 %collective-permute-start.3 = (f32[1,4,32,32]{3,2,1,0:T(8,128)}, f32[1,4,32,32]{3,2,1,0:T(8,128)S(1)}, u32[]{:S(2)}, u32[]{:S(2)}) collective-permute-start(f32[1,4,32,32]{3,2,1,0:T(8,128)} %bitcast.74), channel_id=1, source_target_pairs={{0,2},{2,0},{1,3},{3,1},{4,6},{6,4},{5,7},{7,5},{8,10},{10,8},{9,1... | collective-permute-start | bytes 49160 | tf_op jit(solution)/shard_map/gradient_exchange/ppermute | solution.py:291
  38.4 1.3 %collective-permute-start.4 = (f32[1,4,32,32]{3,2,1,0:T(8,128)S(1)}, f32[1,4,32,32]{3,2,1,0:T(8,128)S(1)}, u32[]{:S(2)}, u32[]{:S(2)}) collective-permute-start(f32[1,4,32,32]{3,2,1,0:T(8,128)S(1)} %bitcast_add_fusion), channel_id=1, source_target_pairs={{0,1},{1,0},{2,3},{3,2},{4,5},{5,4},{6,7},{7,6},{8,9},{9,8},{10,11... | collective-permute-start | bytes 49160 | tf_op jit(solution)/shard_map/gradient_exchange/ppermute | solution.py:280
  40.6 5.2 %collective-permute-start.5 = (f32[1,2,32,32]{3,2,1,0:T(8,128)S(1)}, f32[1,2,32,32]{3,2,1,0:T(8,128)S(1)}, u32[]{:S(2)}, u32[]{:S(2)}) collective-permute-start(f32[1,2,32,32]{3,2,1,0:T(8,128)S(1)} %get-tuple-element.8), channel_id=1, source_target_pairs={{0,8},{4,12},{8,0},{12,4},{1,5},{5,1},{9,13},{13,9},{2,10},{6,14},... | collective-permute-start | bytes 24584 | tf_op jit(solution)/shard_map/gradient_exchange/ppermute | solution.py:357
  41.0 4.8 %collective-permute-start.6 = (f32[1,2,32,32]{3,2,1,0:T(8,128)S(1)}, f32[1,2,32,32]{3,2,1,0:T(8,128)S(1)}, u32[]{:S(2)}, u32[]{:S(2)}) collective-permute-start(f32[1,2,32,32]{3,2,1,0:T(8,128)S(1)} %get-tuple-element.9), channel_id=1, source_target_pairs={{1,13},{5,9},{9,5},{13,1},{3,15},{7,11},{11,7},{15,3},{17,29},{21,... | collective-permute-start | bytes 24584 | tf_op jit(solution)/shard_map/gradient_exchange/ppermute | solution.py:357
  45.8 2.8 %copy-start.10 = (f32[1,2,32,32]{3,2,1,0:T(8,128)}, f32[1,2,32,32]{3,2,1,0:T(8,128)S(1)}, u32[]{:S(2)}) copy-start(f32[1,2,32,32]{3,2,1,0:T(8,128)S(1)} %add_add_fusion.refs_0_) | copy-start | bytes 24580
  45.8 2.8 %collective-permute-start.7 = (f32[1,2,32,32]{3,2,1,0:T(8,128)S(1)}, f32[1,2,32,32]{3,2,1,0:T(8,128)S(1)}, u32[]{:S(2)}, u32[]{:S(2)}) collective-permute-start(f32[1,2,32,32]{3,2,1,0:T(8,128)S(1)} %add_add_fusion.refs_0_), channel_id=1, source_target_pairs={{0,1},{1,0},{2,3},{3,2},{4,5},{5,4},{6,7},{7,6},{8,9},{9,8},{10,11... | collective-permute-start | bytes 24584 | tf_op jit(solution)/shard_map/gradient_exchange/ppermute | solution.py:298
  48.6 0.6 %copy-start.11 = (f32[1,2,32,32]{3,2,1,0:T(8,128)}, f32[1,2,32,32]{3,2,1,0:T(8,128)S(1)}, u32[]{:S(2)}) copy-start(f32[1,2,32,32]{3,2,1,0:T(8,128)S(1)} %collective-permute-done.7.refs_1_) | copy-start | bytes 24580

commit v13 on v12

--- a/solution.py
+++ b/solution.py
@@ -415,8 +415,18 @@
 
     with jax.named_scope("gradient_exchange"):
         corner_count = lax.axis_size("corner")
-        comp = sum_all(comp, "corner", corner_count, lax.axis_index("corner"))
-        both = gather_all(comp, "kern", kern_count, kern_pos)
+        corner_pos = lax.axis_index("corner")
+        if corner_count == 2 and kern_count == 2 and per_dev == 1:
+            got = [
+                lax.ppermute(comp, ("corner", "kern"), [(i, i ^ step) for i in range(4)])
+                for step in (1, 2, 3)
+            ]
+            mine = comp + got[1]
+            other = got[0] + got[2]
+            both = jnp.where(kern_pos == 0, jnp.concatenate([mine, other]), jnp.concatenate([other, mine]))
+        else:
+            comp = sum_all(comp, "corner", corner_count, corner_pos)
+            both = gather_all(comp, "kern", kern_count, kern_pos)
         mine_tiles = both[:, 0:2]
         owner_pick = (
             inst_master[:, None] == jnp.arange(region_masters, dtype=jnp.int32)[None, :]

time: 52 us -> 51 us (0.981)
  waiting for transfers between devices: 5.5 us -> 3.78 us
  starting transfers between devices: 11.5 us -> 12.4 us
    ppermute x2 -> x3, waiting for transfers between devices: 4.11 us -> 2.4 us  [on_device(): lax.ppermute(comp, ('corner', 'kern'), [(i, i ^ step) for i in range(4)])]
    ppermute x2 -> x3, starting transfers between devices: 1.64 us -> 2.26 us  [on_device(): lax.ppermute(comp, ('corner', 'kern'), [(i, i ^ step) for i in range(4)])]
  transfers between devices with their start and end apart: 8 -> 9, of which waited for: 4 -> 4; matrix products, arithmetic and copies ran while one was open for 9% -> 11% of each run, Pallas kernels for 6% -> 6%
where the time goes in v13:
time: 51 us; the launch traced here: 50.6 us
  Pallas kernels  20 us (39%)
  starting transfers between devices  12.4 us (24%)
  local copies, waits for them, and re-layouts  4.85 us (10%)
  matrix products  4.4 us (9%)
  waiting for transfers between devices  3.78 us (7%)
  other arithmetic  2.81 us (6%)
  between operations  2.33 us (5%)
    pallas_call x1, Pallas kernels, imaging(): pl.pallas_call(imaging_body, out_shape=jax.ShapeDtypeStruct((4, B, B), jn...  14.8 us
    ppermute x2, starting transfers between devices, gather_split(): got = lax.ppermute(x, ('tile', 'kern'), pairs)  4.75 us
    ppermute x2, starting transfers between devices, sum_parts(): return (x, lax.ppermute(x, axis, [(0, 1), (1, 0)]))  4.25 us
    unnamed x28, local copies, waits for them, and re-layouts  3.86 us
    pallas_call x1, Pallas kernels, pixels(): pl.pallas_call(functools.partial(pixel_body, passes=True), out_shape=(sha...  2.89 us
    ppermute x3, waiting for transfers between devices, on_device(): lax.ppermute(comp, ('corner', 'kern'), [(i, i ^ step) for i in range(4)])  2.4 us
    pallas_call x1, Pallas kernels, pixels(): pl.pallas_call(functools.partial(pixel_body, passes=False), out_shape=sha...  2.31 us
    ppermute x3, starting transfers between devices, on_device(): lax.ppermute(comp, ('corner', 'kern'), [(i, i ^ step) for i in range(4)])  2.26 us
  transfers between devices with their start and end apart: 9, of which 4 were waited for; matrix products, arithmetic and copies ran while one was open for 11% of the time, Pallas kernels for 6%

profile of v13, /device:TPU:0, one launch (start us, length us, event | category | flops | bytes accessed | tf_op | source)
XLA Modules:
  0.0 50.6 jit_solution(8329245300880028989)
XLA Ops:
  0.7 0.8 %copy-done.2 = f32[32,256]{1,0:T(8,128)S(1)} copy-done((f32[32,256]{1,0:T(8,128)S(1)}, f32[32,256]{1,0:T(8,128)}, u32[]{:S(2)}) %copy-start.2) | copy-done | bytes 32792
  1.4 1.1 %fusion.8 = f32[32,256]{1,0:T(8,128)S(1)} fusion(f32[32,256]{1,0:T(8,128)S(1)} %copy-done.2, bf16[1,256,256]{2,1,0:T(8,128)(2,1)} %param.27), kind=kOutput, calls=%fused_computation.19 | convolution fusion | flops 25165824 | bytes 196608 | tf_op jit(solution)/shard_map/master_spectra/bx,nxy->nby/dot_general | solution.py:39
  2.6 0.2 fusion.6
  3.5 4.1 %collective-permute-start = (f32[1,2,32,32]{3,2,1,0:T(8,128)S(1)}, f32[1,2,32,32]{3,2,1,0:T(8,128)S(1)}, u32[]{:S(2)}, u32[]{:S(2)}) collective-permute-start(f32[1,2,32,32]{3,2,1,0:T(8,128)S(1)} %pad_maximum_fusion.1.own_ref), channel_id=1, source_target_pairs={{8,0},{12,4},{0,8},{4,12},{5,1},{1,5},{13,9},{9,13},{10,2},{14,6},... | collective-permute-start | bytes 24584 | tf_op jit(solution)/shard_map/master_spectra/ppermute | solution.py:338
  7.6 0.7 %collective-permute-start.1 = (f32[1,2,32,32]{3,2,1,0:T(8,128)S(1)}, f32[1,2,32,32]{3,2,1,0:T(8,128)S(1)}, u32[]{:S(2)}, u32[]{:S(2)}) collective-permute-start(f32[1,2,32,32]{3,2,1,0:T(8,128)S(1)} %pad_maximum_fusion.1.own_ref), channel_id=1, source_target_pairs={{13,1},{9,5},{5,9},{1,13},{15,3},{11,7},{7,11},{3,15},{29,17},{25,... | collective-permute-start | bytes 24584 | tf_op jit(solution)/shard_map/master_spectra/ppermute | solution.py:338
  8.3 0.6 %copy-done.12 = f32[1,12]{1,0:T(1,128)S(1)} copy-done((f32[1,12]{1,0:T(1,128)S(1)}, f32[1,12]{1,0:T(1,128)}, u32[]{:S(2)}) %copy-start.12) | copy-done | bytes 72
  9.1 0.7 %copy-done.7 = f32[32,256,1]{1,0,2:T(8,128)S(1)} copy-done((f32[32,256,1]{1,0,2:T(8,128)S(1)}, f32[32,256,1]{1,0,2:T(8,128)}, u32[]{:S(2)}) %copy-start.7) | copy-done | bytes 32792
  9.8 0.2 convolution_bitcast_fusion.1
  10.0 0.5 %copy-done.6 = f32[32,256,1]{1,0,2:T(8,128)S(1)} copy-done((f32[32,256,1]{1,0,2:T(8,128)S(1)}, f32[32,256,1]{1,0,2:T(8,128)}, u32[]{:S(2)}) %copy-start.6) | copy-done | bytes 32792
  10.6 0.2 convolution_bitcast_fusion
  10.8 0.2 fusion.14
  11.6 0.8 %convolution_add_fusion.ti_ref = f32[2,32,32]{2,1,0:T(8,128)} fusion(f32[2,32,32]{2,1,0:T(8,128)S(1)} %fusion.14, f32[2,32,256]{2,1,0:T(8,128)S(1)} %convolution_bitcast_fusion, f32[32,256,1]{1,0,2:T(8,128)S(1)} %copy-done.7), kind=kOutput, calls=%fused_computation.2 | convolution fusion | flops 6293504 | bytes 114688 | tf_op jit(solution)/shard_map/tile_spectra/nby,cy->nbc/dot_general | solution.py:44
  12.4 0.8 %convolution_subtract_fusion.tr_ref = f32[2,32,32]{2,1,0:T(8,128)} fusion(f32[2,32,32]{2,1,0:T(8,128)S(1)} %fusion.13, f32[2,32,256]{2,1,0:T(8,128)S(1)} %convolution_bitcast_fusion, f32[32,256,1]{1,0,2:T(8,128)S(1)} %copy-done.6), kind=kOutput, calls=%fused_computation.3 | convolution fusion | flops 6293504 | bytes 114688 | tf_op jit(solution)/shard_map/tile_spectra/nby,cy->nbc/dot_general | solution.py:41
  13.2 0.9 %pad_maximum_fusion = f32[12,32,128]{2,1,0:T(8,128)} fusion(f32[12,32,32]{2,1,0:T(8,128)S(1)} %copy.39, f32[12,32,32]{2,1,0:T(8,128)S(1)} %copy.38, f32[12,32,32]{2,1,0:T(8,128)S(1)} %copy.36), kind=kLoop, calls=%fused_computation.15 | loop fusion | flops 147456 | bytes 344064 | tf_op jit(solution)/shard_map/imaging_kernel/concatenate | solution.py:404
  14.2 2.0 %collective-permute-start.2 = (f32[4,2,32,32]{3,2,1,0:T(8,128)S(1)}, f32[4,2,32,32]{3,2,1,0:T(8,128)S(1)}, u32[]{:S(2)}, u32[]{:S(2)}) collective-permute-start(f32[4,2,32,32]{3,2,1,0:T(8,128)S(1)} %select_add_fusion.ev_ref), channel_id=1, source_target_pairs={{0,1},{1,0},{2,3},{3,2},{4,5},{5,4},{6,7},{7,6},{8,9},{9,8},{10,11... | collective-permute-start | bytes 98312 | tf_op jit(solution)/shard_map/master_spectra/ppermute | solution.py:298
  16.2 0.6 %pad_add_fusion.pos_ref = s32[2]{0:T(128)} fusion(s32[1]{0:T(128)} %bitcast.1, s32[1]{0:T(128)} %bitcast), kind=kLoop, calls=%fused_computation.27 | loop fusion | flops 2 | bytes 16 | tf_op jit(solution)/shard_map/imaging_kernel/stack | solution.py:407
  17.5 0.6 %copy-done.9 = f32[4,2,32,32]{3,2,1,0:T(8,128)} copy-done((f32[4,2,32,32]{3,2,1,0:T(8,128)}, f32[4,2,32,32]{3,2,1,0:T(8,128)S(1)}, u32[]{:S(2)}) %copy-start.9) | copy-done | bytes 32792
  18.1 14.8 %imaging_kernel.1 = f32[4,32,32]{2,1,0:T(8,128)} custom-call(s32[2]{0:T(128)} %pad_add_fusion.pos_ref, s32[2]{0:T(128)} %im_ref.1, s32[2,2]{1,0:T(2,128)} %sh_ref.1, f32[12]{0:T(128)} %bitcast.77, f32[1]{0:T(128)S(6)} %copy.41.dose_ref, f32[2,32,32]{2,1,0:T(8,128)} %convolution_subtract_fusion.tr_ref, f32[2,32,32]{2,1,0:T(8,128)} %convolution_add_fusion.ti_ref, ...), custom_call_target="tpu_custom_call" | custom-call | tf_op jit(solution)/shard_map/imaging_kernel/pallas_call | solution.py:206
  33.0 1.5 %collective-permute-start.3 = (f32[1,4,32,32]{3,2,1,0:T(8,128)}, f32[1,4,32,32]{3,2,1,0:T(8,128)S(1)}, u32[]{:S(2)}, u32[]{:S(2)}) collective-permute-start(f32[1,4,32,32]{3,2,1,0:T(8,128)} %bitcast.72), channel_id=1, source_target_pairs={{0,2},{1,3},{2,0},{3,1},{4,6},{5,7},{6,4},{7,5},{8,10},{9,11},{10,... | collective-permute-start | bytes 49160 | tf_op jit(solution)/shard_map/gradient_exchange/ppermute | solution.py:421
  34.6 0.7 %collective-permute-start.5 = (f32[1,4,32,32]{3,2,1,0:T(8,128)}, f32[1,4,32,32]{3,2,1,0:T(8,128)S(1)}, u32[]{:S(2)}, u32[]{:S(2)}) collective-permute-start(f32[1,4,32,32]{3,2,1,0:T(8,128)} %bitcast.74), channel_id=1, source_target_pairs={{0,3},{1,2},{2,1},{3,0},{4,7},{5,6},{6,5},{7,4},{8,11},{9,10},{10,... | collective-permute-start | bytes 49160 | tf_op jit(solution)/shard_map/gradient_exchange/ppermute | solution.py:421
  35.3 2.2 %collective-permute-done.3 = f32[1,4,32,32]{3,2,1,0:T(8,128)S(1)} collective-permute-done((f32[1,4,32,32]{3,2,1,0:T(8,128)}, f32[1,4,32,32]{3,2,1,0:T(8,128)S(1)}, u32[]{:S(2)}, u32[]{:S(2)}) %collective-permute-start.3) | collective-permute-done | bytes 16416 | tf_op jit(solution)/shard_map/gradient_exchange/ppermute | solution.py:421
  37.5 0.8 %bitcast_add_fusion = f32[1,4,32,32]{3,2,1,0:T(8,128)S(1)} fusion(f32[1,4,32,32]{3,2,1,0:T(8,128)S(1)} %collective-permute-done.3, f32[4,32,32]{2,1,0:T(8,128)} %imaging_kernel.1), kind=kLoop, calls=%fused_computation.31 | loop fusion | flops 4096 | bytes 49152 | tf_op jit(solution)/shard_map/gradient_exchange/add | solution.py:424
  38.4 0.2 collective-permute-done.5
  38.6 0.6 %fusion.12 = (f32[2,2,32,32]{3,2,1,0:T(8,128)S(1)}, f32[2,2,32,32]{3,2,1,0:T(8,128)}) fusion(f32[2,4,32,32]{3,2,1,0:T(8,128)S(1)} %maximum_select_fusion), kind=kLoop, calls=%fused_computation.33 | loop fusion | bytes 65536 | tf_op jit(solution)/shard_map/gradient_exchange/slice | solution.py:434
  39.4 0.5 collective-permute-start.6
  39.8 0.7 %collective-permute-start.7 = (f32[1,2,32,32]{3,2,1,0:T(8,128)S(1)}, f32[1,2,32,32]{3,2,1,0:T(8,128)S(1)}, u32[]{:S(2)}, u32[]{:S(2)}) collective-permute-start(f32[1,2,32,32]{3,2,1,0:T(8,128)S(1)} %get-tuple-element.9), channel_id=1, source_target_pairs={{1,13},{5,9},{9,5},{13,1},{3,15},{7,11},{11,7},{15,3},{17,29},{21,... | collective-permute-start | bytes 24584 | tf_op jit(solution)/shard_map/gradient_exchange/ppermute | solution.py:357
  40.5 2.9 %gradient_exchange.1 = (f32[2,256,256]{2,1,0:T(8,128)}, f32[1,1,1,1]{3,2,1,0:T(1,128)}) custom-call(f32[2,2,32,32]{3,2,1,0:T(8,128)} %get-tuple-element.11.refs_0_, f32[32,256]{1,0:T(8,128)} %constant.61.clone.c_re_ref.refs_1_.refs_2_, f32[32,256]{1,0:T(8,128)} %constant.62.clone.c_im_ref.refs_2_.refs_3_, bf16[256,384]{1,0:T(8,128)(2,1)} %constant.71.clone.refs_3_.refs_4_), custom_call_target="tpu_custom_call" | custom-call | tf_op jit(solution)/shard_map/gradient_exchange/pallas_call | solution.py:261
  44.1 0.5 %collective-permute-done.6 = f32[1,2,32,32]{3,2,1,0:T(8,128)S(1)} collective-permute-done((f32[1,2,32,32]{3,2,1,0:T(8,128)S(1)}, f32[1,2,32,32]{3,2,1,0:T(8,128)S(1)}, u32[]{:S(2)}, u32[]{:S(2)}) %collective-permute-start.6) | collective-permute-done | bytes 8224 | tf_op jit(solution)/shard_map/gradient_exchange/ppermute | solution.py:357
  44.6 2.2 %collective-permute-start.8 = (f32[1,2,32,32]{3,2,1,0:T(8,128)S(1)}, f32[1,2,32,32]{3,2,1,0:T(8,128)S(1)}, u32[]{:S(2)}, u32[]{:S(2)}) collective-permute-start(f32[1,2,32,32]{3,2,1,0:T(8,128)S(1)} %add_add_fusion.refs_0_), channel_id=1, source_target_pairs={{0,1},{1,0},{2,3},{3,2},{4,5},{5,4},{6,7},{7,6},{8,9},{9,8},{10,11... | collective-permute-start | bytes 24584 | tf_op jit(solution)/shard_map/gradient_exchange/ppermute | solution.py:298
  46.8 0.9 %collective-permute-done.8.refs_1_ = f32[1,2,32,32]{3,2,1,0:T(8,128)S(1)} collective-permute-done((f32[1,2,32,32]{3,2,1,0:T(8,128)S(1)}, f32[1,2,32,32]{3,2,1,0:T(8,128)S(1)}, u32[]{:S(2)}, u32[]{:S(2)}) %collective-permute-start.8) | collective-permute-done | bytes 8224 | tf_op jit(solution)/shard_map/gradient_exchange/ppermute | solution.py:298
  47.7 0.6 %copy-done.11 = f32[1,2,32,32]{3,2,1,0:T(8,128)} copy-done((f32[1,2,32,32]{3,2,1,0:T(8,128)}, f32[1,2,32,32]{3,2,1,0:T(8,128)S(1)}, u32[]{:S(2)}) %copy-start.11) | copy-done | bytes 8216
  48.3 2.3 %pixel_gradients.1 = f32[1,256,256]{2,1,0:T(8,128)} custom-call(f32[1,2,32,32]{3,2,1,0:T(8,128)} %copy-done.10, f32[1,2,32,32]{3,2,1,0:T(8,128)} %copy-done.11, f32[32,256]{1,0:T(8,128)} %constant.61.clone.c_re_ref.refs_1_.refs_2_, f32[32,256]{1,0:T(8,128)} %constant.62.clone.c_im_ref.refs_2_.refs_3_, bf16[256,384]{1,0:T(8,128)(2,1)} %constant.71.clone.refs_3_.refs_4_), custom_call_target="tpu_custom_call" | custom-call | tf_op jit(solution)/shard_map/pixel_gradients/pallas_call | solution.py:255
  (48 shorter events, 1.7 us)
Async XLA Ops:
  0.6 8.5 %copy-start = (bf16[2,256,256]{2,1,0:T(8,128)(2,1)S(1)}, bf16[2,256,256]{2,1,0:T(8,128)(2,1)}, u32[]{:S(2)}) copy-start(bf16[2,256,256]{2,1,0:T(8,128)(2,1)} %param.26) | copy-start | bytes 786436
  0.6 0.8 %copy-start.2 = (f32[32,256]{1,0:T(8,128)S(1)}, f32[32,256]{1,0:T(8,128)}, u32[]{:S(2)}) copy-start(f32[32,256]{1,0:T(8,128)} %constant.61.clone.c_re_ref.refs_1_.refs_2_) | copy-start | bytes 98308
  0.7 1.9 %copy-start.3 = (f32[32,256]{1,0:T(8,128)S(1)}, f32[32,256]{1,0:T(8,128)}, u32[]{:S(2)}) copy-start(f32[32,256]{1,0:T(8,128)} %constant.62.clone.c_im_ref.refs_2_.refs_3_) | copy-start | bytes 98308
  0.7 1.9 %copy-start.5 = (bf16[1,256,256]{2,1,0:T(8,128)(2,1)S(1)}, bf16[1,256,256]{2,1,0:T(8,128)(2,1)}, u32[]{:S(2)}) copy-start(bf16[1,256,256]{2,1,0:T(8,128)(2,1)} %param.27) | copy-start | bytes 393220
  0.7 8.2 %copy-start.1 = (f32[1,12,2,32,32]{4,3,2,1,0:T(8,128)S(1)}, f32[1,12,2,32,32]{4,3,2,1,0:T(8,128)}, u32[]{:S(2)}) copy-start(f32[1,12,2,32,32]{4,3,2,1,0:T(8,128)} %param.31) | copy-start | bytes 294916
  3.5 5.6 %copy-start.8 = (f32[1,2,32,32]{3,2,1,0:T(8,128)}, f32[1,2,32,32]{3,2,1,0:T(8,128)S(1)}, u32[]{:S(2)}) copy-start(f32[1,2,32,32]{3,2,1,0:T(8,128)S(1)} %pad_maximum_fusion.1.own_ref) | copy-start | bytes 24580
  3.5 10.6 %collective-permute-start = (f32[1,2,32,32]{3,2,1,0:T(8,128)S(1)}, f32[1,2,32,32]{3,2,1,0:T(8,128)S(1)}, u32[]{:S(2)}, u32[]{:S(2)}) collective-permute-start(f32[1,2,32,32]{3,2,1,0:T(8,128)S(1)} %pad_maximum_fusion.1.own_ref), channel_id=1, source_target_pairs={{8,0},{12,4},{0,8},{4,12},{5,1},{1,5},{13,9},{9,13},{10,2},{14,6},... | collective-permute-start | bytes 24584 | tf_op jit(solution)/shard_map/master_spectra/ppermute | solution.py:338
  7.6 6.5 %collective-permute-start.1 = (f32[1,2,32,32]{3,2,1,0:T(8,128)S(1)}, f32[1,2,32,32]{3,2,1,0:T(8,128)S(1)}, u32[]{:S(2)}, u32[]{:S(2)}) collective-permute-start(f32[1,2,32,32]{3,2,1,0:T(8,128)S(1)} %pad_maximum_fusion.1.own_ref), channel_id=1, source_target_pairs={{13,1},{9,5},{5,9},{1,13},{15,3},{11,7},{7,11},{3,15},{29,17},{25,... | collective-permute-start | bytes 24584 | tf_op jit(solution)/shard_map/master_spectra/ppermute | solution.py:338
  8.3 0.7 %copy-start.12 = (f32[1,12]{1,0:T(1,128)S(1)}, f32[1,12]{1,0:T(1,128)}, u32[]{:S(2)}) copy-start(f32[1,12]{1,0:T(1,128)} %param.32) | copy-start | bytes 148
  9.0 0.8 %copy-start.7 = (f32[32,256,1]{1,0,2:T(8,128)S(1)}, f32[32,256,1]{1,0,2:T(8,128)}, u32[]{:S(2)}) copy-start(f32[32,256,1]{1,0,2:T(8,128)} %constant.80) | copy-start | bytes 98308
  9.8 0.8 %copy-start.6 = (f32[32,256,1]{1,0,2:T(8,128)S(1)}, f32[32,256,1]{1,0,2:T(8,128)}, u32[]{:S(2)}) copy-start(f32[32,256,1]{1,0,2:T(8,128)} %constant.81) | copy-start | bytes 98308
  14.2 3.3 %copy-start.4 = (f32[4,2,32,32]{3,2,1,0:T(8,128)}, f32[4,2,32,32]{3,2,1,0:T(8,128)S(1)}, u32[]{:S(2)}) copy-start(f32[4,2,32,32]{3,2,1,0:T(8,128)S(1)} %select_add_fusion.ev_ref) | copy-start | bytes 98308
  14.2 3.3 %collective-permute-start.2 = (f32[4,2,32,32]{3,2,1,0:T(8,128)S(1)}, f32[4,2,32,32]{3,2,1,0:T(8,128)S(1)}, u32[]{:S(2)}, u32[]{:S(2)}) collective-permute-start(f32[4,2,32,32]{3,2,1,0:T(8,128)S(1)} %select_add_fusion.ev_ref), channel_id=1, source_target_pairs={{0,1},{1,0},{2,3},{3,2},{4,5},{5,4},{6,7},{7,6},{8,9},{9,8},{10,11... | collective-permute-start | bytes 98312 | tf_op jit(solution)/shard_map/master_spectra/ppermute | solution.py:298
  17.5 0.6 %copy-start.9 = (f32[4,2,32,32]{3,2,1,0:T(8,128)}, f32[4,2,32,32]{3,2,1,0:T(8,128)S(1)}, u32[]{:S(2)}) copy-start(f32[4,2,32,32]{3,2,1,0:T(8,128)S(1)} %collective-permute-done.2.ev2_ref) | copy-start | bytes 98308
  33.0 1.6 %copy-start.13 = (s32[2]{0:T(128)S(1)}, s32[2]{0:T(128)}, u32[]{:S(2)}) copy-start(s32[2]{0:T(128)} %im_ref.1) | copy-start | bytes 28
  33.0 4.5 %collective-permute-start.3 = (f32[1,4,32,32]{3,2,1,0:T(8,128)}, f32[1,4,32,32]{3,2,1,0:T(8,128)S(1)}, u32[]{:S(2)}, u32[]{:S(2)}) collective-permute-start(f32[1,4,32,32]{3,2,1,0:T(8,128)} %bitcast.72), channel_id=1, source_target_pairs={{0,2},{1,3},{2,0},{3,1},{4,6},{5,7},{6,4},{7,5},{8,10},{9,11},{10,... | collective-permute-start | bytes 49160 | tf_op jit(solution)/shard_map/gradient_exchange/ppermute | solution.py:421
  34.6 3.8 %collective-permute-start.4 = (f32[1,4,32,32]{3,2,1,0:T(8,128)}, f32[1,4,32,32]{3,2,1,0:T(8,128)S(1)}, u32[]{:S(2)}, u32[]{:S(2)}) collective-permute-start(f32[1,4,32,32]{3,2,1,0:T(8,128)} %bitcast.73), channel_id=1, source_target_pairs={{0,1},{1,0},{2,3},{3,2},{4,5},{5,4},{6,7},{7,6},{8,9},{9,8},{10,11... | collective-permute-start | bytes 49160 | tf_op jit(solution)/shard_map/gradient_exchange/ppermute | solution.py:421
  34.6 4.0 %collective-permute-start.5 = (f32[1,4,32,32]{3,2,1,0:T(8,128)}, f32[1,4,32,32]{3,2,1,0:T(8,128)S(1)}, u32[]{:S(2)}, u32[]{:S(2)}) collective-permute-start(f32[1,4,32,32]{3,2,1,0:T(8,128)} %bitcast.74), channel_id=1, source_target_pairs={{0,3},{1,2},{2,1},{3,0},{4,7},{5,6},{6,5},{7,4},{8,11},{9,10},{10,... | collective-permute-start | bytes 49160 | tf_op jit(solution)/shard_map/gradient_exchange/ppermute | solution.py:421
  39.4 5.2 %collective-permute-start.6 = (f32[1,2,32,32]{3,2,1,0:T(8,128)S(1)}, f32[1,2,32,32]{3,2,1,0:T(8,128)S(1)}, u32[]{:S(2)}, u32[]{:S(2)}) collective-permute-start(f32[1,2,32,32]{3,2,1,0:T(8,128)S(1)} %get-tuple-element.8), channel_id=1, source_target_pairs={{0,8},{4,12},{8,0},{12,4},{1,5},{5,1},{9,13},{13,9},{2,10},{6,14},... | collective-permute-start | bytes 24584 | tf_op jit(solution)/shard_map/gradient_exchange/ppermute | solution.py:357
  39.8 4.8 %collective-permute-start.7 = (f32[1,2,32,32]{3,2,1,0:T(8,128)S(1)}, f32[1,2,32,32]{3,2,1,0:T(8,128)S(1)}, u32[]{:S(2)}, u32[]{:S(2)}) collective-permute-start(f32[1,2,32,32]{3,2,1,0:T(8,128)S(1)} %get-tuple-element.9), channel_id=1, source_target_pairs={{1,13},{5,9},{9,5},{13,1},{3,15},{7,11},{11,7},{15,3},{17,29},{21,... | collective-permute-start | bytes 24584 | tf_op jit(solution)/shard_map/gradient_exchange/ppermute | solution.py:357
  44.6 3.1 %copy-start.10 = (f32[1,2,32,32]{3,2,1,0:T(8,128)}, f32[1,2,32,32]{3,2,1,0:T(8,128)S(1)}, u32[]{:S(2)}) copy-start(f32[1,2,32,32]{3,2,1,0:T(8,128)S(1)} %add_add_fusion.refs_0_) | copy-start | bytes 24580
  44.6 3.1 %collective-permute-start.8 = (f32[1,2,32,32]{3,2,1,0:T(8,128)S(1)}, f32[1,2,32,32]{3,2,1,0:T(8,128)S(1)}, u32[]{:S(2)}, u32[]{:S(2)}) collective-permute-start(f32[1,2,32,32]{3,2,1,0:T(8,128)S(1)} %add_add_fusion.refs_0_), channel_id=1, source_target_pairs={{0,1},{1,0},{2,3},{3,2},{4,5},{5,4},{6,7},{7,6},{8,9},{9,8},{10,11... | collective-permute-start | bytes 24584 | tf_op jit(solution)/shard_map/gradient_exchange/ppermute | solution.py:298
  47.7 0.6 %copy-start.11 = (f32[1,2,32,32]{3,2,1,0:T(8,128)}, f32[1,2,32,32]{3,2,1,0:T(8,128)S(1)}, u32[]{:S(2)}) copy-start(f32[1,2,32,32]{3,2,1,0:T(8,128)S(1)} %collective-permute-done.8.refs_1_) | copy-start | bytes 24580

commit v14 on v13

--- a/solution.py
+++ b/solution.py
@@ -116,14 +116,19 @@
     b_hi, b_mid, b_lo = table_three(right_b)
     right_hm = np.concatenate([b_hi, b_mid], axis=1)
     right_lh = np.concatenate([b_lo, b_hi], axis=0)
+    parts_re = table_three(c_re)
+    parts_im = table_three(c_im)
+    rows_three = np.concatenate(
+        [np.concatenate(parts_re, axis=1), np.concatenate(parts_im, axis=1)], axis=0
+    )
     plain = (c_re, c_im, c_re.T, c_im.T, right_w[:B], right_w[B : 2 * B], right_c)
     out = [jnp.asarray(table, jnp.float32) for table in plain]
-    return out + [jnp.asarray(table) for table in (left_three, right_hm, right_lh)]
+    return out + [jnp.asarray(table) for table in (left_three, right_hm, right_lh, rows_three)]
 
 
 def imaging_body(
-    pos_ref, im_ref, sh_ref, w_ref, dose_ref, tr_ref, ti_ref, ev_ref, ev2_ref, own_ref, goal_ref, h_ref, hc_ref,
-    c_re_ref, c_im_ref, ct_re_ref, ct_im_ref, rw_top, rw_bot, rc_ref, la_ref, rhm_ref, rlh_ref,
+    pos_ref, im_ref, sh_ref, w_ref, dose_ref, mask_ref, ev_ref, ev2_ref, own_ref, goal_ref, h_ref, hc_ref,
+    c_re_ref, c_im_ref, ct_re_ref, ct_im_ref, rw_top, rw_bot, rc_ref, la_ref, rhm_ref, rlh_ref, rows_ref,
     slots_ref, f_buf, i_buf, u_buf, w_buf, xr_buf, xi_buf,
 ):
     count = f_buf.shape[0]
@@ -141,8 +146,12 @@
     is_own = master // local_masters == pos_ref[1]
     m_re = ev_ref[master, 0] + ev2_ref[master, 0] + jnp.where(is_own, own_ref[master % local_masters, 0], 0.0)
     m_im = ev_ref[master, 1] + ev2_ref[master, 1] + jnp.where(is_own, own_ref[master % local_masters, 1], 0.0)
-    s_re = tr_ref[pos] + (ph_re * m_re - ph_im * m_im)
-    s_im = ti_ref[pos] + (ph_re * m_im + ph_im * m_re)
+    mask = mask_ref[pos]
+    rows = dot_parts(rows_ref[...], jnp.concatenate([mask, mask, mask], axis=0))
+    t_one = dot_full(rows, ct_re_ref[...])
+    t_two = dot_full(rows, ct_im_ref[...])
+    s_re = t_one[:B] - t_two[B:] + (ph_re * m_re - ph_im * m_im)
+    s_im = t_two[:B] + t_one[B:] + (ph_re * m_im + ph_im * m_re)
     i_buf[...] = jnp.zeros(i_buf.shape, jnp.float32)
 
     def spectrum(k, carry):
@@ -196,7 +205,7 @@
     slots_ref[3] = ph_re * g_im - ph_im * g_re
 
 
-def imaging(pos, inst_master, inst_shift, weights, dose, tile_spec, every, own, target, kerns, h_cat):
+def imaging(pos, inst_master, inst_shift, weights, dose, tile_mask, every, own, target, kerns, h_cat):
     if len(every) == 1:
         every = (every[0], jnp.zeros_like(every[0]))
     count = weights.shape[0]
@@ -206,7 +215,7 @@
     return pl.pallas_call(
         imaging_body,
         out_shape=jax.ShapeDtypeStruct((4, B, B), jnp.float32),
-        in_specs=[smem] * 5 + [vmem] * 8 + [vmem] * len(tables),
+        in_specs=[smem] * 5 + [vmem] * 7 + [vmem] * len(tables),
         out_specs=vmem,
         scratch_shapes=[
             pltpu.VMEM((count, P_SIZE, 2 * P_SIZE), jnp.float32),
@@ -216,7 +225,7 @@
             pltpu.VMEM((count * B, B), jnp.float32),
             pltpu.VMEM((count * B, B), jnp.float32),
         ],
-    )(pos, inst_master, inst_shift, weights, dose, *tile_spec, *every, own, target, kerns, h_cat, *tables)
+    )(pos, inst_master, inst_shift, weights, dose, tile_mask, *every, own, target, kerns, h_cat, *tables)
 
 
 def pixel_body(*refs, passes):
@@ -386,10 +395,6 @@
             every = (gather_all(own, "tile", tile_count, tile_pos),)
             own_part = jnp.zeros_like(own)
 
-    with jax.named_scope("tile_spectra"):
-        tile_re, tile_im = spectra(tile_mask.astype(jnp.float32), cos_tab, sin_tab)
-        tile_spec = (tile_re, tile_im)
-
     dose = corner_dose[0]
     kerns = kernels[0]
     h_re = kerns[:, 0]
@@ -407,7 +412,7 @@
             pos = jnp.stack([first + j, tile_pos]).astype(jnp.int32)
             parts.append(
                 imaging(
-                    pos, inst_master, inst_shift, weights, corner_dose, tile_spec, every, own_part, target,
+                    pos, inst_master, inst_shift, weights, corner_dose, tile_mask, every, own_part, target,
                     kerns, h_cat,
                 )
             )

time: 51 us -> 47.9 us (0.939)
  matrix products: 4.4 us -> 1.03 us
  starting transfers between devices: 12.4 us -> 13.8 us
  local copies, waits for them, and re-layouts: 4.85 us -> 3.8 us
    dot_general x2 -> x1, matrix products: 1.33 us -> 0.19 us  [spectra(): rows_re = jnp.einsum('bx,nxy->nby', cos_tab, masks, precision=precise)]
    ppermute x2, starting transfers between devices: 4.25 us -> 5.32 us  [sum_parts(): return (x, lax.ppermute(x, axis, [(0, 1), (1, 0)]))]
    unnamed x28 -> x22, local copies, waits for them, and re-layouts: 3.86 us -> 2.81 us
    dot_general x2 -> x1, matrix products: 0.97 us -> 0.16 us  [spectra(): jnp.einsum('nby,cy->nbc', rows_im, cos_tab, precision=precise)]
    dot_general x2 -> x1, matrix products: 0.96 us -> 0.16 us  [spectra(): jnp.einsum('nby,cy->nbc', rows_im, sin_tab, precision=precise)]
  transfers between devices with their start and end apart: 9 -> 9, of which waited for: 4 -> 4; matrix products, arithmetic and copies ran while one was open for 11% -> 6% of each run, Pallas kernels for 6% -> 6%
where the time goes in v14:
time: 47.9 us; the launch traced here: 47.6 us
  Pallas kernels  20.5 us (43%)
  starting transfers between devices  13.8 us (29%)
  local copies, waits for them, and re-layouts  3.8 us (8%)
  waiting for transfers between devices  3.43 us (7%)
  other arithmetic  2.87 us (6%)
  between operations  2.23 us (5%)
  matrix products  1.03 us (2%)
    pallas_call x1, Pallas kernels, imaging(): pl.pallas_call(imaging_body, out_shape=jax.ShapeDtypeStruct((4, B, B), jn...  15.3 us
    ppermute x2, starting transfers between devices, sum_parts(): return (x, lax.ppermute(x, axis, [(0, 1), (1, 0)]))  5.32 us
    ppermute x2, starting transfers between devices, gather_split(): got = lax.ppermute(x, ('tile', 'kern'), pairs)  4.75 us
    pallas_call x1, Pallas kernels, pixels(): pl.pallas_call(functools.partial(pixel_body, passes=True), out_shape=(sha...  2.89 us
    unnamed x22, local copies, waits for them, and re-layouts  2.81 us
    ppermute x3, waiting for transfers between devices, on_device(): lax.ppermute(comp, ('corner', 'kern'), [(i, i ^ step) for i in range(4)])  2.42 us
    pallas_call x1, Pallas kernels, pixels(): pl.pallas_call(functools.partial(pixel_body, passes=False), out_shape=sha...  2.31 us
    ppermute x3, starting transfers between devices, on_device(): lax.ppermute(comp, ('corner', 'kern'), [(i, i ^ step) for i in range(4)])  2.25 us
  transfers between devices with their start and end apart: 9, of which 4 were waited for; matrix products, arithmetic and copies ran while one was open for 6% of the time, Pallas kernels for 6%

profile of v14, /device:TPU:0, one launch (start us, length us, event | category | flops | bytes accessed | tf_op | source)
XLA Modules:
  0.0 47.6 jit_solution(15955145300148627877)
XLA Ops:
  0.7 0.9 %copy-done = bf16[1,256,256]{2,1,0:T(8,128)(2,1)S(1)} copy-done((bf16[1,256,256]{2,1,0:T(8,128)(2,1)S(1)}, bf16[1,256,256]{2,1,0:T(8,128)(2,1)}, u32[]{:S(2)}) %copy-start) | copy-done | bytes 131096
  1.5 0.2 fusion.8
  1.8 0.2 fusion.6
  2.0 0.2 fusion.14
  2.1 0.2 fusion.13
  2.3 0.2 fusion
  2.5 0.2 fusion.1
  2.7 4.1 %collective-permute-start = (f32[1,2,32,32]{3,2,1,0:T(8,128)S(1)}, f32[1,2,32,32]{3,2,1,0:T(8,128)S(1)}, u32[]{:S(2)}, u32[]{:S(2)}) collective-permute-start(f32[1,2,32,32]{3,2,1,0:T(8,128)S(1)} %pad_maximum_fusion.1.own_ref), channel_id=1, source_target_pairs={{8,0},{12,4},{0,8},{4,12},{5,1},{1,5},{13,9},{9,13},{10,2},{14,6},... | collective-permute-start | bytes 24584 | tf_op jit(solution)/shard_map/master_spectra/ppermute | solution.py:347
  6.8 0.7 %collective-permute-start.1 = (f32[1,2,32,32]{3,2,1,0:T(8,128)S(1)}, f32[1,2,32,32]{3,2,1,0:T(8,128)S(1)}, u32[]{:S(2)}, u32[]{:S(2)}) collective-permute-start(f32[1,2,32,32]{3,2,1,0:T(8,128)S(1)} %pad_maximum_fusion.1.own_ref), channel_id=1, source_target_pairs={{13,1},{9,5},{5,9},{1,13},{15,3},{11,7},{7,11},{3,15},{29,17},{25,... | collective-permute-start | bytes 24584 | tf_op jit(solution)/shard_map/master_spectra/ppermute | solution.py:347
  7.5 0.6 %copy-done.9 = f32[1,12]{1,0:T(1,128)S(1)} copy-done((f32[1,12]{1,0:T(1,128)S(1)}, f32[1,12]{1,0:T(1,128)}, u32[]{:S(2)}) %copy-start.9) | copy-done | bytes 72
  8.3 0.1 copy.39
  8.4 0.1 copy.40
  8.5 0.1 copy.37
  8.7 0.9 %pad_maximum_fusion = f32[12,32,128]{2,1,0:T(8,128)} fusion(f32[12,32,32]{2,1,0:T(8,128)S(1)} %copy.40, f32[12,32,32]{2,1,0:T(8,128)S(1)} %copy.39, f32[12,32,32]{2,1,0:T(8,128)S(1)} %copy.37), kind=kLoop, calls=%fused_computation.11 | loop fusion | flops 147456 | bytes 344064 | tf_op jit(solution)/shard_map/imaging_kernel/concatenate | solution.py:409
  9.7 2.2 %collective-permute-start.2 = (f32[4,2,32,32]{3,2,1,0:T(8,128)S(1)}, f32[4,2,32,32]{3,2,1,0:T(8,128)S(1)}, u32[]{:S(2)}, u32[]{:S(2)}) collective-permute-start(f32[4,2,32,32]{3,2,1,0:T(8,128)S(1)} %select_add_fusion.ev_ref), channel_id=1, source_target_pairs={{0,1},{1,0},{2,3},{3,2},{4,5},{5,4},{6,7},{7,6},{8,9},{9,8},{10,11... | collective-permute-start | bytes 98312 | tf_op jit(solution)/shard_map/master_spectra/ppermute | solution.py:307
  11.9 0.7 %pad_add_fusion.pos_ref = s32[2]{0:T(128)} fusion(s32[1]{0:T(128)} %bitcast.1, s32[1]{0:T(128)} %bitcast), kind=kLoop, calls=%fused_computation.23 | loop fusion | flops 2 | bytes 16 | tf_op jit(solution)/shard_map/imaging_kernel/stack | solution.py:412
  13.2 0.6 %copy-done.6 = f32[4,2,32,32]{3,2,1,0:T(8,128)} copy-done((f32[4,2,32,32]{3,2,1,0:T(8,128)}, f32[4,2,32,32]{3,2,1,0:T(8,128)S(1)}, u32[]{:S(2)}) %copy-start.6) | copy-done | bytes 32792
  13.9 15.3 %imaging_kernel.1 = f32[4,32,32]{2,1,0:T(8,128)} custom-call(s32[2]{0:T(128)} %pad_add_fusion.pos_ref, s32[2]{0:T(128)} %im_ref.1, s32[2,2]{1,0:T(2,128)} %sh_ref.1, f32[12]{0:T(128)} %bitcast.59, f32[1]{0:T(128)S(6)} %copy.42.dose_ref, bf16[2,256,256]{2,1,0:T(8,128)(2,1)} %mask_ref.1, f32[4,2,32,32]{3,2,1,0:T(8,128)} %copy-done.4, ...), custom_call_target="tpu_custom_call" | custom-call | tf_op jit(solution)/shard_map/imaging_kernel/pallas_call | solution.py:215
  29.1 1.6 %collective-permute-start.3 = (f32[1,4,32,32]{3,2,1,0:T(8,128)}, f32[1,4,32,32]{3,2,1,0:T(8,128)S(1)}, u32[]{:S(2)}, u32[]{:S(2)}) collective-permute-start(f32[1,4,32,32]{3,2,1,0:T(8,128)} %bitcast.54), channel_id=1, source_target_pairs={{0,2},{1,3},{2,0},{3,1},{4,6},{5,7},{6,4},{7,5},{8,10},{9,11},{10,... | collective-permute-start | bytes 49160 | tf_op jit(solution)/shard_map/gradient_exchange/ppermute | solution.py:426
  30.8 0.7 %collective-permute-start.5 = (f32[1,4,32,32]{3,2,1,0:T(8,128)}, f32[1,4,32,32]{3,2,1,0:T(8,128)S(1)}, u32[]{:S(2)}, u32[]{:S(2)}) collective-permute-start(f32[1,4,32,32]{3,2,1,0:T(8,128)} %bitcast.56), channel_id=1, source_target_pairs={{0,3},{1,2},{2,1},{3,0},{4,7},{5,6},{6,5},{7,4},{8,11},{9,10},{10,... | collective-permute-start | bytes 49160 | tf_op jit(solution)/shard_map/gradient_exchange/ppermute | solution.py:426
  31.5 2.2 %collective-permute-done.3 = f32[1,4,32,32]{3,2,1,0:T(8,128)S(1)} collective-permute-done((f32[1,4,32,32]{3,2,1,0:T(8,128)}, f32[1,4,32,32]{3,2,1,0:T(8,128)S(1)}, u32[]{:S(2)}, u32[]{:S(2)}) %collective-permute-start.3) | collective-permute-done | bytes 16416 | tf_op jit(solution)/shard_map/gradient_exchange/ppermute | solution.py:426
  33.7 0.8 %bitcast_add_fusion = f32[1,4,32,32]{3,2,1,0:T(8,128)S(1)} fusion(f32[1,4,32,32]{3,2,1,0:T(8,128)S(1)} %collective-permute-done.3, f32[4,32,32]{2,1,0:T(8,128)} %imaging_kernel.1), kind=kLoop, calls=%fused_computation.27 | loop fusion | flops 4096 | bytes 49152 | tf_op jit(solution)/shard_map/gradient_exchange/add | solution.py:429
  34.5 0.2 collective-permute-done.5
  34.8 0.6 %fusion.12 = (f32[2,2,32,32]{3,2,1,0:T(8,128)S(1)}, f32[2,2,32,32]{3,2,1,0:T(8,128)}) fusion(f32[2,4,32,32]{3,2,1,0:T(8,128)S(1)} %maximum_select_fusion), kind=kLoop, calls=%fused_computation.29 | loop fusion | bytes 65536 | tf_op jit(solution)/shard_map/gradient_exchange/slice | solution.py:439
  35.5 0.8 %collective-permute-start.6 = (f32[1,2,32,32]{3,2,1,0:T(8,128)S(1)}, f32[1,2,32,32]{3,2,1,0:T(8,128)S(1)}, u32[]{:S(2)}, u32[]{:S(2)}) collective-permute-start(f32[1,2,32,32]{3,2,1,0:T(8,128)S(1)} %get-tuple-element.8), channel_id=1, source_target_pairs={{0,8},{4,12},{8,0},{12,4},{1,5},{5,1},{9,13},{13,9},{2,10},{6,14},... | collective-permute-start | bytes 24584 | tf_op jit(solution)/shard_map/gradient_exchange/ppermute | solution.py:366
  36.4 0.7 %collective-permute-start.7 = (f32[1,2,32,32]{3,2,1,0:T(8,128)S(1)}, f32[1,2,32,32]{3,2,1,0:T(8,128)S(1)}, u32[]{:S(2)}, u32[]{:S(2)}) collective-permute-start(f32[1,2,32,32]{3,2,1,0:T(8,128)S(1)} %get-tuple-element.9), channel_id=1, source_target_pairs={{1,13},{5,9},{9,5},{13,1},{3,15},{7,11},{11,7},{15,3},{17,29},{21,... | collective-permute-start | bytes 24584 | tf_op jit(solution)/shard_map/gradient_exchange/ppermute | solution.py:366
  37.0 2.9 %gradient_exchange.1 = (f32[2,256,256]{2,1,0:T(8,128)}, f32[1,1,1,1]{3,2,1,0:T(1,128)}) custom-call(f32[2,2,32,32]{3,2,1,0:T(8,128)} %get-tuple-element.11.refs_0_, f32[32,256]{1,0:T(8,128)} %constant.63.clone.c_re_ref.refs_1_.refs_2_, f32[32,256]{1,0:T(8,128)} %constant.64.clone.c_im_ref.refs_2_.refs_3_, bf16[256,384]{1,0:T(8,128)(2,1)} %constant.74.clone.refs_3_.refs_4_), custom_call_target="tpu_custom_call" | custom-call | tf_op jit(solution)/shard_map/gradient_exchange/pallas_call | solution.py:270
  40.6 0.1 collective-permute-done.6
  40.7 3.1 %collective-permute-start.8 = (f32[1,2,32,32]{3,2,1,0:T(8,128)S(1)}, f32[1,2,32,32]{3,2,1,0:T(8,128)S(1)}, u32[]{:S(2)}, u32[]{:S(2)}) collective-permute-start(f32[1,2,32,32]{3,2,1,0:T(8,128)S(1)} %add_add_fusion.refs_0_), channel_id=1, source_target_pairs={{0,1},{1,0},{2,3},{3,2},{4,5},{5,4},{6,7},{7,6},{8,9},{9,8},{10,11... | collective-permute-start | bytes 24584 | tf_op jit(solution)/shard_map/gradient_exchange/ppermute | solution.py:307
  43.8 0.9 %collective-permute-done.8.refs_1_ = f32[1,2,32,32]{3,2,1,0:T(8,128)S(1)} collective-permute-done((f32[1,2,32,32]{3,2,1,0:T(8,128)S(1)}, f32[1,2,32,32]{3,2,1,0:T(8,128)S(1)}, u32[]{:S(2)}, u32[]{:S(2)}) %collective-permute-start.8) | collective-permute-done | bytes 8224 | tf_op jit(solution)/shard_map/gradient_exchange/ppermute | solution.py:307
  44.7 0.6 %copy-done.8 = f32[1,2,32,32]{3,2,1,0:T(8,128)} copy-done((f32[1,2,32,32]{3,2,1,0:T(8,128)}, f32[1,2,32,32]{3,2,1,0:T(8,128)S(1)}, u32[]{:S(2)}) %copy-start.8) | copy-done | bytes 8216
  45.3 2.3 %pixel_gradients.1 = f32[1,256,256]{2,1,0:T(8,128)} custom-call(f32[1,2,32,32]{3,2,1,0:T(8,128)} %copy-done.7, f32[1,2,32,32]{3,2,1,0:T(8,128)} %copy-done.8, f32[32,256]{1,0:T(8,128)} %constant.63.clone.c_re_ref.refs_1_.refs_2_, f32[32,256]{1,0:T(8,128)} %constant.64.clone.c_im_ref.refs_2_.refs_3_, bf16[256,384]{1,0:T(8,128)(2,1)} %constant.74.clone.refs_3_.refs_4_), custom_call_target="tpu_custom_call" | custom-call | tf_op jit(solution)/shard_map/pixel_gradients/pallas_call | solution.py:264
  (36 shorter events, 0.6 us)
Async XLA Ops:
  0.6 0.9 %copy-start = (bf16[1,256,256]{2,1,0:T(8,128)(2,1)S(1)}, bf16[1,256,256]{2,1,0:T(8,128)(2,1)}, u32[]{:S(2)}) copy-start(bf16[1,256,256]{2,1,0:T(8,128)(2,1)} %param.28) | copy-start | bytes 393220
  0.6 0.9 %copy-start.2 = (f32[32,256]{1,0:T(8,128)S(1)}, f32[32,256]{1,0:T(8,128)}, u32[]{:S(2)}) copy-start(f32[32,256]{1,0:T(8,128)} %constant.63.clone.c_re_ref.refs_1_.refs_2_) | copy-start | bytes 98308
  0.7 1.1 %copy-start.3 = (f32[32,256]{1,0:T(8,128)S(1)}, f32[32,256]{1,0:T(8,128)}, u32[]{:S(2)}) copy-start(f32[32,256]{1,0:T(8,128)} %constant.64.clone.c_im_ref.refs_2_.refs_3_) | copy-start | bytes 98308
  0.7 7.4 %copy-start.1 = (f32[1,12,2,32,32]{4,3,2,1,0:T(8,128)S(1)}, f32[1,12,2,32,32]{4,3,2,1,0:T(8,128)}, u32[]{:S(2)}) copy-start(f32[1,12,2,32,32]{4,3,2,1,0:T(8,128)} %param.32) | copy-start | bytes 294916
  2.6 5.6 %copy-start.5 = (f32[1,2,32,32]{3,2,1,0:T(8,128)}, f32[1,2,32,32]{3,2,1,0:T(8,128)S(1)}, u32[]{:S(2)}) copy-start(f32[1,2,32,32]{3,2,1,0:T(8,128)S(1)} %pad_maximum_fusion.1.own_ref) | copy-start | bytes 24580
  2.7 6.9 %collective-permute-start = (f32[1,2,32,32]{3,2,1,0:T(8,128)S(1)}, f32[1,2,32,32]{3,2,1,0:T(8,128)S(1)}, u32[]{:S(2)}, u32[]{:S(2)}) collective-permute-start(f32[1,2,32,32]{3,2,1,0:T(8,128)S(1)} %pad_maximum_fusion.1.own_ref), channel_id=1, source_target_pairs={{8,0},{12,4},{0,8},{4,12},{5,1},{1,5},{13,9},{9,13},{10,2},{14,6},... | collective-permute-start | bytes 24584 | tf_op jit(solution)/shard_map/master_spectra/ppermute | solution.py:347
  6.8 2.8 %collective-permute-start.1 = (f32[1,2,32,32]{3,2,1,0:T(8,128)S(1)}, f32[1,2,32,32]{3,2,1,0:T(8,128)S(1)}, u32[]{:S(2)}, u32[]{:S(2)}) collective-permute-start(f32[1,2,32,32]{3,2,1,0:T(8,128)S(1)} %pad_maximum_fusion.1.own_ref), channel_id=1, source_target_pairs={{13,1},{9,5},{5,9},{1,13},{15,3},{11,7},{7,11},{3,15},{29,17},{25,... | collective-permute-start | bytes 24584 | tf_op jit(solution)/shard_map/master_spectra/ppermute | solution.py:347
  7.4 0.7 %copy-start.9 = (f32[1,12]{1,0:T(1,128)S(1)}, f32[1,12]{1,0:T(1,128)}, u32[]{:S(2)}) copy-start(f32[1,12]{1,0:T(1,128)} %param.33) | copy-start | bytes 148
  9.7 3.6 %copy-start.4 = (f32[4,2,32,32]{3,2,1,0:T(8,128)}, f32[4,2,32,32]{3,2,1,0:T(8,128)S(1)}, u32[]{:S(2)}) copy-start(f32[4,2,32,32]{3,2,1,0:T(8,128)S(1)} %select_add_fusion.ev_ref) | copy-start | bytes 98308
  9.7 3.5 %collective-permute-start.2 = (f32[4,2,32,32]{3,2,1,0:T(8,128)S(1)}, f32[4,2,32,32]{3,2,1,0:T(8,128)S(1)}, u32[]{:S(2)}, u32[]{:S(2)}) collective-permute-start(f32[4,2,32,32]{3,2,1,0:T(8,128)S(1)} %select_add_fusion.ev_ref), channel_id=1, source_target_pairs={{0,1},{1,0},{2,3},{3,2},{4,5},{5,4},{6,7},{7,6},{8,9},{9,8},{10,11... | collective-permute-start | bytes 98312 | tf_op jit(solution)/shard_map/master_spectra/ppermute | solution.py:307
  13.2 0.7 %copy-start.6 = (f32[4,2,32,32]{3,2,1,0:T(8,128)}, f32[4,2,32,32]{3,2,1,0:T(8,128)S(1)}, u32[]{:S(2)}) copy-start(f32[4,2,32,32]{3,2,1,0:T(8,128)S(1)} %collective-permute-done.2.ev2_ref) | copy-start | bytes 98308
  29.1 1.6 %copy-start.10 = (s32[2]{0:T(128)S(1)}, s32[2]{0:T(128)}, u32[]{:S(2)}) copy-start(s32[2]{0:T(128)} %im_ref.1) | copy-start | bytes 28
  29.1 4.5 %collective-permute-start.3 = (f32[1,4,32,32]{3,2,1,0:T(8,128)}, f32[1,4,32,32]{3,2,1,0:T(8,128)S(1)}, u32[]{:S(2)}, u32[]{:S(2)}) collective-permute-start(f32[1,4,32,32]{3,2,1,0:T(8,128)} %bitcast.54), channel_id=1, source_target_pairs={{0,2},{1,3},{2,0},{3,1},{4,6},{5,7},{6,4},{7,5},{8,10},{9,11},{10,... | collective-permute-start | bytes 49160 | tf_op jit(solution)/shard_map/gradient_exchange/ppermute | solution.py:426
  30.8 3.8 %collective-permute-start.4 = (f32[1,4,32,32]{3,2,1,0:T(8,128)}, f32[1,4,32,32]{3,2,1,0:T(8,128)S(1)}, u32[]{:S(2)}, u32[]{:S(2)}) collective-permute-start(f32[1,4,32,32]{3,2,1,0:T(8,128)} %bitcast.55), channel_id=1, source_target_pairs={{0,1},{1,0},{2,3},{3,2},{4,5},{5,4},{6,7},{7,6},{8,9},{9,8},{10,11... | collective-permute-start | bytes 49160 | tf_op jit(solution)/shard_map/gradient_exchange/ppermute | solution.py:426
  30.8 4.0 %collective-permute-start.5 = (f32[1,4,32,32]{3,2,1,0:T(8,128)}, f32[1,4,32,32]{3,2,1,0:T(8,128)S(1)}, u32[]{:S(2)}, u32[]{:S(2)}) collective-permute-start(f32[1,4,32,32]{3,2,1,0:T(8,128)} %bitcast.56), channel_id=1, source_target_pairs={{0,3},{1,2},{2,1},{3,0},{4,7},{5,6},{6,5},{7,4},{8,11},{9,10},{10,... | collective-permute-start | bytes 49160 | tf_op jit(solution)/shard_map/gradient_exchange/ppermute | solution.py:426
  35.5 5.2 %collective-permute-start.6 = (f32[1,2,32,32]{3,2,1,0:T(8,128)S(1)}, f32[1,2,32,32]{3,2,1,0:T(8,128)S(1)}, u32[]{:S(2)}, u32[]{:S(2)}) collective-permute-start(f32[1,2,32,32]{3,2,1,0:T(8,128)S(1)} %get-tuple-element.8), channel_id=1, source_target_pairs={{0,8},{4,12},{8,0},{12,4},{1,5},{5,1},{9,13},{13,9},{2,10},{6,14},... | collective-permute-start | bytes 24584 | tf_op jit(solution)/shard_map/gradient_exchange/ppermute | solution.py:366
  36.4 4.3 %collective-permute-start.7 = (f32[1,2,32,32]{3,2,1,0:T(8,128)S(1)}, f32[1,2,32,32]{3,2,1,0:T(8,128)S(1)}, u32[]{:S(2)}, u32[]{:S(2)}) collective-permute-start(f32[1,2,32,32]{3,2,1,0:T(8,128)S(1)} %get-tuple-element.9), channel_id=1, source_target_pairs={{1,13},{5,9},{9,5},{13,1},{3,15},{7,11},{11,7},{15,3},{17,29},{21,... | collective-permute-start | bytes 24584 | tf_op jit(solution)/shard_map/gradient_exchange/ppermute | solution.py:366
  40.7 4.0 %copy-start.7 = (f32[1,2,32,32]{3,2,1,0:T(8,128)}, f32[1,2,32,32]{3,2,1,0:T(8,128)S(1)}, u32[]{:S(2)}) copy-start(f32[1,2,32,32]{3,2,1,0:T(8,128)S(1)} %add_add_fusion.refs_0_) | copy-start | bytes 24580
  40.7 4.0 %collective-permute-start.8 = (f32[1,2,32,32]{3,2,1,0:T(8,128)S(1)}, f32[1,2,32,32]{3,2,1,0:T(8,128)S(1)}, u32[]{:S(2)}, u32[]{:S(2)}) collective-permute-start(f32[1,2,32,32]{3,2,1,0:T(8,128)S(1)} %add_add_fusion.refs_0_), channel_id=1, source_target_pairs={{0,1},{1,0},{2,3},{3,2},{4,5},{5,4},{6,7},{7,6},{8,9},{9,8},{10,11... | collective-permute-start | bytes 24584 | tf_op jit(solution)/shard_map/gradient_exchange/ppermute | solution.py:307
  44.7 0.6 %copy-start.8 = (f32[1,2,32,32]{3,2,1,0:T(8,128)}, f32[1,2,32,32]{3,2,1,0:T(8,128)S(1)}, u32[]{:S(2)}) copy-start(f32[1,2,32,32]{3,2,1,0:T(8,128)S(1)} %collective-permute-done.8.refs_1_) | copy-start | bytes 24580

commit v15 on v14

--- a/solution.py
+++ b/solution.py
@@ -127,12 +127,12 @@
 
 
 def imaging_body(
-    pos_ref, im_ref, sh_ref, w_ref, dose_ref, mask_ref, ev_ref, ev2_ref, own_ref, goal_ref, h_ref, hc_ref,
+    im_ref, sh_ref, w_ref, dose_ref, mask_ref, ev_ref, ev2_ref, own_ref, goal_ref, h_ref, hc_ref,
     c_re_ref, c_im_ref, ct_re_ref, ct_im_ref, rw_top, rw_bot, rc_ref, la_ref, rhm_ref, rlh_ref, rows_ref,
-    slots_ref, f_buf, i_buf, u_buf, w_buf, xr_buf, xi_buf,
+    slots_ref, f_buf, i_buf, u_buf, w_buf, xr_buf, xi_buf, *, per_dev, offset,
 ):
     count = f_buf.shape[0]
-    pos = pos_ref[0]
+    pos = lax.axis_index("kern") * per_dev + offset
     master = im_ref[pos]
     pick0 = (lax.broadcasted_iota(jnp.int32, (P_SIZE, 128), 0) == sh_ref[pos, 0]).astype(jnp.float32)
     pick1 = (lax.broadcasted_iota(jnp.int32, (8, P_SIZE), 1) == sh_ref[pos, 1]).astype(jnp.float32)
@@ -143,7 +143,7 @@
     ph_re = e0_re * e1_re - e0_im * e1_im
     ph_im = e0_re * e1_im + e0_im * e1_re
     local_masters = own_ref.shape[0]
-    is_own = master // local_masters == pos_ref[1]
+    is_own = master // local_masters == lax.axis_index("tile")
     m_re = ev_ref[master, 0] + ev2_ref[master, 0] + jnp.where(is_own, own_ref[master % local_masters, 0], 0.0)
     m_im = ev_ref[master, 1] + ev2_ref[master, 1] + jnp.where(is_own, own_ref[master % local_masters, 1], 0.0)
     mask = mask_ref[pos]
@@ -205,7 +205,7 @@
     slots_ref[3] = ph_re * g_im - ph_im * g_re
 
 
-def imaging(pos, inst_master, inst_shift, weights, dose, tile_mask, every, own, target, kerns, h_cat):
+def imaging(per_dev, offset, inst_master, inst_shift, weights, dose, tile_mask, every, own, target, kerns, h_cat):
     if len(every) == 1:
         every = (every[0], jnp.zeros_like(every[0]))
     count = weights.shape[0]
@@ -213,9 +213,9 @@
     vmem = pl.BlockSpec(memory_space=pltpu.VMEM)
     smem = pl.BlockSpec(memory_space=pltpu.SMEM)
     return pl.pallas_call(
-        imaging_body,
+        functools.partial(imaging_body, per_dev=per_dev, offset=offset),
         out_shape=jax.ShapeDtypeStruct((4, B, B), jnp.float32),
-        in_specs=[smem] * 5 + [vmem] * 7 + [vmem] * len(tables),
+        in_specs=[smem] * 4 + [vmem] * 7 + [vmem] * len(tables),
         out_specs=vmem,
         scratch_shapes=[
             pltpu.VMEM((count, P_SIZE, 2 * P_SIZE), jnp.float32),
@@ -225,7 +225,7 @@
             pltpu.VMEM((count * B, B), jnp.float32),
             pltpu.VMEM((count * B, B), jnp.float32),
         ],
-    )(pos, inst_master, inst_shift, weights, dose, tile_mask, *every, own, target, kerns, h_cat, *tables)
+    )(inst_master, inst_shift, weights, dose, tile_mask, *every, own, target, kerns, h_cat, *tables)
 
 
 def pixel_body(*refs, passes):
@@ -409,10 +409,9 @@
         h_cat = jnp.concatenate([ht_re, ht_re, ht_im, -ht_im], axis=-1).reshape(count * B, 128)
         parts = []
         for j in range(per_dev):
-            pos = jnp.stack([first + j, tile_pos]).astype(jnp.int32)
             parts.append(
                 imaging(
-                    pos, inst_master, inst_shift, weights, corner_dose, tile_mask, every, own_part, target,
+                    per_dev, j, inst_master, inst_shift, weights, corner_dose, tile_mask, every, own_part, target,
                     kerns, h_cat,
                 )
             )

time: 47.9 us -> 48.2 us (level)
  starting transfers between devices: 13.8 us -> 14.8 us
  other arithmetic: 2.87 us -> 2.22 us
    ppermute x2, starting transfers between devices: 5.32 us -> 6.31 us  [sum_parts(): return (x, lax.ppermute(x, axis, [(0, 1), (1, 0)]))]
    another operation x1 -> x0, other arithmetic: 0.65 us -> none  [on_device(): pos = jnp.stack([first + j, tile_pos]).astype(jnp.int32)]
  transfers between devices with their start and end apart: 9 -> 9, of which waited for: 4 -> 3; matrix products, arithmetic and copies ran while one was open for 6% -> 5% of each run, Pallas kernels for 6% -> 6%
where the time goes in v15:
time: 48.2 us; the launch traced here: 47.9 us
  Pallas kernels  20.4 us (42%)
  starting transfers between devices  14.8 us (31%)
  local copies, waits for them, and re-layouts  3.81 us (8%)
  waiting for transfers between devices  3.29 us (7%)
  between operations  2.26 us (5%)
  other arithmetic  2.22 us (5%)
  matrix products  1.03 us (2%)
    pallas_call x1, Pallas kernels, imaging(): pl.pallas_call(functools.partial(imaging_body, per_dev=per_dev, offset=of...  15.2 us
    ppermute x2, starting transfers between devices, sum_parts(): return (x, lax.ppermute(x, axis, [(0, 1), (1, 0)]))  6.31 us
    ppermute x2, starting transfers between devices, gather_split(): got = lax.ppermute(x, ('tile', 'kern'), pairs)  4.75 us
    pallas_call x1, Pallas kernels, pixels(): pl.pallas_call(functools.partial(pixel_body, passes=True), out_shape=(sha...  2.89 us
    unnamed x22, local copies, waits for them, and re-layouts  2.82 us
    ppermute x3, waiting for transfers between devices, on_device(): lax.ppermute(comp, ('corner', 'kern'), [(i, i ^ step) for i in range(4)])  2.42 us
    pallas_call x1, Pallas kernels, pixels(): pl.pallas_call(functools.partial(pixel_body, passes=False), out_shape=sha...  2.31 us
    ppermute x3, starting transfers between devices, on_device(): lax.ppermute(comp, ('corner', 'kern'), [(i, i ^ step) for i in range(4)])  2.26 us
  transfers between devices with their start and end apart: 9, of which 3 were waited for; matrix products, arithmetic and copies ran while one was open for 5% of the time, Pallas kernels for 6%

profile of v15, /device:TPU:0, one launch (start us, length us, event | category | flops | bytes accessed | tf_op | source)
XLA Modules:
  0.0 47.9 jit_solution(12826892775469802709)
XLA Ops:
  0.7 0.9 %copy-done = bf16[1,256,256]{2,1,0:T(8,128)(2,1)S(1)} copy-done((bf16[1,256,256]{2,1,0:T(8,128)(2,1)S(1)}, bf16[1,256,256]{2,1,0:T(8,128)(2,1)}, u32[]{:S(2)}) %copy-start) | copy-done | bytes 131096
  1.5 0.2 fusion.8
  1.8 0.2 fusion.6
  2.0 0.2 fusion.14
  2.1 0.2 fusion.13
  2.3 0.2 fusion
  2.5 0.2 fusion.1
  2.7 4.1 %collective-permute-start = (f32[1,2,32,32]{3,2,1,0:T(8,128)S(1)}, f32[1,2,32,32]{3,2,1,0:T(8,128)S(1)}, u32[]{:S(2)}, u32[]{:S(2)}) collective-permute-start(f32[1,2,32,32]{3,2,1,0:T(8,128)S(1)} %pad_maximum_fusion.1.own_ref), channel_id=1, source_target_pairs={{8,0},{12,4},{0,8},{4,12},{5,1},{1,5},{13,9},{9,13},{10,2},{14,6},... | collective-permute-start | bytes 24584 | tf_op jit(solution)/shard_map/master_spectra/ppermute | solution.py:347
  6.8 0.7 %collective-permute-start.1 = (f32[1,2,32,32]{3,2,1,0:T(8,128)S(1)}, f32[1,2,32,32]{3,2,1,0:T(8,128)S(1)}, u32[]{:S(2)}, u32[]{:S(2)}) collective-permute-start(f32[1,2,32,32]{3,2,1,0:T(8,128)S(1)} %pad_maximum_fusion.1.own_ref), channel_id=1, source_target_pairs={{13,1},{9,5},{5,9},{1,13},{15,3},{11,7},{7,11},{3,15},{29,17},{25,... | collective-permute-start | bytes 24584 | tf_op jit(solution)/shard_map/master_spectra/ppermute | solution.py:347
  7.5 0.6 %copy-done.9 = f32[1,12]{1,0:T(1,128)S(1)} copy-done((f32[1,12]{1,0:T(1,128)S(1)}, f32[1,12]{1,0:T(1,128)}, u32[]{:S(2)}) %copy-start.9) | copy-done | bytes 72
  8.1 0.1 fusion.10
  8.3 0.1 copy.39
  8.4 0.1 copy.40
  8.6 0.1 copy.37
  8.8 3.1 %collective-permute-start.2 = (f32[4,2,32,32]{3,2,1,0:T(8,128)S(1)}, f32[4,2,32,32]{3,2,1,0:T(8,128)S(1)}, u32[]{:S(2)}, u32[]{:S(2)}) collective-permute-start(f32[4,2,32,32]{3,2,1,0:T(8,128)S(1)} %select_add_fusion.ev_ref), channel_id=1, source_target_pairs={{0,1},{1,0},{2,3},{3,2},{4,5},{5,4},{6,7},{7,6},{8,9},{9,8},{10,11... | collective-permute-start | bytes 98312 | tf_op jit(solution)/shard_map/master_spectra/ppermute | solution.py:307
  11.9 0.9 %pad_maximum_fusion = f32[12,32,128]{2,1,0:T(8,128)} fusion(f32[12,32,32]{2,1,0:T(8,128)S(1)} %copy.40, f32[12,32,32]{2,1,0:T(8,128)S(1)} %copy.39, f32[12,32,32]{2,1,0:T(8,128)S(1)} %copy.37), kind=kLoop, calls=%fused_computation.11 | loop fusion | flops 147456 | bytes 344064 | tf_op jit(solution)/shard_map/imaging_kernel/concatenate | solution.py:409
  13.5 0.6 %copy-done.6 = f32[4,2,32,32]{3,2,1,0:T(8,128)} copy-done((f32[4,2,32,32]{3,2,1,0:T(8,128)}, f32[4,2,32,32]{3,2,1,0:T(8,128)S(1)}, u32[]{:S(2)}) %copy-start.6) | copy-done | bytes 32792
  14.1 15.2 %imaging_kernel.1 = f32[4,32,32]{2,1,0:T(8,128)} custom-call(s32[2]{0:T(128)} %im_ref.1, s32[2,2]{1,0:T(2,128)} %sh_ref.1, f32[12]{0:T(128)} %bitcast.57, f32[1]{0:T(128)S(6)} %copy.42.dose_ref, bf16[2,256,256]{2,1,0:T(8,128)(2,1)} %mask_ref.1, f32[4,2,32,32]{3,2,1,0:T(8,128)} %copy-done.4, f32[4,2,32,32]{3,2,1,0:T(8,128)} %copy-done.6, ...), custom_call_target="tpu_custom_call" | custom-call | tf_op jit(solution)/shard_map/imaging_kernel/pallas_call | solution.py:215
  29.4 1.6 %collective-permute-start.3 = (f32[1,4,32,32]{3,2,1,0:T(8,128)}, f32[1,4,32,32]{3,2,1,0:T(8,128)S(1)}, u32[]{:S(2)}, u32[]{:S(2)}) collective-permute-start(f32[1,4,32,32]{3,2,1,0:T(8,128)} %bitcast.52), channel_id=1, source_target_pairs={{0,2},{1,3},{2,0},{3,1},{4,6},{5,7},{6,4},{7,5},{8,10},{9,11},{10,... | collective-permute-start | bytes 49160 | tf_op jit(solution)/shard_map/gradient_exchange/ppermute | solution.py:425
  31.0 0.7 %collective-permute-start.5 = (f32[1,4,32,32]{3,2,1,0:T(8,128)}, f32[1,4,32,32]{3,2,1,0:T(8,128)S(1)}, u32[]{:S(2)}, u32[]{:S(2)}) collective-permute-start(f32[1,4,32,32]{3,2,1,0:T(8,128)} %bitcast.54), channel_id=1, source_target_pairs={{0,3},{1,2},{2,1},{3,0},{4,7},{5,6},{6,5},{7,4},{8,11},{9,10},{10,... | collective-permute-start | bytes 49160 | tf_op jit(solution)/shard_map/gradient_exchange/ppermute | solution.py:425
  31.7 2.2 %collective-permute-done.3 = f32[1,4,32,32]{3,2,1,0:T(8,128)S(1)} collective-permute-done((f32[1,4,32,32]{3,2,1,0:T(8,128)}, f32[1,4,32,32]{3,2,1,0:T(8,128)S(1)}, u32[]{:S(2)}, u32[]{:S(2)}) %collective-permute-start.3) | collective-permute-done | bytes 16416 | tf_op jit(solution)/shard_map/gradient_exchange/ppermute | solution.py:425
  33.9 0.8 %bitcast_add_fusion = f32[1,4,32,32]{3,2,1,0:T(8,128)S(1)} fusion(f32[1,4,32,32]{3,2,1,0:T(8,128)S(1)} %collective-permute-done.3, f32[4,32,32]{2,1,0:T(8,128)} %imaging_kernel.1), kind=kLoop, calls=%fused_computation.26 | loop fusion | flops 4096 | bytes 49152 | tf_op jit(solution)/shard_map/gradient_exchange/add | solution.py:428
  34.8 0.2 collective-permute-done.5
  35.0 0.6 %fusion.12 = (f32[2,2,32,32]{3,2,1,0:T(8,128)S(1)}, f32[2,2,32,32]{3,2,1,0:T(8,128)}) fusion(f32[2,4,32,32]{3,2,1,0:T(8,128)S(1)} %maximum_select_fusion), kind=kLoop, calls=%fused_computation.28 | loop fusion | bytes 65536 | tf_op jit(solution)/shard_map/gradient_exchange/slice | solution.py:438
  35.7 0.1 multiply_reduce_fusion
  35.8 0.9 %collective-permute-start.6 = (f32[1,2,32,32]{3,2,1,0:T(8,128)S(1)}, f32[1,2,32,32]{3,2,1,0:T(8,128)S(1)}, u32[]{:S(2)}, u32[]{:S(2)}) collective-permute-start(f32[1,2,32,32]{3,2,1,0:T(8,128)S(1)} %get-tuple-element.8), channel_id=1, source_target_pairs={{0,8},{4,12},{8,0},{12,4},{1,5},{5,1},{9,13},{13,9},{2,10},{6,14},... | collective-permute-start | bytes 24584 | tf_op jit(solution)/shard_map/gradient_exchange/ppermute | solution.py:366
  36.6 0.7 %collective-permute-start.7 = (f32[1,2,32,32]{3,2,1,0:T(8,128)S(1)}, f32[1,2,32,32]{3,2,1,0:T(8,128)S(1)}, u32[]{:S(2)}, u32[]{:S(2)}) collective-permute-start(f32[1,2,32,32]{3,2,1,0:T(8,128)S(1)} %get-tuple-element.9), channel_id=1, source_target_pairs={{1,13},{5,9},{9,5},{13,1},{3,15},{7,11},{11,7},{15,3},{17,29},{21,... | collective-permute-start | bytes 24584 | tf_op jit(solution)/shard_map/gradient_exchange/ppermute | solution.py:366
  37.3 2.9 %gradient_exchange.1 = (f32[2,256,256]{2,1,0:T(8,128)}, f32[1,1,1,1]{3,2,1,0:T(1,128)}) custom-call(f32[2,2,32,32]{3,2,1,0:T(8,128)} %get-tuple-element.11.refs_0_, f32[32,256]{1,0:T(8,128)} %constant.63.clone.c_re_ref.refs_1_.refs_2_, f32[32,256]{1,0:T(8,128)} %constant.64.clone.c_im_ref.refs_2_.refs_3_, bf16[256,384]{1,0:T(8,128)(2,1)} %constant.74.clone.refs_3_.refs_4_), custom_call_target="tpu_custom_call" | custom-call | tf_op jit(solution)/shard_map/gradient_exchange/pallas_call | solution.py:270
  40.9 3.2 %collective-permute-start.8 = (f32[1,2,32,32]{3,2,1,0:T(8,128)S(1)}, f32[1,2,32,32]{3,2,1,0:T(8,128)S(1)}, u32[]{:S(2)}, u32[]{:S(2)}) collective-permute-start(f32[1,2,32,32]{3,2,1,0:T(8,128)S(1)} %add_add_fusion.refs_0_), channel_id=1, source_target_pairs={{0,1},{1,0},{2,3},{3,2},{4,5},{5,4},{6,7},{7,6},{8,9},{9,8},{10,11... | collective-permute-start | bytes 24584 | tf_op jit(solution)/shard_map/gradient_exchange/ppermute | solution.py:307
  44.1 0.9 %collective-permute-done.8.refs_1_ = f32[1,2,32,32]{3,2,1,0:T(8,128)S(1)} collective-permute-done((f32[1,2,32,32]{3,2,1,0:T(8,128)S(1)}, f32[1,2,32,32]{3,2,1,0:T(8,128)S(1)}, u32[]{:S(2)}, u32[]{:S(2)}) %collective-permute-start.8) | collective-permute-done | bytes 8224 | tf_op jit(solution)/shard_map/gradient_exchange/ppermute | solution.py:307
  44.9 0.6 %copy-done.8 = f32[1,2,32,32]{3,2,1,0:T(8,128)} copy-done((f32[1,2,32,32]{3,2,1,0:T(8,128)}, f32[1,2,32,32]{3,2,1,0:T(8,128)S(1)}, u32[]{:S(2)}) %copy-start.8) | copy-done | bytes 8216
  45.6 2.3 %pixel_gradients.1 = f32[1,256,256]{2,1,0:T(8,128)} custom-call(f32[1,2,32,32]{3,2,1,0:T(8,128)} %copy-done.7, f32[1,2,32,32]{3,2,1,0:T(8,128)} %copy-done.8, f32[32,256]{1,0:T(8,128)} %constant.63.clone.c_re_ref.refs_1_.refs_2_, f32[32,256]{1,0:T(8,128)} %constant.64.clone.c_im_ref.refs_2_.refs_3_, bf16[256,384]{1,0:T(8,128)(2,1)} %constant.74.clone.refs_3_.refs_4_), custom_call_target="tpu_custom_call" | custom-call | tf_op jit(solution)/shard_map/pixel_gradients/pallas_call | solution.py:264
  (35 shorter events, 0.4 us)
Async XLA Ops:
  0.6 0.9 %copy-start = (bf16[1,256,256]{2,1,0:T(8,128)(2,1)S(1)}, bf16[1,256,256]{2,1,0:T(8,128)(2,1)}, u32[]{:S(2)}) copy-start(bf16[1,256,256]{2,1,0:T(8,128)(2,1)} %param.28) | copy-start | bytes 393220
  0.6 0.9 %copy-start.2 = (f32[32,256]{1,0:T(8,128)S(1)}, f32[32,256]{1,0:T(8,128)}, u32[]{:S(2)}) copy-start(f32[32,256]{1,0:T(8,128)} %constant.63.clone.c_re_ref.refs_1_.refs_2_) | copy-start | bytes 98308
  0.7 1.1 %copy-start.3 = (f32[32,256]{1,0:T(8,128)S(1)}, f32[32,256]{1,0:T(8,128)}, u32[]{:S(2)}) copy-start(f32[32,256]{1,0:T(8,128)} %constant.64.clone.c_im_ref.refs_2_.refs_3_) | copy-start | bytes 98308
  0.7 7.4 %copy-start.1 = (f32[1,12,2,32,32]{4,3,2,1,0:T(8,128)S(1)}, f32[1,12,2,32,32]{4,3,2,1,0:T(8,128)}, u32[]{:S(2)}) copy-start(f32[1,12,2,32,32]{4,3,2,1,0:T(8,128)} %param.32) | copy-start | bytes 294916
  2.6 5.6 %copy-start.5 = (f32[1,2,32,32]{3,2,1,0:T(8,128)}, f32[1,2,32,32]{3,2,1,0:T(8,128)S(1)}, u32[]{:S(2)}) copy-start(f32[1,2,32,32]{3,2,1,0:T(8,128)S(1)} %pad_maximum_fusion.1.own_ref) | copy-start | bytes 24580
  2.7 6.0 %collective-permute-start = (f32[1,2,32,32]{3,2,1,0:T(8,128)S(1)}, f32[1,2,32,32]{3,2,1,0:T(8,128)S(1)}, u32[]{:S(2)}, u32[]{:S(2)}) collective-permute-start(f32[1,2,32,32]{3,2,1,0:T(8,128)S(1)} %pad_maximum_fusion.1.own_ref), channel_id=1, source_target_pairs={{8,0},{12,4},{0,8},{4,12},{5,1},{1,5},{13,9},{9,13},{10,2},{14,6},... | collective-permute-start | bytes 24584 | tf_op jit(solution)/shard_map/master_spectra/ppermute | solution.py:347
  6.8 1.9 %collective-permute-start.1 = (f32[1,2,32,32]{3,2,1,0:T(8,128)S(1)}, f32[1,2,32,32]{3,2,1,0:T(8,128)S(1)}, u32[]{:S(2)}, u32[]{:S(2)}) collective-permute-start(f32[1,2,32,32]{3,2,1,0:T(8,128)S(1)} %pad_maximum_fusion.1.own_ref), channel_id=1, source_target_pairs={{13,1},{9,5},{5,9},{1,13},{15,3},{11,7},{7,11},{3,15},{29,17},{25,... | collective-permute-start | bytes 24584 | tf_op jit(solution)/shard_map/master_spectra/ppermute | solution.py:347
  7.4 0.7 %copy-start.9 = (f32[1,12]{1,0:T(1,128)S(1)}, f32[1,12]{1,0:T(1,128)}, u32[]{:S(2)}) copy-start(f32[1,12]{1,0:T(1,128)} %param.33) | copy-start | bytes 148
  8.8 4.0 %copy-start.4 = (f32[4,2,32,32]{3,2,1,0:T(8,128)}, f32[4,2,32,32]{3,2,1,0:T(8,128)S(1)}, u32[]{:S(2)}) copy-start(f32[4,2,32,32]{3,2,1,0:T(8,128)S(1)} %select_add_fusion.ev_ref) | copy-start | bytes 98308
  8.8 4.7 %collective-permute-start.2 = (f32[4,2,32,32]{3,2,1,0:T(8,128)S(1)}, f32[4,2,32,32]{3,2,1,0:T(8,128)S(1)}, u32[]{:S(2)}, u32[]{:S(2)}) collective-permute-start(f32[4,2,32,32]{3,2,1,0:T(8,128)S(1)} %select_add_fusion.ev_ref), channel_id=1, source_target_pairs={{0,1},{1,0},{2,3},{3,2},{4,5},{5,4},{6,7},{7,6},{8,9},{9,8},{10,11... | collective-permute-start | bytes 98312 | tf_op jit(solution)/shard_map/master_spectra/ppermute | solution.py:307
  13.5 0.7 %copy-start.6 = (f32[4,2,32,32]{3,2,1,0:T(8,128)}, f32[4,2,32,32]{3,2,1,0:T(8,128)S(1)}, u32[]{:S(2)}) copy-start(f32[4,2,32,32]{3,2,1,0:T(8,128)S(1)} %collective-permute-done.2.ev2_ref) | copy-start | bytes 98308
  29.4 1.6 %copy-start.10 = (s32[2]{0:T(128)S(1)}, s32[2]{0:T(128)}, u32[]{:S(2)}) copy-start(s32[2]{0:T(128)} %im_ref.1) | copy-start | bytes 28
  29.4 4.5 %collective-permute-start.3 = (f32[1,4,32,32]{3,2,1,0:T(8,128)}, f32[1,4,32,32]{3,2,1,0:T(8,128)S(1)}, u32[]{:S(2)}, u32[]{:S(2)}) collective-permute-start(f32[1,4,32,32]{3,2,1,0:T(8,128)} %bitcast.52), channel_id=1, source_target_pairs={{0,2},{1,3},{2,0},{3,1},{4,6},{5,7},{6,4},{7,5},{8,10},{9,11},{10,... | collective-permute-start | bytes 49160 | tf_op jit(solution)/shard_map/gradient_exchange/ppermute | solution.py:425
  31.0 3.8 %collective-permute-start.4 = (f32[1,4,32,32]{3,2,1,0:T(8,128)}, f32[1,4,32,32]{3,2,1,0:T(8,128)S(1)}, u32[]{:S(2)}, u32[]{:S(2)}) collective-permute-start(f32[1,4,32,32]{3,2,1,0:T(8,128)} %bitcast.53), channel_id=1, source_target_pairs={{0,1},{1,0},{2,3},{3,2},{4,5},{5,4},{6,7},{7,6},{8,9},{9,8},{10,11... | collective-permute-start | bytes 49160 | tf_op jit(solution)/shard_map/gradient_exchange/ppermute | solution.py:425
  31.0 4.0 %collective-permute-start.5 = (f32[1,4,32,32]{3,2,1,0:T(8,128)}, f32[1,4,32,32]{3,2,1,0:T(8,128)S(1)}, u32[]{:S(2)}, u32[]{:S(2)}) collective-permute-start(f32[1,4,32,32]{3,2,1,0:T(8,128)} %bitcast.54), channel_id=1, source_target_pairs={{0,3},{1,2},{2,1},{3,0},{4,7},{5,6},{6,5},{7,4},{8,11},{9,10},{10,... | collective-permute-start | bytes 49160 | tf_op jit(solution)/shard_map/gradient_exchange/ppermute | solution.py:425
  35.8 5.0 %collective-permute-start.6 = (f32[1,2,32,32]{3,2,1,0:T(8,128)S(1)}, f32[1,2,32,32]{3,2,1,0:T(8,128)S(1)}, u32[]{:S(2)}, u32[]{:S(2)}) collective-permute-start(f32[1,2,32,32]{3,2,1,0:T(8,128)S(1)} %get-tuple-element.8), channel_id=1, source_target_pairs={{0,8},{4,12},{8,0},{12,4},{1,5},{5,1},{9,13},{13,9},{2,10},{6,14},... | collective-permute-start | bytes 24584 | tf_op jit(solution)/shard_map/gradient_exchange/ppermute | solution.py:366
  36.6 4.2 %collective-permute-start.7 = (f32[1,2,32,32]{3,2,1,0:T(8,128)S(1)}, f32[1,2,32,32]{3,2,1,0:T(8,128)S(1)}, u32[]{:S(2)}, u32[]{:S(2)}) collective-permute-start(f32[1,2,32,32]{3,2,1,0:T(8,128)S(1)} %get-tuple-element.9), channel_id=1, source_target_pairs={{1,13},{5,9},{9,5},{13,1},{3,15},{7,11},{11,7},{15,3},{17,29},{21,... | collective-permute-start | bytes 24584 | tf_op jit(solution)/shard_map/gradient_exchange/ppermute | solution.py:366
  40.9 4.1 %copy-start.7 = (f32[1,2,32,32]{3,2,1,0:T(8,128)}, f32[1,2,32,32]{3,2,1,0:T(8,128)S(1)}, u32[]{:S(2)}) copy-start(f32[1,2,32,32]{3,2,1,0:T(8,128)S(1)} %add_add_fusion.refs_0_) | copy-start | bytes 24580
  40.9 4.1 %collective-permute-start.8 = (f32[1,2,32,32]{3,2,1,0:T(8,128)S(1)}, f32[1,2,32,32]{3,2,1,0:T(8,128)S(1)}, u32[]{:S(2)}, u32[]{:S(2)}) collective-permute-start(f32[1,2,32,32]{3,2,1,0:T(8,128)S(1)} %add_add_fusion.refs_0_), channel_id=1, source_target_pairs={{0,1},{1,0},{2,3},{3,2},{4,5},{5,4},{6,7},{7,6},{8,9},{9,8},{10,11... | collective-permute-start | bytes 24584 | tf_op jit(solution)/shard_map/gradient_exchange/ppermute | solution.py:307
  44.9 0.6 %copy-start.8 = (f32[1,2,32,32]{3,2,1,0:T(8,128)}, f32[1,2,32,32]{3,2,1,0:T(8,128)S(1)}, u32[]{:S(2)}) copy-start(f32[1,2,32,32]{3,2,1,0:T(8,128)S(1)} %collective-permute-done.8.refs_1_) | copy-start | bytes 24580

commit v16 on v14

--- a/solution.py
+++ b/solution.py
@@ -249,6 +249,45 @@
         out_ref[n] = dot_parts(left_ref[...], stacked)
 
 
+def group_pixel_body(comp_ref, g0_ref, g1_ref, g2_ref, c_re_ref, c_im_ref, left_ref, out_ref, token_ref):
+    token_ref[...] = jnp.zeros(token_ref.shape, jnp.float32)
+    own = lax.axis_index("kern")
+    for n in range(out_ref.shape[0]):
+        mine = n == own
+        planes = []
+        for c in range(2):
+            planes.append(
+                jnp.where(mine, comp_ref[0, c] + g1_ref[0, c], g0_ref[0, c] + g2_ref[0, c])
+            )
+        x_both = jnp.concatenate(planes, axis=0)
+        p_re = dot_full(x_both, c_re_ref[...])
+        p_im = dot_full(x_both, c_im_ref[...])
+        y_re = p_re[:B] + p_im[B:]
+        y_im = p_re[B:] - p_im[:B]
+        y_hi, y_mid, y_lo = split_three(jnp.concatenate([y_re, y_im], axis=0))
+        stacked = jnp.concatenate([y_hi, y_mid, y_hi, y_lo, y_hi, y_mid], axis=0)
+        out_ref[n] = dot_parts(left_ref[...], stacked)
+
+
+def group_pixels(comp, got):
+    freq = np.arange(B, dtype=np.int64) - B // 2
+    pixel = np.arange(P_SIZE, dtype=np.int64)
+    angle = (2.0 * math.pi / P_SIZE) * np.mod(freq[:, None] * pixel[None, :], P_SIZE).astype(np.float64)
+    c_re = np.cos(angle)
+    c_im = -np.sin(angle)
+    a_hi, a_mid, a_lo = table_three(np.concatenate([c_re.T, c_im.T], axis=1))
+    left = np.concatenate([a_hi, a_hi, a_mid, a_hi, a_lo, a_mid], axis=1)
+    tables = [jnp.asarray(c_re, jnp.float32), jnp.asarray(c_im, jnp.float32), jnp.asarray(left)]
+    vmem = pl.BlockSpec(memory_space=pltpu.VMEM)
+    shape = jax.ShapeDtypeStruct((2, P_SIZE, P_SIZE), jnp.float32)
+    return pl.pallas_call(
+        group_pixel_body,
+        out_shape=(shape, jax.ShapeDtypeStruct((1, 1, 1, 1), jnp.float32)),
+        in_specs=[vmem] * 7,
+        out_specs=(vmem, vmem),
+    )(comp, *got, *tables)
+
+
 def pixels(*parts, token=False):
     freq = np.arange(B, dtype=np.int64) - B // 2
     pixel = np.arange(P_SIZE, dtype=np.int64)
@@ -429,18 +468,28 @@
             mine = comp + got[1]
             other = got[0] + got[2]
             both = jnp.where(kern_pos == 0, jnp.concatenate([mine, other]), jnp.concatenate([other, mine]))
+            tile_pixels = lambda: group_pixels(comp, got)
         else:
             comp = sum_all(comp, "corner", corner_count, corner_pos)
             both = gather_all(comp, "kern", kern_count, kern_pos)
+            tile_pixels = lambda: pixels(both[:, 0:2], token=True)
         mine_tiles = both[:, 0:2]
         owner_pick = (
             inst_master[:, None] == jnp.arange(region_masters, dtype=jnp.int32)[None, :]
         ).astype(jnp.float32)
-        terms = jnp.sum(owner_pick[:, :, None, None, None] * both[:, None, 2:4], axis=0)
+        if corner_count == 2 and kern_count == 2 and per_dev == 1:
+            pick_mine = jnp.where(kern_pos == 0, owner_pick[0], owner_pick[1])
+            pick_other = jnp.where(kern_pos == 0, owner_pick[1], owner_pick[0])
+            terms = (
+                pick_mine[:, None, None, None] * (comp[0, 2:4] + got[1][0, 2:4])[None]
+                + pick_other[:, None, None, None] * (got[0][0, 2:4] + got[2][0, 2:4])[None]
+            )
+        else:
+            terms = jnp.sum(owner_pick[:, :, None, None, None] * both[:, None, 2:4], axis=0)
         if xor_partners(tile_count) and xor_partners(kern_count) and tile_count > 2:
             tile_grad, mine_masters = scatter_split(
                 terms, tile_count, tile_pos, kern_count, kern_pos, local_masters,
-                lambda: pixels(mine_tiles, token=True),
+                tile_pixels,
             )
         else:
             tile_grad = pixels(mine_tiles)

time: 47.9 us -> 47.7 us (level)
  starting transfers between devices: 13.8 us -> 12.6 us
  waiting for transfers between devices: 3.43 us -> 4.02 us
    unnamed x22 -> x28, local copies, waits for them, and re-layouts: 2.81 us -> 3.83 us
    add x2 -> x1, other arithmetic: 0.86 us -> 0.08 us  [on_device(): pick_mine[:, None, None, None] * (comp[0, 2:4] + got[1][0, 2:4])[None]]
    mul x0 -> x2, other arithmetic: none -> 0.77 us  [the longest x1 0.76 us: on_device(): pick_mine[:, None, None, None] * (comp[0, 2:4] + got[1][0, 2:4])[None]]
    slice x1 -> x0, local copies, waits for them, and re-layouts: 0.64 us -> none  [on_device(): both[:, None, 2:4]]
    ppermute x2, starting transfers between devices: 5.32 us -> 4.68 us  [sum_parts(): return (x, lax.ppermute(x, axis, [(0, 1), (1, 0)]))]
where the time goes in v16:
time: 47.7 us; the launch traced here: 47.3 us
  Pallas kernels  20.5 us (43%)
  starting transfers between devices  12.6 us (26%)
  local copies, waits for them, and re-layouts  4.17 us (9%)
  waiting for transfers between devices  4.02 us (8%)
  other arithmetic  2.7 us (6%)
  between operations  2.21 us (5%)
  matrix products  1.03 us (2%)
    pallas_call x1, Pallas kernels, imaging(): pl.pallas_call(imaging_body, out_shape=jax.ShapeDtypeStruct((4, B, B), jn...  15.2 us
    ppermute x2, starting transfers between devices, gather_split(): got = lax.ppermute(x, ('tile', 'kern'), pairs)  4.75 us
    ppermute x2, starting transfers between devices, sum_parts(): return (x, lax.ppermute(x, axis, [(0, 1), (1, 0)]))  4.68 us
    unnamed x28, local copies, waits for them, and re-layouts  3.83 us
    pallas_call x1, Pallas kernels, group_pixels(): pl.pallas_call(group_pixel_body, out_shape=(shape, jax.ShapeDtypeStruct((...  2.99 us
    ppermute x3, waiting for transfers between devices, on_device(): lax.ppermute(comp, ('corner', 'kern'), [(i, i ^ step) for i in range(4)])  2.67 us
    pallas_call x1, Pallas kernels, pixels(): pl.pallas_call(functools.partial(pixel_body, passes=False), out_shape=sha...  2.31 us
    ppermute x3, starting transfers between devices, on_device(): lax.ppermute(comp, ('corner', 'kern'), [(i, i ^ step) for i in range(4)])  2.14 us
  transfers between devices with their start and end apart: 9, of which 4 were waited for; matrix products, arithmetic and copies ran while one was open for 6% of the time, Pallas kernels for 6%

profile of v16, /device:TPU:0, one launch (start us, length us, event | category | flops | bytes accessed | tf_op | source)
XLA Modules:
  0.0 47.3 jit_solution(16319316681302050789)
XLA Ops:
  0.7 0.9 %copy-done = bf16[1,256,256]{2,1,0:T(8,128)(2,1)S(1)} copy-done((bf16[1,256,256]{2,1,0:T(8,128)(2,1)S(1)}, bf16[1,256,256]{2,1,0:T(8,128)(2,1)}, u32[]{:S(2)}) %copy-start) | copy-done | bytes 131096
  1.5 0.2 fusion.8
  1.8 0.2 fusion.6
  2.0 0.2 fusion.17
  2.1 0.2 fusion.16
  2.3 0.2 fusion
  2.5 0.2 fusion.1
  2.7 4.1 %collective-permute-start = (f32[1,2,32,32]{3,2,1,0:T(8,128)S(1)}, f32[1,2,32,32]{3,2,1,0:T(8,128)S(1)}, u32[]{:S(2)}, u32[]{:S(2)}) collective-permute-start(f32[1,2,32,32]{3,2,1,0:T(8,128)S(1)} %pad_maximum_fusion.1.own_ref), channel_id=1, source_target_pairs={{8,0},{12,4},{0,8},{4,12},{5,1},{1,5},{13,9},{9,13},{10,2},{14,6},... | collective-permute-start | bytes 24584 | tf_op jit(solution)/shard_map/master_spectra/ppermute | solution.py:386
  6.8 0.7 %collective-permute-start.1 = (f32[1,2,32,32]{3,2,1,0:T(8,128)S(1)}, f32[1,2,32,32]{3,2,1,0:T(8,128)S(1)}, u32[]{:S(2)}, u32[]{:S(2)}) collective-permute-start(f32[1,2,32,32]{3,2,1,0:T(8,128)S(1)} %pad_maximum_fusion.1.own_ref), channel_id=1, source_target_pairs={{13,1},{9,5},{5,9},{1,13},{15,3},{11,7},{7,11},{3,15},{29,17},{25,... | collective-permute-start | bytes 24584 | tf_op jit(solution)/shard_map/master_spectra/ppermute | solution.py:386
  7.5 0.6 %copy-done.13 = f32[1,12]{1,0:T(1,128)S(1)} copy-done((f32[1,12]{1,0:T(1,128)S(1)}, f32[1,12]{1,0:T(1,128)}, u32[]{:S(2)}) %copy-start.13) | copy-done | bytes 72
  8.3 0.1 copy.34
  8.7 0.5 %copy-done.12 = s32[2]{0:T(128)S(1)} copy-done((s32[2]{0:T(128)S(1)}, s32[2]{0:T(128)}, u32[]{:S(2)}) %copy-start.12) | copy-done | bytes 32
  9.3 0.9 %pad_maximum_fusion = f32[12,32,128]{2,1,0:T(8,128)} fusion(f32[12,32,32]{2,1,0:T(8,128)S(1)} %copy.35, f32[12,32,32]{2,1,0:T(8,128)S(1)} %copy.34, f32[12,32,32]{2,1,0:T(8,128)S(1)} %copy.32), kind=kLoop, calls=%fused_computation.10 | loop fusion | flops 147456 | bytes 344064 | tf_op jit(solution)/shard_map/imaging_kernel/concatenate | solution.py:448
  10.3 2.0 %collective-permute-start.2 = (f32[4,2,32,32]{3,2,1,0:T(8,128)S(1)}, f32[4,2,32,32]{3,2,1,0:T(8,128)S(1)}, u32[]{:S(2)}, u32[]{:S(2)}) collective-permute-start(f32[4,2,32,32]{3,2,1,0:T(8,128)S(1)} %select_add_fusion.ev_ref), channel_id=1, source_target_pairs={{0,1},{1,0},{2,3},{3,2},{4,5},{5,4},{6,7},{7,6},{8,9},{9,8},{10,11... | collective-permute-start | bytes 98312 | tf_op jit(solution)/shard_map/master_spectra/ppermute | solution.py:346
  12.3 0.6 %pad_add_fusion.pos_ref = s32[2]{0:T(128)} fusion(s32[1]{0:T(128)} %bitcast.1, s32[1]{0:T(128)} %bitcast), kind=kLoop, calls=%fused_computation.30 | loop fusion | flops 2 | bytes 16 | tf_op jit(solution)/shard_map/imaging_kernel/stack | solution.py:451
  13.6 0.6 %copy-done.9 = f32[4,2,32,32]{3,2,1,0:T(8,128)} copy-done((f32[4,2,32,32]{3,2,1,0:T(8,128)}, f32[4,2,32,32]{3,2,1,0:T(8,128)S(1)}, u32[]{:S(2)}) %copy-start.9) | copy-done | bytes 32792
  14.2 15.2 %imaging_kernel.1 = f32[4,32,32]{2,1,0:T(8,128)} custom-call(s32[2]{0:T(128)} %pad_add_fusion.pos_ref, s32[2]{0:T(128)} %im_ref.1, s32[2,2]{1,0:T(2,128)} %sh_ref.1, f32[12]{0:T(128)} %bitcast.68, f32[1]{0:T(128)S(6)} %copy.37.dose_ref, bf16[2,256,256]{2,1,0:T(8,128)(2,1)} %mask_ref.1, f32[4,2,32,32]{3,2,1,0:T(8,128)} %copy-done.4, ...), custom_call_target="tpu_custom_call" | custom-call | tf_op jit(solution)/shard_map/imaging_kernel/pallas_call | solution.py:215
  29.5 1.5 %collective-permute-start.4 = (f32[1,4,32,32]{3,2,1,0:T(8,128)}, f32[1,4,32,32]{3,2,1,0:T(8,128)S(1)}, u32[]{:S(2)}, u32[]{:S(2)}) collective-permute-start(f32[1,4,32,32]{3,2,1,0:T(8,128)} %bitcast.61), channel_id=1, source_target_pairs={{0,2},{1,3},{2,0},{3,1},{4,6},{5,7},{6,4},{7,5},{8,10},{9,11},{10,... | collective-permute-start | bytes 49160 | tf_op jit(solution)/shard_map/gradient_exchange/ppermute | solution.py:465
  31.0 0.6 %collective-permute-start.5 = (f32[1,4,32,32]{3,2,1,0:T(8,128)}, f32[1,4,32,32]{3,2,1,0:T(8,128)S(1)}, u32[]{:S(2)}, u32[]{:S(2)}) collective-permute-start(f32[1,4,32,32]{3,2,1,0:T(8,128)} %bitcast.63), channel_id=1, source_target_pairs={{0,3},{1,2},{2,1},{3,0},{4,7},{5,6},{6,5},{7,4},{8,11},{9,10},{10,... | collective-permute-start | bytes 49160 | tf_op jit(solution)/shard_map/gradient_exchange/ppermute | solution.py:465
  31.6 2.3 %collective-permute-done.4.g1_ref = f32[1,4,32,32]{3,2,1,0:T(8,128)S(1)} collective-permute-done((f32[1,4,32,32]{3,2,1,0:T(8,128)}, f32[1,4,32,32]{3,2,1,0:T(8,128)S(1)}, u32[]{:S(2)}, u32[]{:S(2)}) %collective-permute-start.4) | collective-permute-done | bytes 16416 | tf_op jit(solution)/shard_map/gradient_exchange/ppermute | solution.py:465
  34.0 0.8 %fusion.11 = f32[2,32,32]{2,1,0:T(8,128)S(1)} fusion(f32[1,4,32,32]{3,2,1,0:T(8,128)S(1)} %collective-permute-done.4.g1_ref, f32[1,4,32,32]{3,2,1,0:T(8,128)} %bitcast.64), kind=kLoop, calls=%fused_computation.20 | loop fusion | flops 2048 | bytes 24576 | tf_op jit(solution)/shard_map/gradient_exchange/mul | solution.py:484
  34.7 0.3 collective-permute-done.5.g2_ref
  35.2 0.2 copy-done.6
  35.4 0.3 copy-done.7
  35.7 0.4 collective-permute-start.6
  36.1 0.7 %collective-permute-start.7 = (f32[1,2,32,32]{3,2,1,0:T(8,128)S(1)}, f32[1,2,32,32]{3,2,1,0:T(8,128)S(1)}, u32[]{:S(2)}, u32[]{:S(2)}) collective-permute-start(f32[1,2,32,32]{3,2,1,0:T(8,128)S(1)} %get-tuple-element.9), channel_id=1, source_target_pairs={{1,13},{5,9},{9,5},{13,1},{3,15},{7,11},{11,7},{15,3},{17,29},{21,... | collective-permute-start | bytes 24584 | tf_op jit(solution)/shard_map/gradient_exchange/ppermute | solution.py:405
  36.8 3.0 %gradient_exchange.1 = (f32[2,256,256]{2,1,0:T(8,128)}, f32[1,1,1,1]{3,2,1,0:T(1,128)}) custom-call(f32[1,4,32,32]{3,2,1,0:T(8,128)} %bitcast.65, f32[1,4,32,32]{3,2,1,0:T(8,128)} %copy-done.6, f32[1,4,32,32]{3,2,1,0:T(8,128)} %copy-done.5, f32[1,4,32,32]{3,2,1,0:T(8,128)} %copy-done.7, f32[32,256]{1,0:T(8,128)} %constant.63.clone.c_re_ref.refs_2_, ...), custom_call_target="tpu_custom_call" | custom-call | tf_op jit(solution)/shard_map/gradient_exchange/pallas_call | solution.py:283
  40.4 0.5 %collective-permute-done.6 = f32[1,2,32,32]{3,2,1,0:T(8,128)S(1)} collective-permute-done((f32[1,2,32,32]{3,2,1,0:T(8,128)S(1)}, f32[1,2,32,32]{3,2,1,0:T(8,128)S(1)}, u32[]{:S(2)}, u32[]{:S(2)}) %collective-permute-start.6) | collective-permute-done | bytes 8224 | tf_op jit(solution)/shard_map/gradient_exchange/ppermute | solution.py:405
  40.9 2.6 %collective-permute-start.8 = (f32[1,2,32,32]{3,2,1,0:T(8,128)S(1)}, f32[1,2,32,32]{3,2,1,0:T(8,128)S(1)}, u32[]{:S(2)}, u32[]{:S(2)}) collective-permute-start(f32[1,2,32,32]{3,2,1,0:T(8,128)S(1)} %add_add_fusion.refs_0_), channel_id=1, source_target_pairs={{0,1},{1,0},{2,3},{3,2},{4,5},{5,4},{6,7},{7,6},{8,9},{9,8},{10,11... | collective-permute-start | bytes 24584 | tf_op jit(solution)/shard_map/gradient_exchange/ppermute | solution.py:346
  43.5 0.9 %collective-permute-done.8.refs_1_ = f32[1,2,32,32]{3,2,1,0:T(8,128)S(1)} collective-permute-done((f32[1,2,32,32]{3,2,1,0:T(8,128)S(1)}, f32[1,2,32,32]{3,2,1,0:T(8,128)S(1)}, u32[]{:S(2)}, u32[]{:S(2)}) %collective-permute-start.8) | collective-permute-done | bytes 8224 | tf_op jit(solution)/shard_map/gradient_exchange/ppermute | solution.py:346
  44.4 0.6 %copy-done.11 = f32[1,2,32,32]{3,2,1,0:T(8,128)} copy-done((f32[1,2,32,32]{3,2,1,0:T(8,128)}, f32[1,2,32,32]{3,2,1,0:T(8,128)S(1)}, u32[]{:S(2)}) %copy-start.11) | copy-done | bytes 8216
  45.0 2.3 %pixel_gradients.1 = f32[1,256,256]{2,1,0:T(8,128)} custom-call(f32[1,2,32,32]{3,2,1,0:T(8,128)} %copy-done.10, f32[1,2,32,32]{3,2,1,0:T(8,128)} %copy-done.11, f32[32,256]{1,0:T(8,128)} %constant.63.clone.c_re_ref.refs_2_, f32[32,256]{1,0:T(8,128)} %constant.64.clone.c_im_ref.refs_3_, bf16[256,384]{1,0:T(8,128)(2,1)} %constant.74.clone.left_ref.refs_4_), custom_call_target="tpu_custom_call" | custom-call | tf_op jit(solution)/shard_map/pixel_gradients/pallas_call | solution.py:303
  (41 shorter events, 0.8 us)
Async XLA Ops:
  0.6 0.9 %copy-start = (bf16[1,256,256]{2,1,0:T(8,128)(2,1)S(1)}, bf16[1,256,256]{2,1,0:T(8,128)(2,1)}, u32[]{:S(2)}) copy-start(bf16[1,256,256]{2,1,0:T(8,128)(2,1)} %param.28) | copy-start | bytes 393220
  0.6 0.9 %copy-start.2 = (f32[32,256]{1,0:T(8,128)S(1)}, f32[32,256]{1,0:T(8,128)}, u32[]{:S(2)}) copy-start(f32[32,256]{1,0:T(8,128)} %constant.63.clone.c_re_ref.refs_2_) | copy-start | bytes 98308
  0.7 1.1 %copy-start.3 = (f32[32,256]{1,0:T(8,128)S(1)}, f32[32,256]{1,0:T(8,128)}, u32[]{:S(2)}) copy-start(f32[32,256]{1,0:T(8,128)} %constant.64.clone.c_im_ref.refs_3_) | copy-start | bytes 98308
  0.7 7.4 %copy-start.1 = (f32[1,12,2,32,32]{4,3,2,1,0:T(8,128)S(1)}, f32[1,12,2,32,32]{4,3,2,1,0:T(8,128)}, u32[]{:S(2)}) copy-start(f32[1,12,2,32,32]{4,3,2,1,0:T(8,128)} %param.32) | copy-start | bytes 294916
  2.6 5.6 %copy-start.8 = (f32[1,2,32,32]{3,2,1,0:T(8,128)}, f32[1,2,32,32]{3,2,1,0:T(8,128)S(1)}, u32[]{:S(2)}) copy-start(f32[1,2,32,32]{3,2,1,0:T(8,128)S(1)} %pad_maximum_fusion.1.own_ref) | copy-start | bytes 24580
  2.7 7.5 %collective-permute-start = (f32[1,2,32,32]{3,2,1,0:T(8,128)S(1)}, f32[1,2,32,32]{3,2,1,0:T(8,128)S(1)}, u32[]{:S(2)}, u32[]{:S(2)}) collective-permute-start(f32[1,2,32,32]{3,2,1,0:T(8,128)S(1)} %pad_maximum_fusion.1.own_ref), channel_id=1, source_target_pairs={{8,0},{12,4},{0,8},{4,12},{5,1},{1,5},{13,9},{9,13},{10,2},{14,6},... | collective-permute-start | bytes 24584 | tf_op jit(solution)/shard_map/master_spectra/ppermute | solution.py:386
  6.8 3.4 %collective-permute-start.1 = (f32[1,2,32,32]{3,2,1,0:T(8,128)S(1)}, f32[1,2,32,32]{3,2,1,0:T(8,128)S(1)}, u32[]{:S(2)}, u32[]{:S(2)}) collective-permute-start(f32[1,2,32,32]{3,2,1,0:T(8,128)S(1)} %pad_maximum_fusion.1.own_ref), channel_id=1, source_target_pairs={{13,1},{9,5},{5,9},{1,13},{15,3},{11,7},{7,11},{3,15},{29,17},{25,... | collective-permute-start | bytes 24584 | tf_op jit(solution)/shard_map/master_spectra/ppermute | solution.py:386
  7.4 0.7 %copy-start.13 = (f32[1,12]{1,0:T(1,128)S(1)}, f32[1,12]{1,0:T(1,128)}, u32[]{:S(2)}) copy-start(f32[1,12]{1,0:T(1,128)} %param.33) | copy-start | bytes 148
  8.5 0.7 %copy-start.12 = (s32[2]{0:T(128)S(1)}, s32[2]{0:T(128)}, u32[]{:S(2)}) copy-start(s32[2]{0:T(128)} %im_ref.1) | copy-start | bytes 28
  10.3 3.3 %copy-start.4 = (f32[4,2,32,32]{3,2,1,0:T(8,128)}, f32[4,2,32,32]{3,2,1,0:T(8,128)S(1)}, u32[]{:S(2)}) copy-start(f32[4,2,32,32]{3,2,1,0:T(8,128)S(1)} %select_add_fusion.ev_ref) | copy-start | bytes 98308
  10.3 3.3 %collective-permute-start.2 = (f32[4,2,32,32]{3,2,1,0:T(8,128)S(1)}, f32[4,2,32,32]{3,2,1,0:T(8,128)S(1)}, u32[]{:S(2)}, u32[]{:S(2)}) collective-permute-start(f32[4,2,32,32]{3,2,1,0:T(8,128)S(1)} %select_add_fusion.ev_ref), channel_id=1, source_target_pairs={{0,1},{1,0},{2,3},{3,2},{4,5},{5,4},{6,7},{7,6},{8,9},{9,8},{10,11... | collective-permute-start | bytes 98312 | tf_op jit(solution)/shard_map/master_spectra/ppermute | solution.py:346
  13.6 0.6 %copy-start.9 = (f32[4,2,32,32]{3,2,1,0:T(8,128)}, f32[4,2,32,32]{3,2,1,0:T(8,128)S(1)}, u32[]{:S(2)}) copy-start(f32[4,2,32,32]{3,2,1,0:T(8,128)S(1)} %collective-permute-done.2.ev2_ref) | copy-start | bytes 98308
  29.5 4.5 %collective-permute-start.4 = (f32[1,4,32,32]{3,2,1,0:T(8,128)}, f32[1,4,32,32]{3,2,1,0:T(8,128)S(1)}, u32[]{:S(2)}, u32[]{:S(2)}) collective-permute-start(f32[1,4,32,32]{3,2,1,0:T(8,128)} %bitcast.61), channel_id=1, source_target_pairs={{0,2},{1,3},{2,0},{3,1},{4,6},{5,7},{6,4},{7,5},{8,10},{9,11},{10,... | collective-permute-start | bytes 49160 | tf_op jit(solution)/shard_map/gradient_exchange/ppermute | solution.py:465
  31.0 3.7 %collective-permute-start.3 = (f32[1,4,32,32]{3,2,1,0:T(8,128)}, f32[1,4,32,32]{3,2,1,0:T(8,128)S(1)}, u32[]{:S(2)}, u32[]{:S(2)}) collective-permute-start(f32[1,4,32,32]{3,2,1,0:T(8,128)} %bitcast.62), channel_id=1, source_target_pairs={{0,1},{1,0},{2,3},{3,2},{4,5},{5,4},{6,7},{7,6},{8,9},{9,8},{10,11... | collective-permute-start | bytes 49160 | tf_op jit(solution)/shard_map/gradient_exchange/ppermute | solution.py:465
  31.0 4.1 %collective-permute-start.5 = (f32[1,4,32,32]{3,2,1,0:T(8,128)}, f32[1,4,32,32]{3,2,1,0:T(8,128)S(1)}, u32[]{:S(2)}, u32[]{:S(2)}) collective-permute-start(f32[1,4,32,32]{3,2,1,0:T(8,128)} %bitcast.63), channel_id=1, source_target_pairs={{0,3},{1,2},{2,1},{3,0},{4,7},{5,6},{6,5},{7,4},{8,11},{9,10},{10,... | collective-permute-start | bytes 49160 | tf_op jit(solution)/shard_map/gradient_exchange/ppermute | solution.py:465
  34.0 1.1 %copy-start.5 = (f32[1,4,32,32]{3,2,1,0:T(8,128)}, f32[1,4,32,32]{3,2,1,0:T(8,128)S(1)}, u32[]{:S(2)}) copy-start(f32[1,4,32,32]{3,2,1,0:T(8,128)S(1)} %collective-permute-done.4.g1_ref) | copy-start | bytes 49156
  34.7 0.6 %copy-start.6 = (f32[1,4,32,32]{3,2,1,0:T(8,128)}, f32[1,4,32,32]{3,2,1,0:T(8,128)S(1)}, u32[]{:S(2)}) copy-start(f32[1,4,32,32]{3,2,1,0:T(8,128)S(1)} %collective-permute-done.3.g0_ref) | copy-start | bytes 49156
  35.1 0.6 %copy-start.7 = (f32[1,4,32,32]{3,2,1,0:T(8,128)}, f32[1,4,32,32]{3,2,1,0:T(8,128)S(1)}, u32[]{:S(2)}) copy-start(f32[1,4,32,32]{3,2,1,0:T(8,128)S(1)} %collective-permute-done.5.g2_ref) | copy-start | bytes 49156
  35.7 5.2 %collective-permute-start.6 = (f32[1,2,32,32]{3,2,1,0:T(8,128)S(1)}, f32[1,2,32,32]{3,2,1,0:T(8,128)S(1)}, u32[]{:S(2)}, u32[]{:S(2)}) collective-permute-start(f32[1,2,32,32]{3,2,1,0:T(8,128)S(1)} %get-tuple-element.8), channel_id=1, source_target_pairs={{0,8},{4,12},{8,0},{12,4},{1,5},{5,1},{9,13},{13,9},{2,10},{6,14},... | collective-permute-start | bytes 24584 | tf_op jit(solution)/shard_map/gradient_exchange/ppermute | solution.py:405
  36.1 4.8 %collective-permute-start.7 = (f32[1,2,32,32]{3,2,1,0:T(8,128)S(1)}, f32[1,2,32,32]{3,2,1,0:T(8,128)S(1)}, u32[]{:S(2)}, u32[]{:S(2)}) collective-permute-start(f32[1,2,32,32]{3,2,1,0:T(8,128)S(1)} %get-tuple-element.9), channel_id=1, source_target_pairs={{1,13},{5,9},{9,5},{13,1},{3,15},{7,11},{11,7},{15,3},{17,29},{21,... | collective-permute-start | bytes 24584 | tf_op jit(solution)/shard_map/gradient_exchange/ppermute | solution.py:405
  40.9 3.5 %copy-start.10 = (f32[1,2,32,32]{3,2,1,0:T(8,128)}, f32[1,2,32,32]{3,2,1,0:T(8,128)S(1)}, u32[]{:S(2)}) copy-start(f32[1,2,32,32]{3,2,1,0:T(8,128)S(1)} %add_add_fusion.refs_0_) | copy-start | bytes 24580
  40.9 3.5 %collective-permute-start.8 = (f32[1,2,32,32]{3,2,1,0:T(8,128)S(1)}, f32[1,2,32,32]{3,2,1,0:T(8,128)S(1)}, u32[]{:S(2)}, u32[]{:S(2)}) collective-permute-start(f32[1,2,32,32]{3,2,1,0:T(8,128)S(1)} %add_add_fusion.refs_0_), channel_id=1, source_target_pairs={{0,1},{1,0},{2,3},{3,2},{4,5},{5,4},{6,7},{7,6},{8,9},{9,8},{10,11... | collective-permute-start | bytes 24584 | tf_op jit(solution)/shard_map/gradient_exchange/ppermute | solution.py:346
  44.4 0.6 %copy-start.11 = (f32[1,2,32,32]{3,2,1,0:T(8,128)}, f32[1,2,32,32]{3,2,1,0:T(8,128)S(1)}, u32[]{:S(2)}) copy-start(f32[1,2,32,32]{3,2,1,0:T(8,128)S(1)} %collective-permute-done.8.refs_1_) | copy-start | bytes 24580

commit v17 on v16

--- a/solution.py
+++ b/solution.py
@@ -126,11 +126,19 @@
     return out + [jnp.asarray(table) for table in (left_three, right_hm, right_lh, rows_three)]
 
 
-def imaging_body(
-    pos_ref, im_ref, sh_ref, w_ref, dose_ref, mask_ref, ev_ref, ev2_ref, own_ref, goal_ref, h_ref, hc_ref,
-    c_re_ref, c_im_ref, ct_re_ref, ct_im_ref, rw_top, rw_bot, rc_ref, la_ref, rhm_ref, rlh_ref, rows_ref,
-    slots_ref, f_buf, i_buf, u_buf, w_buf, xr_buf, xi_buf,
-):
+def imaging_body(*refs, group):
+    if group:
+        pos_ref, im_ref, sh_ref, w_ref, dose_ref, mask_ref = refs[:6]
+        fetched_ref, r1_ref, r2_ref, r3_ref = refs[6:10]
+        rest = refs[10:]
+    else:
+        pos_ref, im_ref, sh_ref, w_ref, dose_ref, mask_ref, ev_ref, ev2_ref = refs[:8]
+        rest = refs[8:]
+    (
+        own_ref, goal_ref, h_ref, hc_ref,
+        c_re_ref, c_im_ref, ct_re_ref, ct_im_ref, rw_top, rw_bot, rc_ref, la_ref, rhm_ref, rlh_ref, rows_ref,
+        slots_ref, f_buf, i_buf, u_buf, w_buf, xr_buf, xi_buf,
+    ) = rest
     count = f_buf.shape[0]
     pos = pos_ref[0]
     master = im_ref[pos]
@@ -144,8 +152,20 @@
     ph_im = e0_re * e1_im + e0_im * e1_re
     local_masters = own_ref.shape[0]
     is_own = master // local_masters == pos_ref[1]
-    m_re = ev_ref[master, 0] + ev2_ref[master, 0] + jnp.where(is_own, own_ref[master % local_masters, 0], 0.0)
-    m_im = ev_ref[master, 1] + ev2_ref[master, 1] + jnp.where(is_own, own_ref[master % local_masters, 1], 0.0)
+    if group:
+        far = jnp.bitwise_xor(master, pos_ref[1])
+        step = jnp.bitwise_xor(lax.axis_index("corner") * 2 + lax.axis_index("kern"), far)
+
+        def choose(c):
+            picked = jnp.where(step == 1, r1_ref[0, c], jnp.where(step == 2, r2_ref[0, c], r3_ref[0, c]))
+            picked = jnp.where(step == 0, fetched_ref[0, c], picked)
+            return jnp.where(far == 0, own_ref[0, c], picked)
+
+        m_re = choose(0)
+        m_im = choose(1)
+    else:
+        m_re = ev_ref[master, 0] + ev2_ref[master, 0] + jnp.where(is_own, own_ref[master % local_masters, 0], 0.0)
+        m_im = ev_ref[master, 1] + ev2_ref[master, 1] + jnp.where(is_own, own_ref[master % local_masters, 1], 0.0)
     mask = mask_ref[pos]
     rows = dot_parts(rows_ref[...], jnp.concatenate([mask, mask, mask], axis=0))
     t_one = dot_full(rows, ct_re_ref[...])
@@ -206,6 +226,7 @@
 
 
 def imaging(pos, inst_master, inst_shift, weights, dose, tile_mask, every, own, target, kerns, h_cat):
+    group = len(every) == 4
     if len(every) == 1:
         every = (every[0], jnp.zeros_like(every[0]))
     count = weights.shape[0]
@@ -213,9 +234,9 @@
     vmem = pl.BlockSpec(memory_space=pltpu.VMEM)
     smem = pl.BlockSpec(memory_space=pltpu.SMEM)
     return pl.pallas_call(
-        imaging_body,
+        functools.partial(imaging_body, group=group),
         out_shape=jax.ShapeDtypeStruct((4, B, B), jnp.float32),
-        in_specs=[smem] * 5 + [vmem] * 7 + [vmem] * len(tables),
+        in_specs=[smem] * 5 + [vmem] * (5 + len(every)) + [vmem] * len(tables),
         out_specs=vmem,
         scratch_shapes=[
             pltpu.VMEM((count, P_SIZE, 2 * P_SIZE), jnp.float32),
@@ -427,7 +448,16 @@
     with jax.named_scope("master_spectra"):
         own_re, own_im = spectra(master_mask.astype(jnp.float32), cos_tab, sin_tab)
         own = jnp.stack([own_re, own_im], axis=1)
-        if xor_partners(tile_count) and xor_partners(kern_count) and tile_count > 2:
+        corner_count = lax.axis_size("corner")
+        if tile_count == 4 and corner_count == 2 and kern_count == 2 and local_masters == 1:
+            pairs = [((t ^ g) * 4 + g, t * 4 + g) for t in range(4) for g in range(1, 4)]
+            fetched = lax.ppermute(own, ("tile", "corner", "kern"), pairs)
+            every = (fetched,) + tuple(
+                lax.ppermute(fetched, ("corner", "kern"), [(i, i ^ step) for i in range(4)])
+                for step in (1, 2, 3)
+            )
+            own_part = own
+        elif xor_partners(tile_count) and xor_partners(kern_count) and tile_count > 2:
             every = gather_split(own, tile_count, tile_pos, kern_count, kern_pos)
             own_part = own
         else:

time: 47.7 us -> 51.4 us (1.078)
  starting transfers between devices: 12.6 us -> 15.2 us
  waiting for transfers between devices: 4.02 us -> 6.03 us
  local copies, waits for them, and re-layouts: 4.17 us -> 3.47 us
    ppermute x2 -> x4, starting transfers between devices: 4.75 us -> 8.01 us  [the longest x3 7.34 us: on_device(): lax.ppermute(fetched, ('corner', 'kern'), [(i, i ^ step) for i in range(4)])]
    ppermute x2 -> x1, starting transfers between devices: 4.68 us -> 2.31 us  [sum_parts(): return (x, lax.ppermute(x, axis, [(0, 1), (1, 0)]))]
    ppermute x2 -> x4, waiting for transfers between devices: 0.01 us -> 2.26 us  [the longest x3 2.26 us: on_device(): lax.ppermute(fetched, ('corner', 'kern'), [(i, i ^ step) for i in range(4)])]
    ppermute x2, starting transfers between devices: 1.06 us -> 2.71 us  [scatter_split(): total = total + lax.ppermute(part, ('tile', 'kern'), pairs)]
    unnamed x28 -> x32, local copies, waits for them, and re-layouts: 3.83 us -> 3.13 us
  transfers between devices with their start and end apart: 9 -> 10, of which waited for: 4 -> 4; matrix products, arithmetic and copies ran while one was open for 6% -> 6% of each run, Pallas kernels for 6% -> 6%
where the time goes in v17:
time: 51.4 us; the launch traced here: 51.1 us
  Pallas kernels  20.5 us (40%)
  starting transfers between devices  15.2 us (30%)
  waiting for transfers between devices  6.03 us (12%)
  local copies, waits for them, and re-layouts  3.47 us (7%)
  other arithmetic  2.65 us (5%)
  between operations  2.24 us (4%)
  matrix products  1.03 us (2%)
    pallas_call x1, Pallas kernels, imaging(): pl.pallas_call(functools.partial(imaging_body, group=group), out_shape=ja...  15.2 us
    ppermute x3, starting transfers between devices, on_device(): lax.ppermute(fetched, ('corner', 'kern'), [(i, i ^ step) for i in range(4)])  7.34 us
    unnamed x32, local copies, waits for them, and re-layouts  3.13 us
    pallas_call x1, Pallas kernels, group_pixels(): pl.pallas_call(group_pixel_body, out_shape=(shape, jax.ShapeDtypeStruct((...  2.98 us
    ppermute x3, waiting for transfers between devices, on_device(): lax.ppermute(comp, ('corner', 'kern'), [(i, i ^ step) for i in range(4)])  2.9 us
    ppermute x2, starting transfers between devices, scatter_split(): total = total + lax.ppermute(part, ('tile', 'kern'), pairs)  2.71 us
    ppermute x1, starting transfers between devices, sum_parts(): return (x, lax.ppermute(x, axis, [(0, 1), (1, 0)]))  2.31 us
    pallas_call x1, Pallas kernels, pixels(): pl.pallas_call(functools.partial(pixel_body, passes=False), out_shape=sha...  2.31 us
  transfers between devices with their start and end apart: 10, of which 4 were waited for; matrix products, arithmetic and copies ran while one was open for 6% of the time, Pallas kernels for 6%

profile of v17, /device:TPU:0, one launch (start us, length us, event | category | flops | bytes accessed | tf_op | source)
XLA Modules:
  0.0 51.1 jit_solution(712294030159061407)
XLA Ops:
  0.7 0.9 %copy-done = bf16[1,256,256]{2,1,0:T(8,128)(2,1)S(1)} copy-done((bf16[1,256,256]{2,1,0:T(8,128)(2,1)S(1)}, bf16[1,256,256]{2,1,0:T(8,128)(2,1)}, u32[]{:S(2)}) %copy-start) | copy-done | bytes 131096
  1.5 0.2 fusion.8
  1.8 0.2 fusion.6
  2.0 0.2 fusion.17
  2.1 0.2 fusion.16
  2.3 0.2 fusion
  2.5 0.2 fusion.1
  2.7 0.7 %collective-permute-start = (f32[1,2,32,32]{3,2,1,0:T(8,128)S(1)}, f32[1,2,32,32]{3,2,1,0:T(8,128)S(1)}, u32[]{:S(2)}, u32[]{:S(2)}) collective-permute-start(f32[1,2,32,32]{3,2,1,0:T(8,128)S(1)} %pad_maximum_fusion.1.refs_10_), channel_id=1, source_target_pairs={{5,1},{10,2},{15,3},{1,5},{14,6},{11,7},{13,9},{2,10},{7,11},{9,13... | collective-permute-start | bytes 24584 | tf_op jit(solution)/shard_map/master_spectra/ppermute | solution.py:454
  3.6 0.1 copy.35
  3.7 0.1 copy.34
  3.8 0.1 copy.32
  3.9 0.5 %copy-done.14 = s32[2]{0:T(128)S(1)} copy-done((s32[2]{0:T(128)S(1)}, s32[2]{0:T(128)}, u32[]{:S(2)}) %copy-start.14) | copy-done | bytes 32
  4.5 0.9 %pad_maximum_fusion = f32[12,32,128]{2,1,0:T(8,128)} fusion(f32[12,32,32]{2,1,0:T(8,128)S(1)} %copy.35, f32[12,32,32]{2,1,0:T(8,128)S(1)} %copy.34, f32[12,32,32]{2,1,0:T(8,128)S(1)} %copy.32), kind=kLoop, calls=%fused_computation.10 | loop fusion | flops 147456 | bytes 344064 | tf_op jit(solution)/shard_map/imaging_kernel/concatenate | solution.py:478
  5.4 3.8 %collective-permute-start.1 = (f32[1,2,32,32]{3,2,1,0:T(8,128)S(1)}, f32[1,2,32,32]{3,2,1,0:T(8,128)S(1)}, u32[]{:S(2)}, u32[]{:S(2)}) collective-permute-start(f32[1,2,32,32]{3,2,1,0:T(8,128)S(1)} %collective-permute-done.refs_6_), channel_id=1, source_target_pairs={{0,1},{1,0},{2,3},{3,2},{4,5},{5,4},{6,7},{7,6},{8,9},{9,8},{10,11... | collective-permute-start | bytes 24584 | tf_op jit(solution)/shard_map/master_spectra/ppermute | solution.py:456
  9.3 3.5 %collective-permute-start.2 = (f32[1,2,32,32]{3,2,1,0:T(8,128)S(1)}, f32[1,2,32,32]{3,2,1,0:T(8,128)S(1)}, u32[]{:S(2)}, u32[]{:S(2)}) collective-permute-start(f32[1,2,32,32]{3,2,1,0:T(8,128)S(1)} %collective-permute-done.refs_6_), channel_id=1, source_target_pairs={{0,2},{1,3},{2,0},{3,1},{4,6},{5,7},{6,4},{7,5},{8,10},{9,11},{10,... | collective-permute-start | bytes 24584 | tf_op jit(solution)/shard_map/master_spectra/ppermute | solution.py:456
  12.8 0.6 %pad_add_fusion.refs_0_ = s32[2]{0:T(128)} fusion(s32[1]{0:T(128)} %bitcast.1, s32[1]{0:T(128)} %bitcast), kind=kLoop, calls=%fused_computation.29 | loop fusion | flops 2 | bytes 16 | tf_op jit(solution)/shard_map/imaging_kernel/stack | solution.py:481
  14.1 0.6 %collective-permute-done.2.refs_8_ = f32[1,2,32,32]{3,2,1,0:T(8,128)S(1)} collective-permute-done((f32[1,2,32,32]{3,2,1,0:T(8,128)S(1)}, f32[1,2,32,32]{3,2,1,0:T(8,128)S(1)}, u32[]{:S(2)}, u32[]{:S(2)}) %collective-permute-start.2) | collective-permute-done | bytes 8224 | tf_op jit(solution)/shard_map/master_spectra/ppermute | solution.py:456
  14.7 1.7 %collective-permute-done.3.refs_9_ = f32[1,2,32,32]{3,2,1,0:T(8,128)S(1)} collective-permute-done((f32[1,2,32,32]{3,2,1,0:T(8,128)S(1)}, f32[1,2,32,32]{3,2,1,0:T(8,128)S(1)}, u32[]{:S(2)}, u32[]{:S(2)}) %collective-permute-start.3) | collective-permute-done | bytes 8224 | tf_op jit(solution)/shard_map/master_spectra/ppermute | solution.py:456
  16.4 0.6 %copy-done.12 = f32[1,2,32,32]{3,2,1,0:T(8,128)} copy-done((f32[1,2,32,32]{3,2,1,0:T(8,128)}, f32[1,2,32,32]{3,2,1,0:T(8,128)S(1)}, u32[]{:S(2)}) %copy-start.12) | copy-done | bytes 8216
  16.9 15.2 %imaging_kernel.1 = f32[4,32,32]{2,1,0:T(8,128)} custom-call(s32[2]{0:T(128)} %pad_add_fusion.refs_0_, s32[2]{0:T(128)} %refs_1_.1, s32[2,2]{1,0:T(2,128)} %refs_2_.2, f32[12]{0:T(128)} %bitcast.64, f32[1]{0:T(128)S(6)} %copy.37.refs_4_, bf16[2,256,256]{2,1,0:T(8,128)(2,1)} %refs_5_.1, f32[1,2,32,32]{3,2,1,0:T(8,128)} %copy-done.9, ...), custom_call_target="tpu_custom_call" | custom-call | tf_op jit(solution)/shard_map/imaging_kernel/pallas_call | solution.py:236
  32.1 0.4 collective-permute-start.5
  32.5 1.8 %collective-permute-start.6 = (f32[1,4,32,32]{3,2,1,0:T(8,128)}, f32[1,4,32,32]{3,2,1,0:T(8,128)S(1)}, u32[]{:S(2)}, u32[]{:S(2)}) collective-permute-start(f32[1,4,32,32]{3,2,1,0:T(8,128)} %bitcast.61), channel_id=1, source_target_pairs={{0,3},{1,2},{2,1},{3,0},{4,7},{5,6},{6,5},{7,4},{8,11},{9,10},{10,... | collective-permute-start | bytes 49160 | tf_op jit(solution)/shard_map/gradient_exchange/ppermute | solution.py:495
  34.3 2.9 %collective-permute-done.5.g1_ref = f32[1,4,32,32]{3,2,1,0:T(8,128)S(1)} collective-permute-done((f32[1,4,32,32]{3,2,1,0:T(8,128)}, f32[1,4,32,32]{3,2,1,0:T(8,128)S(1)}, u32[]{:S(2)}, u32[]{:S(2)}) %collective-permute-start.5) | collective-permute-done | bytes 16416 | tf_op jit(solution)/shard_map/gradient_exchange/ppermute | solution.py:495
  37.2 0.8 %fusion.11 = f32[2,32,32]{2,1,0:T(8,128)S(1)} fusion(f32[1,4,32,32]{3,2,1,0:T(8,128)S(1)} %collective-permute-done.5.g1_ref, f32[1,4,32,32]{3,2,1,0:T(8,128)} %bitcast.62), kind=kLoop, calls=%fused_computation.19 | loop fusion | flops 2048 | bytes 24576 | tf_op jit(solution)/shard_map/gradient_exchange/mul | solution.py:514
  38.1 0.5 copy-done.5
  38.6 0.7 %collective-permute-start.8 = (f32[1,2,32,32]{3,2,1,0:T(8,128)S(1)}, f32[1,2,32,32]{3,2,1,0:T(8,128)S(1)}, u32[]{:S(2)}, u32[]{:S(2)}) collective-permute-start(f32[1,2,32,32]{3,2,1,0:T(8,128)S(1)} %get-tuple-element.9), channel_id=1, source_target_pairs={{1,13},{5,9},{9,5},{13,1},{3,15},{7,11},{11,7},{15,3},{17,29},{21,... | collective-permute-start | bytes 24584 | tf_op jit(solution)/shard_map/gradient_exchange/ppermute | solution.py:426
  39.3 2.0 %collective-permute-start.7 = (f32[1,2,32,32]{3,2,1,0:T(8,128)S(1)}, f32[1,2,32,32]{3,2,1,0:T(8,128)S(1)}, u32[]{:S(2)}, u32[]{:S(2)}) collective-permute-start(f32[1,2,32,32]{3,2,1,0:T(8,128)S(1)} %get-tuple-element.8), channel_id=1, source_target_pairs={{0,8},{4,12},{8,0},{12,4},{1,5},{5,1},{9,13},{13,9},{2,10},{6,14},... | collective-permute-start | bytes 24584 | tf_op jit(solution)/shard_map/gradient_exchange/ppermute | solution.py:426
  41.3 3.0 %gradient_exchange.1 = (f32[2,256,256]{2,1,0:T(8,128)}, f32[1,1,1,1]{3,2,1,0:T(1,128)}) custom-call(f32[1,4,32,32]{3,2,1,0:T(8,128)} %bitcast.63, f32[1,4,32,32]{3,2,1,0:T(8,128)} %copy-done.5, f32[1,4,32,32]{3,2,1,0:T(8,128)} %copy-done.4, f32[1,4,32,32]{3,2,1,0:T(8,128)} %copy-done.6, f32[32,256]{1,0:T(8,128)} %constant.51.clone.refs_14_.c_re_ref.refs_2_, ...), custom_call_target="tpu_custom_call" | custom-call | tf_op jit(solution)/shard_map/gradient_exchange/pallas_call | solution.py:304
  45.0 2.3 %collective-permute-start.9 = (f32[1,2,32,32]{3,2,1,0:T(8,128)S(1)}, f32[1,2,32,32]{3,2,1,0:T(8,128)S(1)}, u32[]{:S(2)}, u32[]{:S(2)}) collective-permute-start(f32[1,2,32,32]{3,2,1,0:T(8,128)S(1)} %add_add_fusion.refs_0_), channel_id=1, source_target_pairs={{0,1},{1,0},{2,3},{3,2},{4,5},{5,4},{6,7},{7,6},{8,9},{9,8},{10,11... | collective-permute-start | bytes 24584 | tf_op jit(solution)/shard_map/gradient_exchange/ppermute | solution.py:367
  47.3 0.9 %collective-permute-done.9.refs_1_ = f32[1,2,32,32]{3,2,1,0:T(8,128)S(1)} collective-permute-done((f32[1,2,32,32]{3,2,1,0:T(8,128)S(1)}, f32[1,2,32,32]{3,2,1,0:T(8,128)S(1)}, u32[]{:S(2)}, u32[]{:S(2)}) %collective-permute-start.9) | collective-permute-done | bytes 8224 | tf_op jit(solution)/shard_map/gradient_exchange/ppermute | solution.py:367
  48.2 0.6 %copy-done.13 = f32[1,2,32,32]{3,2,1,0:T(8,128)} copy-done((f32[1,2,32,32]{3,2,1,0:T(8,128)}, f32[1,2,32,32]{3,2,1,0:T(8,128)S(1)}, u32[]{:S(2)}) %copy-start.13) | copy-done | bytes 8216
  48.8 2.3 %pixel_gradients.1 = f32[1,256,256]{2,1,0:T(8,128)} custom-call(f32[1,2,32,32]{3,2,1,0:T(8,128)} %copy-done.8, f32[1,2,32,32]{3,2,1,0:T(8,128)} %copy-done.13, f32[32,256]{1,0:T(8,128)} %constant.51.clone.refs_14_.c_re_ref.refs_2_, f32[32,256]{1,0:T(8,128)} %constant.52.clone.refs_15_.c_im_ref.refs_3_, bf16[256,384]{1,0:T(8,128)(2,1)} %constant.62.clone.left_ref.refs_4_), custom_call_target="tpu_custom_call" | custom-call | tf_op jit(solution)/shard_map/pixel_gradients/pallas_call | solution.py:324
  (45 shorter events, 0.5 us)
Async XLA Ops:
  0.6 0.9 %copy-start = (bf16[1,256,256]{2,1,0:T(8,128)(2,1)S(1)}, bf16[1,256,256]{2,1,0:T(8,128)(2,1)}, u32[]{:S(2)}) copy-start(bf16[1,256,256]{2,1,0:T(8,128)(2,1)} %param.28) | copy-start | bytes 393220
  0.6 0.9 %copy-start.2 = (f32[32,256]{1,0:T(8,128)S(1)}, f32[32,256]{1,0:T(8,128)}, u32[]{:S(2)}) copy-start(f32[32,256]{1,0:T(8,128)} %constant.51.clone.refs_14_.c_re_ref.refs_2_) | copy-start | bytes 98308
  0.7 1.1 %copy-start.3 = (f32[32,256]{1,0:T(8,128)S(1)}, f32[32,256]{1,0:T(8,128)}, u32[]{:S(2)}) copy-start(f32[32,256]{1,0:T(8,128)} %constant.52.clone.refs_15_.c_im_ref.refs_3_) | copy-start | bytes 98308
  0.7 2.7 %copy-start.1 = (f32[1,12,2,32,32]{4,3,2,1,0:T(8,128)S(1)}, f32[1,12,2,32,32]{4,3,2,1,0:T(8,128)}, u32[]{:S(2)}) copy-start(f32[1,12,2,32,32]{4,3,2,1,0:T(8,128)} %param.32) | copy-start | bytes 294916
  2.6 0.7 %copy-start.15 = (f32[1,12]{1,0:T(1,128)S(1)}, f32[1,12]{1,0:T(1,128)}, u32[]{:S(2)}) copy-start(f32[1,12]{1,0:T(1,128)} %param.33) | copy-start | bytes 148
  2.7 0.8 %copy-start.7 = (f32[1,2,32,32]{3,2,1,0:T(8,128)}, f32[1,2,32,32]{3,2,1,0:T(8,128)S(1)}, u32[]{:S(2)}) copy-start(f32[1,2,32,32]{3,2,1,0:T(8,128)S(1)} %pad_maximum_fusion.1.refs_10_) | copy-start | bytes 24580
  2.7 2.8 %collective-permute-start = (f32[1,2,32,32]{3,2,1,0:T(8,128)S(1)}, f32[1,2,32,32]{3,2,1,0:T(8,128)S(1)}, u32[]{:S(2)}, u32[]{:S(2)}) collective-permute-start(f32[1,2,32,32]{3,2,1,0:T(8,128)S(1)} %pad_maximum_fusion.1.refs_10_), channel_id=1, source_target_pairs={{5,1},{10,2},{15,3},{1,5},{14,6},{11,7},{13,9},{2,10},{7,11},{9,13... | collective-permute-start | bytes 24584 | tf_op jit(solution)/shard_map/master_spectra/ppermute | solution.py:454
  3.8 0.7 %copy-start.14 = (s32[2]{0:T(128)S(1)}, s32[2]{0:T(128)}, u32[]{:S(2)}) copy-start(s32[2]{0:T(128)} %refs_1_.1) | copy-start | bytes 28
  5.4 10.9 %copy-start.9 = (f32[1,2,32,32]{3,2,1,0:T(8,128)}, f32[1,2,32,32]{3,2,1,0:T(8,128)S(1)}, u32[]{:S(2)}) copy-start(f32[1,2,32,32]{3,2,1,0:T(8,128)S(1)} %collective-permute-done.refs_6_) | copy-start | bytes 24580
  5.4 8.6 %collective-permute-start.1 = (f32[1,2,32,32]{3,2,1,0:T(8,128)S(1)}, f32[1,2,32,32]{3,2,1,0:T(8,128)S(1)}, u32[]{:S(2)}, u32[]{:S(2)}) collective-permute-start(f32[1,2,32,32]{3,2,1,0:T(8,128)S(1)} %collective-permute-done.refs_6_), channel_id=1, source_target_pairs={{0,1},{1,0},{2,3},{3,2},{4,5},{5,4},{6,7},{7,6},{8,9},{9,8},{10,11... | collective-permute-start | bytes 24584 | tf_op jit(solution)/shard_map/master_spectra/ppermute | solution.py:456
  9.3 5.4 %collective-permute-start.2 = (f32[1,2,32,32]{3,2,1,0:T(8,128)S(1)}, f32[1,2,32,32]{3,2,1,0:T(8,128)S(1)}, u32[]{:S(2)}, u32[]{:S(2)}) collective-permute-start(f32[1,2,32,32]{3,2,1,0:T(8,128)S(1)} %collective-permute-done.refs_6_), channel_id=1, source_target_pairs={{0,2},{1,3},{2,0},{3,1},{4,6},{5,7},{6,4},{7,5},{8,10},{9,11},{10,... | collective-permute-start | bytes 24584 | tf_op jit(solution)/shard_map/master_spectra/ppermute | solution.py:456
  12.8 3.6 %collective-permute-start.3 = (f32[1,2,32,32]{3,2,1,0:T(8,128)S(1)}, f32[1,2,32,32]{3,2,1,0:T(8,128)S(1)}, u32[]{:S(2)}, u32[]{:S(2)}) collective-permute-start(f32[1,2,32,32]{3,2,1,0:T(8,128)S(1)} %collective-permute-done.refs_6_), channel_id=1, source_target_pairs={{0,3},{1,2},{2,1},{3,0},{4,7},{5,6},{6,5},{7,4},{8,11},{9,10},{10,... | collective-permute-start | bytes 24584 | tf_op jit(solution)/shard_map/master_spectra/ppermute | solution.py:456
  14.1 2.3 %copy-start.10 = (f32[1,2,32,32]{3,2,1,0:T(8,128)}, f32[1,2,32,32]{3,2,1,0:T(8,128)S(1)}, u32[]{:S(2)}) copy-start(f32[1,2,32,32]{3,2,1,0:T(8,128)S(1)} %collective-permute-done.1.refs_7_) | copy-start | bytes 24580
  14.7 1.7 %copy-start.11 = (f32[1,2,32,32]{3,2,1,0:T(8,128)}, f32[1,2,32,32]{3,2,1,0:T(8,128)S(1)}, u32[]{:S(2)}) copy-start(f32[1,2,32,32]{3,2,1,0:T(8,128)S(1)} %collective-permute-done.2.refs_8_) | copy-start | bytes 24580
  16.3 0.6 %copy-start.12 = (f32[1,2,32,32]{3,2,1,0:T(8,128)}, f32[1,2,32,32]{3,2,1,0:T(8,128)S(1)}, u32[]{:S(2)}) copy-start(f32[1,2,32,32]{3,2,1,0:T(8,128)S(1)} %collective-permute-done.3.refs_9_) | copy-start | bytes 24580
  32.1 5.0 %collective-permute-start.5 = (f32[1,4,32,32]{3,2,1,0:T(8,128)}, f32[1,4,32,32]{3,2,1,0:T(8,128)S(1)}, u32[]{:S(2)}, u32[]{:S(2)}) collective-permute-start(f32[1,4,32,32]{3,2,1,0:T(8,128)} %bitcast.59), channel_id=1, source_target_pairs={{0,2},{1,3},{2,0},{3,1},{4,6},{5,7},{6,4},{7,5},{8,10},{9,11},{10,... | collective-permute-start | bytes 49160 | tf_op jit(solution)/shard_map/gradient_exchange/ppermute | solution.py:495
  32.5 5.4 %collective-permute-start.4 = (f32[1,4,32,32]{3,2,1,0:T(8,128)}, f32[1,4,32,32]{3,2,1,0:T(8,128)S(1)}, u32[]{:S(2)}, u32[]{:S(2)}) collective-permute-start(f32[1,4,32,32]{3,2,1,0:T(8,128)} %bitcast.60), channel_id=1, source_target_pairs={{0,1},{1,0},{2,3},{3,2},{4,5},{5,4},{6,7},{7,6},{8,9},{9,8},{10,11... | collective-permute-start | bytes 49160 | tf_op jit(solution)/shard_map/gradient_exchange/ppermute | solution.py:495
  32.5 5.4 %collective-permute-start.6 = (f32[1,4,32,32]{3,2,1,0:T(8,128)}, f32[1,4,32,32]{3,2,1,0:T(8,128)S(1)}, u32[]{:S(2)}, u32[]{:S(2)}) collective-permute-start(f32[1,4,32,32]{3,2,1,0:T(8,128)} %bitcast.61), channel_id=1, source_target_pairs={{0,3},{1,2},{2,1},{3,0},{4,7},{5,6},{6,5},{7,4},{8,11},{9,10},{10,... | collective-permute-start | bytes 49160 | tf_op jit(solution)/shard_map/gradient_exchange/ppermute | solution.py:495
  37.2 0.8 %copy-start.4 = (f32[1,4,32,32]{3,2,1,0:T(8,128)}, f32[1,4,32,32]{3,2,1,0:T(8,128)S(1)}, u32[]{:S(2)}) copy-start(f32[1,4,32,32]{3,2,1,0:T(8,128)S(1)} %collective-permute-done.5.g1_ref) | copy-start | bytes 49156
  38.0 0.6 %copy-start.5 = (f32[1,4,32,32]{3,2,1,0:T(8,128)}, f32[1,4,32,32]{3,2,1,0:T(8,128)S(1)}, u32[]{:S(2)}) copy-start(f32[1,4,32,32]{3,2,1,0:T(8,128)S(1)} %collective-permute-done.4.g0_ref) | copy-start | bytes 49156
  38.0 0.6 %copy-start.6 = (f32[1,4,32,32]{3,2,1,0:T(8,128)}, f32[1,4,32,32]{3,2,1,0:T(8,128)S(1)}, u32[]{:S(2)}) copy-start(f32[1,4,32,32]{3,2,1,0:T(8,128)S(1)} %collective-permute-done.6.g2_ref) | copy-start | bytes 49156
  38.6 6.3 %collective-permute-start.8 = (f32[1,2,32,32]{3,2,1,0:T(8,128)S(1)}, f32[1,2,32,32]{3,2,1,0:T(8,128)S(1)}, u32[]{:S(2)}, u32[]{:S(2)}) collective-permute-start(f32[1,2,32,32]{3,2,1,0:T(8,128)S(1)} %get-tuple-element.9), channel_id=1, source_target_pairs={{1,13},{5,9},{9,5},{13,1},{3,15},{7,11},{11,7},{15,3},{17,29},{21,... | collective-permute-start | bytes 24584 | tf_op jit(solution)/shard_map/gradient_exchange/ppermute | solution.py:426
  39.3 5.7 %collective-permute-start.7 = (f32[1,2,32,32]{3,2,1,0:T(8,128)S(1)}, f32[1,2,32,32]{3,2,1,0:T(8,128)S(1)}, u32[]{:S(2)}, u32[]{:S(2)}) collective-permute-start(f32[1,2,32,32]{3,2,1,0:T(8,128)S(1)} %get-tuple-element.8), channel_id=1, source_target_pairs={{0,8},{4,12},{8,0},{12,4},{1,5},{5,1},{9,13},{13,9},{2,10},{6,14},... | collective-permute-start | bytes 24584 | tf_op jit(solution)/shard_map/gradient_exchange/ppermute | solution.py:426
  45.0 3.2 %copy-start.8 = (f32[1,2,32,32]{3,2,1,0:T(8,128)}, f32[1,2,32,32]{3,2,1,0:T(8,128)S(1)}, u32[]{:S(2)}) copy-start(f32[1,2,32,32]{3,2,1,0:T(8,128)S(1)} %add_add_fusion.refs_0_) | copy-start | bytes 24580
  45.0 3.2 %collective-permute-start.9 = (f32[1,2,32,32]{3,2,1,0:T(8,128)S(1)}, f32[1,2,32,32]{3,2,1,0:T(8,128)S(1)}, u32[]{:S(2)}, u32[]{:S(2)}) collective-permute-start(f32[1,2,32,32]{3,2,1,0:T(8,128)S(1)} %add_add_fusion.refs_0_), channel_id=1, source_target_pairs={{0,1},{1,0},{2,3},{3,2},{4,5},{5,4},{6,7},{7,6},{8,9},{9,8},{10,11... | collective-permute-start | bytes 24584 | tf_op jit(solution)/shard_map/gradient_exchange/ppermute | solution.py:367
  48.2 0.6 %copy-start.13 = (f32[1,2,32,32]{3,2,1,0:T(8,128)}, f32[1,2,32,32]{3,2,1,0:T(8,128)S(1)}, u32[]{:S(2)}) copy-start(f32[1,2,32,32]{3,2,1,0:T(8,128)S(1)} %collective-permute-done.9.refs_1_) | copy-start | bytes 24580

commit v18 on v16

--- a/solution.py
+++ b/solution.py
@@ -121,25 +121,30 @@
     rows_three = np.concatenate(
         [np.concatenate(parts_re, axis=1), np.concatenate(parts_im, axis=1)], axis=0
     )
+    cols_re = np.concatenate(table_three(c_re.T), axis=0)
+    cols_im = np.concatenate(table_three(c_im.T), axis=0)
     plain = (c_re, c_im, c_re.T, c_im.T, right_w[:B], right_w[B : 2 * B], right_c)
     out = [jnp.asarray(table, jnp.float32) for table in plain]
-    return out + [jnp.asarray(table) for table in (left_three, right_hm, right_lh, rows_three)]
+    bf = (left_three, right_hm, right_lh, rows_three, cols_re, cols_im)
+    return out + [jnp.asarray(table) for table in bf]
 
 
 def imaging_body(
     pos_ref, im_ref, sh_ref, w_ref, dose_ref, mask_ref, ev_ref, ev2_ref, own_ref, goal_ref, h_ref, hc_ref,
-    c_re_ref, c_im_ref, ct_re_ref, ct_im_ref, rw_top, rw_bot, rc_ref, la_ref, rhm_ref, rlh_ref, rows_ref,
+    c_re_ref, c_im_ref, ct_re_ref, ct_im_ref, rw_top, rw_bot, rc_ref, la_ref, rhm_ref, rlh_ref, rows_ref, cre_ref, cim_ref,
     slots_ref, f_buf, i_buf, u_buf, w_buf, xr_buf, xi_buf,
 ):
     count = f_buf.shape[0]
     pos = pos_ref[0]
     master = im_ref[pos]
-    pick0 = (lax.broadcasted_iota(jnp.int32, (P_SIZE, 128), 0) == sh_ref[pos, 0]).astype(jnp.float32)
-    pick1 = (lax.broadcasted_iota(jnp.int32, (8, P_SIZE), 1) == sh_ref[pos, 1]).astype(jnp.float32)
-    e0_re = dot_full(c_re_ref[...], pick0)[:, 0:1]
-    e0_im = dot_full(c_im_ref[...], pick0)[:, 0:1]
-    e1_re = dot_full(pick1, ct_re_ref[...])[0:1, :]
-    e1_im = dot_full(pick1, ct_im_ref[...])[0:1, :]
+    pick0 = (lax.broadcasted_iota(jnp.int32, (P_SIZE, 128), 0) == sh_ref[pos, 0]).astype(jnp.bfloat16)
+    pick1 = (lax.broadcasted_iota(jnp.int32, (8, P_SIZE), 1) == sh_ref[pos, 1]).astype(jnp.bfloat16)
+    e0 = dot_parts(rows_ref[...], jnp.concatenate([pick0, pick0, pick0], axis=0))
+    e0_re = e0[:B, 0:1]
+    e0_im = e0[B:, 0:1]
+    pick1 = jnp.concatenate([pick1, pick1, pick1], axis=1)
+    e1_re = dot_parts(pick1, cre_ref[...])[0:1, :]
+    e1_im = dot_parts(pick1, cim_ref[...])[0:1, :]
     ph_re = e0_re * e1_re - e0_im * e1_im
     ph_im = e0_re * e1_im + e0_im * e1_re
     local_masters = own_ref.shape[0]

time: 47.7 us -> 47.6 us (level)
  no operation moved by 1% of the time
where the time goes in v18:
time: 47.6 us; the launch traced here: 47.3 us
  Pallas kernels  20.5 us (43%)
  starting transfers between devices  12.6 us (26%)
  local copies, waits for them, and re-layouts  4.17 us (9%)
  waiting for transfers between devices  4.01 us (8%)
  other arithmetic  2.7 us (6%)
  between operations  2.21 us (5%)
  matrix products  1.03 us (2%)
    pallas_call x1, Pallas kernels, imaging(): pl.pallas_call(imaging_body, out_shape=jax.ShapeDtypeStruct((4, B, B), jn...  15.2 us
    ppermute x2, starting transfers between devices, gather_split(): got = lax.ppermute(x, ('tile', 'kern'), pairs)  4.75 us
    ppermute x2, starting transfers between devices, sum_parts(): return (x, lax.ppermute(x, axis, [(0, 1), (1, 0)]))  4.68 us
    unnamed x28, local copies, waits for them, and re-layouts  3.83 us
    pallas_call x1, Pallas kernels, group_pixels(): pl.pallas_call(group_pixel_body, out_shape=(shape, jax.ShapeDtypeStruct((...  2.99 us
    ppermute x3, waiting for transfers between devices, on_device(): lax.ppermute(comp, ('corner', 'kern'), [(i, i ^ step) for i in range(4)])  2.66 us
    pallas_call x1, Pallas kernels, pixels(): pl.pallas_call(functools.partial(pixel_body, passes=False), out_shape=sha...  2.31 us
    ppermute x3, starting transfers between devices, on_device(): lax.ppermute(comp, ('corner', 'kern'), [(i, i ^ step) for i in range(4)])  2.14 us
  transfers between devices with their start and end apart: 9, of which 4 were waited for; matrix products, arithmetic and copies ran while one was open for 6% of the time, Pallas kernels for 6%

profile of v18, /device:TPU:0, one launch (start us, length us, event | category | flops | bytes accessed | tf_op | source)
XLA Modules:
  0.0 47.3 jit_solution(9649807503097638824)
XLA Ops:
  0.7 0.9 %copy-done = bf16[1,256,256]{2,1,0:T(8,128)(2,1)S(1)} copy-done((bf16[1,256,256]{2,1,0:T(8,128)(2,1)S(1)}, bf16[1,256,256]{2,1,0:T(8,128)(2,1)}, u32[]{:S(2)}) %copy-start) | copy-done | bytes 131096
  1.5 0.2 fusion.8
  1.8 0.2 fusion.6
  2.0 0.2 fusion.17
  2.1 0.2 fusion.16
  2.3 0.2 fusion
  2.5 0.2 fusion.1
  2.7 4.1 %collective-permute-start = (f32[1,2,32,32]{3,2,1,0:T(8,128)S(1)}, f32[1,2,32,32]{3,2,1,0:T(8,128)S(1)}, u32[]{:S(2)}, u32[]{:S(2)}) collective-permute-start(f32[1,2,32,32]{3,2,1,0:T(8,128)S(1)} %pad_maximum_fusion.1.own_ref), channel_id=1, source_target_pairs={{8,0},{12,4},{0,8},{4,12},{5,1},{1,5},{13,9},{9,13},{10,2},{14,6},... | collective-permute-start | bytes 24584 | tf_op jit(solution)/shard_map/master_spectra/ppermute | solution.py:391
  6.8 0.7 %collective-permute-start.1 = (f32[1,2,32,32]{3,2,1,0:T(8,128)S(1)}, f32[1,2,32,32]{3,2,1,0:T(8,128)S(1)}, u32[]{:S(2)}, u32[]{:S(2)}) collective-permute-start(f32[1,2,32,32]{3,2,1,0:T(8,128)S(1)} %pad_maximum_fusion.1.own_ref), channel_id=1, source_target_pairs={{13,1},{9,5},{5,9},{1,13},{15,3},{11,7},{7,11},{3,15},{29,17},{25,... | collective-permute-start | bytes 24584 | tf_op jit(solution)/shard_map/master_spectra/ppermute | solution.py:391
  7.5 0.6 %copy-done.13 = f32[1,12]{1,0:T(1,128)S(1)} copy-done((f32[1,12]{1,0:T(1,128)S(1)}, f32[1,12]{1,0:T(1,128)}, u32[]{:S(2)}) %copy-start.13) | copy-done | bytes 72
  8.3 0.1 copy.36
  8.7 0.5 %copy-done.12 = s32[2]{0:T(128)S(1)} copy-done((s32[2]{0:T(128)S(1)}, s32[2]{0:T(128)}, u32[]{:S(2)}) %copy-start.12) | copy-done | bytes 32
  9.3 0.9 %pad_maximum_fusion = f32[12,32,128]{2,1,0:T(8,128)} fusion(f32[12,32,32]{2,1,0:T(8,128)S(1)} %copy.37, f32[12,32,32]{2,1,0:T(8,128)S(1)} %copy.36, f32[12,32,32]{2,1,0:T(8,128)S(1)} %copy.34), kind=kLoop, calls=%fused_computation.10 | loop fusion | flops 147456 | bytes 344064 | tf_op jit(solution)/shard_map/imaging_kernel/concatenate | solution.py:453
  10.3 2.0 %collective-permute-start.2 = (f32[4,2,32,32]{3,2,1,0:T(8,128)S(1)}, f32[4,2,32,32]{3,2,1,0:T(8,128)S(1)}, u32[]{:S(2)}, u32[]{:S(2)}) collective-permute-start(f32[4,2,32,32]{3,2,1,0:T(8,128)S(1)} %select_add_fusion.ev_ref), channel_id=1, source_target_pairs={{0,1},{1,0},{2,3},{3,2},{4,5},{5,4},{6,7},{7,6},{8,9},{9,8},{10,11... | collective-permute-start | bytes 98312 | tf_op jit(solution)/shard_map/master_spectra/ppermute | solution.py:351
  12.3 0.6 %pad_add_fusion.pos_ref = s32[2]{0:T(128)} fusion(s32[1]{0:T(128)} %bitcast.1, s32[1]{0:T(128)} %bitcast), kind=kLoop, calls=%fused_computation.30 | loop fusion | flops 2 | bytes 16 | tf_op jit(solution)/shard_map/imaging_kernel/stack | solution.py:456
  13.6 0.6 %copy-done.9 = f32[4,2,32,32]{3,2,1,0:T(8,128)} copy-done((f32[4,2,32,32]{3,2,1,0:T(8,128)}, f32[4,2,32,32]{3,2,1,0:T(8,128)S(1)}, u32[]{:S(2)}) %copy-start.9) | copy-done | bytes 32792
  14.2 15.2 %imaging_kernel.1 = f32[4,32,32]{2,1,0:T(8,128)} custom-call(s32[2]{0:T(128)} %pad_add_fusion.pos_ref, s32[2]{0:T(128)} %im_ref.1, s32[2,2]{1,0:T(2,128)} %sh_ref.1, f32[12]{0:T(128)} %bitcast.68, f32[1]{0:T(128)S(6)} %copy.39.dose_ref, bf16[2,256,256]{2,1,0:T(8,128)(2,1)} %mask_ref.1, f32[4,2,32,32]{3,2,1,0:T(8,128)} %copy-done.4, ...), custom_call_target="tpu_custom_call" | custom-call | tf_op jit(solution)/shard_map/imaging_kernel/pallas_call | solution.py:220
  29.5 1.5 %collective-permute-start.4 = (f32[1,4,32,32]{3,2,1,0:T(8,128)}, f32[1,4,32,32]{3,2,1,0:T(8,128)S(1)}, u32[]{:S(2)}, u32[]{:S(2)}) collective-permute-start(f32[1,4,32,32]{3,2,1,0:T(8,128)} %bitcast.61), channel_id=1, source_target_pairs={{0,2},{1,3},{2,0},{3,1},{4,6},{5,7},{6,4},{7,5},{8,10},{9,11},{10,... | collective-permute-start | bytes 49160 | tf_op jit(solution)/shard_map/gradient_exchange/ppermute | solution.py:470
  31.0 0.7 %collective-permute-start.5 = (f32[1,4,32,32]{3,2,1,0:T(8,128)}, f32[1,4,32,32]{3,2,1,0:T(8,128)S(1)}, u32[]{:S(2)}, u32[]{:S(2)}) collective-permute-start(f32[1,4,32,32]{3,2,1,0:T(8,128)} %bitcast.63), channel_id=1, source_target_pairs={{0,3},{1,2},{2,1},{3,0},{4,7},{5,6},{6,5},{7,4},{8,11},{9,10},{10,... | collective-permute-start | bytes 49160 | tf_op jit(solution)/shard_map/gradient_exchange/ppermute | solution.py:470
  31.6 2.3 %collective-permute-done.4.g1_ref = f32[1,4,32,32]{3,2,1,0:T(8,128)S(1)} collective-permute-done((f32[1,4,32,32]{3,2,1,0:T(8,128)}, f32[1,4,32,32]{3,2,1,0:T(8,128)S(1)}, u32[]{:S(2)}, u32[]{:S(2)}) %collective-permute-start.4) | collective-permute-done | bytes 16416 | tf_op jit(solution)/shard_map/gradient_exchange/ppermute | solution.py:470
  33.9 0.8 %fusion.11 = f32[2,32,32]{2,1,0:T(8,128)S(1)} fusion(f32[1,4,32,32]{3,2,1,0:T(8,128)S(1)} %collective-permute-done.4.g1_ref, f32[1,4,32,32]{3,2,1,0:T(8,128)} %bitcast.64), kind=kLoop, calls=%fused_computation.20 | loop fusion | flops 2048 | bytes 24576 | tf_op jit(solution)/shard_map/gradient_exchange/mul | solution.py:489
  34.7 0.3 collective-permute-done.5.g2_ref
  35.2 0.2 copy-done.6
  35.3 0.3 copy-done.7
  35.7 0.4 collective-permute-start.6
  36.1 0.7 %collective-permute-start.7 = (f32[1,2,32,32]{3,2,1,0:T(8,128)S(1)}, f32[1,2,32,32]{3,2,1,0:T(8,128)S(1)}, u32[]{:S(2)}, u32[]{:S(2)}) collective-permute-start(f32[1,2,32,32]{3,2,1,0:T(8,128)S(1)} %get-tuple-element.9), channel_id=1, source_target_pairs={{1,13},{5,9},{9,5},{13,1},{3,15},{7,11},{11,7},{15,3},{17,29},{21,... | collective-permute-start | bytes 24584 | tf_op jit(solution)/shard_map/gradient_exchange/ppermute | solution.py:410
  36.7 3.0 %gradient_exchange.1 = (f32[2,256,256]{2,1,0:T(8,128)}, f32[1,1,1,1]{3,2,1,0:T(1,128)}) custom-call(f32[1,4,32,32]{3,2,1,0:T(8,128)} %bitcast.65, f32[1,4,32,32]{3,2,1,0:T(8,128)} %copy-done.6, f32[1,4,32,32]{3,2,1,0:T(8,128)} %copy-done.5, f32[1,4,32,32]{3,2,1,0:T(8,128)} %copy-done.7, f32[32,256]{1,0:T(8,128)} %constant.67.clone.c_re_ref.refs_2_, ...), custom_call_target="tpu_custom_call" | custom-call | tf_op jit(solution)/shard_map/gradient_exchange/pallas_call | solution.py:288
  40.4 0.5 %collective-permute-done.6 = f32[1,2,32,32]{3,2,1,0:T(8,128)S(1)} collective-permute-done((f32[1,2,32,32]{3,2,1,0:T(8,128)S(1)}, f32[1,2,32,32]{3,2,1,0:T(8,128)S(1)}, u32[]{:S(2)}, u32[]{:S(2)}) %collective-permute-start.6) | collective-permute-done | bytes 8224 | tf_op jit(solution)/shard_map/gradient_exchange/ppermute | solution.py:410
  40.9 2.6 %collective-permute-start.8 = (f32[1,2,32,32]{3,2,1,0:T(8,128)S(1)}, f32[1,2,32,32]{3,2,1,0:T(8,128)S(1)}, u32[]{:S(2)}, u32[]{:S(2)}) collective-permute-start(f32[1,2,32,32]{3,2,1,0:T(8,128)S(1)} %add_add_fusion.refs_0_), channel_id=1, source_target_pairs={{0,1},{1,0},{2,3},{3,2},{4,5},{5,4},{6,7},{7,6},{8,9},{9,8},{10,11... | collective-permute-start | bytes 24584 | tf_op jit(solution)/shard_map/gradient_exchange/ppermute | solution.py:351
  43.5 0.9 %collective-permute-done.8.refs_1_ = f32[1,2,32,32]{3,2,1,0:T(8,128)S(1)} collective-permute-done((f32[1,2,32,32]{3,2,1,0:T(8,128)S(1)}, f32[1,2,32,32]{3,2,1,0:T(8,128)S(1)}, u32[]{:S(2)}, u32[]{:S(2)}) %collective-permute-start.8) | collective-permute-done | bytes 8224 | tf_op jit(solution)/shard_map/gradient_exchange/ppermute | solution.py:351
  44.4 0.6 %copy-done.11 = f32[1,2,32,32]{3,2,1,0:T(8,128)} copy-done((f32[1,2,32,32]{3,2,1,0:T(8,128)}, f32[1,2,32,32]{3,2,1,0:T(8,128)S(1)}, u32[]{:S(2)}) %copy-start.11) | copy-done | bytes 8216
  45.0 2.3 %pixel_gradients.1 = f32[1,256,256]{2,1,0:T(8,128)} custom-call(f32[1,2,32,32]{3,2,1,0:T(8,128)} %copy-done.10, f32[1,2,32,32]{3,2,1,0:T(8,128)} %copy-done.11, f32[32,256]{1,0:T(8,128)} %constant.67.clone.c_re_ref.refs_2_, f32[32,256]{1,0:T(8,128)} %constant.68.clone.c_im_ref.refs_3_, bf16[256,384]{1,0:T(8,128)(2,1)} %constant.80.clone.left_ref.refs_4_), custom_call_target="tpu_custom_call" | custom-call | tf_op jit(solution)/shard_map/pixel_gradients/pallas_call | solution.py:308
  (41 shorter events, 0.8 us)
Async XLA Ops:
  0.6 0.9 %copy-start = (bf16[1,256,256]{2,1,0:T(8,128)(2,1)S(1)}, bf16[1,256,256]{2,1,0:T(8,128)(2,1)}, u32[]{:S(2)}) copy-start(bf16[1,256,256]{2,1,0:T(8,128)(2,1)} %param.30) | copy-start | bytes 393220
  0.6 0.9 %copy-start.2 = (f32[32,256]{1,0:T(8,128)S(1)}, f32[32,256]{1,0:T(8,128)}, u32[]{:S(2)}) copy-start(f32[32,256]{1,0:T(8,128)} %constant.67.clone.c_re_ref.refs_2_) | copy-start | bytes 98308
  0.7 1.1 %copy-start.3 = (f32[32,256]{1,0:T(8,128)S(1)}, f32[32,256]{1,0:T(8,128)}, u32[]{:S(2)}) copy-start(f32[32,256]{1,0:T(8,128)} %constant.68.clone.c_im_ref.refs_3_) | copy-start | bytes 98308
  0.7 7.4 %copy-start.1 = (f32[1,12,2,32,32]{4,3,2,1,0:T(8,128)S(1)}, f32[1,12,2,32,32]{4,3,2,1,0:T(8,128)}, u32[]{:S(2)}) copy-start(f32[1,12,2,32,32]{4,3,2,1,0:T(8,128)} %param.34) | copy-start | bytes 294916
  2.6 5.6 %copy-start.8 = (f32[1,2,32,32]{3,2,1,0:T(8,128)}, f32[1,2,32,32]{3,2,1,0:T(8,128)S(1)}, u32[]{:S(2)}) copy-start(f32[1,2,32,32]{3,2,1,0:T(8,128)S(1)} %pad_maximum_fusion.1.own_ref) | copy-start | bytes 24580
  2.7 7.5 %collective-permute-start = (f32[1,2,32,32]{3,2,1,0:T(8,128)S(1)}, f32[1,2,32,32]{3,2,1,0:T(8,128)S(1)}, u32[]{:S(2)}, u32[]{:S(2)}) collective-permute-start(f32[1,2,32,32]{3,2,1,0:T(8,128)S(1)} %pad_maximum_fusion.1.own_ref), channel_id=1, source_target_pairs={{8,0},{12,4},{0,8},{4,12},{5,1},{1,5},{13,9},{9,13},{10,2},{14,6},... | collective-permute-start | bytes 24584 | tf_op jit(solution)/shard_map/master_spectra/ppermute | solution.py:391
  6.8 3.4 %collective-permute-start.1 = (f32[1,2,32,32]{3,2,1,0:T(8,128)S(1)}, f32[1,2,32,32]{3,2,1,0:T(8,128)S(1)}, u32[]{:S(2)}, u32[]{:S(2)}) collective-permute-start(f32[1,2,32,32]{3,2,1,0:T(8,128)S(1)} %pad_maximum_fusion.1.own_ref), channel_id=1, source_target_pairs={{13,1},{9,5},{5,9},{1,13},{15,3},{11,7},{7,11},{3,15},{29,17},{25,... | collective-permute-start | bytes 24584 | tf_op jit(solution)/shard_map/master_spectra/ppermute | solution.py:391
  7.4 0.7 %copy-start.13 = (f32[1,12]{1,0:T(1,128)S(1)}, f32[1,12]{1,0:T(1,128)}, u32[]{:S(2)}) copy-start(f32[1,12]{1,0:T(1,128)} %param.35) | copy-start | bytes 148
  8.5 0.7 %copy-start.12 = (s32[2]{0:T(128)S(1)}, s32[2]{0:T(128)}, u32[]{:S(2)}) copy-start(s32[2]{0:T(128)} %im_ref.1) | copy-start | bytes 28
  10.3 3.3 %copy-start.4 = (f32[4,2,32,32]{3,2,1,0:T(8,128)}, f32[4,2,32,32]{3,2,1,0:T(8,128)S(1)}, u32[]{:S(2)}) copy-start(f32[4,2,32,32]{3,2,1,0:T(8,128)S(1)} %select_add_fusion.ev_ref) | copy-start | bytes 98308
  10.3 3.3 %collective-permute-start.2 = (f32[4,2,32,32]{3,2,1,0:T(8,128)S(1)}, f32[4,2,32,32]{3,2,1,0:T(8,128)S(1)}, u32[]{:S(2)}, u32[]{:S(2)}) collective-permute-start(f32[4,2,32,32]{3,2,1,0:T(8,128)S(1)} %select_add_fusion.ev_ref), channel_id=1, source_target_pairs={{0,1},{1,0},{2,3},{3,2},{4,5},{5,4},{6,7},{7,6},{8,9},{9,8},{10,11... | collective-permute-start | bytes 98312 | tf_op jit(solution)/shard_map/master_spectra/ppermute | solution.py:351
  13.6 0.6 %copy-start.9 = (f32[4,2,32,32]{3,2,1,0:T(8,128)}, f32[4,2,32,32]{3,2,1,0:T(8,128)S(1)}, u32[]{:S(2)}) copy-start(f32[4,2,32,32]{3,2,1,0:T(8,128)S(1)} %collective-permute-done.2.ev2_ref) | copy-start | bytes 98308
  29.5 4.5 %collective-permute-start.4 = (f32[1,4,32,32]{3,2,1,0:T(8,128)}, f32[1,4,32,32]{3,2,1,0:T(8,128)S(1)}, u32[]{:S(2)}, u32[]{:S(2)}) collective-permute-start(f32[1,4,32,32]{3,2,1,0:T(8,128)} %bitcast.61), channel_id=1, source_target_pairs={{0,2},{1,3},{2,0},{3,1},{4,6},{5,7},{6,4},{7,5},{8,10},{9,11},{10,... | collective-permute-start | bytes 49160 | tf_op jit(solution)/shard_map/gradient_exchange/ppermute | solution.py:470
  31.0 3.8 %collective-permute-start.3 = (f32[1,4,32,32]{3,2,1,0:T(8,128)}, f32[1,4,32,32]{3,2,1,0:T(8,128)S(1)}, u32[]{:S(2)}, u32[]{:S(2)}) collective-permute-start(f32[1,4,32,32]{3,2,1,0:T(8,128)} %bitcast.62), channel_id=1, source_target_pairs={{0,1},{1,0},{2,3},{3,2},{4,5},{5,4},{6,7},{7,6},{8,9},{9,8},{10,11... | collective-permute-start | bytes 49160 | tf_op jit(solution)/shard_map/gradient_exchange/ppermute | solution.py:470
  31.0 4.1 %collective-permute-start.5 = (f32[1,4,32,32]{3,2,1,0:T(8,128)}, f32[1,4,32,32]{3,2,1,0:T(8,128)S(1)}, u32[]{:S(2)}, u32[]{:S(2)}) collective-permute-start(f32[1,4,32,32]{3,2,1,0:T(8,128)} %bitcast.63), channel_id=1, source_target_pairs={{0,3},{1,2},{2,1},{3,0},{4,7},{5,6},{6,5},{7,4},{8,11},{9,10},{10,... | collective-permute-start | bytes 49160 | tf_op jit(solution)/shard_map/gradient_exchange/ppermute | solution.py:470
  33.9 1.1 %copy-start.5 = (f32[1,4,32,32]{3,2,1,0:T(8,128)}, f32[1,4,32,32]{3,2,1,0:T(8,128)S(1)}, u32[]{:S(2)}) copy-start(f32[1,4,32,32]{3,2,1,0:T(8,128)S(1)} %collective-permute-done.4.g1_ref) | copy-start | bytes 49156
  34.7 0.6 %copy-start.6 = (f32[1,4,32,32]{3,2,1,0:T(8,128)}, f32[1,4,32,32]{3,2,1,0:T(8,128)S(1)}, u32[]{:S(2)}) copy-start(f32[1,4,32,32]{3,2,1,0:T(8,128)S(1)} %collective-permute-done.3.g0_ref) | copy-start | bytes 49156
  35.1 0.6 %copy-start.7 = (f32[1,4,32,32]{3,2,1,0:T(8,128)}, f32[1,4,32,32]{3,2,1,0:T(8,128)S(1)}, u32[]{:S(2)}) copy-start(f32[1,4,32,32]{3,2,1,0:T(8,128)S(1)} %collective-permute-done.5.g2_ref) | copy-start | bytes 49156
  35.7 5.2 %collective-permute-start.6 = (f32[1,2,32,32]{3,2,1,0:T(8,128)S(1)}, f32[1,2,32,32]{3,2,1,0:T(8,128)S(1)}, u32[]{:S(2)}, u32[]{:S(2)}) collective-permute-start(f32[1,2,32,32]{3,2,1,0:T(8,128)S(1)} %get-tuple-element.8), channel_id=1, source_target_pairs={{0,8},{4,12},{8,0},{12,4},{1,5},{5,1},{9,13},{13,9},{2,10},{6,14},... | collective-permute-start | bytes 24584 | tf_op jit(solution)/shard_map/gradient_exchange/ppermute | solution.py:410
  36.1 4.8 %collective-permute-start.7 = (f32[1,2,32,32]{3,2,1,0:T(8,128)S(1)}, f32[1,2,32,32]{3,2,1,0:T(8,128)S(1)}, u32[]{:S(2)}, u32[]{:S(2)}) collective-permute-start(f32[1,2,32,32]{3,2,1,0:T(8,128)S(1)} %get-tuple-element.9), channel_id=1, source_target_pairs={{1,13},{5,9},{9,5},{13,1},{3,15},{7,11},{11,7},{15,3},{17,29},{21,... | collective-permute-start | bytes 24584 | tf_op jit(solution)/shard_map/gradient_exchange/ppermute | solution.py:410
  40.9 3.5 %copy-start.10 = (f32[1,2,32,32]{3,2,1,0:T(8,128)}, f32[1,2,32,32]{3,2,1,0:T(8,128)S(1)}, u32[]{:S(2)}) copy-start(f32[1,2,32,32]{3,2,1,0:T(8,128)S(1)} %add_add_fusion.refs_0_) | copy-start | bytes 24580
  40.9 3.5 %collective-permute-start.8 = (f32[1,2,32,32]{3,2,1,0:T(8,128)S(1)}, f32[1,2,32,32]{3,2,1,0:T(8,128)S(1)}, u32[]{:S(2)}, u32[]{:S(2)}) collective-permute-start(f32[1,2,32,32]{3,2,1,0:T(8,128)S(1)} %add_add_fusion.refs_0_), channel_id=1, source_target_pairs={{0,1},{1,0},{2,3},{3,2},{4,5},{5,4},{6,7},{7,6},{8,9},{9,8},{10,11... | collective-permute-start | bytes 24584 | tf_op jit(solution)/shard_map/gradient_exchange/ppermute | solution.py:351
  44.4 0.6 %copy-start.11 = (f32[1,2,32,32]{3,2,1,0:T(8,128)}, f32[1,2,32,32]{3,2,1,0:T(8,128)S(1)}, u32[]{:S(2)}) copy-start(f32[1,2,32,32]{3,2,1,0:T(8,128)S(1)} %collective-permute-done.8.refs_1_) | copy-start | bytes 24580

commit v19 on v18

--- a/solution.py
+++ b/solution.py
@@ -125,13 +125,21 @@
     cols_im = np.concatenate(table_three(c_im.T), axis=0)
     plain = (c_re, c_im, c_re.T, c_im.T, right_w[:B], right_w[B : 2 * B], right_c)
     out = [jnp.asarray(table, jnp.float32) for table in plain]
-    bf = (left_three, right_hm, right_lh, rows_three, cols_re, cols_im)
+    six = []
+    for table in (c_re.T, c_im.T):
+        t_hi, t_mid, t_lo = table_three(table)
+        six.append(np.concatenate([t_hi, t_mid, t_hi, t_lo, t_hi, t_mid], axis=0))
+    c_hi, c_mid, c_lo = table_three(right_c)
+    c_hm = np.concatenate([c_hi, c_mid], axis=1)
+    c_lh = np.concatenate([c_lo, c_hi], axis=0)
+    bf = (left_three, right_hm, right_lh, rows_three, cols_re, cols_im, six[0], six[1], c_hm, c_lh)
     return out + [jnp.asarray(table) for table in bf]
 
 
 def imaging_body(
     pos_ref, im_ref, sh_ref, w_ref, dose_ref, mask_ref, ev_ref, ev2_ref, own_ref, goal_ref, h_ref, hc_ref,
     c_re_ref, c_im_ref, ct_re_ref, ct_im_ref, rw_top, rw_bot, rc_ref, la_ref, rhm_ref, rlh_ref, rows_ref, cre_ref, cim_ref,
+        six_re, six_im, chm_ref, clh_ref,
     slots_ref, f_buf, i_buf, u_buf, w_buf, xr_buf, xi_buf,
 ):
     count = f_buf.shape[0]
@@ -153,8 +161,10 @@
     m_im = ev_ref[master, 1] + ev2_ref[master, 1] + jnp.where(is_own, own_ref[master % local_masters, 1], 0.0)
     mask = mask_ref[pos]
     rows = dot_parts(rows_ref[...], jnp.concatenate([mask, mask, mask], axis=0))
-    t_one = dot_full(rows, ct_re_ref[...])
-    t_two = dot_full(rows, ct_im_ref[...])
+    r_hi, r_mid, r_lo = split_three(rows)
+    packed = jnp.concatenate([r_hi, r_hi, r_mid, r_hi, r_lo, r_mid], axis=1)
+    t_one = dot_parts(packed, six_re[...])
+    t_two = dot_parts(packed, six_im[...])
     s_re = t_one[:B] - t_two[B:] + (ph_re * m_re - ph_im * m_im)
     s_im = t_two[:B] + t_one[B:] + (ph_re * m_im + ph_im * m_re)
     i_buf[...] = jnp.zeros(i_buf.shape, jnp.float32)
@@ -199,7 +209,9 @@
         return carry
 
     lax.fori_loop(0, count, backward, 0)
-    out = dot_full(u_buf[...], rc_ref[...])
+    u_hi, u_mid, u_lo = split_three(u_buf[...])
+    first = dot_parts(u_hi, chm_ref[...]) + dot_parts(u_mid, chm_ref[...])
+    out = first[:, :128] + first[:, 128:] + dot_parts(jnp.concatenate([u_hi, u_lo], axis=1), clh_ref[...])
     acc = jnp.sum((hc_ref[...] * out).reshape(count, B, 128), axis=0)
     flip = jnp.concatenate([acc, jnp.zeros((128 - B, 128), jnp.float32)], axis=0).T
     g_re = flip[0:B, 0:B] + flip[2 * B : 3 * B, 0:B]

time: 47.6 us -> 47.8 us (level)
  no operation moved by 1% of the time
where the time goes in v19:
time: 47.8 us; the launch traced here: 47.5 us
  Pallas kernels  20.7 us (43%)
  starting transfers between devices  12.7 us (27%)
  local copies, waits for them, and re-layouts  4.17 us (9%)
  waiting for transfers between devices  4.02 us (8%)
  other arithmetic  2.7 us (6%)
  between operations  2.22 us (5%)
  matrix products  1.03 us (2%)
    pallas_call x1, Pallas kernels, imaging(): pl.pallas_call(imaging_body, out_shape=jax.ShapeDtypeStruct((4, B, B), jn...  15.4 us
    ppermute x2, starting transfers between devices, gather_split(): got = lax.ppermute(x, ('tile', 'kern'), pairs)  4.75 us
    ppermute x2, starting transfers between devices, sum_parts(): return (x, lax.ppermute(x, axis, [(0, 1), (1, 0)]))  4.68 us
    unnamed x28, local copies, waits for them, and re-layouts  3.83 us
    pallas_call x1, Pallas kernels, group_pixels(): pl.pallas_call(group_pixel_body, out_shape=(shape, jax.ShapeDtypeStruct((...  2.99 us
    ppermute x3, waiting for transfers between devices, on_device(): lax.ppermute(comp, ('corner', 'kern'), [(i, i ^ step) for i in range(4)])  2.66 us
    pallas_call x1, Pallas kernels, pixels(): pl.pallas_call(functools.partial(pixel_body, passes=False), out_shape=sha...  2.31 us
    ppermute x3, starting transfers between devices, on_device(): lax.ppermute(comp, ('corner', 'kern'), [(i, i ^ step) for i in range(4)])  2.21 us
  transfers between devices with their start and end apart: 9, of which 4 were waited for; matrix products, arithmetic and copies ran while one was open for 6% of the time, Pallas kernels for 6%

profile of v19, /device:TPU:0, one launch (start us, length us, event | category | flops | bytes accessed | tf_op | source)
XLA Modules:
  0.0 47.5 jit_solution(13738858687802265504)
XLA Ops:
  0.7 0.9 %copy-done = bf16[1,256,256]{2,1,0:T(8,128)(2,1)S(1)} copy-done((bf16[1,256,256]{2,1,0:T(8,128)(2,1)S(1)}, bf16[1,256,256]{2,1,0:T(8,128)(2,1)}, u32[]{:S(2)}) %copy-start) | copy-done | bytes 131096
  1.5 0.2 fusion.8
  1.8 0.2 fusion.6
  2.0 0.2 fusion.17
  2.1 0.2 fusion.16
  2.3 0.2 fusion
  2.5 0.2 fusion.1
  2.7 4.1 %collective-permute-start = (f32[1,2,32,32]{3,2,1,0:T(8,128)S(1)}, f32[1,2,32,32]{3,2,1,0:T(8,128)S(1)}, u32[]{:S(2)}, u32[]{:S(2)}) collective-permute-start(f32[1,2,32,32]{3,2,1,0:T(8,128)S(1)} %pad_maximum_fusion.1.own_ref), channel_id=1, source_target_pairs={{8,0},{12,4},{0,8},{4,12},{5,1},{1,5},{13,9},{9,13},{10,2},{14,6},... | collective-permute-start | bytes 24584 | tf_op jit(solution)/shard_map/master_spectra/ppermute | solution.py:403
  6.8 0.7 %collective-permute-start.1 = (f32[1,2,32,32]{3,2,1,0:T(8,128)S(1)}, f32[1,2,32,32]{3,2,1,0:T(8,128)S(1)}, u32[]{:S(2)}, u32[]{:S(2)}) collective-permute-start(f32[1,2,32,32]{3,2,1,0:T(8,128)S(1)} %pad_maximum_fusion.1.own_ref), channel_id=1, source_target_pairs={{13,1},{9,5},{5,9},{1,13},{15,3},{11,7},{7,11},{3,15},{29,17},{25,... | collective-permute-start | bytes 24584 | tf_op jit(solution)/shard_map/master_spectra/ppermute | solution.py:403
  7.5 0.6 %copy-done.13 = f32[1,12]{1,0:T(1,128)S(1)} copy-done((f32[1,12]{1,0:T(1,128)S(1)}, f32[1,12]{1,0:T(1,128)}, u32[]{:S(2)}) %copy-start.13) | copy-done | bytes 72
  8.3 0.1 copy.40
  8.7 0.5 %copy-done.12 = s32[2]{0:T(128)S(1)} copy-done((s32[2]{0:T(128)S(1)}, s32[2]{0:T(128)}, u32[]{:S(2)}) %copy-start.12) | copy-done | bytes 32
  9.3 0.9 %pad_maximum_fusion = f32[12,32,128]{2,1,0:T(8,128)} fusion(f32[12,32,32]{2,1,0:T(8,128)S(1)} %copy.41, f32[12,32,32]{2,1,0:T(8,128)S(1)} %copy.40, f32[12,32,32]{2,1,0:T(8,128)S(1)} %copy.38), kind=kLoop, calls=%fused_computation.10 | loop fusion | flops 147456 | bytes 344064 | tf_op jit(solution)/shard_map/imaging_kernel/concatenate | solution.py:465
  10.3 2.0 %collective-permute-start.2 = (f32[4,2,32,32]{3,2,1,0:T(8,128)S(1)}, f32[4,2,32,32]{3,2,1,0:T(8,128)S(1)}, u32[]{:S(2)}, u32[]{:S(2)}) collective-permute-start(f32[4,2,32,32]{3,2,1,0:T(8,128)S(1)} %select_add_fusion.ev_ref), channel_id=1, source_target_pairs={{0,1},{1,0},{2,3},{3,2},{4,5},{5,4},{6,7},{7,6},{8,9},{9,8},{10,11... | collective-permute-start | bytes 98312 | tf_op jit(solution)/shard_map/master_spectra/ppermute | solution.py:363
  12.3 0.6 %pad_add_fusion.pos_ref = s32[2]{0:T(128)} fusion(s32[1]{0:T(128)} %bitcast.1, s32[1]{0:T(128)} %bitcast), kind=kLoop, calls=%fused_computation.30 | loop fusion | flops 2 | bytes 16 | tf_op jit(solution)/shard_map/imaging_kernel/stack | solution.py:468
  13.6 0.6 %copy-done.9 = f32[4,2,32,32]{3,2,1,0:T(8,128)} copy-done((f32[4,2,32,32]{3,2,1,0:T(8,128)}, f32[4,2,32,32]{3,2,1,0:T(8,128)S(1)}, u32[]{:S(2)}) %copy-start.9) | copy-done | bytes 32792
  14.2 15.4 %imaging_kernel.1 = f32[4,32,32]{2,1,0:T(8,128)} custom-call(s32[2]{0:T(128)} %pad_add_fusion.pos_ref, s32[2]{0:T(128)} %im_ref.1, s32[2,2]{1,0:T(2,128)} %sh_ref.1, f32[12]{0:T(128)} %bitcast.68, f32[1]{0:T(128)S(6)} %copy.43.dose_ref, bf16[2,256,256]{2,1,0:T(8,128)(2,1)} %mask_ref.1, f32[4,2,32,32]{3,2,1,0:T(8,128)} %copy-done.4, ...), custom_call_target="tpu_custom_call" | custom-call | tf_op jit(solution)/shard_map/imaging_kernel/pallas_call | solution.py:232
  29.6 1.6 %collective-permute-start.4 = (f32[1,4,32,32]{3,2,1,0:T(8,128)}, f32[1,4,32,32]{3,2,1,0:T(8,128)S(1)}, u32[]{:S(2)}, u32[]{:S(2)}) collective-permute-start(f32[1,4,32,32]{3,2,1,0:T(8,128)} %bitcast.61), channel_id=1, source_target_pairs={{0,2},{1,3},{2,0},{3,1},{4,6},{5,7},{6,4},{7,5},{8,10},{9,11},{10,... | collective-permute-start | bytes 49160 | tf_op jit(solution)/shard_map/gradient_exchange/ppermute | solution.py:482
  31.2 0.6 %collective-permute-start.5 = (f32[1,4,32,32]{3,2,1,0:T(8,128)}, f32[1,4,32,32]{3,2,1,0:T(8,128)S(1)}, u32[]{:S(2)}, u32[]{:S(2)}) collective-permute-start(f32[1,4,32,32]{3,2,1,0:T(8,128)} %bitcast.63), channel_id=1, source_target_pairs={{0,3},{1,2},{2,1},{3,0},{4,7},{5,6},{6,5},{7,4},{8,11},{9,10},{10,... | collective-permute-start | bytes 49160 | tf_op jit(solution)/shard_map/gradient_exchange/ppermute | solution.py:482
  31.9 2.3 %collective-permute-done.4.g1_ref = f32[1,4,32,32]{3,2,1,0:T(8,128)S(1)} collective-permute-done((f32[1,4,32,32]{3,2,1,0:T(8,128)}, f32[1,4,32,32]{3,2,1,0:T(8,128)S(1)}, u32[]{:S(2)}, u32[]{:S(2)}) %collective-permute-start.4) | collective-permute-done | bytes 16416 | tf_op jit(solution)/shard_map/gradient_exchange/ppermute | solution.py:482
  34.2 0.8 %fusion.11 = f32[2,32,32]{2,1,0:T(8,128)S(1)} fusion(f32[1,4,32,32]{3,2,1,0:T(8,128)S(1)} %collective-permute-done.4.g1_ref, f32[1,4,32,32]{3,2,1,0:T(8,128)} %bitcast.64), kind=kLoop, calls=%fused_computation.20 | loop fusion | flops 2048 | bytes 24576 | tf_op jit(solution)/shard_map/gradient_exchange/mul | solution.py:501
  35.0 0.3 collective-permute-done.5.g2_ref
  35.4 0.2 copy-done.6
  35.6 0.3 copy-done.7
  35.9 0.4 collective-permute-start.6
  36.3 0.7 %collective-permute-start.7 = (f32[1,2,32,32]{3,2,1,0:T(8,128)S(1)}, f32[1,2,32,32]{3,2,1,0:T(8,128)S(1)}, u32[]{:S(2)}, u32[]{:S(2)}) collective-permute-start(f32[1,2,32,32]{3,2,1,0:T(8,128)S(1)} %get-tuple-element.9), channel_id=1, source_target_pairs={{1,13},{5,9},{9,5},{13,1},{3,15},{7,11},{11,7},{15,3},{17,29},{21,... | collective-permute-start | bytes 24584 | tf_op jit(solution)/shard_map/gradient_exchange/ppermute | solution.py:422
  37.0 3.0 %gradient_exchange.1 = (f32[2,256,256]{2,1,0:T(8,128)}, f32[1,1,1,1]{3,2,1,0:T(1,128)}) custom-call(f32[1,4,32,32]{3,2,1,0:T(8,128)} %bitcast.65, f32[1,4,32,32]{3,2,1,0:T(8,128)} %copy-done.6, f32[1,4,32,32]{3,2,1,0:T(8,128)} %copy-done.5, f32[1,4,32,32]{3,2,1,0:T(8,128)} %copy-done.7, f32[32,256]{1,0:T(8,128)} %constant.75.clone.c_re_ref.refs_2_, ...), custom_call_target="tpu_custom_call" | custom-call | tf_op jit(solution)/shard_map/gradient_exchange/pallas_call | solution.py:300
  40.6 0.5 %collective-permute-done.6 = f32[1,2,32,32]{3,2,1,0:T(8,128)S(1)} collective-permute-done((f32[1,2,32,32]{3,2,1,0:T(8,128)S(1)}, f32[1,2,32,32]{3,2,1,0:T(8,128)S(1)}, u32[]{:S(2)}, u32[]{:S(2)}) %collective-permute-start.6) | collective-permute-done | bytes 8224 | tf_op jit(solution)/shard_map/gradient_exchange/ppermute | solution.py:422
  41.1 2.6 %collective-permute-start.8 = (f32[1,2,32,32]{3,2,1,0:T(8,128)S(1)}, f32[1,2,32,32]{3,2,1,0:T(8,128)S(1)}, u32[]{:S(2)}, u32[]{:S(2)}) collective-permute-start(f32[1,2,32,32]{3,2,1,0:T(8,128)S(1)} %add_add_fusion.refs_0_), channel_id=1, source_target_pairs={{0,1},{1,0},{2,3},{3,2},{4,5},{5,4},{6,7},{7,6},{8,9},{9,8},{10,11... | collective-permute-start | bytes 24584 | tf_op jit(solution)/shard_map/gradient_exchange/ppermute | solution.py:363
  43.7 0.9 %collective-permute-done.8.refs_1_ = f32[1,2,32,32]{3,2,1,0:T(8,128)S(1)} collective-permute-done((f32[1,2,32,32]{3,2,1,0:T(8,128)S(1)}, f32[1,2,32,32]{3,2,1,0:T(8,128)S(1)}, u32[]{:S(2)}, u32[]{:S(2)}) %collective-permute-start.8) | collective-permute-done | bytes 8224 | tf_op jit(solution)/shard_map/gradient_exchange/ppermute | solution.py:363
  44.6 0.6 %copy-done.11 = f32[1,2,32,32]{3,2,1,0:T(8,128)} copy-done((f32[1,2,32,32]{3,2,1,0:T(8,128)}, f32[1,2,32,32]{3,2,1,0:T(8,128)S(1)}, u32[]{:S(2)}) %copy-start.11) | copy-done | bytes 8216
  45.2 2.3 %pixel_gradients.1 = f32[1,256,256]{2,1,0:T(8,128)} custom-call(f32[1,2,32,32]{3,2,1,0:T(8,128)} %copy-done.10, f32[1,2,32,32]{3,2,1,0:T(8,128)} %copy-done.11, f32[32,256]{1,0:T(8,128)} %constant.75.clone.c_re_ref.refs_2_, f32[32,256]{1,0:T(8,128)} %constant.76.clone.c_im_ref.refs_3_, bf16[256,384]{1,0:T(8,128)(2,1)} %constant.92.clone.left_ref.refs_4_), custom_call_target="tpu_custom_call" | custom-call | tf_op jit(solution)/shard_map/pixel_gradients/pallas_call | solution.py:320
  (41 shorter events, 0.8 us)
Async XLA Ops:
  0.6 0.9 %copy-start = (bf16[1,256,256]{2,1,0:T(8,128)(2,1)S(1)}, bf16[1,256,256]{2,1,0:T(8,128)(2,1)}, u32[]{:S(2)}) copy-start(bf16[1,256,256]{2,1,0:T(8,128)(2,1)} %param.34) | copy-start | bytes 393220
  0.6 0.9 %copy-start.2 = (f32[32,256]{1,0:T(8,128)S(1)}, f32[32,256]{1,0:T(8,128)}, u32[]{:S(2)}) copy-start(f32[32,256]{1,0:T(8,128)} %constant.75.clone.c_re_ref.refs_2_) | copy-start | bytes 98308
  0.7 1.1 %copy-start.3 = (f32[32,256]{1,0:T(8,128)S(1)}, f32[32,256]{1,0:T(8,128)}, u32[]{:S(2)}) copy-start(f32[32,256]{1,0:T(8,128)} %constant.76.clone.c_im_ref.refs_3_) | copy-start | bytes 98308
  0.7 7.4 %copy-start.1 = (f32[1,12,2,32,32]{4,3,2,1,0:T(8,128)S(1)}, f32[1,12,2,32,32]{4,3,2,1,0:T(8,128)}, u32[]{:S(2)}) copy-start(f32[1,12,2,32,32]{4,3,2,1,0:T(8,128)} %param.38) | copy-start | bytes 294916
  2.6 5.6 %copy-start.8 = (f32[1,2,32,32]{3,2,1,0:T(8,128)}, f32[1,2,32,32]{3,2,1,0:T(8,128)S(1)}, u32[]{:S(2)}) copy-start(f32[1,2,32,32]{3,2,1,0:T(8,128)S(1)} %pad_maximum_fusion.1.own_ref) | copy-start | bytes 24580
  2.7 7.5 %collective-permute-start = (f32[1,2,32,32]{3,2,1,0:T(8,128)S(1)}, f32[1,2,32,32]{3,2,1,0:T(8,128)S(1)}, u32[]{:S(2)}, u32[]{:S(2)}) collective-permute-start(f32[1,2,32,32]{3,2,1,0:T(8,128)S(1)} %pad_maximum_fusion.1.own_ref), channel_id=1, source_target_pairs={{8,0},{12,4},{0,8},{4,12},{5,1},{1,5},{13,9},{9,13},{10,2},{14,6},... | collective-permute-start | bytes 24584 | tf_op jit(solution)/shard_map/master_spectra/ppermute | solution.py:403
  6.8 3.4 %collective-permute-start.1 = (f32[1,2,32,32]{3,2,1,0:T(8,128)S(1)}, f32[1,2,32,32]{3,2,1,0:T(8,128)S(1)}, u32[]{:S(2)}, u32[]{:S(2)}) collective-permute-start(f32[1,2,32,32]{3,2,1,0:T(8,128)S(1)} %pad_maximum_fusion.1.own_ref), channel_id=1, source_target_pairs={{13,1},{9,5},{5,9},{1,13},{15,3},{11,7},{7,11},{3,15},{29,17},{25,... | collective-permute-start | bytes 24584 | tf_op jit(solution)/shard_map/master_spectra/ppermute | solution.py:403
  7.4 0.7 %copy-start.13 = (f32[1,12]{1,0:T(1,128)S(1)}, f32[1,12]{1,0:T(1,128)}, u32[]{:S(2)}) copy-start(f32[1,12]{1,0:T(1,128)} %param.39) | copy-start | bytes 148
  8.5 0.7 %copy-start.12 = (s32[2]{0:T(128)S(1)}, s32[2]{0:T(128)}, u32[]{:S(2)}) copy-start(s32[2]{0:T(128)} %im_ref.1) | copy-start | bytes 28
  10.3 3.3 %copy-start.4 = (f32[4,2,32,32]{3,2,1,0:T(8,128)}, f32[4,2,32,32]{3,2,1,0:T(8,128)S(1)}, u32[]{:S(2)}) copy-start(f32[4,2,32,32]{3,2,1,0:T(8,128)S(1)} %select_add_fusion.ev_ref) | copy-start | bytes 98308
  10.3 3.3 %collective-permute-start.2 = (f32[4,2,32,32]{3,2,1,0:T(8,128)S(1)}, f32[4,2,32,32]{3,2,1,0:T(8,128)S(1)}, u32[]{:S(2)}, u32[]{:S(2)}) collective-permute-start(f32[4,2,32,32]{3,2,1,0:T(8,128)S(1)} %select_add_fusion.ev_ref), channel_id=1, source_target_pairs={{0,1},{1,0},{2,3},{3,2},{4,5},{5,4},{6,7},{7,6},{8,9},{9,8},{10,11... | collective-permute-start | bytes 98312 | tf_op jit(solution)/shard_map/master_spectra/ppermute | solution.py:363
  13.6 0.6 %copy-start.9 = (f32[4,2,32,32]{3,2,1,0:T(8,128)}, f32[4,2,32,32]{3,2,1,0:T(8,128)S(1)}, u32[]{:S(2)}) copy-start(f32[4,2,32,32]{3,2,1,0:T(8,128)S(1)} %collective-permute-done.2.ev2_ref) | copy-start | bytes 98308
  29.6 4.5 %collective-permute-start.4 = (f32[1,4,32,32]{3,2,1,0:T(8,128)}, f32[1,4,32,32]{3,2,1,0:T(8,128)S(1)}, u32[]{:S(2)}, u32[]{:S(2)}) collective-permute-start(f32[1,4,32,32]{3,2,1,0:T(8,128)} %bitcast.61), channel_id=1, source_target_pairs={{0,2},{1,3},{2,0},{3,1},{4,6},{5,7},{6,4},{7,5},{8,10},{9,11},{10,... | collective-permute-start | bytes 49160 | tf_op jit(solution)/shard_map/gradient_exchange/ppermute | solution.py:482
  31.2 3.8 %collective-permute-start.3 = (f32[1,4,32,32]{3,2,1,0:T(8,128)}, f32[1,4,32,32]{3,2,1,0:T(8,128)S(1)}, u32[]{:S(2)}, u32[]{:S(2)}) collective-permute-start(f32[1,4,32,32]{3,2,1,0:T(8,128)} %bitcast.62), channel_id=1, source_target_pairs={{0,1},{1,0},{2,3},{3,2},{4,5},{5,4},{6,7},{7,6},{8,9},{9,8},{10,11... | collective-permute-start | bytes 49160 | tf_op jit(solution)/shard_map/gradient_exchange/ppermute | solution.py:482
  31.2 4.1 %collective-permute-start.5 = (f32[1,4,32,32]{3,2,1,0:T(8,128)}, f32[1,4,32,32]{3,2,1,0:T(8,128)S(1)}, u32[]{:S(2)}, u32[]{:S(2)}) collective-permute-start(f32[1,4,32,32]{3,2,1,0:T(8,128)} %bitcast.63), channel_id=1, source_target_pairs={{0,3},{1,2},{2,1},{3,0},{4,7},{5,6},{6,5},{7,4},{8,11},{9,10},{10,... | collective-permute-start | bytes 49160 | tf_op jit(solution)/shard_map/gradient_exchange/ppermute | solution.py:482
  34.2 1.1 %copy-start.5 = (f32[1,4,32,32]{3,2,1,0:T(8,128)}, f32[1,4,32,32]{3,2,1,0:T(8,128)S(1)}, u32[]{:S(2)}) copy-start(f32[1,4,32,32]{3,2,1,0:T(8,128)S(1)} %collective-permute-done.4.g1_ref) | copy-start | bytes 49156
  35.0 0.6 %copy-start.6 = (f32[1,4,32,32]{3,2,1,0:T(8,128)}, f32[1,4,32,32]{3,2,1,0:T(8,128)S(1)}, u32[]{:S(2)}) copy-start(f32[1,4,32,32]{3,2,1,0:T(8,128)S(1)} %collective-permute-done.3.g0_ref) | copy-start | bytes 49156
  35.3 0.6 %copy-start.7 = (f32[1,4,32,32]{3,2,1,0:T(8,128)}, f32[1,4,32,32]{3,2,1,0:T(8,128)S(1)}, u32[]{:S(2)}) copy-start(f32[1,4,32,32]{3,2,1,0:T(8,128)S(1)} %collective-permute-done.5.g2_ref) | copy-start | bytes 49156
  35.9 5.2 %collective-permute-start.6 = (f32[1,2,32,32]{3,2,1,0:T(8,128)S(1)}, f32[1,2,32,32]{3,2,1,0:T(8,128)S(1)}, u32[]{:S(2)}, u32[]{:S(2)}) collective-permute-start(f32[1,2,32,32]{3,2,1,0:T(8,128)S(1)} %get-tuple-element.8), channel_id=1, source_target_pairs={{0,8},{4,12},{8,0},{12,4},{1,5},{5,1},{9,13},{13,9},{2,10},{6,14},... | collective-permute-start | bytes 24584 | tf_op jit(solution)/shard_map/gradient_exchange/ppermute | solution.py:422
  36.3 4.8 %collective-permute-start.7 = (f32[1,2,32,32]{3,2,1,0:T(8,128)S(1)}, f32[1,2,32,32]{3,2,1,0:T(8,128)S(1)}, u32[]{:S(2)}, u32[]{:S(2)}) collective-permute-start(f32[1,2,32,32]{3,2,1,0:T(8,128)S(1)} %get-tuple-element.9), channel_id=1, source_target_pairs={{1,13},{5,9},{9,5},{13,1},{3,15},{7,11},{11,7},{15,3},{17,29},{21,... | collective-permute-start | bytes 24584 | tf_op jit(solution)/shard_map/gradient_exchange/ppermute | solution.py:422
  41.1 3.5 %copy-start.10 = (f32[1,2,32,32]{3,2,1,0:T(8,128)}, f32[1,2,32,32]{3,2,1,0:T(8,128)S(1)}, u32[]{:S(2)}) copy-start(f32[1,2,32,32]{3,2,1,0:T(8,128)S(1)} %add_add_fusion.refs_0_) | copy-start | bytes 24580
  41.1 3.5 %collective-permute-start.8 = (f32[1,2,32,32]{3,2,1,0:T(8,128)S(1)}, f32[1,2,32,32]{3,2,1,0:T(8,128)S(1)}, u32[]{:S(2)}, u32[]{:S(2)}) collective-permute-start(f32[1,2,32,32]{3,2,1,0:T(8,128)S(1)} %add_add_fusion.refs_0_), channel_id=1, source_target_pairs={{0,1},{1,0},{2,3},{3,2},{4,5},{5,4},{6,7},{7,6},{8,9},{9,8},{10,11... | collective-permute-start | bytes 24584 | tf_op jit(solution)/shard_map/gradient_exchange/ppermute | solution.py:363
  44.6 0.6 %copy-start.11 = (f32[1,2,32,32]{3,2,1,0:T(8,128)}, f32[1,2,32,32]{3,2,1,0:T(8,128)S(1)}, u32[]{:S(2)}) copy-start(f32[1,2,32,32]{3,2,1,0:T(8,128)S(1)} %collective-permute-done.8.refs_1_) | copy-start | bytes 24580

commit v20 on v18

--- a/solution.py
+++ b/solution.py
@@ -121,30 +121,29 @@
     rows_three = np.concatenate(
         [np.concatenate(parts_re, axis=1), np.concatenate(parts_im, axis=1)], axis=0
     )
-    cols_re = np.concatenate(table_three(c_re.T), axis=0)
-    cols_im = np.concatenate(table_three(c_im.T), axis=0)
     plain = (c_re, c_im, c_re.T, c_im.T, right_w[:B], right_w[B : 2 * B], right_c)
     out = [jnp.asarray(table, jnp.float32) for table in plain]
-    bf = (left_three, right_hm, right_lh, rows_three, cols_re, cols_im)
+    bf = (left_three, right_hm, right_lh, rows_three)
     return out + [jnp.asarray(table) for table in bf]
 
 
 def imaging_body(
     pos_ref, im_ref, sh_ref, w_ref, dose_ref, mask_ref, ev_ref, ev2_ref, own_ref, goal_ref, h_ref, hc_ref,
-    c_re_ref, c_im_ref, ct_re_ref, ct_im_ref, rw_top, rw_bot, rc_ref, la_ref, rhm_ref, rlh_ref, rows_ref, cre_ref, cim_ref,
+    c_re_ref, c_im_ref, ct_re_ref, ct_im_ref, rw_top, rw_bot, rc_ref, la_ref, rhm_ref, rlh_ref, rows_ref,
     slots_ref, f_buf, i_buf, u_buf, w_buf, xr_buf, xi_buf,
 ):
     count = f_buf.shape[0]
     pos = pos_ref[0]
     master = im_ref[pos]
     pick0 = (lax.broadcasted_iota(jnp.int32, (P_SIZE, 128), 0) == sh_ref[pos, 0]).astype(jnp.bfloat16)
-    pick1 = (lax.broadcasted_iota(jnp.int32, (8, P_SIZE), 1) == sh_ref[pos, 1]).astype(jnp.bfloat16)
+    pick1 = (lax.broadcasted_iota(jnp.int32, (P_SIZE, 128), 0) == sh_ref[pos, 1]).astype(jnp.bfloat16)
     e0 = dot_parts(rows_ref[...], jnp.concatenate([pick0, pick0, pick0], axis=0))
     e0_re = e0[:B, 0:1]
     e0_im = e0[B:, 0:1]
-    pick1 = jnp.concatenate([pick1, pick1, pick1], axis=1)
-    e1_re = dot_parts(pick1, cre_ref[...])[0:1, :]
-    e1_im = dot_parts(pick1, cim_ref[...])[0:1, :]
+    e1 = dot_parts(rows_ref[...], jnp.concatenate([pick1, pick1, pick1], axis=0))
+    fill = jnp.zeros((128 - B, 128), jnp.float32)
+    e1_re = jnp.concatenate([e1[:B], fill], axis=0).T[0:1, 0:B]
+    e1_im = jnp.concatenate([e1[B:], fill], axis=0).T[0:1, 0:B]
     ph_re = e0_re * e1_re - e0_im * e1_im
     ph_im = e0_re * e1_im + e0_im * e1_re
     local_masters = own_ref.shape[0]

time: 47.6 us -> 47.5 us (level)
  no operation moved by 1% of the time
where the time goes in v20:
time: 47.5 us; the launch traced here: 47.2 us
  Pallas kernels  20.4 us (43%)
  starting transfers between devices  12.6 us (27%)
  local copies, waits for them, and re-layouts  4.17 us (9%)
  waiting for transfers between devices  4.01 us (8%)
  other arithmetic  2.7 us (6%)
  between operations  2.21 us (5%)
  matrix products  1.03 us (2%)
    pallas_call x1, Pallas kernels, imaging(): pl.pallas_call(imaging_body, out_shape=jax.ShapeDtypeStruct((4, B, B), jn...  15.1 us
    ppermute x2, starting transfers between devices, gather_split(): got = lax.ppermute(x, ('tile', 'kern'), pairs)  4.75 us
    ppermute x2, starting transfers between devices, sum_parts(): return (x, lax.ppermute(x, axis, [(0, 1), (1, 0)]))  4.68 us
    unnamed x28, local copies, waits for them, and re-layouts  3.83 us
    pallas_call x1, Pallas kernels, group_pixels(): pl.pallas_call(group_pixel_body, out_shape=(shape, jax.ShapeDtypeStruct((...  2.99 us
    ppermute x3, waiting for transfers between devices, on_device(): lax.ppermute(comp, ('corner', 'kern'), [(i, i ^ step) for i in range(4)])  2.66 us
    pallas_call x1, Pallas kernels, pixels(): pl.pallas_call(functools.partial(pixel_body, passes=False), out_shape=sha...  2.31 us
    ppermute x3, starting transfers between devices, on_device(): lax.ppermute(comp, ('corner', 'kern'), [(i, i ^ step) for i in range(4)])  2.14 us
  transfers between devices with their start and end apart: 9, of which 4 were waited for; matrix products, arithmetic and copies ran while one was open for 6% of the time, Pallas kernels for 6%

profile of v20, /device:TPU:0, one launch (start us, length us, event | category | flops | bytes accessed | tf_op | source)
XLA Modules:
  0.0 47.2 jit_solution(13362738781684438918)
XLA Ops:
  0.7 0.9 %copy-done = bf16[1,256,256]{2,1,0:T(8,128)(2,1)S(1)} copy-done((bf16[1,256,256]{2,1,0:T(8,128)(2,1)S(1)}, bf16[1,256,256]{2,1,0:T(8,128)(2,1)}, u32[]{:S(2)}) %copy-start) | copy-done | bytes 131096
  1.5 0.2 fusion.8
  1.8 0.2 fusion.6
  2.0 0.2 fusion.17
  2.1 0.2 fusion.16
  2.3 0.2 fusion
  2.5 0.2 fusion.1
  2.7 4.1 %collective-permute-start = (f32[1,2,32,32]{3,2,1,0:T(8,128)S(1)}, f32[1,2,32,32]{3,2,1,0:T(8,128)S(1)}, u32[]{:S(2)}, u32[]{:S(2)}) collective-permute-start(f32[1,2,32,32]{3,2,1,0:T(8,128)S(1)} %pad_maximum_fusion.1.own_ref), channel_id=1, source_target_pairs={{8,0},{12,4},{0,8},{4,12},{5,1},{1,5},{13,9},{9,13},{10,2},{14,6},... | collective-permute-start | bytes 24584 | tf_op jit(solution)/shard_map/master_spectra/ppermute | solution.py:390
  6.8 0.7 %collective-permute-start.1 = (f32[1,2,32,32]{3,2,1,0:T(8,128)S(1)}, f32[1,2,32,32]{3,2,1,0:T(8,128)S(1)}, u32[]{:S(2)}, u32[]{:S(2)}) collective-permute-start(f32[1,2,32,32]{3,2,1,0:T(8,128)S(1)} %pad_maximum_fusion.1.own_ref), channel_id=1, source_target_pairs={{13,1},{9,5},{5,9},{1,13},{15,3},{11,7},{7,11},{3,15},{29,17},{25,... | collective-permute-start | bytes 24584 | tf_op jit(solution)/shard_map/master_spectra/ppermute | solution.py:390
  7.5 0.6 %copy-done.13 = f32[1,12]{1,0:T(1,128)S(1)} copy-done((f32[1,12]{1,0:T(1,128)S(1)}, f32[1,12]{1,0:T(1,128)}, u32[]{:S(2)}) %copy-start.13) | copy-done | bytes 72
  8.3 0.1 copy.34
  8.7 0.5 %copy-done.12 = s32[2]{0:T(128)S(1)} copy-done((s32[2]{0:T(128)S(1)}, s32[2]{0:T(128)}, u32[]{:S(2)}) %copy-start.12) | copy-done | bytes 32
  9.3 0.9 %pad_maximum_fusion = f32[12,32,128]{2,1,0:T(8,128)} fusion(f32[12,32,32]{2,1,0:T(8,128)S(1)} %copy.35, f32[12,32,32]{2,1,0:T(8,128)S(1)} %copy.34, f32[12,32,32]{2,1,0:T(8,128)S(1)} %copy.32), kind=kLoop, calls=%fused_computation.10 | loop fusion | flops 147456 | bytes 344064 | tf_op jit(solution)/shard_map/imaging_kernel/concatenate | solution.py:452
  10.3 2.0 %collective-permute-start.2 = (f32[4,2,32,32]{3,2,1,0:T(8,128)S(1)}, f32[4,2,32,32]{3,2,1,0:T(8,128)S(1)}, u32[]{:S(2)}, u32[]{:S(2)}) collective-permute-start(f32[4,2,32,32]{3,2,1,0:T(8,128)S(1)} %select_add_fusion.ev_ref), channel_id=1, source_target_pairs={{0,1},{1,0},{2,3},{3,2},{4,5},{5,4},{6,7},{7,6},{8,9},{9,8},{10,11... | collective-permute-start | bytes 98312 | tf_op jit(solution)/shard_map/master_spectra/ppermute | solution.py:350
  12.3 0.6 %pad_add_fusion.pos_ref = s32[2]{0:T(128)} fusion(s32[1]{0:T(128)} %bitcast.1, s32[1]{0:T(128)} %bitcast), kind=kLoop, calls=%fused_computation.30 | loop fusion | flops 2 | bytes 16 | tf_op jit(solution)/shard_map/imaging_kernel/stack | solution.py:455
  13.6 0.6 %copy-done.9 = f32[4,2,32,32]{3,2,1,0:T(8,128)} copy-done((f32[4,2,32,32]{3,2,1,0:T(8,128)}, f32[4,2,32,32]{3,2,1,0:T(8,128)S(1)}, u32[]{:S(2)}) %copy-start.9) | copy-done | bytes 32792
  14.2 15.1 %imaging_kernel.1 = f32[4,32,32]{2,1,0:T(8,128)} custom-call(s32[2]{0:T(128)} %pad_add_fusion.pos_ref, s32[2]{0:T(128)} %im_ref.1, s32[2,2]{1,0:T(2,128)} %sh_ref.1, f32[12]{0:T(128)} %bitcast.68, f32[1]{0:T(128)S(6)} %copy.37.dose_ref, bf16[2,256,256]{2,1,0:T(8,128)(2,1)} %mask_ref.1, f32[4,2,32,32]{3,2,1,0:T(8,128)} %copy-done.4, ...), custom_call_target="tpu_custom_call" | custom-call | tf_op jit(solution)/shard_map/imaging_kernel/pallas_call | solution.py:219
  29.4 1.5 %collective-permute-start.4 = (f32[1,4,32,32]{3,2,1,0:T(8,128)}, f32[1,4,32,32]{3,2,1,0:T(8,128)S(1)}, u32[]{:S(2)}, u32[]{:S(2)}) collective-permute-start(f32[1,4,32,32]{3,2,1,0:T(8,128)} %bitcast.61), channel_id=1, source_target_pairs={{0,2},{1,3},{2,0},{3,1},{4,6},{5,7},{6,4},{7,5},{8,10},{9,11},{10,... | collective-permute-start | bytes 49160 | tf_op jit(solution)/shard_map/gradient_exchange/ppermute | solution.py:469
  30.8 0.7 %collective-permute-start.5 = (f32[1,4,32,32]{3,2,1,0:T(8,128)}, f32[1,4,32,32]{3,2,1,0:T(8,128)S(1)}, u32[]{:S(2)}, u32[]{:S(2)}) collective-permute-start(f32[1,4,32,32]{3,2,1,0:T(8,128)} %bitcast.63), channel_id=1, source_target_pairs={{0,3},{1,2},{2,1},{3,0},{4,7},{5,6},{6,5},{7,4},{8,11},{9,10},{10,... | collective-permute-start | bytes 49160 | tf_op jit(solution)/shard_map/gradient_exchange/ppermute | solution.py:469
  31.5 2.3 %collective-permute-done.4.g1_ref = f32[1,4,32,32]{3,2,1,0:T(8,128)S(1)} collective-permute-done((f32[1,4,32,32]{3,2,1,0:T(8,128)}, f32[1,4,32,32]{3,2,1,0:T(8,128)S(1)}, u32[]{:S(2)}, u32[]{:S(2)}) %collective-permute-start.4) | collective-permute-done | bytes 16416 | tf_op jit(solution)/shard_map/gradient_exchange/ppermute | solution.py:469
  33.8 0.8 %fusion.11 = f32[2,32,32]{2,1,0:T(8,128)S(1)} fusion(f32[1,4,32,32]{3,2,1,0:T(8,128)S(1)} %collective-permute-done.4.g1_ref, f32[1,4,32,32]{3,2,1,0:T(8,128)} %bitcast.64), kind=kLoop, calls=%fused_computation.20 | loop fusion | flops 2048 | bytes 24576 | tf_op jit(solution)/shard_map/gradient_exchange/mul | solution.py:488
  34.6 0.3 collective-permute-done.5.g2_ref
  35.0 0.2 copy-done.6
  35.2 0.3 copy-done.7
  35.6 0.4 collective-permute-start.6
  36.0 0.7 %collective-permute-start.7 = (f32[1,2,32,32]{3,2,1,0:T(8,128)S(1)}, f32[1,2,32,32]{3,2,1,0:T(8,128)S(1)}, u32[]{:S(2)}, u32[]{:S(2)}) collective-permute-start(f32[1,2,32,32]{3,2,1,0:T(8,128)S(1)} %get-tuple-element.9), channel_id=1, source_target_pairs={{1,13},{5,9},{9,5},{13,1},{3,15},{7,11},{11,7},{15,3},{17,29},{21,... | collective-permute-start | bytes 24584 | tf_op jit(solution)/shard_map/gradient_exchange/ppermute | solution.py:409
  36.6 3.0 %gradient_exchange.1 = (f32[2,256,256]{2,1,0:T(8,128)}, f32[1,1,1,1]{3,2,1,0:T(1,128)}) custom-call(f32[1,4,32,32]{3,2,1,0:T(8,128)} %bitcast.65, f32[1,4,32,32]{3,2,1,0:T(8,128)} %copy-done.6, f32[1,4,32,32]{3,2,1,0:T(8,128)} %copy-done.5, f32[1,4,32,32]{3,2,1,0:T(8,128)} %copy-done.7, f32[32,256]{1,0:T(8,128)} %constant.63.clone.c_re_ref.refs_2_, ...), custom_call_target="tpu_custom_call" | custom-call | tf_op jit(solution)/shard_map/gradient_exchange/pallas_call | solution.py:287
  40.3 0.5 %collective-permute-done.6 = f32[1,2,32,32]{3,2,1,0:T(8,128)S(1)} collective-permute-done((f32[1,2,32,32]{3,2,1,0:T(8,128)S(1)}, f32[1,2,32,32]{3,2,1,0:T(8,128)S(1)}, u32[]{:S(2)}, u32[]{:S(2)}) %collective-permute-start.6) | collective-permute-done | bytes 8224 | tf_op jit(solution)/shard_map/gradient_exchange/ppermute | solution.py:409
  40.8 2.6 %collective-permute-start.8 = (f32[1,2,32,32]{3,2,1,0:T(8,128)S(1)}, f32[1,2,32,32]{3,2,1,0:T(8,128)S(1)}, u32[]{:S(2)}, u32[]{:S(2)}) collective-permute-start(f32[1,2,32,32]{3,2,1,0:T(8,128)S(1)} %add_add_fusion.refs_0_), channel_id=1, source_target_pairs={{0,1},{1,0},{2,3},{3,2},{4,5},{5,4},{6,7},{7,6},{8,9},{9,8},{10,11... | collective-permute-start | bytes 24584 | tf_op jit(solution)/shard_map/gradient_exchange/ppermute | solution.py:350
  43.4 0.9 %collective-permute-done.8.refs_1_ = f32[1,2,32,32]{3,2,1,0:T(8,128)S(1)} collective-permute-done((f32[1,2,32,32]{3,2,1,0:T(8,128)S(1)}, f32[1,2,32,32]{3,2,1,0:T(8,128)S(1)}, u32[]{:S(2)}, u32[]{:S(2)}) %collective-permute-start.8) | collective-permute-done | bytes 8224 | tf_op jit(solution)/shard_map/gradient_exchange/ppermute | solution.py:350
  44.3 0.6 %copy-done.11 = f32[1,2,32,32]{3,2,1,0:T(8,128)} copy-done((f32[1,2,32,32]{3,2,1,0:T(8,128)}, f32[1,2,32,32]{3,2,1,0:T(8,128)S(1)}, u32[]{:S(2)}) %copy-start.11) | copy-done | bytes 8216
  44.9 2.3 %pixel_gradients.1 = f32[1,256,256]{2,1,0:T(8,128)} custom-call(f32[1,2,32,32]{3,2,1,0:T(8,128)} %copy-done.10, f32[1,2,32,32]{3,2,1,0:T(8,128)} %copy-done.11, f32[32,256]{1,0:T(8,128)} %constant.63.clone.c_re_ref.refs_2_, f32[32,256]{1,0:T(8,128)} %constant.64.clone.c_im_ref.refs_3_, bf16[256,384]{1,0:T(8,128)(2,1)} %constant.74.clone.left_ref.refs_4_), custom_call_target="tpu_custom_call" | custom-call | tf_op jit(solution)/shard_map/pixel_gradients/pallas_call | solution.py:307
  (41 shorter events, 0.8 us)
Async XLA Ops:
  0.6 0.9 %copy-start = (bf16[1,256,256]{2,1,0:T(8,128)(2,1)S(1)}, bf16[1,256,256]{2,1,0:T(8,128)(2,1)}, u32[]{:S(2)}) copy-start(bf16[1,256,256]{2,1,0:T(8,128)(2,1)} %param.28) | copy-start | bytes 393220
  0.6 0.9 %copy-start.2 = (f32[32,256]{1,0:T(8,128)S(1)}, f32[32,256]{1,0:T(8,128)}, u32[]{:S(2)}) copy-start(f32[32,256]{1,0:T(8,128)} %constant.63.clone.c_re_ref.refs_2_) | copy-start | bytes 98308
  0.7 1.1 %copy-start.3 = (f32[32,256]{1,0:T(8,128)S(1)}, f32[32,256]{1,0:T(8,128)}, u32[]{:S(2)}) copy-start(f32[32,256]{1,0:T(8,128)} %constant.64.clone.c_im_ref.refs_3_) | copy-start | bytes 98308
  0.7 7.4 %copy-start.1 = (f32[1,12,2,32,32]{4,3,2,1,0:T(8,128)S(1)}, f32[1,12,2,32,32]{4,3,2,1,0:T(8,128)}, u32[]{:S(2)}) copy-start(f32[1,12,2,32,32]{4,3,2,1,0:T(8,128)} %param.32) | copy-start | bytes 294916
  2.6 5.6 %copy-start.8 = (f32[1,2,32,32]{3,2,1,0:T(8,128)}, f32[1,2,32,32]{3,2,1,0:T(8,128)S(1)}, u32[]{:S(2)}) copy-start(f32[1,2,32,32]{3,2,1,0:T(8,128)S(1)} %pad_maximum_fusion.1.own_ref) | copy-start | bytes 24580
  2.7 7.5 %collective-permute-start = (f32[1,2,32,32]{3,2,1,0:T(8,128)S(1)}, f32[1,2,32,32]{3,2,1,0:T(8,128)S(1)}, u32[]{:S(2)}, u32[]{:S(2)}) collective-permute-start(f32[1,2,32,32]{3,2,1,0:T(8,128)S(1)} %pad_maximum_fusion.1.own_ref), channel_id=1, source_target_pairs={{8,0},{12,4},{0,8},{4,12},{5,1},{1,5},{13,9},{9,13},{10,2},{14,6},... | collective-permute-start | bytes 24584 | tf_op jit(solution)/shard_map/master_spectra/ppermute | solution.py:390
  6.8 3.4 %collective-permute-start.1 = (f32[1,2,32,32]{3,2,1,0:T(8,128)S(1)}, f32[1,2,32,32]{3,2,1,0:T(8,128)S(1)}, u32[]{:S(2)}, u32[]{:S(2)}) collective-permute-start(f32[1,2,32,32]{3,2,1,0:T(8,128)S(1)} %pad_maximum_fusion.1.own_ref), channel_id=1, source_target_pairs={{13,1},{9,5},{5,9},{1,13},{15,3},{11,7},{7,11},{3,15},{29,17},{25,... | collective-permute-start | bytes 24584 | tf_op jit(solution)/shard_map/master_spectra/ppermute | solution.py:390
  7.4 0.7 %copy-start.13 = (f32[1,12]{1,0:T(1,128)S(1)}, f32[1,12]{1,0:T(1,128)}, u32[]{:S(2)}) copy-start(f32[1,12]{1,0:T(1,128)} %param.33) | copy-start | bytes 148
  8.5 0.7 %copy-start.12 = (s32[2]{0:T(128)S(1)}, s32[2]{0:T(128)}, u32[]{:S(2)}) copy-start(s32[2]{0:T(128)} %im_ref.1) | copy-start | bytes 28
  10.3 3.3 %copy-start.4 = (f32[4,2,32,32]{3,2,1,0:T(8,128)}, f32[4,2,32,32]{3,2,1,0:T(8,128)S(1)}, u32[]{:S(2)}) copy-start(f32[4,2,32,32]{3,2,1,0:T(8,128)S(1)} %select_add_fusion.ev_ref) | copy-start | bytes 98308
  10.3 3.3 %collective-permute-start.2 = (f32[4,2,32,32]{3,2,1,0:T(8,128)S(1)}, f32[4,2,32,32]{3,2,1,0:T(8,128)S(1)}, u32[]{:S(2)}, u32[]{:S(2)}) collective-permute-start(f32[4,2,32,32]{3,2,1,0:T(8,128)S(1)} %select_add_fusion.ev_ref), channel_id=1, source_target_pairs={{0,1},{1,0},{2,3},{3,2},{4,5},{5,4},{6,7},{7,6},{8,9},{9,8},{10,11... | collective-permute-start | bytes 98312 | tf_op jit(solution)/shard_map/master_spectra/ppermute | solution.py:350
  13.6 0.6 %copy-start.9 = (f32[4,2,32,32]{3,2,1,0:T(8,128)}, f32[4,2,32,32]{3,2,1,0:T(8,128)S(1)}, u32[]{:S(2)}) copy-start(f32[4,2,32,32]{3,2,1,0:T(8,128)S(1)} %collective-permute-done.2.ev2_ref) | copy-start | bytes 98308
  29.4 4.5 %collective-permute-start.4 = (f32[1,4,32,32]{3,2,1,0:T(8,128)}, f32[1,4,32,32]{3,2,1,0:T(8,128)S(1)}, u32[]{:S(2)}, u32[]{:S(2)}) collective-permute-start(f32[1,4,32,32]{3,2,1,0:T(8,128)} %bitcast.61), channel_id=1, source_target_pairs={{0,2},{1,3},{2,0},{3,1},{4,6},{5,7},{6,4},{7,5},{8,10},{9,11},{10,... | collective-permute-start | bytes 49160 | tf_op jit(solution)/shard_map/gradient_exchange/ppermute | solution.py:469
  30.8 3.8 %collective-permute-start.3 = (f32[1,4,32,32]{3,2,1,0:T(8,128)}, f32[1,4,32,32]{3,2,1,0:T(8,128)S(1)}, u32[]{:S(2)}, u32[]{:S(2)}) collective-permute-start(f32[1,4,32,32]{3,2,1,0:T(8,128)} %bitcast.62), channel_id=1, source_target_pairs={{0,1},{1,0},{2,3},{3,2},{4,5},{5,4},{6,7},{7,6},{8,9},{9,8},{10,11... | collective-permute-start | bytes 49160 | tf_op jit(solution)/shard_map/gradient_exchange/ppermute | solution.py:469
  30.8 4.1 %collective-permute-start.5 = (f32[1,4,32,32]{3,2,1,0:T(8,128)}, f32[1,4,32,32]{3,2,1,0:T(8,128)S(1)}, u32[]{:S(2)}, u32[]{:S(2)}) collective-permute-start(f32[1,4,32,32]{3,2,1,0:T(8,128)} %bitcast.63), channel_id=1, source_target_pairs={{0,3},{1,2},{2,1},{3,0},{4,7},{5,6},{6,5},{7,4},{8,11},{9,10},{10,... | collective-permute-start | bytes 49160 | tf_op jit(solution)/shard_map/gradient_exchange/ppermute | solution.py:469
  33.8 1.1 %copy-start.5 = (f32[1,4,32,32]{3,2,1,0:T(8,128)}, f32[1,4,32,32]{3,2,1,0:T(8,128)S(1)}, u32[]{:S(2)}) copy-start(f32[1,4,32,32]{3,2,1,0:T(8,128)S(1)} %collective-permute-done.4.g1_ref) | copy-start | bytes 49156
  34.6 0.6 %copy-start.6 = (f32[1,4,32,32]{3,2,1,0:T(8,128)}, f32[1,4,32,32]{3,2,1,0:T(8,128)S(1)}, u32[]{:S(2)}) copy-start(f32[1,4,32,32]{3,2,1,0:T(8,128)S(1)} %collective-permute-done.3.g0_ref) | copy-start | bytes 49156
  34.9 0.6 %copy-start.7 = (f32[1,4,32,32]{3,2,1,0:T(8,128)}, f32[1,4,32,32]{3,2,1,0:T(8,128)S(1)}, u32[]{:S(2)}) copy-start(f32[1,4,32,32]{3,2,1,0:T(8,128)S(1)} %collective-permute-done.5.g2_ref) | copy-start | bytes 49156
  35.6 5.2 %collective-permute-start.6 = (f32[1,2,32,32]{3,2,1,0:T(8,128)S(1)}, f32[1,2,32,32]{3,2,1,0:T(8,128)S(1)}, u32[]{:S(2)}, u32[]{:S(2)}) collective-permute-start(f32[1,2,32,32]{3,2,1,0:T(8,128)S(1)} %get-tuple-element.8), channel_id=1, source_target_pairs={{0,8},{4,12},{8,0},{12,4},{1,5},{5,1},{9,13},{13,9},{2,10},{6,14},... | collective-permute-start | bytes 24584 | tf_op jit(solution)/shard_map/gradient_exchange/ppermute | solution.py:409
  36.0 4.8 %collective-permute-start.7 = (f32[1,2,32,32]{3,2,1,0:T(8,128)S(1)}, f32[1,2,32,32]{3,2,1,0:T(8,128)S(1)}, u32[]{:S(2)}, u32[]{:S(2)}) collective-permute-start(f32[1,2,32,32]{3,2,1,0:T(8,128)S(1)} %get-tuple-element.9), channel_id=1, source_target_pairs={{1,13},{5,9},{9,5},{13,1},{3,15},{7,11},{11,7},{15,3},{17,29},{21,... | collective-permute-start | bytes 24584 | tf_op jit(solution)/shard_map/gradient_exchange/ppermute | solution.py:409
  40.7 3.5 %copy-start.10 = (f32[1,2,32,32]{3,2,1,0:T(8,128)}, f32[1,2,32,32]{3,2,1,0:T(8,128)S(1)}, u32[]{:S(2)}) copy-start(f32[1,2,32,32]{3,2,1,0:T(8,128)S(1)} %add_add_fusion.refs_0_) | copy-start | bytes 24580
  40.8 3.5 %collective-permute-start.8 = (f32[1,2,32,32]{3,2,1,0:T(8,128)S(1)}, f32[1,2,32,32]{3,2,1,0:T(8,128)S(1)}, u32[]{:S(2)}, u32[]{:S(2)}) collective-permute-start(f32[1,2,32,32]{3,2,1,0:T(8,128)S(1)} %add_add_fusion.refs_0_), channel_id=1, source_target_pairs={{0,1},{1,0},{2,3},{3,2},{4,5},{5,4},{6,7},{7,6},{8,9},{9,8},{10,11... | collective-permute-start | bytes 24584 | tf_op jit(solution)/shard_map/gradient_exchange/ppermute | solution.py:350
  44.3 0.6 %copy-start.11 = (f32[1,2,32,32]{3,2,1,0:T(8,128)}, f32[1,2,32,32]{3,2,1,0:T(8,128)S(1)}, u32[]{:S(2)}) copy-start(f32[1,2,32,32]{3,2,1,0:T(8,128)S(1)} %collective-permute-done.8.refs_1_) | copy-start | bytes 24580

commit v21 on v18

--- a/solution.py
+++ b/solution.py
@@ -125,13 +125,17 @@
     cols_im = np.concatenate(table_three(c_im.T), axis=0)
     plain = (c_re, c_im, c_re.T, c_im.T, right_w[:B], right_w[B : 2 * B], right_c)
     out = [jnp.asarray(table, jnp.float32) for table in plain]
-    bf = (left_three, right_hm, right_lh, rows_three, cols_re, cols_im)
+    c_hi, c_mid, c_lo = table_three(right_c)
+    c_hm = np.concatenate([c_hi, c_mid], axis=1)
+    c_lh = np.concatenate([c_lo, c_hi], axis=0)
+    bf = (left_three, right_hm, right_lh, rows_three, cols_re, cols_im, c_hm, c_lh)
     return out + [jnp.asarray(table) for table in bf]
 
 
 def imaging_body(
     pos_ref, im_ref, sh_ref, w_ref, dose_ref, mask_ref, ev_ref, ev2_ref, own_ref, goal_ref, h_ref, hc_ref,
     c_re_ref, c_im_ref, ct_re_ref, ct_im_ref, rw_top, rw_bot, rc_ref, la_ref, rhm_ref, rlh_ref, rows_ref, cre_ref, cim_ref,
+    chm_ref, clh_ref,
     slots_ref, f_buf, i_buf, u_buf, w_buf, xr_buf, xi_buf,
 ):
     count = f_buf.shape[0]
@@ -199,7 +203,9 @@
         return carry
 
     lax.fori_loop(0, count, backward, 0)
-    out = dot_full(u_buf[...], rc_ref[...])
+    u_hi, u_mid, u_lo = split_three(u_buf[...])
+    first = dot_parts(u_hi, chm_ref[...]) + dot_parts(u_mid, chm_ref[...])
+    out = first[:, :128] + first[:, 128:] + dot_parts(jnp.concatenate([u_hi, u_lo], axis=1), clh_ref[...])
     acc = jnp.sum((hc_ref[...] * out).reshape(count, B, 128), axis=0)
     flip = jnp.concatenate([acc, jnp.zeros((128 - B, 128), jnp.float32)], axis=0).T
     g_re = flip[0:B, 0:B] + flip[2 * B : 3 * B, 0:B]

time: 47.6 us -> 47.6 us (level)
  no operation moved by 1% of the time
where the time goes in v21:
time: 47.6 us; the launch traced here: 47.3 us
  Pallas kernels  20.4 us (43%)
  starting transfers between devices  12.7 us (27%)
  local copies, waits for them, and re-layouts  4.17 us (9%)
  waiting for transfers between devices  4.03 us (8%)
  other arithmetic  2.7 us (6%)
  between operations  2.21 us (5%)
  matrix products  1.03 us (2%)
    pallas_call x1, Pallas kernels, imaging(): pl.pallas_call(imaging_body, out_shape=jax.ShapeDtypeStruct((4, B, B), jn...  15.1 us
    ppermute x2, starting transfers between devices, gather_split(): got = lax.ppermute(x, ('tile', 'kern'), pairs)  4.75 us
    ppermute x2, starting transfers between devices, sum_parts(): return (x, lax.ppermute(x, axis, [(0, 1), (1, 0)]))  4.68 us
    unnamed x28, local copies, waits for them, and re-layouts  3.83 us
    pallas_call x1, Pallas kernels, group_pixels(): pl.pallas_call(group_pixel_body, out_shape=(shape, jax.ShapeDtypeStruct((...  2.99 us
    ppermute x3, waiting for transfers between devices, on_device(): lax.ppermute(comp, ('corner', 'kern'), [(i, i ^ step) for i in range(4)])  2.67 us
    pallas_call x1, Pallas kernels, pixels(): pl.pallas_call(functools.partial(pixel_body, passes=False), out_shape=sha...  2.31 us
    ppermute x3, starting transfers between devices, on_device(): lax.ppermute(comp, ('corner', 'kern'), [(i, i ^ step) for i in range(4)])  2.2 us
  transfers between devices with their start and end apart: 9, of which 4 were waited for; matrix products, arithmetic and copies ran while one was open for 6% of the time, Pallas kernels for 6%

profile of v21, /device:TPU:0, one launch (start us, length us, event | category | flops | bytes accessed | tf_op | source)
XLA Modules:
  0.0 47.3 jit_solution(460188339678462512)
XLA Ops:
  0.7 0.9 %copy-done = bf16[1,256,256]{2,1,0:T(8,128)(2,1)S(1)} copy-done((bf16[1,256,256]{2,1,0:T(8,128)(2,1)S(1)}, bf16[1,256,256]{2,1,0:T(8,128)(2,1)}, u32[]{:S(2)}) %copy-start) | copy-done | bytes 131096
  1.5 0.2 fusion.8
  1.8 0.2 fusion.6
  2.0 0.2 fusion.17
  2.1 0.2 fusion.16
  2.3 0.2 fusion
  2.5 0.2 fusion.1
  2.7 4.1 %collective-permute-start = (f32[1,2,32,32]{3,2,1,0:T(8,128)S(1)}, f32[1,2,32,32]{3,2,1,0:T(8,128)S(1)}, u32[]{:S(2)}, u32[]{:S(2)}) collective-permute-start(f32[1,2,32,32]{3,2,1,0:T(8,128)S(1)} %pad_maximum_fusion.1.own_ref), channel_id=1, source_target_pairs={{8,0},{12,4},{0,8},{4,12},{5,1},{1,5},{13,9},{9,13},{10,2},{14,6},... | collective-permute-start | bytes 24584 | tf_op jit(solution)/shard_map/master_spectra/ppermute | solution.py:397
  6.8 0.7 %collective-permute-start.1 = (f32[1,2,32,32]{3,2,1,0:T(8,128)S(1)}, f32[1,2,32,32]{3,2,1,0:T(8,128)S(1)}, u32[]{:S(2)}, u32[]{:S(2)}) collective-permute-start(f32[1,2,32,32]{3,2,1,0:T(8,128)S(1)} %pad_maximum_fusion.1.own_ref), channel_id=1, source_target_pairs={{13,1},{9,5},{5,9},{1,13},{15,3},{11,7},{7,11},{3,15},{29,17},{25,... | collective-permute-start | bytes 24584 | tf_op jit(solution)/shard_map/master_spectra/ppermute | solution.py:397
  7.5 0.6 %copy-done.13 = f32[1,12]{1,0:T(1,128)S(1)} copy-done((f32[1,12]{1,0:T(1,128)S(1)}, f32[1,12]{1,0:T(1,128)}, u32[]{:S(2)}) %copy-start.13) | copy-done | bytes 72
  8.3 0.1 copy.38
  8.7 0.5 %copy-done.12 = s32[2]{0:T(128)S(1)} copy-done((s32[2]{0:T(128)S(1)}, s32[2]{0:T(128)}, u32[]{:S(2)}) %copy-start.12) | copy-done | bytes 32
  9.3 0.9 %pad_maximum_fusion = f32[12,32,128]{2,1,0:T(8,128)} fusion(f32[12,32,32]{2,1,0:T(8,128)S(1)} %copy.39, f32[12,32,32]{2,1,0:T(8,128)S(1)} %copy.38, f32[12,32,32]{2,1,0:T(8,128)S(1)} %copy.36), kind=kLoop, calls=%fused_computation.10 | loop fusion | flops 147456 | bytes 344064 | tf_op jit(solution)/shard_map/imaging_kernel/concatenate | solution.py:459
  10.3 2.0 %collective-permute-start.2 = (f32[4,2,32,32]{3,2,1,0:T(8,128)S(1)}, f32[4,2,32,32]{3,2,1,0:T(8,128)S(1)}, u32[]{:S(2)}, u32[]{:S(2)}) collective-permute-start(f32[4,2,32,32]{3,2,1,0:T(8,128)S(1)} %select_add_fusion.ev_ref), channel_id=1, source_target_pairs={{0,1},{1,0},{2,3},{3,2},{4,5},{5,4},{6,7},{7,6},{8,9},{9,8},{10,11... | collective-permute-start | bytes 98312 | tf_op jit(solution)/shard_map/master_spectra/ppermute | solution.py:357
  12.3 0.6 %pad_add_fusion.pos_ref = s32[2]{0:T(128)} fusion(s32[1]{0:T(128)} %bitcast.1, s32[1]{0:T(128)} %bitcast), kind=kLoop, calls=%fused_computation.30 | loop fusion | flops 2 | bytes 16 | tf_op jit(solution)/shard_map/imaging_kernel/stack | solution.py:462
  13.6 0.6 %copy-done.9 = f32[4,2,32,32]{3,2,1,0:T(8,128)} copy-done((f32[4,2,32,32]{3,2,1,0:T(8,128)}, f32[4,2,32,32]{3,2,1,0:T(8,128)S(1)}, u32[]{:S(2)}) %copy-start.9) | copy-done | bytes 32792
  14.2 15.1 %imaging_kernel.1 = f32[4,32,32]{2,1,0:T(8,128)} custom-call(s32[2]{0:T(128)} %pad_add_fusion.pos_ref, s32[2]{0:T(128)} %im_ref.1, s32[2,2]{1,0:T(2,128)} %sh_ref.1, f32[12]{0:T(128)} %bitcast.68, f32[1]{0:T(128)S(6)} %copy.41.dose_ref, bf16[2,256,256]{2,1,0:T(8,128)(2,1)} %mask_ref.1, f32[4,2,32,32]{3,2,1,0:T(8,128)} %copy-done.4, ...), custom_call_target="tpu_custom_call" | custom-call | tf_op jit(solution)/shard_map/imaging_kernel/pallas_call | solution.py:226
  29.4 1.6 %collective-permute-start.4 = (f32[1,4,32,32]{3,2,1,0:T(8,128)}, f32[1,4,32,32]{3,2,1,0:T(8,128)S(1)}, u32[]{:S(2)}, u32[]{:S(2)}) collective-permute-start(f32[1,4,32,32]{3,2,1,0:T(8,128)} %bitcast.61), channel_id=1, source_target_pairs={{0,2},{1,3},{2,0},{3,1},{4,6},{5,7},{6,4},{7,5},{8,10},{9,11},{10,... | collective-permute-start | bytes 49160 | tf_op jit(solution)/shard_map/gradient_exchange/ppermute | solution.py:476
  31.0 0.6 %collective-permute-start.5 = (f32[1,4,32,32]{3,2,1,0:T(8,128)}, f32[1,4,32,32]{3,2,1,0:T(8,128)S(1)}, u32[]{:S(2)}, u32[]{:S(2)}) collective-permute-start(f32[1,4,32,32]{3,2,1,0:T(8,128)} %bitcast.63), channel_id=1, source_target_pairs={{0,3},{1,2},{2,1},{3,0},{4,7},{5,6},{6,5},{7,4},{8,11},{9,10},{10,... | collective-permute-start | bytes 49160 | tf_op jit(solution)/shard_map/gradient_exchange/ppermute | solution.py:476
  31.6 2.3 %collective-permute-done.4.g1_ref = f32[1,4,32,32]{3,2,1,0:T(8,128)S(1)} collective-permute-done((f32[1,4,32,32]{3,2,1,0:T(8,128)}, f32[1,4,32,32]{3,2,1,0:T(8,128)S(1)}, u32[]{:S(2)}, u32[]{:S(2)}) %collective-permute-start.4) | collective-permute-done | bytes 16416 | tf_op jit(solution)/shard_map/gradient_exchange/ppermute | solution.py:476
  33.9 0.8 %fusion.11 = f32[2,32,32]{2,1,0:T(8,128)S(1)} fusion(f32[1,4,32,32]{3,2,1,0:T(8,128)S(1)} %collective-permute-done.4.g1_ref, f32[1,4,32,32]{3,2,1,0:T(8,128)} %bitcast.64), kind=kLoop, calls=%fused_computation.20 | loop fusion | flops 2048 | bytes 24576 | tf_op jit(solution)/shard_map/gradient_exchange/mul | solution.py:495
  34.7 0.3 collective-permute-done.5.g2_ref
  35.2 0.2 copy-done.6
  35.3 0.3 copy-done.7
  35.7 0.4 collective-permute-start.6
  36.1 0.7 %collective-permute-start.7 = (f32[1,2,32,32]{3,2,1,0:T(8,128)S(1)}, f32[1,2,32,32]{3,2,1,0:T(8,128)S(1)}, u32[]{:S(2)}, u32[]{:S(2)}) collective-permute-start(f32[1,2,32,32]{3,2,1,0:T(8,128)S(1)} %get-tuple-element.9), channel_id=1, source_target_pairs={{1,13},{5,9},{9,5},{13,1},{3,15},{7,11},{11,7},{15,3},{17,29},{21,... | collective-permute-start | bytes 24584 | tf_op jit(solution)/shard_map/gradient_exchange/ppermute | solution.py:416
  36.7 3.0 %gradient_exchange.1 = (f32[2,256,256]{2,1,0:T(8,128)}, f32[1,1,1,1]{3,2,1,0:T(1,128)}) custom-call(f32[1,4,32,32]{3,2,1,0:T(8,128)} %bitcast.65, f32[1,4,32,32]{3,2,1,0:T(8,128)} %copy-done.6, f32[1,4,32,32]{3,2,1,0:T(8,128)} %copy-done.5, f32[1,4,32,32]{3,2,1,0:T(8,128)} %copy-done.7, f32[32,256]{1,0:T(8,128)} %constant.71.clone.c_re_ref.refs_2_, ...), custom_call_target="tpu_custom_call" | custom-call | tf_op jit(solution)/shard_map/gradient_exchange/pallas_call | solution.py:294
  40.4 0.5 %collective-permute-done.6 = f32[1,2,32,32]{3,2,1,0:T(8,128)S(1)} collective-permute-done((f32[1,2,32,32]{3,2,1,0:T(8,128)S(1)}, f32[1,2,32,32]{3,2,1,0:T(8,128)S(1)}, u32[]{:S(2)}, u32[]{:S(2)}) %collective-permute-start.6) | collective-permute-done | bytes 8224 | tf_op jit(solution)/shard_map/gradient_exchange/ppermute | solution.py:416
  40.9 2.6 %collective-permute-start.8 = (f32[1,2,32,32]{3,2,1,0:T(8,128)S(1)}, f32[1,2,32,32]{3,2,1,0:T(8,128)S(1)}, u32[]{:S(2)}, u32[]{:S(2)}) collective-permute-start(f32[1,2,32,32]{3,2,1,0:T(8,128)S(1)} %add_add_fusion.refs_0_), channel_id=1, source_target_pairs={{0,1},{1,0},{2,3},{3,2},{4,5},{5,4},{6,7},{7,6},{8,9},{9,8},{10,11... | collective-permute-start | bytes 24584 | tf_op jit(solution)/shard_map/gradient_exchange/ppermute | solution.py:357
  43.5 0.9 %collective-permute-done.8.refs_1_ = f32[1,2,32,32]{3,2,1,0:T(8,128)S(1)} collective-permute-done((f32[1,2,32,32]{3,2,1,0:T(8,128)S(1)}, f32[1,2,32,32]{3,2,1,0:T(8,128)S(1)}, u32[]{:S(2)}, u32[]{:S(2)}) %collective-permute-start.8) | collective-permute-done | bytes 8224 | tf_op jit(solution)/shard_map/gradient_exchange/ppermute | solution.py:357
  44.4 0.6 %copy-done.11 = f32[1,2,32,32]{3,2,1,0:T(8,128)} copy-done((f32[1,2,32,32]{3,2,1,0:T(8,128)}, f32[1,2,32,32]{3,2,1,0:T(8,128)S(1)}, u32[]{:S(2)}) %copy-start.11) | copy-done | bytes 8216
  45.0 2.3 %pixel_gradients.1 = f32[1,256,256]{2,1,0:T(8,128)} custom-call(f32[1,2,32,32]{3,2,1,0:T(8,128)} %copy-done.10, f32[1,2,32,32]{3,2,1,0:T(8,128)} %copy-done.11, f32[32,256]{1,0:T(8,128)} %constant.71.clone.c_re_ref.refs_2_, f32[32,256]{1,0:T(8,128)} %constant.72.clone.c_im_ref.refs_3_, bf16[256,384]{1,0:T(8,128)(2,1)} %constant.86.clone.left_ref.refs_4_), custom_call_target="tpu_custom_call" | custom-call | tf_op jit(solution)/shard_map/pixel_gradients/pallas_call | solution.py:314
  (41 shorter events, 0.8 us)
Async XLA Ops:
  0.6 0.9 %copy-start = (bf16[1,256,256]{2,1,0:T(8,128)(2,1)S(1)}, bf16[1,256,256]{2,1,0:T(8,128)(2,1)}, u32[]{:S(2)}) copy-start(bf16[1,256,256]{2,1,0:T(8,128)(2,1)} %param.32) | copy-start | bytes 393220
  0.6 0.9 %copy-start.2 = (f32[32,256]{1,0:T(8,128)S(1)}, f32[32,256]{1,0:T(8,128)}, u32[]{:S(2)}) copy-start(f32[32,256]{1,0:T(8,128)} %constant.71.clone.c_re_ref.refs_2_) | copy-start | bytes 98308
  0.7 1.1 %copy-start.3 = (f32[32,256]{1,0:T(8,128)S(1)}, f32[32,256]{1,0:T(8,128)}, u32[]{:S(2)}) copy-start(f32[32,256]{1,0:T(8,128)} %constant.72.clone.c_im_ref.refs_3_) | copy-start | bytes 98308
  0.7 7.4 %copy-start.1 = (f32[1,12,2,32,32]{4,3,2,1,0:T(8,128)S(1)}, f32[1,12,2,32,32]{4,3,2,1,0:T(8,128)}, u32[]{:S(2)}) copy-start(f32[1,12,2,32,32]{4,3,2,1,0:T(8,128)} %param.36) | copy-start | bytes 294916
  2.6 5.6 %copy-start.8 = (f32[1,2,32,32]{3,2,1,0:T(8,128)}, f32[1,2,32,32]{3,2,1,0:T(8,128)S(1)}, u32[]{:S(2)}) copy-start(f32[1,2,32,32]{3,2,1,0:T(8,128)S(1)} %pad_maximum_fusion.1.own_ref) | copy-start | bytes 24580
  2.7 7.5 %collective-permute-start = (f32[1,2,32,32]{3,2,1,0:T(8,128)S(1)}, f32[1,2,32,32]{3,2,1,0:T(8,128)S(1)}, u32[]{:S(2)}, u32[]{:S(2)}) collective-permute-start(f32[1,2,32,32]{3,2,1,0:T(8,128)S(1)} %pad_maximum_fusion.1.own_ref), channel_id=1, source_target_pairs={{8,0},{12,4},{0,8},{4,12},{5,1},{1,5},{13,9},{9,13},{10,2},{14,6},... | collective-permute-start | bytes 24584 | tf_op jit(solution)/shard_map/master_spectra/ppermute | solution.py:397
  6.8 3.4 %collective-permute-start.1 = (f32[1,2,32,32]{3,2,1,0:T(8,128)S(1)}, f32[1,2,32,32]{3,2,1,0:T(8,128)S(1)}, u32[]{:S(2)}, u32[]{:S(2)}) collective-permute-start(f32[1,2,32,32]{3,2,1,0:T(8,128)S(1)} %pad_maximum_fusion.1.own_ref), channel_id=1, source_target_pairs={{13,1},{9,5},{5,9},{1,13},{15,3},{11,7},{7,11},{3,15},{29,17},{25,... | collective-permute-start | bytes 24584 | tf_op jit(solution)/shard_map/master_spectra/ppermute | solution.py:397
  7.4 0.7 %copy-start.13 = (f32[1,12]{1,0:T(1,128)S(1)}, f32[1,12]{1,0:T(1,128)}, u32[]{:S(2)}) copy-start(f32[1,12]{1,0:T(1,128)} %param.37) | copy-start | bytes 148
  8.5 0.7 %copy-start.12 = (s32[2]{0:T(128)S(1)}, s32[2]{0:T(128)}, u32[]{:S(2)}) copy-start(s32[2]{0:T(128)} %im_ref.1) | copy-start | bytes 28
  10.3 3.3 %copy-start.4 = (f32[4,2,32,32]{3,2,1,0:T(8,128)}, f32[4,2,32,32]{3,2,1,0:T(8,128)S(1)}, u32[]{:S(2)}) copy-start(f32[4,2,32,32]{3,2,1,0:T(8,128)S(1)} %select_add_fusion.ev_ref) | copy-start | bytes 98308
  10.3 3.3 %collective-permute-start.2 = (f32[4,2,32,32]{3,2,1,0:T(8,128)S(1)}, f32[4,2,32,32]{3,2,1,0:T(8,128)S(1)}, u32[]{:S(2)}, u32[]{:S(2)}) collective-permute-start(f32[4,2,32,32]{3,2,1,0:T(8,128)S(1)} %select_add_fusion.ev_ref), channel_id=1, source_target_pairs={{0,1},{1,0},{2,3},{3,2},{4,5},{5,4},{6,7},{7,6},{8,9},{9,8},{10,11... | collective-permute-start | bytes 98312 | tf_op jit(solution)/shard_map/master_spectra/ppermute | solution.py:357
  13.6 0.6 %copy-start.9 = (f32[4,2,32,32]{3,2,1,0:T(8,128)}, f32[4,2,32,32]{3,2,1,0:T(8,128)S(1)}, u32[]{:S(2)}) copy-start(f32[4,2,32,32]{3,2,1,0:T(8,128)S(1)} %collective-permute-done.2.ev2_ref) | copy-start | bytes 98308
  29.4 4.5 %collective-permute-start.4 = (f32[1,4,32,32]{3,2,1,0:T(8,128)}, f32[1,4,32,32]{3,2,1,0:T(8,128)S(1)}, u32[]{:S(2)}, u32[]{:S(2)}) collective-permute-start(f32[1,4,32,32]{3,2,1,0:T(8,128)} %bitcast.61), channel_id=1, source_target_pairs={{0,2},{1,3},{2,0},{3,1},{4,6},{5,7},{6,4},{7,5},{8,10},{9,11},{10,... | collective-permute-start | bytes 49160 | tf_op jit(solution)/shard_map/gradient_exchange/ppermute | solution.py:476
  31.0 3.7 %collective-permute-start.3 = (f32[1,4,32,32]{3,2,1,0:T(8,128)}, f32[1,4,32,32]{3,2,1,0:T(8,128)S(1)}, u32[]{:S(2)}, u32[]{:S(2)}) collective-permute-start(f32[1,4,32,32]{3,2,1,0:T(8,128)} %bitcast.62), channel_id=1, source_target_pairs={{0,1},{1,0},{2,3},{3,2},{4,5},{5,4},{6,7},{7,6},{8,9},{9,8},{10,11... | collective-permute-start | bytes 49160 | tf_op jit(solution)/shard_map/gradient_exchange/ppermute | solution.py:476
  31.0 4.1 %collective-permute-start.5 = (f32[1,4,32,32]{3,2,1,0:T(8,128)}, f32[1,4,32,32]{3,2,1,0:T(8,128)S(1)}, u32[]{:S(2)}, u32[]{:S(2)}) collective-permute-start(f32[1,4,32,32]{3,2,1,0:T(8,128)} %bitcast.63), channel_id=1, source_target_pairs={{0,3},{1,2},{2,1},{3,0},{4,7},{5,6},{6,5},{7,4},{8,11},{9,10},{10,... | collective-permute-start | bytes 49160 | tf_op jit(solution)/shard_map/gradient_exchange/ppermute | solution.py:476
  33.9 1.1 %copy-start.5 = (f32[1,4,32,32]{3,2,1,0:T(8,128)}, f32[1,4,32,32]{3,2,1,0:T(8,128)S(1)}, u32[]{:S(2)}) copy-start(f32[1,4,32,32]{3,2,1,0:T(8,128)S(1)} %collective-permute-done.4.g1_ref) | copy-start | bytes 49156
  34.7 0.6 %copy-start.6 = (f32[1,4,32,32]{3,2,1,0:T(8,128)}, f32[1,4,32,32]{3,2,1,0:T(8,128)S(1)}, u32[]{:S(2)}) copy-start(f32[1,4,32,32]{3,2,1,0:T(8,128)S(1)} %collective-permute-done.3.g0_ref) | copy-start | bytes 49156
  35.0 0.6 %copy-start.7 = (f32[1,4,32,32]{3,2,1,0:T(8,128)}, f32[1,4,32,32]{3,2,1,0:T(8,128)S(1)}, u32[]{:S(2)}) copy-start(f32[1,4,32,32]{3,2,1,0:T(8,128)S(1)} %collective-permute-done.5.g2_ref) | copy-start | bytes 49156
  35.7 5.2 %collective-permute-start.6 = (f32[1,2,32,32]{3,2,1,0:T(8,128)S(1)}, f32[1,2,32,32]{3,2,1,0:T(8,128)S(1)}, u32[]{:S(2)}, u32[]{:S(2)}) collective-permute-start(f32[1,2,32,32]{3,2,1,0:T(8,128)S(1)} %get-tuple-element.8), channel_id=1, source_target_pairs={{0,8},{4,12},{8,0},{12,4},{1,5},{5,1},{9,13},{13,9},{2,10},{6,14},... | collective-permute-start | bytes 24584 | tf_op jit(solution)/shard_map/gradient_exchange/ppermute | solution.py:416
  36.1 4.8 %collective-permute-start.7 = (f32[1,2,32,32]{3,2,1,0:T(8,128)S(1)}, f32[1,2,32,32]{3,2,1,0:T(8,128)S(1)}, u32[]{:S(2)}, u32[]{:S(2)}) collective-permute-start(f32[1,2,32,32]{3,2,1,0:T(8,128)S(1)} %get-tuple-element.9), channel_id=1, source_target_pairs={{1,13},{5,9},{9,5},{13,1},{3,15},{7,11},{11,7},{15,3},{17,29},{21,... | collective-permute-start | bytes 24584 | tf_op jit(solution)/shard_map/gradient_exchange/ppermute | solution.py:416
  40.9 3.5 %copy-start.10 = (f32[1,2,32,32]{3,2,1,0:T(8,128)}, f32[1,2,32,32]{3,2,1,0:T(8,128)S(1)}, u32[]{:S(2)}) copy-start(f32[1,2,32,32]{3,2,1,0:T(8,128)S(1)} %add_add_fusion.refs_0_) | copy-start | bytes 24580
  40.9 3.5 %collective-permute-start.8 = (f32[1,2,32,32]{3,2,1,0:T(8,128)S(1)}, f32[1,2,32,32]{3,2,1,0:T(8,128)S(1)}, u32[]{:S(2)}, u32[]{:S(2)}) collective-permute-start(f32[1,2,32,32]{3,2,1,0:T(8,128)S(1)} %add_add_fusion.refs_0_), channel_id=1, source_target_pairs={{0,1},{1,0},{2,3},{3,2},{4,5},{5,4},{6,7},{7,6},{8,9},{9,8},{10,11... | collective-permute-start | bytes 24584 | tf_op jit(solution)/shard_map/gradient_exchange/ppermute | solution.py:357
  44.4 0.6 %copy-start.11 = (f32[1,2,32,32]{3,2,1,0:T(8,128)}, f32[1,2,32,32]{3,2,1,0:T(8,128)S(1)}, u32[]{:S(2)}) copy-start(f32[1,2,32,32]{3,2,1,0:T(8,128)S(1)} %collective-permute-done.8.refs_1_) | copy-start | bytes 24580

commit v22 on v18

--- a/solution.py
+++ b/solution.py
@@ -167,7 +167,7 @@
         xi_buf[rows, :] = h_re * s_im + h_im * s_re
         return carry
 
-    lax.fori_loop(0, count, spectrum, 0)
+    lax.fori_loop(0, count, spectrum, 0, unroll=True)
     w_buf[...] = dot_full(xr_buf[...], rw_top[...]) + dot_full(xi_buf[...], rw_bot[...])
 
     def forward(k, carry):
@@ -181,7 +181,7 @@
         i_buf[...] += w_ref[k] * (power[:, :P_SIZE] + power[:, P_SIZE:])
         return carry
 
-    lax.fori_loop(0, count, forward, 0)
+    lax.fori_loop(0, count, forward, 0, unroll=2)
     dose = dose_ref[0]
     resist = 1.0 / (1.0 + jnp.exp(-(steepness * (dose * i_buf[...] - threshold))))
     goal = goal_ref[pos].astype(jnp.float32)
@@ -198,7 +198,7 @@
         u_buf[pl.ds(pl.multiple_of(k * B, B), B), :] = jnp.concatenate([flip[:B], flip[B : 2 * B]], axis=1)
         return carry
 
-    lax.fori_loop(0, count, backward, 0)
+    lax.fori_loop(0, count, backward, 0, unroll=2)
     out = dot_full(u_buf[...], rc_ref[...])
     acc = jnp.sum((hc_ref[...] * out).reshape(count, B, 128), axis=0)
     flip = jnp.concatenate([acc, jnp.zeros((128 - B, 128), jnp.float32)], axis=0).T

time: 47.6 us -> 45.2 us (0.950)
  Pallas kernels: 20.5 us -> 18.1 us
    pallas_call x1, Pallas kernels: 15.2 us -> 12.8 us  [imaging(): pl.pallas_call(imaging_body, out_shape=jax.ShapeDtypeStruct((4, B, B), jn...]
  transfers between devices with their start and end apart: 9 -> 9, of which waited for: 4 -> 4; matrix products, arithmetic and copies ran while one was open for 6% -> 6% of each run, Pallas kernels for 6% -> 7%
where the time goes in v22:
time: 45.2 us; the launch traced here: 44.8 us
  Pallas kernels  18.1 us (40%)
  starting transfers between devices  12.6 us (28%)
  local copies, waits for them, and re-layouts  4.17 us (9%)
  waiting for transfers between devices  4.01 us (9%)
  other arithmetic  2.7 us (6%)
  between operations  2.21 us (5%)
  matrix products  1.03 us (2%)
    pallas_call x1, Pallas kernels, imaging(): pl.pallas_call(imaging_body, out_shape=jax.ShapeDtypeStruct((4, B, B), jn...  12.8 us
    ppermute x2, starting transfers between devices, gather_split(): got = lax.ppermute(x, ('tile', 'kern'), pairs)  4.75 us
    ppermute x2, starting transfers between devices, sum_parts(): return (x, lax.ppermute(x, axis, [(0, 1), (1, 0)]))  4.68 us
    unnamed x28, local copies, waits for them, and re-layouts  3.83 us
    pallas_call x1, Pallas kernels, group_pixels(): pl.pallas_call(group_pixel_body, out_shape=(shape, jax.ShapeDtypeStruct((...  2.99 us
    ppermute x3, waiting for transfers between devices, on_device(): lax.ppermute(comp, ('corner', 'kern'), [(i, i ^ step) for i in range(4)])  2.66 us
    pallas_call x1, Pallas kernels, pixels(): pl.pallas_call(functools.partial(pixel_body, passes=False), out_shape=sha...  2.31 us
    ppermute x3, starting transfers between devices, on_device(): lax.ppermute(comp, ('corner', 'kern'), [(i, i ^ step) for i in range(4)])  2.14 us
  transfers between devices with their start and end apart: 9, of which 4 were waited for; matrix products, arithmetic and copies ran while one was open for 6% of the time, Pallas kernels for 7%

profile of v22, /device:TPU:0, one launch (start us, length us, event | category | flops | bytes accessed | tf_op | source)
XLA Modules:
  0.0 44.8 jit_solution(7314886285164339908)
XLA Ops:
  0.7 0.9 %copy-done = bf16[1,256,256]{2,1,0:T(8,128)(2,1)S(1)} copy-done((bf16[1,256,256]{2,1,0:T(8,128)(2,1)S(1)}, bf16[1,256,256]{2,1,0:T(8,128)(2,1)}, u32[]{:S(2)}) %copy-start) | copy-done | bytes 131096
  1.5 0.2 fusion.8
  1.8 0.2 fusion.6
  2.0 0.2 fusion.17
  2.1 0.2 fusion.16
  2.3 0.2 fusion
  2.5 0.2 fusion.1
  2.7 4.1 %collective-permute-start = (f32[1,2,32,32]{3,2,1,0:T(8,128)S(1)}, f32[1,2,32,32]{3,2,1,0:T(8,128)S(1)}, u32[]{:S(2)}, u32[]{:S(2)}) collective-permute-start(f32[1,2,32,32]{3,2,1,0:T(8,128)S(1)} %pad_maximum_fusion.1.own_ref), channel_id=1, source_target_pairs={{8,0},{12,4},{0,8},{4,12},{5,1},{1,5},{13,9},{9,13},{10,2},{14,6},... | collective-permute-start | bytes 24584 | tf_op jit(solution)/shard_map/master_spectra/ppermute | solution.py:391
  6.8 0.7 %collective-permute-start.1 = (f32[1,2,32,32]{3,2,1,0:T(8,128)S(1)}, f32[1,2,32,32]{3,2,1,0:T(8,128)S(1)}, u32[]{:S(2)}, u32[]{:S(2)}) collective-permute-start(f32[1,2,32,32]{3,2,1,0:T(8,128)S(1)} %pad_maximum_fusion.1.own_ref), channel_id=1, source_target_pairs={{13,1},{9,5},{5,9},{1,13},{15,3},{11,7},{7,11},{3,15},{29,17},{25,... | collective-permute-start | bytes 24584 | tf_op jit(solution)/shard_map/master_spectra/ppermute | solution.py:391
  7.5 0.6 %copy-done.13 = f32[1,12]{1,0:T(1,128)S(1)} copy-done((f32[1,12]{1,0:T(1,128)S(1)}, f32[1,12]{1,0:T(1,128)}, u32[]{:S(2)}) %copy-start.13) | copy-done | bytes 72
  8.3 0.1 copy.36
  8.7 0.5 %copy-done.12 = s32[2]{0:T(128)S(1)} copy-done((s32[2]{0:T(128)S(1)}, s32[2]{0:T(128)}, u32[]{:S(2)}) %copy-start.12) | copy-done | bytes 32
  9.3 0.9 %pad_maximum_fusion = f32[12,32,128]{2,1,0:T(8,128)} fusion(f32[12,32,32]{2,1,0:T(8,128)S(1)} %copy.37, f32[12,32,32]{2,1,0:T(8,128)S(1)} %copy.36, f32[12,32,32]{2,1,0:T(8,128)S(1)} %copy.34), kind=kLoop, calls=%fused_computation.10 | loop fusion | flops 147456 | bytes 344064 | tf_op jit(solution)/shard_map/imaging_kernel/concatenate | solution.py:453
  10.3 2.0 %collective-permute-start.2 = (f32[4,2,32,32]{3,2,1,0:T(8,128)S(1)}, f32[4,2,32,32]{3,2,1,0:T(8,128)S(1)}, u32[]{:S(2)}, u32[]{:S(2)}) collective-permute-start(f32[4,2,32,32]{3,2,1,0:T(8,128)S(1)} %select_add_fusion.ev_ref), channel_id=1, source_target_pairs={{0,1},{1,0},{2,3},{3,2},{4,5},{5,4},{6,7},{7,6},{8,9},{9,8},{10,11... | collective-permute-start | bytes 98312 | tf_op jit(solution)/shard_map/master_spectra/ppermute | solution.py:351
  12.3 0.6 %pad_add_fusion.pos_ref = s32[2]{0:T(128)} fusion(s32[1]{0:T(128)} %bitcast.1, s32[1]{0:T(128)} %bitcast), kind=kLoop, calls=%fused_computation.30 | loop fusion | flops 2 | bytes 16 | tf_op jit(solution)/shard_map/imaging_kernel/stack | solution.py:456
  13.6 0.6 %copy-done.9 = f32[4,2,32,32]{3,2,1,0:T(8,128)} copy-done((f32[4,2,32,32]{3,2,1,0:T(8,128)}, f32[4,2,32,32]{3,2,1,0:T(8,128)S(1)}, u32[]{:S(2)}) %copy-start.9) | copy-done | bytes 32792
  14.2 12.8 %imaging_kernel.1 = f32[4,32,32]{2,1,0:T(8,128)} custom-call(s32[2]{0:T(128)} %pad_add_fusion.pos_ref, s32[2]{0:T(128)} %im_ref.1, s32[2,2]{1,0:T(2,128)} %sh_ref.1, f32[12]{0:T(128)} %bitcast.68, f32[1]{0:T(128)S(6)} %copy.39.dose_ref, bf16[2,256,256]{2,1,0:T(8,128)(2,1)} %mask_ref.1, f32[4,2,32,32]{3,2,1,0:T(8,128)} %copy-done.4, ...), custom_call_target="tpu_custom_call" | custom-call | tf_op jit(solution)/shard_map/imaging_kernel/pallas_call | solution.py:220
  27.0 1.5 %collective-permute-start.4 = (f32[1,4,32,32]{3,2,1,0:T(8,128)}, f32[1,4,32,32]{3,2,1,0:T(8,128)S(1)}, u32[]{:S(2)}, u32[]{:S(2)}) collective-permute-start(f32[1,4,32,32]{3,2,1,0:T(8,128)} %bitcast.61), channel_id=1, source_target_pairs={{0,2},{1,3},{2,0},{3,1},{4,6},{5,7},{6,4},{7,5},{8,10},{9,11},{10,... | collective-permute-start | bytes 49160 | tf_op jit(solution)/shard_map/gradient_exchange/ppermute | solution.py:470
  28.5 0.7 %collective-permute-start.5 = (f32[1,4,32,32]{3,2,1,0:T(8,128)}, f32[1,4,32,32]{3,2,1,0:T(8,128)S(1)}, u32[]{:S(2)}, u32[]{:S(2)}) collective-permute-start(f32[1,4,32,32]{3,2,1,0:T(8,128)} %bitcast.63), channel_id=1, source_target_pairs={{0,3},{1,2},{2,1},{3,0},{4,7},{5,6},{6,5},{7,4},{8,11},{9,10},{10,... | collective-permute-start | bytes 49160 | tf_op jit(solution)/shard_map/gradient_exchange/ppermute | solution.py:470
  29.2 2.3 %collective-permute-done.4.g1_ref = f32[1,4,32,32]{3,2,1,0:T(8,128)S(1)} collective-permute-done((f32[1,4,32,32]{3,2,1,0:T(8,128)}, f32[1,4,32,32]{3,2,1,0:T(8,128)S(1)}, u32[]{:S(2)}, u32[]{:S(2)}) %collective-permute-start.4) | collective-permute-done | bytes 16416 | tf_op jit(solution)/shard_map/gradient_exchange/ppermute | solution.py:470
  31.5 0.8 %fusion.11 = f32[2,32,32]{2,1,0:T(8,128)S(1)} fusion(f32[1,4,32,32]{3,2,1,0:T(8,128)S(1)} %collective-permute-done.4.g1_ref, f32[1,4,32,32]{3,2,1,0:T(8,128)} %bitcast.64), kind=kLoop, calls=%fused_computation.20 | loop fusion | flops 2048 | bytes 24576 | tf_op jit(solution)/shard_map/gradient_exchange/mul | solution.py:489
  32.3 0.3 collective-permute-done.5.g2_ref
  32.7 0.2 copy-done.6
  32.9 0.3 copy-done.7
  33.2 0.4 collective-permute-start.6
  33.7 0.7 %collective-permute-start.7 = (f32[1,2,32,32]{3,2,1,0:T(8,128)S(1)}, f32[1,2,32,32]{3,2,1,0:T(8,128)S(1)}, u32[]{:S(2)}, u32[]{:S(2)}) collective-permute-start(f32[1,2,32,32]{3,2,1,0:T(8,128)S(1)} %get-tuple-element.9), channel_id=1, source_target_pairs={{1,13},{5,9},{9,5},{13,1},{3,15},{7,11},{11,7},{15,3},{17,29},{21,... | collective-permute-start | bytes 24584 | tf_op jit(solution)/shard_map/gradient_exchange/ppermute | solution.py:410
  34.3 3.0 %gradient_exchange.1 = (f32[2,256,256]{2,1,0:T(8,128)}, f32[1,1,1,1]{3,2,1,0:T(1,128)}) custom-call(f32[1,4,32,32]{3,2,1,0:T(8,128)} %bitcast.65, f32[1,4,32,32]{3,2,1,0:T(8,128)} %copy-done.6, f32[1,4,32,32]{3,2,1,0:T(8,128)} %copy-done.5, f32[1,4,32,32]{3,2,1,0:T(8,128)} %copy-done.7, f32[32,256]{1,0:T(8,128)} %constant.67.clone.c_re_ref.refs_2_, ...), custom_call_target="tpu_custom_call" | custom-call | tf_op jit(solution)/shard_map/gradient_exchange/pallas_call | solution.py:288
  37.9 0.5 %collective-permute-done.6 = f32[1,2,32,32]{3,2,1,0:T(8,128)S(1)} collective-permute-done((f32[1,2,32,32]{3,2,1,0:T(8,128)S(1)}, f32[1,2,32,32]{3,2,1,0:T(8,128)S(1)}, u32[]{:S(2)}, u32[]{:S(2)}) %collective-permute-start.6) | collective-permute-done | bytes 8224 | tf_op jit(solution)/shard_map/gradient_exchange/ppermute | solution.py:410
  38.4 2.6 %collective-permute-start.8 = (f32[1,2,32,32]{3,2,1,0:T(8,128)S(1)}, f32[1,2,32,32]{3,2,1,0:T(8,128)S(1)}, u32[]{:S(2)}, u32[]{:S(2)}) collective-permute-start(f32[1,2,32,32]{3,2,1,0:T(8,128)S(1)} %add_add_fusion.refs_0_), channel_id=1, source_target_pairs={{0,1},{1,0},{2,3},{3,2},{4,5},{5,4},{6,7},{7,6},{8,9},{9,8},{10,11... | collective-permute-start | bytes 24584 | tf_op jit(solution)/shard_map/gradient_exchange/ppermute | solution.py:351
  41.1 0.9 %collective-permute-done.8.refs_1_ = f32[1,2,32,32]{3,2,1,0:T(8,128)S(1)} collective-permute-done((f32[1,2,32,32]{3,2,1,0:T(8,128)S(1)}, f32[1,2,32,32]{3,2,1,0:T(8,128)S(1)}, u32[]{:S(2)}, u32[]{:S(2)}) %collective-permute-start.8) | collective-permute-done | bytes 8224 | tf_op jit(solution)/shard_map/gradient_exchange/ppermute | solution.py:351
  41.9 0.6 %copy-done.11 = f32[1,2,32,32]{3,2,1,0:T(8,128)} copy-done((f32[1,2,32,32]{3,2,1,0:T(8,128)}, f32[1,2,32,32]{3,2,1,0:T(8,128)S(1)}, u32[]{:S(2)}) %copy-start.11) | copy-done | bytes 8216
  42.5 2.3 %pixel_gradients.1 = f32[1,256,256]{2,1,0:T(8,128)} custom-call(f32[1,2,32,32]{3,2,1,0:T(8,128)} %copy-done.10, f32[1,2,32,32]{3,2,1,0:T(8,128)} %copy-done.11, f32[32,256]{1,0:T(8,128)} %constant.67.clone.c_re_ref.refs_2_, f32[32,256]{1,0:T(8,128)} %constant.68.clone.c_im_ref.refs_3_, bf16[256,384]{1,0:T(8,128)(2,1)} %constant.80.clone.left_ref.refs_4_), custom_call_target="tpu_custom_call" | custom-call | tf_op jit(solution)/shard_map/pixel_gradients/pallas_call | solution.py:308
  (41 shorter events, 0.8 us)
Async XLA Ops:
  0.6 0.9 %copy-start = (bf16[1,256,256]{2,1,0:T(8,128)(2,1)S(1)}, bf16[1,256,256]{2,1,0:T(8,128)(2,1)}, u32[]{:S(2)}) copy-start(bf16[1,256,256]{2,1,0:T(8,128)(2,1)} %param.30) | copy-start | bytes 393220
  0.6 0.9 %copy-start.2 = (f32[32,256]{1,0:T(8,128)S(1)}, f32[32,256]{1,0:T(8,128)}, u32[]{:S(2)}) copy-start(f32[32,256]{1,0:T(8,128)} %constant.67.clone.c_re_ref.refs_2_) | copy-start | bytes 98308
  0.7 1.1 %copy-start.3 = (f32[32,256]{1,0:T(8,128)S(1)}, f32[32,256]{1,0:T(8,128)}, u32[]{:S(2)}) copy-start(f32[32,256]{1,0:T(8,128)} %constant.68.clone.c_im_ref.refs_3_) | copy-start | bytes 98308
  0.7 7.4 %copy-start.1 = (f32[1,12,2,32,32]{4,3,2,1,0:T(8,128)S(1)}, f32[1,12,2,32,32]{4,3,2,1,0:T(8,128)}, u32[]{:S(2)}) copy-start(f32[1,12,2,32,32]{4,3,2,1,0:T(8,128)} %param.34) | copy-start | bytes 294916
  2.6 5.6 %copy-start.8 = (f32[1,2,32,32]{3,2,1,0:T(8,128)}, f32[1,2,32,32]{3,2,1,0:T(8,128)S(1)}, u32[]{:S(2)}) copy-start(f32[1,2,32,32]{3,2,1,0:T(8,128)S(1)} %pad_maximum_fusion.1.own_ref) | copy-start | bytes 24580
  2.7 7.5 %collective-permute-start = (f32[1,2,32,32]{3,2,1,0:T(8,128)S(1)}, f32[1,2,32,32]{3,2,1,0:T(8,128)S(1)}, u32[]{:S(2)}, u32[]{:S(2)}) collective-permute-start(f32[1,2,32,32]{3,2,1,0:T(8,128)S(1)} %pad_maximum_fusion.1.own_ref), channel_id=1, source_target_pairs={{8,0},{12,4},{0,8},{4,12},{5,1},{1,5},{13,9},{9,13},{10,2},{14,6},... | collective-permute-start | bytes 24584 | tf_op jit(solution)/shard_map/master_spectra/ppermute | solution.py:391
  6.8 3.4 %collective-permute-start.1 = (f32[1,2,32,32]{3,2,1,0:T(8,128)S(1)}, f32[1,2,32,32]{3,2,1,0:T(8,128)S(1)}, u32[]{:S(2)}, u32[]{:S(2)}) collective-permute-start(f32[1,2,32,32]{3,2,1,0:T(8,128)S(1)} %pad_maximum_fusion.1.own_ref), channel_id=1, source_target_pairs={{13,1},{9,5},{5,9},{1,13},{15,3},{11,7},{7,11},{3,15},{29,17},{25,... | collective-permute-start | bytes 24584 | tf_op jit(solution)/shard_map/master_spectra/ppermute | solution.py:391
  7.4 0.7 %copy-start.13 = (f32[1,12]{1,0:T(1,128)S(1)}, f32[1,12]{1,0:T(1,128)}, u32[]{:S(2)}) copy-start(f32[1,12]{1,0:T(1,128)} %param.35) | copy-start | bytes 148
  8.5 0.7 %copy-start.12 = (s32[2]{0:T(128)S(1)}, s32[2]{0:T(128)}, u32[]{:S(2)}) copy-start(s32[2]{0:T(128)} %im_ref.1) | copy-start | bytes 28
  10.3 3.3 %copy-start.4 = (f32[4,2,32,32]{3,2,1,0:T(8,128)}, f32[4,2,32,32]{3,2,1,0:T(8,128)S(1)}, u32[]{:S(2)}) copy-start(f32[4,2,32,32]{3,2,1,0:T(8,128)S(1)} %select_add_fusion.ev_ref) | copy-start | bytes 98308
  10.3 3.3 %collective-permute-start.2 = (f32[4,2,32,32]{3,2,1,0:T(8,128)S(1)}, f32[4,2,32,32]{3,2,1,0:T(8,128)S(1)}, u32[]{:S(2)}, u32[]{:S(2)}) collective-permute-start(f32[4,2,32,32]{3,2,1,0:T(8,128)S(1)} %select_add_fusion.ev_ref), channel_id=1, source_target_pairs={{0,1},{1,0},{2,3},{3,2},{4,5},{5,4},{6,7},{7,6},{8,9},{9,8},{10,11... | collective-permute-start | bytes 98312 | tf_op jit(solution)/shard_map/master_spectra/ppermute | solution.py:351
  13.6 0.6 %copy-start.9 = (f32[4,2,32,32]{3,2,1,0:T(8,128)}, f32[4,2,32,32]{3,2,1,0:T(8,128)S(1)}, u32[]{:S(2)}) copy-start(f32[4,2,32,32]{3,2,1,0:T(8,128)S(1)} %collective-permute-done.2.ev2_ref) | copy-start | bytes 98308
  27.0 4.5 %collective-permute-start.4 = (f32[1,4,32,32]{3,2,1,0:T(8,128)}, f32[1,4,32,32]{3,2,1,0:T(8,128)S(1)}, u32[]{:S(2)}, u32[]{:S(2)}) collective-permute-start(f32[1,4,32,32]{3,2,1,0:T(8,128)} %bitcast.61), channel_id=1, source_target_pairs={{0,2},{1,3},{2,0},{3,1},{4,6},{5,7},{6,4},{7,5},{8,10},{9,11},{10,... | collective-permute-start | bytes 49160 | tf_op jit(solution)/shard_map/gradient_exchange/ppermute | solution.py:470
  28.5 3.8 %collective-permute-start.3 = (f32[1,4,32,32]{3,2,1,0:T(8,128)}, f32[1,4,32,32]{3,2,1,0:T(8,128)S(1)}, u32[]{:S(2)}, u32[]{:S(2)}) collective-permute-start(f32[1,4,32,32]{3,2,1,0:T(8,128)} %bitcast.62), channel_id=1, source_target_pairs={{0,1},{1,0},{2,3},{3,2},{4,5},{5,4},{6,7},{7,6},{8,9},{9,8},{10,11... | collective-permute-start | bytes 49160 | tf_op jit(solution)/shard_map/gradient_exchange/ppermute | solution.py:470
  28.5 4.1 %collective-permute-start.5 = (f32[1,4,32,32]{3,2,1,0:T(8,128)}, f32[1,4,32,32]{3,2,1,0:T(8,128)S(1)}, u32[]{:S(2)}, u32[]{:S(2)}) collective-permute-start(f32[1,4,32,32]{3,2,1,0:T(8,128)} %bitcast.63), channel_id=1, source_target_pairs={{0,3},{1,2},{2,1},{3,0},{4,7},{5,6},{6,5},{7,4},{8,11},{9,10},{10,... | collective-permute-start | bytes 49160 | tf_op jit(solution)/shard_map/gradient_exchange/ppermute | solution.py:470
  31.5 1.1 %copy-start.5 = (f32[1,4,32,32]{3,2,1,0:T(8,128)}, f32[1,4,32,32]{3,2,1,0:T(8,128)S(1)}, u32[]{:S(2)}) copy-start(f32[1,4,32,32]{3,2,1,0:T(8,128)S(1)} %collective-permute-done.4.g1_ref) | copy-start | bytes 49156
  32.3 0.6 %copy-start.6 = (f32[1,4,32,32]{3,2,1,0:T(8,128)}, f32[1,4,32,32]{3,2,1,0:T(8,128)S(1)}, u32[]{:S(2)}) copy-start(f32[1,4,32,32]{3,2,1,0:T(8,128)S(1)} %collective-permute-done.3.g0_ref) | copy-start | bytes 49156
  32.6 0.6 %copy-start.7 = (f32[1,4,32,32]{3,2,1,0:T(8,128)}, f32[1,4,32,32]{3,2,1,0:T(8,128)S(1)}, u32[]{:S(2)}) copy-start(f32[1,4,32,32]{3,2,1,0:T(8,128)S(1)} %collective-permute-done.5.g2_ref) | copy-start | bytes 49156
  33.2 5.2 %collective-permute-start.6 = (f32[1,2,32,32]{3,2,1,0:T(8,128)S(1)}, f32[1,2,32,32]{3,2,1,0:T(8,128)S(1)}, u32[]{:S(2)}, u32[]{:S(2)}) collective-permute-start(f32[1,2,32,32]{3,2,1,0:T(8,128)S(1)} %get-tuple-element.8), channel_id=1, source_target_pairs={{0,8},{4,12},{8,0},{12,4},{1,5},{5,1},{9,13},{13,9},{2,10},{6,14},... | collective-permute-start | bytes 24584 | tf_op jit(solution)/shard_map/gradient_exchange/ppermute | solution.py:410
  33.7 4.8 %collective-permute-start.7 = (f32[1,2,32,32]{3,2,1,0:T(8,128)S(1)}, f32[1,2,32,32]{3,2,1,0:T(8,128)S(1)}, u32[]{:S(2)}, u32[]{:S(2)}) collective-permute-start(f32[1,2,32,32]{3,2,1,0:T(8,128)S(1)} %get-tuple-element.9), channel_id=1, source_target_pairs={{1,13},{5,9},{9,5},{13,1},{3,15},{7,11},{11,7},{15,3},{17,29},{21,... | collective-permute-start | bytes 24584 | tf_op jit(solution)/shard_map/gradient_exchange/ppermute | solution.py:410
  38.4 3.5 %copy-start.10 = (f32[1,2,32,32]{3,2,1,0:T(8,128)}, f32[1,2,32,32]{3,2,1,0:T(8,128)S(1)}, u32[]{:S(2)}) copy-start(f32[1,2,32,32]{3,2,1,0:T(8,128)S(1)} %add_add_fusion.refs_0_) | copy-start | bytes 24580
  38.4 3.5 %collective-permute-start.8 = (f32[1,2,32,32]{3,2,1,0:T(8,128)S(1)}, f32[1,2,32,32]{3,2,1,0:T(8,128)S(1)}, u32[]{:S(2)}, u32[]{:S(2)}) collective-permute-start(f32[1,2,32,32]{3,2,1,0:T(8,128)S(1)} %add_add_fusion.refs_0_), channel_id=1, source_target_pairs={{0,1},{1,0},{2,3},{3,2},{4,5},{5,4},{6,7},{7,6},{8,9},{9,8},{10,11... | collective-permute-start | bytes 24584 | tf_op jit(solution)/shard_map/gradient_exchange/ppermute | solution.py:351
  41.9 0.6 %copy-start.11 = (f32[1,2,32,32]{3,2,1,0:T(8,128)}, f32[1,2,32,32]{3,2,1,0:T(8,128)S(1)}, u32[]{:S(2)}) copy-start(f32[1,2,32,32]{3,2,1,0:T(8,128)S(1)} %collective-permute-done.8.refs_1_) | copy-start | bytes 24580

commit v23 on v22

--- a/solution.py
+++ b/solution.py
@@ -181,7 +181,7 @@
         i_buf[...] += w_ref[k] * (power[:, :P_SIZE] + power[:, P_SIZE:])
         return carry
 
-    lax.fori_loop(0, count, forward, 0, unroll=2)
+    lax.fori_loop(0, count, forward, 0, unroll=4)
     dose = dose_ref[0]
     resist = 1.0 / (1.0 + jnp.exp(-(steepness * (dose * i_buf[...] - threshold))))
     goal = goal_ref[pos].astype(jnp.float32)
@@ -198,7 +198,7 @@
         u_buf[pl.ds(pl.multiple_of(k * B, B), B), :] = jnp.concatenate([flip[:B], flip[B : 2 * B]], axis=1)
         return carry
 
-    lax.fori_loop(0, count, backward, 0, unroll=2)
+    lax.fori_loop(0, count, backward, 0, unroll=4)
     out = dot_full(u_buf[...], rc_ref[...])
     acc = jnp.sum((hc_ref[...] * out).reshape(count, B, 128), axis=0)
     flip = jnp.concatenate([acc, jnp.zeros((128 - B, 128), jnp.float32)], axis=0).T

time: 45.2 us -> 44.1 us (0.976)
  Pallas kernels: 18.1 us -> 17 us
    pallas_call x1, Pallas kernels: 12.8 us -> 11.7 us  [imaging(): pl.pallas_call(imaging_body, out_shape=jax.ShapeDtypeStruct((4, B, B), jn...]
  transfers between devices with their start and end apart: 9 -> 9, of which waited for: 4 -> 4; matrix products, arithmetic and copies ran while one was open for 6% -> 7% of each run, Pallas kernels for 7% -> 7%
where the time goes in v23:
time: 44.1 us; the launch traced here: 43.7 us
  Pallas kernels  17 us (39%)
  starting transfers between devices  12.6 us (29%)
  local copies, waits for them, and re-layouts  4.17 us (9%)
  waiting for transfers between devices  4.01 us (9%)
  other arithmetic  2.7 us (6%)
  between operations  2.21 us (5%)
  matrix products  1.03 us (2%)
    pallas_call x1, Pallas kernels, imaging(): pl.pallas_call(imaging_body, out_shape=jax.ShapeDtypeStruct((4, B, B), jn...  11.7 us
    ppermute x2, starting transfers between devices, gather_split(): got = lax.ppermute(x, ('tile', 'kern'), pairs)  4.75 us
    ppermute x2, starting transfers between devices, sum_parts(): return (x, lax.ppermute(x, axis, [(0, 1), (1, 0)]))  4.68 us
    unnamed x28, local copies, waits for them, and re-layouts  3.83 us
    pallas_call x1, Pallas kernels, group_pixels(): pl.pallas_call(group_pixel_body, out_shape=(shape, jax.ShapeDtypeStruct((...  2.99 us
    ppermute x3, waiting for transfers between devices, on_device(): lax.ppermute(comp, ('corner', 'kern'), [(i, i ^ step) for i in range(4)])  2.66 us
    pallas_call x1, Pallas kernels, pixels(): pl.pallas_call(functools.partial(pixel_body, passes=False), out_shape=sha...  2.31 us
    ppermute x3, starting transfers between devices, on_device(): lax.ppermute(comp, ('corner', 'kern'), [(i, i ^ step) for i in range(4)])  2.14 us
  transfers between devices with their start and end apart: 9, of which 4 were waited for; matrix products, arithmetic and copies ran while one was open for 7% of the time, Pallas kernels for 7%

profile of v23, /device:TPU:0, one launch (start us, length us, event | category | flops | bytes accessed | tf_op | source)
XLA Modules:
  0.0 43.7 jit_solution(8624509871354325943)
XLA Ops:
  0.7 0.9 %copy-done = bf16[1,256,256]{2,1,0:T(8,128)(2,1)S(1)} copy-done((bf16[1,256,256]{2,1,0:T(8,128)(2,1)S(1)}, bf16[1,256,256]{2,1,0:T(8,128)(2,1)}, u32[]{:S(2)}) %copy-start) | copy-done | bytes 131096
  1.5 0.2 fusion.8
  1.8 0.2 fusion.6
  2.0 0.2 fusion.17
  2.1 0.2 fusion.16
  2.3 0.2 fusion
  2.5 0.2 fusion.1
  2.7 4.1 %collective-permute-start = (f32[1,2,32,32]{3,2,1,0:T(8,128)S(1)}, f32[1,2,32,32]{3,2,1,0:T(8,128)S(1)}, u32[]{:S(2)}, u32[]{:S(2)}) collective-permute-start(f32[1,2,32,32]{3,2,1,0:T(8,128)S(1)} %pad_maximum_fusion.1.own_ref), channel_id=1, source_target_pairs={{8,0},{12,4},{0,8},{4,12},{5,1},{1,5},{13,9},{9,13},{10,2},{14,6},... | collective-permute-start | bytes 24584 | tf_op jit(solution)/shard_map/master_spectra/ppermute | solution.py:391
  6.8 0.7 %collective-permute-start.1 = (f32[1,2,32,32]{3,2,1,0:T(8,128)S(1)}, f32[1,2,32,32]{3,2,1,0:T(8,128)S(1)}, u32[]{:S(2)}, u32[]{:S(2)}) collective-permute-start(f32[1,2,32,32]{3,2,1,0:T(8,128)S(1)} %pad_maximum_fusion.1.own_ref), channel_id=1, source_target_pairs={{13,1},{9,5},{5,9},{1,13},{15,3},{11,7},{7,11},{3,15},{29,17},{25,... | collective-permute-start | bytes 24584 | tf_op jit(solution)/shard_map/master_spectra/ppermute | solution.py:391
  7.5 0.6 %copy-done.13 = f32[1,12]{1,0:T(1,128)S(1)} copy-done((f32[1,12]{1,0:T(1,128)S(1)}, f32[1,12]{1,0:T(1,128)}, u32[]{:S(2)}) %copy-start.13) | copy-done | bytes 72
  8.3 0.1 copy.36
  8.7 0.5 %copy-done.12 = s32[2]{0:T(128)S(1)} copy-done((s32[2]{0:T(128)S(1)}, s32[2]{0:T(128)}, u32[]{:S(2)}) %copy-start.12) | copy-done | bytes 32
  9.3 0.9 %pad_maximum_fusion = f32[12,32,128]{2,1,0:T(8,128)} fusion(f32[12,32,32]{2,1,0:T(8,128)S(1)} %copy.37, f32[12,32,32]{2,1,0:T(8,128)S(1)} %copy.36, f32[12,32,32]{2,1,0:T(8,128)S(1)} %copy.34), kind=kLoop, calls=%fused_computation.10 | loop fusion | flops 147456 | bytes 344064 | tf_op jit(solution)/shard_map/imaging_kernel/concatenate | solution.py:453
  10.3 2.0 %collective-permute-start.2 = (f32[4,2,32,32]{3,2,1,0:T(8,128)S(1)}, f32[4,2,32,32]{3,2,1,0:T(8,128)S(1)}, u32[]{:S(2)}, u32[]{:S(2)}) collective-permute-start(f32[4,2,32,32]{3,2,1,0:T(8,128)S(1)} %select_add_fusion.ev_ref), channel_id=1, source_target_pairs={{0,1},{1,0},{2,3},{3,2},{4,5},{5,4},{6,7},{7,6},{8,9},{9,8},{10,11... | collective-permute-start | bytes 98312 | tf_op jit(solution)/shard_map/master_spectra/ppermute | solution.py:351
  12.3 0.6 %pad_add_fusion.pos_ref = s32[2]{0:T(128)} fusion(s32[1]{0:T(128)} %bitcast.1, s32[1]{0:T(128)} %bitcast), kind=kLoop, calls=%fused_computation.30 | loop fusion | flops 2 | bytes 16 | tf_op jit(solution)/shard_map/imaging_kernel/stack | solution.py:456
  13.6 0.6 %copy-done.9 = f32[4,2,32,32]{3,2,1,0:T(8,128)} copy-done((f32[4,2,32,32]{3,2,1,0:T(8,128)}, f32[4,2,32,32]{3,2,1,0:T(8,128)S(1)}, u32[]{:S(2)}) %copy-start.9) | copy-done | bytes 32792
  14.2 11.7 %imaging_kernel.1 = f32[4,32,32]{2,1,0:T(8,128)} custom-call(s32[2]{0:T(128)} %pad_add_fusion.pos_ref, s32[2]{0:T(128)} %im_ref.1, s32[2,2]{1,0:T(2,128)} %sh_ref.1, f32[12]{0:T(128)} %bitcast.68, f32[1]{0:T(128)S(6)} %copy.39.dose_ref, bf16[2,256,256]{2,1,0:T(8,128)(2,1)} %mask_ref.1, f32[4,2,32,32]{3,2,1,0:T(8,128)} %copy-done.4, ...), custom_call_target="tpu_custom_call" | custom-call | tf_op jit(solution)/shard_map/imaging_kernel/pallas_call | solution.py:220
  25.9 1.5 %collective-permute-start.4 = (f32[1,4,32,32]{3,2,1,0:T(8,128)}, f32[1,4,32,32]{3,2,1,0:T(8,128)S(1)}, u32[]{:S(2)}, u32[]{:S(2)}) collective-permute-start(f32[1,4,32,32]{3,2,1,0:T(8,128)} %bitcast.61), channel_id=1, source_target_pairs={{0,2},{1,3},{2,0},{3,1},{4,6},{5,7},{6,4},{7,5},{8,10},{9,11},{10,... | collective-permute-start | bytes 49160 | tf_op jit(solution)/shard_map/gradient_exchange/ppermute | solution.py:470
  27.4 0.6 %collective-permute-start.5 = (f32[1,4,32,32]{3,2,1,0:T(8,128)}, f32[1,4,32,32]{3,2,1,0:T(8,128)S(1)}, u32[]{:S(2)}, u32[]{:S(2)}) collective-permute-start(f32[1,4,32,32]{3,2,1,0:T(8,128)} %bitcast.63), channel_id=1, source_target_pairs={{0,3},{1,2},{2,1},{3,0},{4,7},{5,6},{6,5},{7,4},{8,11},{9,10},{10,... | collective-permute-start | bytes 49160 | tf_op jit(solution)/shard_map/gradient_exchange/ppermute | solution.py:470
  28.0 2.3 %collective-permute-done.4.g1_ref = f32[1,4,32,32]{3,2,1,0:T(8,128)S(1)} collective-permute-done((f32[1,4,32,32]{3,2,1,0:T(8,128)}, f32[1,4,32,32]{3,2,1,0:T(8,128)S(1)}, u32[]{:S(2)}, u32[]{:S(2)}) %collective-permute-start.4) | collective-permute-done | bytes 16416 | tf_op jit(solution)/shard_map/gradient_exchange/ppermute | solution.py:470
  30.4 0.8 %fusion.11 = f32[2,32,32]{2,1,0:T(8,128)S(1)} fusion(f32[1,4,32,32]{3,2,1,0:T(8,128)S(1)} %collective-permute-done.4.g1_ref, f32[1,4,32,32]{3,2,1,0:T(8,128)} %bitcast.64), kind=kLoop, calls=%fused_computation.20 | loop fusion | flops 2048 | bytes 24576 | tf_op jit(solution)/shard_map/gradient_exchange/mul | solution.py:489
  31.2 0.3 collective-permute-done.5.g2_ref
  31.6 0.2 copy-done.6
  31.8 0.3 copy-done.7
  32.1 0.4 collective-permute-start.6
  32.5 0.7 %collective-permute-start.7 = (f32[1,2,32,32]{3,2,1,0:T(8,128)S(1)}, f32[1,2,32,32]{3,2,1,0:T(8,128)S(1)}, u32[]{:S(2)}, u32[]{:S(2)}) collective-permute-start(f32[1,2,32,32]{3,2,1,0:T(8,128)S(1)} %get-tuple-element.9), channel_id=1, source_target_pairs={{1,13},{5,9},{9,5},{13,1},{3,15},{7,11},{11,7},{15,3},{17,29},{21,... | collective-permute-start | bytes 24584 | tf_op jit(solution)/shard_map/gradient_exchange/ppermute | solution.py:410
  33.2 3.0 %gradient_exchange.1 = (f32[2,256,256]{2,1,0:T(8,128)}, f32[1,1,1,1]{3,2,1,0:T(1,128)}) custom-call(f32[1,4,32,32]{3,2,1,0:T(8,128)} %bitcast.65, f32[1,4,32,32]{3,2,1,0:T(8,128)} %copy-done.6, f32[1,4,32,32]{3,2,1,0:T(8,128)} %copy-done.5, f32[1,4,32,32]{3,2,1,0:T(8,128)} %copy-done.7, f32[32,256]{1,0:T(8,128)} %constant.67.clone.c_re_ref.refs_2_, ...), custom_call_target="tpu_custom_call" | custom-call | tf_op jit(solution)/shard_map/gradient_exchange/pallas_call | solution.py:288
  36.8 0.5 %collective-permute-done.6 = f32[1,2,32,32]{3,2,1,0:T(8,128)S(1)} collective-permute-done((f32[1,2,32,32]{3,2,1,0:T(8,128)S(1)}, f32[1,2,32,32]{3,2,1,0:T(8,128)S(1)}, u32[]{:S(2)}, u32[]{:S(2)}) %collective-permute-start.6) | collective-permute-done | bytes 8224 | tf_op jit(solution)/shard_map/gradient_exchange/ppermute | solution.py:410
  37.3 2.6 %collective-permute-start.8 = (f32[1,2,32,32]{3,2,1,0:T(8,128)S(1)}, f32[1,2,32,32]{3,2,1,0:T(8,128)S(1)}, u32[]{:S(2)}, u32[]{:S(2)}) collective-permute-start(f32[1,2,32,32]{3,2,1,0:T(8,128)S(1)} %add_add_fusion.refs_0_), channel_id=1, source_target_pairs={{0,1},{1,0},{2,3},{3,2},{4,5},{5,4},{6,7},{7,6},{8,9},{9,8},{10,11... | collective-permute-start | bytes 24584 | tf_op jit(solution)/shard_map/gradient_exchange/ppermute | solution.py:351
  39.9 0.9 %collective-permute-done.8.refs_1_ = f32[1,2,32,32]{3,2,1,0:T(8,128)S(1)} collective-permute-done((f32[1,2,32,32]{3,2,1,0:T(8,128)S(1)}, f32[1,2,32,32]{3,2,1,0:T(8,128)S(1)}, u32[]{:S(2)}, u32[]{:S(2)}) %collective-permute-start.8) | collective-permute-done | bytes 8224 | tf_op jit(solution)/shard_map/gradient_exchange/ppermute | solution.py:351
  40.8 0.6 %copy-done.11 = f32[1,2,32,32]{3,2,1,0:T(8,128)} copy-done((f32[1,2,32,32]{3,2,1,0:T(8,128)}, f32[1,2,32,32]{3,2,1,0:T(8,128)S(1)}, u32[]{:S(2)}) %copy-start.11) | copy-done | bytes 8216
  41.4 2.3 %pixel_gradients.1 = f32[1,256,256]{2,1,0:T(8,128)} custom-call(f32[1,2,32,32]{3,2,1,0:T(8,128)} %copy-done.10, f32[1,2,32,32]{3,2,1,0:T(8,128)} %copy-done.11, f32[32,256]{1,0:T(8,128)} %constant.67.clone.c_re_ref.refs_2_, f32[32,256]{1,0:T(8,128)} %constant.68.clone.c_im_ref.refs_3_, bf16[256,384]{1,0:T(8,128)(2,1)} %constant.80.clone.left_ref.refs_4_), custom_call_target="tpu_custom_call" | custom-call | tf_op jit(solution)/shard_map/pixel_gradients/pallas_call | solution.py:308
  (41 shorter events, 0.8 us)
Async XLA Ops:
  0.6 0.9 %copy-start = (bf16[1,256,256]{2,1,0:T(8,128)(2,1)S(1)}, bf16[1,256,256]{2,1,0:T(8,128)(2,1)}, u32[]{:S(2)}) copy-start(bf16[1,256,256]{2,1,0:T(8,128)(2,1)} %param.30) | copy-start | bytes 393220
  0.6 0.9 %copy-start.2 = (f32[32,256]{1,0:T(8,128)S(1)}, f32[32,256]{1,0:T(8,128)}, u32[]{:S(2)}) copy-start(f32[32,256]{1,0:T(8,128)} %constant.67.clone.c_re_ref.refs_2_) | copy-start | bytes 98308
  0.7 1.1 %copy-start.3 = (f32[32,256]{1,0:T(8,128)S(1)}, f32[32,256]{1,0:T(8,128)}, u32[]{:S(2)}) copy-start(f32[32,256]{1,0:T(8,128)} %constant.68.clone.c_im_ref.refs_3_) | copy-start | bytes 98308
  0.7 7.4 %copy-start.1 = (f32[1,12,2,32,32]{4,3,2,1,0:T(8,128)S(1)}, f32[1,12,2,32,32]{4,3,2,1,0:T(8,128)}, u32[]{:S(2)}) copy-start(f32[1,12,2,32,32]{4,3,2,1,0:T(8,128)} %param.34) | copy-start | bytes 294916
  2.6 5.6 %copy-start.8 = (f32[1,2,32,32]{3,2,1,0:T(8,128)}, f32[1,2,32,32]{3,2,1,0:T(8,128)S(1)}, u32[]{:S(2)}) copy-start(f32[1,2,32,32]{3,2,1,0:T(8,128)S(1)} %pad_maximum_fusion.1.own_ref) | copy-start | bytes 24580
  2.7 7.5 %collective-permute-start = (f32[1,2,32,32]{3,2,1,0:T(8,128)S(1)}, f32[1,2,32,32]{3,2,1,0:T(8,128)S(1)}, u32[]{:S(2)}, u32[]{:S(2)}) collective-permute-start(f32[1,2,32,32]{3,2,1,0:T(8,128)S(1)} %pad_maximum_fusion.1.own_ref), channel_id=1, source_target_pairs={{8,0},{12,4},{0,8},{4,12},{5,1},{1,5},{13,9},{9,13},{10,2},{14,6},... | collective-permute-start | bytes 24584 | tf_op jit(solution)/shard_map/master_spectra/ppermute | solution.py:391
  6.8 3.4 %collective-permute-start.1 = (f32[1,2,32,32]{3,2,1,0:T(8,128)S(1)}, f32[1,2,32,32]{3,2,1,0:T(8,128)S(1)}, u32[]{:S(2)}, u32[]{:S(2)}) collective-permute-start(f32[1,2,32,32]{3,2,1,0:T(8,128)S(1)} %pad_maximum_fusion.1.own_ref), channel_id=1, source_target_pairs={{13,1},{9,5},{5,9},{1,13},{15,3},{11,7},{7,11},{3,15},{29,17},{25,... | collective-permute-start | bytes 24584 | tf_op jit(solution)/shard_map/master_spectra/ppermute | solution.py:391
  7.4 0.7 %copy-start.13 = (f32[1,12]{1,0:T(1,128)S(1)}, f32[1,12]{1,0:T(1,128)}, u32[]{:S(2)}) copy-start(f32[1,12]{1,0:T(1,128)} %param.35) | copy-start | bytes 148
  8.5 0.7 %copy-start.12 = (s32[2]{0:T(128)S(1)}, s32[2]{0:T(128)}, u32[]{:S(2)}) copy-start(s32[2]{0:T(128)} %im_ref.1) | copy-start | bytes 28
  10.3 3.3 %copy-start.4 = (f32[4,2,32,32]{3,2,1,0:T(8,128)}, f32[4,2,32,32]{3,2,1,0:T(8,128)S(1)}, u32[]{:S(2)}) copy-start(f32[4,2,32,32]{3,2,1,0:T(8,128)S(1)} %select_add_fusion.ev_ref) | copy-start | bytes 98308
  10.3 3.3 %collective-permute-start.2 = (f32[4,2,32,32]{3,2,1,0:T(8,128)S(1)}, f32[4,2,32,32]{3,2,1,0:T(8,128)S(1)}, u32[]{:S(2)}, u32[]{:S(2)}) collective-permute-start(f32[4,2,32,32]{3,2,1,0:T(8,128)S(1)} %select_add_fusion.ev_ref), channel_id=1, source_target_pairs={{0,1},{1,0},{2,3},{3,2},{4,5},{5,4},{6,7},{7,6},{8,9},{9,8},{10,11... | collective-permute-start | bytes 98312 | tf_op jit(solution)/shard_map/master_spectra/ppermute | solution.py:351
  13.6 0.6 %copy-start.9 = (f32[4,2,32,32]{3,2,1,0:T(8,128)}, f32[4,2,32,32]{3,2,1,0:T(8,128)S(1)}, u32[]{:S(2)}) copy-start(f32[4,2,32,32]{3,2,1,0:T(8,128)S(1)} %collective-permute-done.2.ev2_ref) | copy-start | bytes 98308
  25.9 4.5 %collective-permute-start.4 = (f32[1,4,32,32]{3,2,1,0:T(8,128)}, f32[1,4,32,32]{3,2,1,0:T(8,128)S(1)}, u32[]{:S(2)}, u32[]{:S(2)}) collective-permute-start(f32[1,4,32,32]{3,2,1,0:T(8,128)} %bitcast.61), channel_id=1, source_target_pairs={{0,2},{1,3},{2,0},{3,1},{4,6},{5,7},{6,4},{7,5},{8,10},{9,11},{10,... | collective-permute-start | bytes 49160 | tf_op jit(solution)/shard_map/gradient_exchange/ppermute | solution.py:470
  27.4 3.8 %collective-permute-start.3 = (f32[1,4,32,32]{3,2,1,0:T(8,128)}, f32[1,4,32,32]{3,2,1,0:T(8,128)S(1)}, u32[]{:S(2)}, u32[]{:S(2)}) collective-permute-start(f32[1,4,32,32]{3,2,1,0:T(8,128)} %bitcast.62), channel_id=1, source_target_pairs={{0,1},{1,0},{2,3},{3,2},{4,5},{5,4},{6,7},{7,6},{8,9},{9,8},{10,11... | collective-permute-start | bytes 49160 | tf_op jit(solution)/shard_map/gradient_exchange/ppermute | solution.py:470
  27.4 4.1 %collective-permute-start.5 = (f32[1,4,32,32]{3,2,1,0:T(8,128)}, f32[1,4,32,32]{3,2,1,0:T(8,128)S(1)}, u32[]{:S(2)}, u32[]{:S(2)}) collective-permute-start(f32[1,4,32,32]{3,2,1,0:T(8,128)} %bitcast.63), channel_id=1, source_target_pairs={{0,3},{1,2},{2,1},{3,0},{4,7},{5,6},{6,5},{7,4},{8,11},{9,10},{10,... | collective-permute-start | bytes 49160 | tf_op jit(solution)/shard_map/gradient_exchange/ppermute | solution.py:470
  30.4 1.1 %copy-start.5 = (f32[1,4,32,32]{3,2,1,0:T(8,128)}, f32[1,4,32,32]{3,2,1,0:T(8,128)S(1)}, u32[]{:S(2)}) copy-start(f32[1,4,32,32]{3,2,1,0:T(8,128)S(1)} %collective-permute-done.4.g1_ref) | copy-start | bytes 49156
  31.1 0.6 %copy-start.6 = (f32[1,4,32,32]{3,2,1,0:T(8,128)}, f32[1,4,32,32]{3,2,1,0:T(8,128)S(1)}, u32[]{:S(2)}) copy-start(f32[1,4,32,32]{3,2,1,0:T(8,128)S(1)} %collective-permute-done.3.g0_ref) | copy-start | bytes 49156
  31.5 0.6 %copy-start.7 = (f32[1,4,32,32]{3,2,1,0:T(8,128)}, f32[1,4,32,32]{3,2,1,0:T(8,128)S(1)}, u32[]{:S(2)}) copy-start(f32[1,4,32,32]{3,2,1,0:T(8,128)S(1)} %collective-permute-done.5.g2_ref) | copy-start | bytes 49156
  32.1 5.2 %collective-permute-start.6 = (f32[1,2,32,32]{3,2,1,0:T(8,128)S(1)}, f32[1,2,32,32]{3,2,1,0:T(8,128)S(1)}, u32[]{:S(2)}, u32[]{:S(2)}) collective-permute-start(f32[1,2,32,32]{3,2,1,0:T(8,128)S(1)} %get-tuple-element.8), channel_id=1, source_target_pairs={{0,8},{4,12},{8,0},{12,4},{1,5},{5,1},{9,13},{13,9},{2,10},{6,14},... | collective-permute-start | bytes 24584 | tf_op jit(solution)/shard_map/gradient_exchange/ppermute | solution.py:410
  32.5 4.8 %collective-permute-start.7 = (f32[1,2,32,32]{3,2,1,0:T(8,128)S(1)}, f32[1,2,32,32]{3,2,1,0:T(8,128)S(1)}, u32[]{:S(2)}, u32[]{:S(2)}) collective-permute-start(f32[1,2,32,32]{3,2,1,0:T(8,128)S(1)} %get-tuple-element.9), channel_id=1, source_target_pairs={{1,13},{5,9},{9,5},{13,1},{3,15},{7,11},{11,7},{15,3},{17,29},{21,... | collective-permute-start | bytes 24584 | tf_op jit(solution)/shard_map/gradient_exchange/ppermute | solution.py:410
  37.3 3.5 %copy-start.10 = (f32[1,2,32,32]{3,2,1,0:T(8,128)}, f32[1,2,32,32]{3,2,1,0:T(8,128)S(1)}, u32[]{:S(2)}) copy-start(f32[1,2,32,32]{3,2,1,0:T(8,128)S(1)} %add_add_fusion.refs_0_) | copy-start | bytes 24580
  37.3 3.5 %collective-permute-start.8 = (f32[1,2,32,32]{3,2,1,0:T(8,128)S(1)}, f32[1,2,32,32]{3,2,1,0:T(8,128)S(1)}, u32[]{:S(2)}, u32[]{:S(2)}) collective-permute-start(f32[1,2,32,32]{3,2,1,0:T(8,128)S(1)} %add_add_fusion.refs_0_), channel_id=1, source_target_pairs={{0,1},{1,0},{2,3},{3,2},{4,5},{5,4},{6,7},{7,6},{8,9},{9,8},{10,11... | collective-permute-start | bytes 24584 | tf_op jit(solution)/shard_map/gradient_exchange/ppermute | solution.py:351
  40.8 0.6 %copy-start.11 = (f32[1,2,32,32]{3,2,1,0:T(8,128)}, f32[1,2,32,32]{3,2,1,0:T(8,128)S(1)}, u32[]{:S(2)}) copy-start(f32[1,2,32,32]{3,2,1,0:T(8,128)S(1)} %collective-permute-done.8.refs_1_) | copy-start | bytes 24580

commit v24 on v23

--- a/solution.py
+++ b/solution.py
@@ -181,7 +181,7 @@
         i_buf[...] += w_ref[k] * (power[:, :P_SIZE] + power[:, P_SIZE:])
         return carry
 
-    lax.fori_loop(0, count, forward, 0, unroll=4)
+    lax.fori_loop(0, count, forward, 0, unroll=True)
     dose = dose_ref[0]
     resist = 1.0 / (1.0 + jnp.exp(-(steepness * (dose * i_buf[...] - threshold))))
     goal = goal_ref[pos].astype(jnp.float32)
@@ -198,7 +198,7 @@
         u_buf[pl.ds(pl.multiple_of(k * B, B), B), :] = jnp.concatenate([flip[:B], flip[B : 2 * B]], axis=1)
         return carry
 
-    lax.fori_loop(0, count, backward, 0, unroll=4)
+    lax.fori_loop(0, count, backward, 0, unroll=True)
     out = dot_full(u_buf[...], rc_ref[...])
     acc = jnp.sum((hc_ref[...] * out).reshape(count, B, 128), axis=0)
     flip = jnp.concatenate([acc, jnp.zeros((128 - B, 128), jnp.float32)], axis=0).T

time: 44.1 us -> 44.3 us (level)
  transfers between devices with their start and end apart: 9 -> 9, of which waited for: 4 -> 4; matrix products, arithmetic and copies ran while one was open for 7% -> 6% of each run, Pallas kernels for 7% -> 7%
where the time goes in v24:
time: 44.3 us; the launch traced here: 44 us
  Pallas kernels  17.2 us (39%)
  starting transfers between devices  12.6 us (28%)
  local copies, waits for them, and re-layouts  4.17 us (9%)
  waiting for transfers between devices  4.02 us (9%)
  other arithmetic  2.7 us (6%)
  between operations  2.21 us (5%)
  matrix products  1.03 us (2%)
    pallas_call x1, Pallas kernels, imaging(): pl.pallas_call(imaging_body, out_shape=jax.ShapeDtypeStruct((4, B, B), jn...  11.9 us
    ppermute x2, starting transfers between devices, gather_split(): got = lax.ppermute(x, ('tile', 'kern'), pairs)  4.75 us
    ppermute x2, starting transfers between devices, sum_parts(): return (x, lax.ppermute(x, axis, [(0, 1), (1, 0)]))  4.68 us
    unnamed x28, local copies, waits for them, and re-layouts  3.83 us
    pallas_call x1, Pallas kernels, group_pixels(): pl.pallas_call(group_pixel_body, out_shape=(shape, jax.ShapeDtypeStruct((...  2.99 us
    ppermute x3, waiting for transfers between devices, on_device(): lax.ppermute(comp, ('corner', 'kern'), [(i, i ^ step) for i in range(4)])  2.67 us
    pallas_call x1, Pallas kernels, pixels(): pl.pallas_call(functools.partial(pixel_body, passes=False), out_shape=sha...  2.31 us
    ppermute x3, starting transfers between devices, on_device(): lax.ppermute(comp, ('corner', 'kern'), [(i, i ^ step) for i in range(4)])  2.14 us
  transfers between devices with their start and end apart: 9, of which 4 were waited for; matrix products, arithmetic and copies ran while one was open for 6% of the time, Pallas kernels for 7%

profile of v24, /device:TPU:0, one launch (start us, length us, event | category | flops | bytes accessed | tf_op | source)
XLA Modules:
  0.0 44.0 jit_solution(18079498797373766627)
XLA Ops:
  0.7 0.9 %copy-done = bf16[1,256,256]{2,1,0:T(8,128)(2,1)S(1)} copy-done((bf16[1,256,256]{2,1,0:T(8,128)(2,1)S(1)}, bf16[1,256,256]{2,1,0:T(8,128)(2,1)}, u32[]{:S(2)}) %copy-start) | copy-done | bytes 131096
  1.5 0.2 fusion.8
  1.8 0.2 fusion.6
  2.0 0.2 fusion.17
  2.1 0.2 fusion.16
  2.3 0.2 fusion
  2.5 0.2 fusion.1
  2.7 4.1 %collective-permute-start = (f32[1,2,32,32]{3,2,1,0:T(8,128)S(1)}, f32[1,2,32,32]{3,2,1,0:T(8,128)S(1)}, u32[]{:S(2)}, u32[]{:S(2)}) collective-permute-start(f32[1,2,32,32]{3,2,1,0:T(8,128)S(1)} %pad_maximum_fusion.1.own_ref), channel_id=1, source_target_pairs={{8,0},{12,4},{0,8},{4,12},{5,1},{1,5},{13,9},{9,13},{10,2},{14,6},... | collective-permute-start | bytes 24584 | tf_op jit(solution)/shard_map/master_spectra/ppermute | solution.py:391
  6.8 0.7 %collective-permute-start.1 = (f32[1,2,32,32]{3,2,1,0:T(8,128)S(1)}, f32[1,2,32,32]{3,2,1,0:T(8,128)S(1)}, u32[]{:S(2)}, u32[]{:S(2)}) collective-permute-start(f32[1,2,32,32]{3,2,1,0:T(8,128)S(1)} %pad_maximum_fusion.1.own_ref), channel_id=1, source_target_pairs={{13,1},{9,5},{5,9},{1,13},{15,3},{11,7},{7,11},{3,15},{29,17},{25,... | collective-permute-start | bytes 24584 | tf_op jit(solution)/shard_map/master_spectra/ppermute | solution.py:391
  7.5 0.6 %copy-done.13 = f32[1,12]{1,0:T(1,128)S(1)} copy-done((f32[1,12]{1,0:T(1,128)S(1)}, f32[1,12]{1,0:T(1,128)}, u32[]{:S(2)}) %copy-start.13) | copy-done | bytes 72
  8.3 0.1 copy.36
  8.7 0.5 %copy-done.12 = s32[2]{0:T(128)S(1)} copy-done((s32[2]{0:T(128)S(1)}, s32[2]{0:T(128)}, u32[]{:S(2)}) %copy-start.12) | copy-done | bytes 32
  9.3 0.9 %pad_maximum_fusion = f32[12,32,128]{2,1,0:T(8,128)} fusion(f32[12,32,32]{2,1,0:T(8,128)S(1)} %copy.37, f32[12,32,32]{2,1,0:T(8,128)S(1)} %copy.36, f32[12,32,32]{2,1,0:T(8,128)S(1)} %copy.34), kind=kLoop, calls=%fused_computation.10 | loop fusion | flops 147456 | bytes 344064 | tf_op jit(solution)/shard_map/imaging_kernel/concatenate | solution.py:453
  10.3 2.0 %collective-permute-start.2 = (f32[4,2,32,32]{3,2,1,0:T(8,128)S(1)}, f32[4,2,32,32]{3,2,1,0:T(8,128)S(1)}, u32[]{:S(2)}, u32[]{:S(2)}) collective-permute-start(f32[4,2,32,32]{3,2,1,0:T(8,128)S(1)} %select_add_fusion.ev_ref), channel_id=1, source_target_pairs={{0,1},{1,0},{2,3},{3,2},{4,5},{5,4},{6,7},{7,6},{8,9},{9,8},{10,11... | collective-permute-start | bytes 98312 | tf_op jit(solution)/shard_map/master_spectra/ppermute | solution.py:351
  12.3 0.6 %pad_add_fusion.pos_ref = s32[2]{0:T(128)} fusion(s32[1]{0:T(128)} %bitcast.1, s32[1]{0:T(128)} %bitcast), kind=kLoop, calls=%fused_computation.30 | loop fusion | flops 2 | bytes 16 | tf_op jit(solution)/shard_map/imaging_kernel/stack | solution.py:456
  13.6 0.6 %copy-done.9 = f32[4,2,32,32]{3,2,1,0:T(8,128)} copy-done((f32[4,2,32,32]{3,2,1,0:T(8,128)}, f32[4,2,32,32]{3,2,1,0:T(8,128)S(1)}, u32[]{:S(2)}) %copy-start.9) | copy-done | bytes 32792
  14.2 11.9 %imaging_kernel.1 = f32[4,32,32]{2,1,0:T(8,128)} custom-call(s32[2]{0:T(128)} %pad_add_fusion.pos_ref, s32[2]{0:T(128)} %im_ref.1, s32[2,2]{1,0:T(2,128)} %sh_ref.1, f32[12]{0:T(128)} %bitcast.68, f32[1]{0:T(128)S(6)} %copy.39.dose_ref, bf16[2,256,256]{2,1,0:T(8,128)(2,1)} %mask_ref.1, f32[4,2,32,32]{3,2,1,0:T(8,128)} %copy-done.4, ...), custom_call_target="tpu_custom_call" | custom-call | tf_op jit(solution)/shard_map/imaging_kernel/pallas_call | solution.py:220
  26.2 1.5 %collective-permute-start.4 = (f32[1,4,32,32]{3,2,1,0:T(8,128)}, f32[1,4,32,32]{3,2,1,0:T(8,128)S(1)}, u32[]{:S(2)}, u32[]{:S(2)}) collective-permute-start(f32[1,4,32,32]{3,2,1,0:T(8,128)} %bitcast.61), channel_id=1, source_target_pairs={{0,2},{1,3},{2,0},{3,1},{4,6},{5,7},{6,4},{7,5},{8,10},{9,11},{10,... | collective-permute-start | bytes 49160 | tf_op jit(solution)/shard_map/gradient_exchange/ppermute | solution.py:470
  27.7 0.6 %collective-permute-start.5 = (f32[1,4,32,32]{3,2,1,0:T(8,128)}, f32[1,4,32,32]{3,2,1,0:T(8,128)S(1)}, u32[]{:S(2)}, u32[]{:S(2)}) collective-permute-start(f32[1,4,32,32]{3,2,1,0:T(8,128)} %bitcast.63), channel_id=1, source_target_pairs={{0,3},{1,2},{2,1},{3,0},{4,7},{5,6},{6,5},{7,4},{8,11},{9,10},{10,... | collective-permute-start | bytes 49160 | tf_op jit(solution)/shard_map/gradient_exchange/ppermute | solution.py:470
  28.3 2.3 %collective-permute-done.4.g1_ref = f32[1,4,32,32]{3,2,1,0:T(8,128)S(1)} collective-permute-done((f32[1,4,32,32]{3,2,1,0:T(8,128)}, f32[1,4,32,32]{3,2,1,0:T(8,128)S(1)}, u32[]{:S(2)}, u32[]{:S(2)}) %collective-permute-start.4) | collective-permute-done | bytes 16416 | tf_op jit(solution)/shard_map/gradient_exchange/ppermute | solution.py:470
  30.6 0.8 %fusion.11 = f32[2,32,32]{2,1,0:T(8,128)S(1)} fusion(f32[1,4,32,32]{3,2,1,0:T(8,128)S(1)} %collective-permute-done.4.g1_ref, f32[1,4,32,32]{3,2,1,0:T(8,128)} %bitcast.64), kind=kLoop, calls=%fused_computation.20 | loop fusion | flops 2048 | bytes 24576 | tf_op jit(solution)/shard_map/gradient_exchange/mul | solution.py:489
  31.4 0.3 collective-permute-done.5.g2_ref
  31.9 0.2 copy-done.6
  32.0 0.3 copy-done.7
  32.4 0.4 collective-permute-start.6
  32.8 0.7 %collective-permute-start.7 = (f32[1,2,32,32]{3,2,1,0:T(8,128)S(1)}, f32[1,2,32,32]{3,2,1,0:T(8,128)S(1)}, u32[]{:S(2)}, u32[]{:S(2)}) collective-permute-start(f32[1,2,32,32]{3,2,1,0:T(8,128)S(1)} %get-tuple-element.9), channel_id=1, source_target_pairs={{1,13},{5,9},{9,5},{13,1},{3,15},{7,11},{11,7},{15,3},{17,29},{21,... | collective-permute-start | bytes 24584 | tf_op jit(solution)/shard_map/gradient_exchange/ppermute | solution.py:410
  33.4 3.0 %gradient_exchange.1 = (f32[2,256,256]{2,1,0:T(8,128)}, f32[1,1,1,1]{3,2,1,0:T(1,128)}) custom-call(f32[1,4,32,32]{3,2,1,0:T(8,128)} %bitcast.65, f32[1,4,32,32]{3,2,1,0:T(8,128)} %copy-done.6, f32[1,4,32,32]{3,2,1,0:T(8,128)} %copy-done.5, f32[1,4,32,32]{3,2,1,0:T(8,128)} %copy-done.7, f32[32,256]{1,0:T(8,128)} %constant.67.clone.c_re_ref.refs_2_, ...), custom_call_target="tpu_custom_call" | custom-call | tf_op jit(solution)/shard_map/gradient_exchange/pallas_call | solution.py:288
  37.1 0.5 %collective-permute-done.6 = f32[1,2,32,32]{3,2,1,0:T(8,128)S(1)} collective-permute-done((f32[1,2,32,32]{3,2,1,0:T(8,128)S(1)}, f32[1,2,32,32]{3,2,1,0:T(8,128)S(1)}, u32[]{:S(2)}, u32[]{:S(2)}) %collective-permute-start.6) | collective-permute-done | bytes 8224 | tf_op jit(solution)/shard_map/gradient_exchange/ppermute | solution.py:410
  37.6 2.6 %collective-permute-start.8 = (f32[1,2,32,32]{3,2,1,0:T(8,128)S(1)}, f32[1,2,32,32]{3,2,1,0:T(8,128)S(1)}, u32[]{:S(2)}, u32[]{:S(2)}) collective-permute-start(f32[1,2,32,32]{3,2,1,0:T(8,128)S(1)} %add_add_fusion.refs_0_), channel_id=1, source_target_pairs={{0,1},{1,0},{2,3},{3,2},{4,5},{5,4},{6,7},{7,6},{8,9},{9,8},{10,11... | collective-permute-start | bytes 24584 | tf_op jit(solution)/shard_map/gradient_exchange/ppermute | solution.py:351
  40.2 0.9 %collective-permute-done.8.refs_1_ = f32[1,2,32,32]{3,2,1,0:T(8,128)S(1)} collective-permute-done((f32[1,2,32,32]{3,2,1,0:T(8,128)S(1)}, f32[1,2,32,32]{3,2,1,0:T(8,128)S(1)}, u32[]{:S(2)}, u32[]{:S(2)}) %collective-permute-start.8) | collective-permute-done | bytes 8224 | tf_op jit(solution)/shard_map/gradient_exchange/ppermute | solution.py:351
  41.1 0.6 %copy-done.11 = f32[1,2,32,32]{3,2,1,0:T(8,128)} copy-done((f32[1,2,32,32]{3,2,1,0:T(8,128)}, f32[1,2,32,32]{3,2,1,0:T(8,128)S(1)}, u32[]{:S(2)}) %copy-start.11) | copy-done | bytes 8216
  41.7 2.3 %pixel_gradients.1 = f32[1,256,256]{2,1,0:T(8,128)} custom-call(f32[1,2,32,32]{3,2,1,0:T(8,128)} %copy-done.10, f32[1,2,32,32]{3,2,1,0:T(8,128)} %copy-done.11, f32[32,256]{1,0:T(8,128)} %constant.67.clone.c_re_ref.refs_2_, f32[32,256]{1,0:T(8,128)} %constant.68.clone.c_im_ref.refs_3_, bf16[256,384]{1,0:T(8,128)(2,1)} %constant.80.clone.left_ref.refs_4_), custom_call_target="tpu_custom_call" | custom-call | tf_op jit(solution)/shard_map/pixel_gradients/pallas_call | solution.py:308
  (41 shorter events, 0.8 us)
Async XLA Ops:
  0.6 0.9 %copy-start = (bf16[1,256,256]{2,1,0:T(8,128)(2,1)S(1)}, bf16[1,256,256]{2,1,0:T(8,128)(2,1)}, u32[]{:S(2)}) copy-start(bf16[1,256,256]{2,1,0:T(8,128)(2,1)} %param.30) | copy-start | bytes 393220
  0.6 0.9 %copy-start.2 = (f32[32,256]{1,0:T(8,128)S(1)}, f32[32,256]{1,0:T(8,128)}, u32[]{:S(2)}) copy-start(f32[32,256]{1,0:T(8,128)} %constant.67.clone.c_re_ref.refs_2_) | copy-start | bytes 98308
  0.7 1.1 %copy-start.3 = (f32[32,256]{1,0:T(8,128)S(1)}, f32[32,256]{1,0:T(8,128)}, u32[]{:S(2)}) copy-start(f32[32,256]{1,0:T(8,128)} %constant.68.clone.c_im_ref.refs_3_) | copy-start | bytes 98308
  0.7 7.4 %copy-start.1 = (f32[1,12,2,32,32]{4,3,2,1,0:T(8,128)S(1)}, f32[1,12,2,32,32]{4,3,2,1,0:T(8,128)}, u32[]{:S(2)}) copy-start(f32[1,12,2,32,32]{4,3,2,1,0:T(8,128)} %param.34) | copy-start | bytes 294916
  2.6 5.6 %copy-start.8 = (f32[1,2,32,32]{3,2,1,0:T(8,128)}, f32[1,2,32,32]{3,2,1,0:T(8,128)S(1)}, u32[]{:S(2)}) copy-start(f32[1,2,32,32]{3,2,1,0:T(8,128)S(1)} %pad_maximum_fusion.1.own_ref) | copy-start | bytes 24580
  2.7 7.5 %collective-permute-start = (f32[1,2,32,32]{3,2,1,0:T(8,128)S(1)}, f32[1,2,32,32]{3,2,1,0:T(8,128)S(1)}, u32[]{:S(2)}, u32[]{:S(2)}) collective-permute-start(f32[1,2,32,32]{3,2,1,0:T(8,128)S(1)} %pad_maximum_fusion.1.own_ref), channel_id=1, source_target_pairs={{8,0},{12,4},{0,8},{4,12},{5,1},{1,5},{13,9},{9,13},{10,2},{14,6},... | collective-permute-start | bytes 24584 | tf_op jit(solution)/shard_map/master_spectra/ppermute | solution.py:391
  6.8 3.4 %collective-permute-start.1 = (f32[1,2,32,32]{3,2,1,0:T(8,128)S(1)}, f32[1,2,32,32]{3,2,1,0:T(8,128)S(1)}, u32[]{:S(2)}, u32[]{:S(2)}) collective-permute-start(f32[1,2,32,32]{3,2,1,0:T(8,128)S(1)} %pad_maximum_fusion.1.own_ref), channel_id=1, source_target_pairs={{13,1},{9,5},{5,9},{1,13},{15,3},{11,7},{7,11},{3,15},{29,17},{25,... | collective-permute-start | bytes 24584 | tf_op jit(solution)/shard_map/master_spectra/ppermute | solution.py:391
  7.4 0.7 %copy-start.13 = (f32[1,12]{1,0:T(1,128)S(1)}, f32[1,12]{1,0:T(1,128)}, u32[]{:S(2)}) copy-start(f32[1,12]{1,0:T(1,128)} %param.35) | copy-start | bytes 148
  8.5 0.7 %copy-start.12 = (s32[2]{0:T(128)S(1)}, s32[2]{0:T(128)}, u32[]{:S(2)}) copy-start(s32[2]{0:T(128)} %im_ref.1) | copy-start | bytes 28
  10.3 3.3 %copy-start.4 = (f32[4,2,32,32]{3,2,1,0:T(8,128)}, f32[4,2,32,32]{3,2,1,0:T(8,128)S(1)}, u32[]{:S(2)}) copy-start(f32[4,2,32,32]{3,2,1,0:T(8,128)S(1)} %select_add_fusion.ev_ref) | copy-start | bytes 98308
  10.3 3.3 %collective-permute-start.2 = (f32[4,2,32,32]{3,2,1,0:T(8,128)S(1)}, f32[4,2,32,32]{3,2,1,0:T(8,128)S(1)}, u32[]{:S(2)}, u32[]{:S(2)}) collective-permute-start(f32[4,2,32,32]{3,2,1,0:T(8,128)S(1)} %select_add_fusion.ev_ref), channel_id=1, source_target_pairs={{0,1},{1,0},{2,3},{3,2},{4,5},{5,4},{6,7},{7,6},{8,9},{9,8},{10,11... | collective-permute-start | bytes 98312 | tf_op jit(solution)/shard_map/master_spectra/ppermute | solution.py:351
  13.6 0.6 %copy-start.9 = (f32[4,2,32,32]{3,2,1,0:T(8,128)}, f32[4,2,32,32]{3,2,1,0:T(8,128)S(1)}, u32[]{:S(2)}) copy-start(f32[4,2,32,32]{3,2,1,0:T(8,128)S(1)} %collective-permute-done.2.ev2_ref) | copy-start | bytes 98308
  26.2 4.5 %collective-permute-start.4 = (f32[1,4,32,32]{3,2,1,0:T(8,128)}, f32[1,4,32,32]{3,2,1,0:T(8,128)S(1)}, u32[]{:S(2)}, u32[]{:S(2)}) collective-permute-start(f32[1,4,32,32]{3,2,1,0:T(8,128)} %bitcast.61), channel_id=1, source_target_pairs={{0,2},{1,3},{2,0},{3,1},{4,6},{5,7},{6,4},{7,5},{8,10},{9,11},{10,... | collective-permute-start | bytes 49160 | tf_op jit(solution)/shard_map/gradient_exchange/ppermute | solution.py:470
  27.7 3.7 %collective-permute-start.3 = (f32[1,4,32,32]{3,2,1,0:T(8,128)}, f32[1,4,32,32]{3,2,1,0:T(8,128)S(1)}, u32[]{:S(2)}, u32[]{:S(2)}) collective-permute-start(f32[1,4,32,32]{3,2,1,0:T(8,128)} %bitcast.62), channel_id=1, source_target_pairs={{0,1},{1,0},{2,3},{3,2},{4,5},{5,4},{6,7},{7,6},{8,9},{9,8},{10,11... | collective-permute-start | bytes 49160 | tf_op jit(solution)/shard_map/gradient_exchange/ppermute | solution.py:470
  27.7 4.1 %collective-permute-start.5 = (f32[1,4,32,32]{3,2,1,0:T(8,128)}, f32[1,4,32,32]{3,2,1,0:T(8,128)S(1)}, u32[]{:S(2)}, u32[]{:S(2)}) collective-permute-start(f32[1,4,32,32]{3,2,1,0:T(8,128)} %bitcast.63), channel_id=1, source_target_pairs={{0,3},{1,2},{2,1},{3,0},{4,7},{5,6},{6,5},{7,4},{8,11},{9,10},{10,... | collective-permute-start | bytes 49160 | tf_op jit(solution)/shard_map/gradient_exchange/ppermute | solution.py:470
  30.6 1.1 %copy-start.5 = (f32[1,4,32,32]{3,2,1,0:T(8,128)}, f32[1,4,32,32]{3,2,1,0:T(8,128)S(1)}, u32[]{:S(2)}) copy-start(f32[1,4,32,32]{3,2,1,0:T(8,128)S(1)} %collective-permute-done.4.g1_ref) | copy-start | bytes 49156
  31.4 0.6 %copy-start.6 = (f32[1,4,32,32]{3,2,1,0:T(8,128)}, f32[1,4,32,32]{3,2,1,0:T(8,128)S(1)}, u32[]{:S(2)}) copy-start(f32[1,4,32,32]{3,2,1,0:T(8,128)S(1)} %collective-permute-done.3.g0_ref) | copy-start | bytes 49156
  31.8 0.6 %copy-start.7 = (f32[1,4,32,32]{3,2,1,0:T(8,128)}, f32[1,4,32,32]{3,2,1,0:T(8,128)S(1)}, u32[]{:S(2)}) copy-start(f32[1,4,32,32]{3,2,1,0:T(8,128)S(1)} %collective-permute-done.5.g2_ref) | copy-start | bytes 49156
  32.4 5.2 %collective-permute-start.6 = (f32[1,2,32,32]{3,2,1,0:T(8,128)S(1)}, f32[1,2,32,32]{3,2,1,0:T(8,128)S(1)}, u32[]{:S(2)}, u32[]{:S(2)}) collective-permute-start(f32[1,2,32,32]{3,2,1,0:T(8,128)S(1)} %get-tuple-element.8), channel_id=1, source_target_pairs={{0,8},{4,12},{8,0},{12,4},{1,5},{5,1},{9,13},{13,9},{2,10},{6,14},... | collective-permute-start | bytes 24584 | tf_op jit(solution)/shard_map/gradient_exchange/ppermute | solution.py:410
  32.8 4.8 %collective-permute-start.7 = (f32[1,2,32,32]{3,2,1,0:T(8,128)S(1)}, f32[1,2,32,32]{3,2,1,0:T(8,128)S(1)}, u32[]{:S(2)}, u32[]{:S(2)}) collective-permute-start(f32[1,2,32,32]{3,2,1,0:T(8,128)S(1)} %get-tuple-element.9), channel_id=1, source_target_pairs={{1,13},{5,9},{9,5},{13,1},{3,15},{7,11},{11,7},{15,3},{17,29},{21,... | collective-permute-start | bytes 24584 | tf_op jit(solution)/shard_map/gradient_exchange/ppermute | solution.py:410
  37.6 3.5 %copy-start.10 = (f32[1,2,32,32]{3,2,1,0:T(8,128)}, f32[1,2,32,32]{3,2,1,0:T(8,128)S(1)}, u32[]{:S(2)}) copy-start(f32[1,2,32,32]{3,2,1,0:T(8,128)S(1)} %add_add_fusion.refs_0_) | copy-start | bytes 24580
  37.6 3.5 %collective-permute-start.8 = (f32[1,2,32,32]{3,2,1,0:T(8,128)S(1)}, f32[1,2,32,32]{3,2,1,0:T(8,128)S(1)}, u32[]{:S(2)}, u32[]{:S(2)}) collective-permute-start(f32[1,2,32,32]{3,2,1,0:T(8,128)S(1)} %add_add_fusion.refs_0_), channel_id=1, source_target_pairs={{0,1},{1,0},{2,3},{3,2},{4,5},{5,4},{6,7},{7,6},{8,9},{9,8},{10,11... | collective-permute-start | bytes 24584 | tf_op jit(solution)/shard_map/gradient_exchange/ppermute | solution.py:351
  41.1 0.6 %copy-start.11 = (f32[1,2,32,32]{3,2,1,0:T(8,128)}, f32[1,2,32,32]{3,2,1,0:T(8,128)S(1)}, u32[]{:S(2)}) copy-start(f32[1,2,32,32]{3,2,1,0:T(8,128)S(1)} %collective-permute-done.8.refs_1_) | copy-start | bytes 24580
